TPU v7x, 32 devices: a whole 2x2x4 slice. The times are simulated.
32 devices in a mesh: sub: 8 (over z, x), grp: 4 (over y, core).
Axes of the slice: x: 2, y: 2, z: 4, core: 2. Of those that a mesh axis runs over, the one named last changes fastest.
Arguments:
- resid: float32 [32768, 256], P(('sub', 'grp')), may hold values from -6 to 6
- schur_inv: bfloat16 [65536, 2048], P(('sub', 'grp')), may hold values from -0.125 to 0.125
- basis: bfloat16 [512, 2048], P(('sub', 'grp')), may hold values from -1.5 to 1.5
- scaling: float32 [65536], P(('sub', 'grp')), may hold values from 0.25 to 1
- coarse_inv: bfloat16 [512, 512], P(('sub', 'grp')), may hold values from -0.5 to 0.5
- source_row: int32 [65536], P(('sub', 'grp')), may hold values from 0 to 3071, as said below
- primal_idx: int32 [512], P(('sub', 'grp')), may hold values from 0 to 2047, as said below
Outputs:
- first_apply: float32 [32768, 256], P(('sub', 'grp'))
- second_apply: float32 [32768, 256], P(('sub', 'grp'))
Inputs may be any that keep to these rules, and one draw needn't show every extreme that they name: `source_row`: within one subdomain the entries are distinct; the first subdomain of each chain has none below 1024, the last none at or above 2048. `primal_idx`: within one subdomain the entries are distinct.
All inputs are finite; a program needn't handle non-finite values.
Results may differ from a plain program's by a relative error of at most 0.0076.
Values may be sent and summed in bfloat16 or wider, within the bound.
No kernel may reach another device: no remote copies, remote signals or barrier semaphores. Data moves between devices by JAX's collectives and lax.ppermute only.
A program may use at most 64 MiB of HBM per device.

v0:
```python
import jax
import jax.numpy as jnp
from jax import lax
from jax.sharding import PartitionSpec as P


def with_halo(cells, sides, width):
    for axis, dim in sides:
        count = lax.axis_size(axis)
        ends = count - 1
        head = lax.slice_in_dim(cells, 0, width, axis=dim)
        tail = lax.slice_in_dim(cells, cells.shape[dim] - width, cells.shape[dim], axis=dim)
        cells = jnp.concatenate(
            [
                lax.ppermute(tail, axis, [(i, (i + 1) % count) for i in range(ends)]),
                cells,
                lax.ppermute(head, axis, [((i + 1) % count, i) for i in range(ends)]),
            ],
            axis=dim,
        )
    return cells


def shifted(shard, axis, by):
    devices = lax.axis_size(axis)
    pairs = [(i, i + by) for i in range(devices) if 0 <= i + by < devices]
    return lax.ppermute(shard, axis, pairs)


def shards(resid, schur_inv, basis, scaling, coarse_inv, source_row, primal_idx):
    own_count = resid.shape[0]
    scale_column = scaling[:, None]

    def add_all(portion):
        return jnp.dot(coarse_inv, portion, preferred_element_type=jnp.float32)

    def precondition(vector_in):
        rounded = vector_in.astype(jnp.bfloat16)
        padded = with_halo(rounded, (("sub", 0),), own_count)
        gathered = padded[source_row]
        scaled = (scale_column * gathered.astype(jnp.float32)).astype(jnp.bfloat16)
        primal = scaled[primal_idx]
        coarse = add_all(lax.all_gather(primal, ("sub", "grp"), axis=0, tiled=True))
        coarse_rounded = coarse.astype(jnp.bfloat16)
        solved = jnp.dot(schur_inv, scaled, preferred_element_type=jnp.float32)
        solved = solved + lax.dot_general(
            basis, coarse_rounded, (((0,), (0,)), ((), ())), preferred_element_type=jnp.float32
        )
        weighted = (scale_column * solved).astype(jnp.bfloat16)
        spread = (
            jnp.zeros((3 * own_count, weighted.shape[1]), jnp.bfloat16).at[source_row].set(weighted)
        )
        from_next = shifted(spread[:own_count], "sub", -1)
        from_previous = shifted(spread[2 * own_count :], "sub", 1)
        return (
            spread[own_count : 2 * own_count].astype(jnp.float32)
            + from_next.astype(jnp.float32)
            + from_previous.astype(jnp.float32)
        )

    first_apply = precondition(resid)
    second_apply = precondition(first_apply)
    return (first_apply, second_apply)


def solution(mesh):
    return jax.shard_map(
        shards,
        mesh=mesh,
        in_specs=(
            P(("sub", "grp"), None),
            P(("sub", "grp"), None),
            P(("sub", "grp"), None),
            P(("sub", "grp")),
            P(("sub", "grp"), None),
            P(("sub", "grp")),
            P(("sub", "grp")),
        ),
        out_specs=(P(("sub", "grp"), None), P(("sub", "grp"), None)),
        check_vma=False,
    )
```

profile of v0, /device:TPU:0, one launch (start us, length us, event | category | flops | bytes accessed | tf_op | source)
XLA Modules:
  0.0 236.3 jit_solution(8052517843796168222)
XLA Ops:
  0.6 1.3 convert_element_type.56
  2.0 1.3 collective-permute-start.1
  3.3 5.5 %collective-permute-start = (bf16[1024,256]{1,0:T(8,128)(2,1)S(1)}, bf16[1024,256]{1,0:T(8,128)(2,1)S(1)}, u32[]{:S(2)}, u32[]{:S(2)}) collective-permute-start(bf16[1024,256]{1,0:T(8,128)(2,1)S(1)} %convert_element_type.56), channel_id=1, source_target_pairs={{0,4},{4,8},{8,12},{12,16},{16,20},{20,24},{24,28},{1,5},{5,9},{9,... | collective-permute-start | bytes 1572872 | tf_op jit(solution)/shard_map/ppermute | solution.py:15
  8.8 0.7 compare_select_fusion.1
  9.4 0.7 broadcast_clamp_fusion
  10.1 8.6 %collective-permute-done.1 = bf16[1024,256]{1,0:T(8,128)(2,1)S(1)} collective-permute-done((bf16[1024,256]{1,0:T(8,128)(2,1)S(1)}, bf16[1024,256]{1,0:T(8,128)(2,1)S(1)}, u32[]{:S(2)}, u32[]{:S(2)}) %collective-permute-start.1) | collective-permute-done | bytes 524320 | tf_op jit(solution)/shard_map/ppermute | solution.py:17
  18.7 11.4 %collective-permute-done = bf16[1024,256]{1,0:T(8,128)(2,1)S(1)} collective-permute-done((bf16[1024,256]{1,0:T(8,128)(2,1)S(1)}, bf16[1024,256]{1,0:T(8,128)(2,1)S(1)}, u32[]{:S(2)}, u32[]{:S(2)}) %collective-permute-start) | collective-permute-done | bytes 524320 | tf_op jit(solution)/shard_map/ppermute | solution.py:15
  30.2 7.5 %gather_fusion = bf16[2048,256]{1,0:T(8,128)(2,1)S(1)} fusion(bf16[3072,256]{1,0:T(8,128)(2,1)S(1)} %pad_maximum_fusion, s32[2048]{0:T(1024)S(1)} %get-tuple-element.8), kind=kCustom, calls=%fused_computation | custom fusion | bytes 2105344 | tf_op jit(solution)/shard_map/gather | solution.py:40
  38.7 40.7 %all-gather = bf16[512,256]{1,0:T(8,128)(2,1)S(1)} all-gather(bf16[16,256]{1,0:T(8,128)(2,1)S(1)} %gather_fusion.1), channel_id=2, replica_groups=mesh['sub'=8,'grp'=4] {'sub','grp'}, dimensions={0}, use_global_device_ids=true | all-gather | bytes 270336 | tf_op jit(solution)/shard_map/all_gather | solution.py:43
  79.4 5.8 %fusion.13 = f32[256,2048]{1,0:T(8,128)S(1)} fusion(bf16[2048,256]{1,0:T(8,128)(2,1)S(1)} %multiply_convert_fusion.1, bf16[2048,2048]{1,0:T(8,128)(2,1)} %param.8), kind=kOutput, calls=%fused_computation.33 | convolution fusion | flops 2147483648 | bytes 11534336 | tf_op jit(solution)/shard_map/dot_general | solution.py:45
  85.2 0.7 fusion.5
  86.5 9.8 %scatter_custom_fusion = bf16[3072,256]{1,0:T(8,128)(2,1)S(1)} fusion(s32[2048]{0:T(1024)S(1)} %get-tuple-element.9, bf16[2048,256]{1,0:T(8,128)(2,1)S(1)} %copy.9, bf16[]{:T(256)} %constant.4.clone.1), kind=kCustom, calls=%fused_computation.24 | custom fusion | bytes 1572866 | tf_op jit(solution)/shard_map/scatter | solution.py:51
  96.4 1.3 collective-permute-start.2
  97.7 4.6 %collective-permute-start.3 = (bf16[1024,256]{1,0:T(8,128)(2,1)S(1)}, bf16[1024,256]{1,0:T(8,128)(2,1)S(1)}, u32[]{:S(2)}, u32[]{:S(2)}) collective-permute-start(bf16[1024,256]{1,0:T(8,128)(2,1)S(1)} %get-tuple-element.7), channel_id=1, source_target_pairs={{0,4},{4,8},{8,12},{12,16},{16,20},{20,24},{24,28},{1,5},{5,9},{9,... | collective-permute-start | bytes 1572872 | tf_op jit(solution)/shard_map/ppermute | solution.py:27
  102.2 10.2 %collective-permute-done.2 = bf16[1024,256]{1,0:T(8,128)(2,1)S(1)} collective-permute-done((bf16[1024,256]{1,0:T(8,128)(2,1)S(1)}, bf16[1024,256]{1,0:T(8,128)(2,1)S(1)}, u32[]{:S(2)}, u32[]{:S(2)}) %collective-permute-start.2) | collective-permute-done | bytes 524320 | tf_op jit(solution)/shard_map/ppermute | solution.py:27
  112.4 7.4 %collective-permute-done.3 = bf16[1024,256]{1,0:T(8,128)(2,1)S(1)} collective-permute-done((bf16[1024,256]{1,0:T(8,128)(2,1)S(1)}, bf16[1024,256]{1,0:T(8,128)(2,1)S(1)}, u32[]{:S(2)}, u32[]{:S(2)}) %collective-permute-start.3) | collective-permute-done | bytes 524320 | tf_op jit(solution)/shard_map/ppermute | solution.py:27
  119.9 1.2 fusion.10
  121.0 1.3 collective-permute-start.5
  122.3 5.0 %collective-permute-start.4 = (bf16[1024,256]{1,0:T(8,128)(2,1)S(1)}, bf16[1024,256]{1,0:T(8,128)(2,1)S(1)}, u32[]{:S(2)}, u32[]{:S(2)}) collective-permute-start(bf16[1024,256]{1,0:T(8,128)(2,1)S(1)} %get-tuple-element.2), channel_id=1, source_target_pairs={{0,4},{4,8},{8,12},{12,16},{16,20},{20,24},{24,28},{1,5},{5,9},{9,... | collective-permute-start | bytes 1572872 | tf_op jit(solution)/shard_map/ppermute | solution.py:15
  127.4 10.1 %collective-permute-done.5 = bf16[1024,256]{1,0:T(8,128)(2,1)S(1)} collective-permute-done((bf16[1024,256]{1,0:T(8,128)(2,1)S(1)}, bf16[1024,256]{1,0:T(8,128)(2,1)S(1)}, u32[]{:S(2)}, u32[]{:S(2)}) %collective-permute-start.5) | collective-permute-done | bytes 524320 | tf_op jit(solution)/shard_map/ppermute | solution.py:17
  137.5 11.4 %collective-permute-done.4 = bf16[1024,256]{1,0:T(8,128)(2,1)S(1)} collective-permute-done((bf16[1024,256]{1,0:T(8,128)(2,1)S(1)}, bf16[1024,256]{1,0:T(8,128)(2,1)S(1)}, u32[]{:S(2)}, u32[]{:S(2)}) %collective-permute-start.4) | collective-permute-done | bytes 524320 | tf_op jit(solution)/shard_map/ppermute | solution.py:15
  149.0 7.5 %gather_fusion.2 = bf16[2048,256]{1,0:T(8,128)(2,1)S(1)} fusion(bf16[3072,256]{1,0:T(8,128)(2,1)S(1)} %pad_maximum_fusion.1, s32[2048]{0:T(1024)S(1)} %get-tuple-element.8), kind=kCustom, calls=%fused_computation.2 | custom fusion | bytes 2105344 | tf_op jit(solution)/shard_map/gather | solution.py:40
  156.8 0.6 gather_fusion.3
  157.4 5.8 %fusion.14 = f32[256,2048]{1,0:T(8,128)S(1)} fusion(bf16[2048,256]{1,0:T(8,128)(2,1)S(1)} %multiply_convert_fusion, bf16[2048,2048]{1,0:T(8,128)(2,1)} %param.8), kind=kOutput, calls=%fused_computation.34 | convolution fusion | flops 2147483648 | bytes 11534336 | tf_op jit(solution)/shard_map/dot_general | solution.py:45
  163.2 37.2 %all-gather.1 = bf16[512,256]{1,0:T(8,128)(2,1)S(1)} all-gather(bf16[16,256]{1,0:T(8,128)(2,1)S(1)} %gather_fusion.3), channel_id=3, replica_groups=mesh['sub'=8,'grp'=4] {'sub','grp'}, dimensions={0}, use_global_device_ids=true | all-gather | bytes 270336 | tf_op jit(solution)/shard_map/all_gather | solution.py:43
  200.4 0.7 fusion.4
  201.7 9.8 %scatter_custom_fusion.1 = bf16[3072,256]{1,0:T(8,128)(2,1)S(1)} fusion(s32[2048]{0:T(1024)S(1)} %get-tuple-element.9, bf16[2048,256]{1,0:T(8,128)(2,1)S(1)} %copy.10, bf16[]{:T(256)} %constant.4.clone.1), kind=kCustom, calls=%fused_computation.22 | custom fusion | bytes 1572866 | tf_op jit(solution)/shard_map/scatter | solution.py:51
  211.6 1.3 collective-permute-start.6
  212.9 4.6 %collective-permute-start.7 = (bf16[1024,256]{1,0:T(8,128)(2,1)S(1)}, bf16[1024,256]{1,0:T(8,128)(2,1)S(1)}, u32[]{:S(2)}, u32[]{:S(2)}) collective-permute-start(bf16[1024,256]{1,0:T(8,128)(2,1)S(1)} %get-tuple-element.5), channel_id=1, source_target_pairs={{0,4},{4,8},{8,12},{12,16},{16,20},{20,24},{24,28},{1,5},{5,9},{9,... | collective-permute-start | bytes 1572872 | tf_op jit(solution)/shard_map/ppermute | solution.py:27
  217.4 10.2 %collective-permute-done.6 = bf16[1024,256]{1,0:T(8,128)(2,1)S(1)} collective-permute-done((bf16[1024,256]{1,0:T(8,128)(2,1)S(1)}, bf16[1024,256]{1,0:T(8,128)(2,1)S(1)}, u32[]{:S(2)}, u32[]{:S(2)}) %collective-permute-start.6) | collective-permute-done | bytes 524320 | tf_op jit(solution)/shard_map/ppermute | solution.py:27
  227.6 7.5 %collective-permute-done.7 = bf16[1024,256]{1,0:T(8,128)(2,1)S(1)} collective-permute-done((bf16[1024,256]{1,0:T(8,128)(2,1)S(1)}, bf16[1024,256]{1,0:T(8,128)(2,1)S(1)}, u32[]{:S(2)}, u32[]{:S(2)}) %collective-permute-start.7) | collective-permute-done | bytes 524320 | tf_op jit(solution)/shard_map/ppermute | solution.py:27
  235.1 1.1 convert_add_fusion
  (16 shorter events, 2.7 us)
Async XLA Ops:
  0.6 84.6 %copy-start = (bf16[16,2048]{1,0:T(8,128)(2,1)S(1)}, bf16[16,2048]{1,0:T(8,128)(2,1)}, u32[]{:S(2)}) copy-start(bf16[16,2048]{1,0:T(8,128)(2,1)} %param.9) | copy-start | bytes 196612
  2.0 16.8 %collective-permute-start.1 = (bf16[1024,256]{1,0:T(8,128)(2,1)S(1)}, bf16[1024,256]{1,0:T(8,128)(2,1)S(1)}, u32[]{:S(2)}, u32[]{:S(2)}) collective-permute-start(bf16[1024,256]{1,0:T(8,128)(2,1)S(1)} %convert_element_type.56), channel_id=1, source_target_pairs={{4,0},{8,4},{12,8},{16,12},{20,16},{24,20},{28,24},{5,1},{9,5},{13... | collective-permute-start | bytes 1572872 | tf_op jit(solution)/shard_map/ppermute | solution.py:17
  3.3 26.8 %collective-permute-start = (bf16[1024,256]{1,0:T(8,128)(2,1)S(1)}, bf16[1024,256]{1,0:T(8,128)(2,1)S(1)}, u32[]{:S(2)}, u32[]{:S(2)}) collective-permute-start(bf16[1024,256]{1,0:T(8,128)(2,1)S(1)} %convert_element_type.56), channel_id=1, source_target_pairs={{0,4},{4,8},{8,12},{12,16},{16,20},{20,24},{24,28},{1,5},{5,9},{9,... | collective-permute-start | bytes 1572872 | tf_op jit(solution)/shard_map/ppermute | solution.py:15
  30.2 7.5 %copy-start.1 = (f32[2048]{0:T(1024)S(1)}, f32[2048]{0:T(1024)}, u32[]{:S(2)}) copy-start(f32[2048]{0:T(1024)} %param.10) | copy-start | bytes 24580
  79.4 5.8 %copy-start.2 = (bf16[16,512]{1,0:T(8,128)(2,1)S(1)}, bf16[16,512]{1,0:T(8,128)(2,1)}, u32[]{:S(2)}) copy-start(bf16[16,512]{1,0:T(8,128)(2,1)} %param.11) | copy-start | bytes 49156
  96.4 16.1 %collective-permute-start.2 = (bf16[1024,256]{1,0:T(8,128)(2,1)S(1)}, bf16[1024,256]{1,0:T(8,128)(2,1)S(1)}, u32[]{:S(2)}, u32[]{:S(2)}) collective-permute-start(bf16[1024,256]{1,0:T(8,128)(2,1)S(1)} %get-tuple-element.6), channel_id=1, source_target_pairs={{4,0},{8,4},{12,8},{16,12},{20,16},{24,20},{28,24},{5,1},{9,5},{13... | collective-permute-start | bytes 1572872 | tf_op jit(solution)/shard_map/ppermute | solution.py:27
  97.7 22.2 %collective-permute-start.3 = (bf16[1024,256]{1,0:T(8,128)(2,1)S(1)}, bf16[1024,256]{1,0:T(8,128)(2,1)S(1)}, u32[]{:S(2)}, u32[]{:S(2)}) collective-permute-start(bf16[1024,256]{1,0:T(8,128)(2,1)S(1)} %get-tuple-element.7), channel_id=1, source_target_pairs={{0,4},{4,8},{8,12},{12,16},{16,20},{20,24},{24,28},{1,5},{5,9},{9,... | collective-permute-start | bytes 1572872 | tf_op jit(solution)/shard_map/ppermute | solution.py:27
  121.0 16.5 %collective-permute-start.5 = (bf16[1024,256]{1,0:T(8,128)(2,1)S(1)}, bf16[1024,256]{1,0:T(8,128)(2,1)S(1)}, u32[]{:S(2)}, u32[]{:S(2)}) collective-permute-start(bf16[1024,256]{1,0:T(8,128)(2,1)S(1)} %get-tuple-element.2), channel_id=1, source_target_pairs={{4,0},{8,4},{12,8},{16,12},{20,16},{24,20},{28,24},{5,1},{9,5},{13... | collective-permute-start | bytes 1572872 | tf_op jit(solution)/shard_map/ppermute | solution.py:17
  122.3 26.6 %collective-permute-start.4 = (bf16[1024,256]{1,0:T(8,128)(2,1)S(1)}, bf16[1024,256]{1,0:T(8,128)(2,1)S(1)}, u32[]{:S(2)}, u32[]{:S(2)}) collective-permute-start(bf16[1024,256]{1,0:T(8,128)(2,1)S(1)} %get-tuple-element.2), channel_id=1, source_target_pairs={{0,4},{4,8},{8,12},{12,16},{16,20},{20,24},{24,28},{1,5},{5,9},{9,... | collective-permute-start | bytes 1572872 | tf_op jit(solution)/shard_map/ppermute | solution.py:15
  211.6 16.1 %collective-permute-start.6 = (bf16[1024,256]{1,0:T(8,128)(2,1)S(1)}, bf16[1024,256]{1,0:T(8,128)(2,1)S(1)}, u32[]{:S(2)}, u32[]{:S(2)}) collective-permute-start(bf16[1024,256]{1,0:T(8,128)(2,1)S(1)} %get-tuple-element.4), channel_id=1, source_target_pairs={{4,0},{8,4},{12,8},{16,12},{20,16},{24,20},{28,24},{5,1},{9,5},{13... | collective-permute-start | bytes 1572872 | tf_op jit(solution)/shard_map/ppermute | solution.py:27
  212.9 22.3 %collective-permute-start.7 = (bf16[1024,256]{1,0:T(8,128)(2,1)S(1)}, bf16[1024,256]{1,0:T(8,128)(2,1)S(1)}, u32[]{:S(2)}, u32[]{:S(2)}) collective-permute-start(bf16[1024,256]{1,0:T(8,128)(2,1)S(1)} %get-tuple-element.5), channel_id=1, source_target_pairs={{0,4},{4,8},{8,12},{12,16},{16,20},{20,24},{24,28},{1,5},{5,9},{9,... | collective-permute-start | bytes 1572872 | tf_op jit(solution)/shard_map/ppermute | solution.py:27
where the time goes:
time: 237 us; the launch traced here: 236 us
  blocking collectives  78 us (33%)
  waiting for transfers between devices  76.8 us (32%)
  local copies, waits for them, and re-layouts  36.9 us (16%)
  starting transfers between devices  24.9 us (11%)
  matrix products  13 us (5%)
  other arithmetic  5.85 us (2%)
    all_gather x2, blocking collectives, precondition(): coarse = add_all(lax.all_gather(primal, ('sub', 'grp'), axis=0, tiled=True))  78 us
    ppermute x4, waiting for transfers between devices, shifted(): return lax.ppermute(shard, axis, pairs)  35.3 us
    ppermute x2, waiting for transfers between devices, with_halo(): lax.ppermute(tail, axis, [(i, (i + 1) % count) for i in range(ends)])  22.8 us
    scatter x2, local copies, waits for them, and re-layouts, precondition(): jnp.zeros((3 * own_count, weighted.shape[1]), jnp.bfloat16).at[source_row]  19.6 us
    ppermute x2, waiting for transfers between devices, with_halo(): lax.ppermute(head, axis, [((i + 1) % count, i) for i in range(ends)])  18.7 us
    gather x2, local copies, waits for them, and re-layouts, precondition(): gathered = padded[source_row]  15 us
    ppermute x4, starting transfers between devices, shifted(): return lax.ppermute(shard, axis, pairs)  11.7 us
    dot_general x2, matrix products, precondition(): solved = jnp.dot(schur_inv, scaled, preferred_element_type=jnp.float32)  11.5 us
  transfers between devices with their start and end apart: 8, of which 8 were waited for; matrix products, arithmetic and copies ran while one was open for 1% of the time, Pallas kernels for 0%

commit v1 on v0

--- a/solution.py
+++ b/solution.py
@@ -40,7 +40,10 @@
         gathered = padded[source_row]
         scaled = (scale_column * gathered.astype(jnp.float32)).astype(jnp.bfloat16)
         primal = scaled[primal_idx]
-        coarse = add_all(lax.all_gather(primal, ("sub", "grp"), axis=0, tiled=True))
+        idx = lax.axis_index("sub") * lax.axis_size("grp") + lax.axis_index("grp")
+        total = lax.axis_size("sub") * lax.axis_size("grp") * primal.shape[0]
+        buf = lax.dynamic_update_slice(jnp.zeros((total, primal.shape[1]), primal.dtype), primal, (idx * primal.shape[0], 0))
+        coarse = add_all(lax.psum(buf, ("sub", "grp")))
         coarse_rounded = coarse.astype(jnp.bfloat16)
         solved = jnp.dot(schur_inv, scaled, preferred_element_type=jnp.float32)
         solved = solved + lax.dot_general(

time: 237 us -> 419 us (1.77)
  waiting for transfers between devices: 76.8 us -> 320 us
  blocking collectives: 78 us -> 0 us
  between operations: 0.86 us -> 14.3 us
    psum x0 -> x2, waiting for transfers between devices: none -> 239 us  [precondition(): coarse = add_all(lax.psum(buf, ('sub', 'grp')))]
    all_gather x2 -> x0, blocking collectives: 78 us -> none  [precondition(): coarse = add_all(lax.all_gather(primal, ('sub', 'grp'), axis=0, tiled=True))]
    ppermute x4, waiting for transfers between devices: 35.3 us -> 40 us  [shifted(): return lax.ppermute(shard, axis, pairs)]
  transfers between devices with their start and end apart: 8 -> 10, of which waited for: 8 -> 10; matrix products, arithmetic and copies ran while one was open for 1% -> 3% of each run, Pallas kernels for 0% -> 0%
where the time goes in v1:
time: 419 us; the launch traced here: 418 us
  waiting for transfers between devices  320 us (76%)
  local copies, waits for them, and re-layouts  38.4 us (9%)
  starting transfers between devices  25.1 us (6%)
  matrix products  14.9 us (4%)
  between operations  14.3 us (3%)
  other arithmetic  5.82 us (1%)
    psum x2, waiting for transfers between devices, precondition(): coarse = add_all(lax.psum(buf, ('sub', 'grp')))  239 us
    ppermute x4, waiting for transfers between devices, shifted(): return lax.ppermute(shard, axis, pairs)  40 us
    ppermute x2, waiting for transfers between devices, with_halo(): lax.ppermute(tail, axis, [(i, (i + 1) % count) for i in range(ends)])  22.8 us
    scatter x2, local copies, waits for them, and re-layouts, precondition(): jnp.zeros((3 * own_count, weighted.shape[1]), jnp.bfloat16).at[source_row]  19.6 us
    ppermute x2, waiting for transfers between devices, with_halo(): lax.ppermute(head, axis, [((i + 1) % count, i) for i in range(ends)])  18.5 us
    gather x2, local copies, waits for them, and re-layouts, precondition(): gathered = padded[source_row]  15 us
    ppermute x4, starting transfers between devices, shifted(): return lax.ppermute(shard, axis, pairs)  11.7 us
    dot_general x2, matrix products, precondition(): solved = jnp.dot(schur_inv, scaled, preferred_element_type=jnp.float32)  11.5 us
  transfers between devices with their start and end apart: 10, of which 10 were waited for; matrix products, arithmetic and copies ran while one was open for 3% of the time, Pallas kernels for 0%

profile of v1, /device:TPU:0, one launch (start us, length us, event | category | flops | bytes accessed | tf_op | source)
XLA Modules:
  0.0 418.4 jit_solution(4887360545982959692)
XLA Ops:
  7.2 1.3 convert_element_type.56
  8.5 1.3 collective-permute-start.1
  9.8 5.5 %collective-permute-start = (bf16[1024,256]{1,0:T(8,128)(2,1)S(1)}, bf16[1024,256]{1,0:T(8,128)(2,1)S(1)}, u32[]{:S(2)}, u32[]{:S(2)}) collective-permute-start(bf16[1024,256]{1,0:T(8,128)(2,1)S(1)} %convert_element_type.56), channel_id=1, source_target_pairs={{0,4},{4,8},{8,12},{12,16},{16,20},{20,24},{24,28},{1,5},{5,9},{9,... | collective-permute-start | bytes 1572872 | tf_op jit(solution)/shard_map/ppermute | solution.py:15
  16.0 0.7 broadcast_clamp_fusion
  16.7 8.6 %collective-permute-done.1 = bf16[1024,256]{1,0:T(8,128)(2,1)S(1)} collective-permute-done((bf16[1024,256]{1,0:T(8,128)(2,1)S(1)}, bf16[1024,256]{1,0:T(8,128)(2,1)S(1)}, u32[]{:S(2)}, u32[]{:S(2)}) %collective-permute-start.1) | collective-permute-done | bytes 524320 | tf_op jit(solution)/shard_map/ppermute | solution.py:17
  25.3 11.4 %collective-permute-done = bf16[1024,256]{1,0:T(8,128)(2,1)S(1)} collective-permute-done((bf16[1024,256]{1,0:T(8,128)(2,1)S(1)}, bf16[1024,256]{1,0:T(8,128)(2,1)S(1)}, u32[]{:S(2)}, u32[]{:S(2)}) %collective-permute-start) | collective-permute-done | bytes 524320 | tf_op jit(solution)/shard_map/ppermute | solution.py:15
  36.8 7.5 %gather_fusion = bf16[2048,256]{1,0:T(8,128)(2,1)S(1)} fusion(bf16[3072,256]{1,0:T(8,128)(2,1)S(1)} %pad_maximum_fusion, s32[2048]{0:T(1024)S(1)} %get-tuple-element.8), kind=kCustom, calls=%fused_computation | custom fusion | bytes 2105344 | tf_op jit(solution)/shard_map/gather | solution.py:40
  45.3 0.7 copy-done.2
  46.1 5.8 %fusion.13 = f32[256,2048]{1,0:T(8,128)S(1)} fusion(bf16[2048,256]{1,0:T(8,128)(2,1)S(1)} %multiply_convert_fusion.1, bf16[2048,2048]{1,0:T(8,128)(2,1)} %param.8), kind=kOutput, calls=%fused_computation.35 | convolution fusion | flops 2147483648 | bytes 11534336 | tf_op jit(solution)/shard_map/dot_general | solution.py:48
  51.8 120.6 %all-reduce.3.cloned.1.call-done = bf16[512,256]{1,0:T(8,128)(2,1)} async-done(((bf16[512,256]{1,0:T(8,128)(2,1)}), bf16[512,256]{1,0:T(8,128)(2,1)}) %all-reduce.3.cloned.1.call-update) | async-done | bytes 262160 | tf_op jit(solution)/shard_map/psum | solution.py:46
  172.4 1.7 fusion.5
  174.6 9.8 %scatter_custom_fusion = bf16[3072,256]{1,0:T(8,128)(2,1)S(1)} fusion(s32[2048]{0:T(1024)S(1)} %get-tuple-element.9, bf16[2048,256]{1,0:T(8,128)(2,1)S(1)} %copy.9, bf16[]{:T(256)} %constant.10.clone.1), kind=kCustom, calls=%fused_computation.24 | custom fusion | bytes 1572866 | tf_op jit(solution)/shard_map/scatter | solution.py:54
  184.5 1.3 collective-permute-start.2
  185.8 4.6 %collective-permute-start.3 = (bf16[1024,256]{1,0:T(8,128)(2,1)S(1)}, bf16[1024,256]{1,0:T(8,128)(2,1)S(1)}, u32[]{:S(2)}, u32[]{:S(2)}) collective-permute-start(bf16[1024,256]{1,0:T(8,128)(2,1)S(1)} %get-tuple-element.7), channel_id=1, source_target_pairs={{0,4},{4,8},{8,12},{12,16},{16,20},{20,24},{24,28},{1,5},{5,9},{9,... | collective-permute-start | bytes 1572872 | tf_op jit(solution)/shard_map/ppermute | solution.py:27
  190.4 8.9 %collective-permute-done.2 = bf16[1024,256]{1,0:T(8,128)(2,1)S(1)} collective-permute-done((bf16[1024,256]{1,0:T(8,128)(2,1)S(1)}, bf16[1024,256]{1,0:T(8,128)(2,1)S(1)}, u32[]{:S(2)}, u32[]{:S(2)}) %collective-permute-start.2) | collective-permute-done | bytes 524320 | tf_op jit(solution)/shard_map/ppermute | solution.py:27
  199.3 11.1 %collective-permute-done.3 = bf16[1024,256]{1,0:T(8,128)(2,1)S(1)} collective-permute-done((bf16[1024,256]{1,0:T(8,128)(2,1)S(1)}, bf16[1024,256]{1,0:T(8,128)(2,1)S(1)}, u32[]{:S(2)}, u32[]{:S(2)}) %collective-permute-start.3) | collective-permute-done | bytes 524320 | tf_op jit(solution)/shard_map/ppermute | solution.py:27
  210.4 1.2 fusion.10
  211.5 1.3 collective-permute-start.5
  212.8 5.2 %collective-permute-start.4 = (bf16[1024,256]{1,0:T(8,128)(2,1)S(1)}, bf16[1024,256]{1,0:T(8,128)(2,1)S(1)}, u32[]{:S(2)}, u32[]{:S(2)}) collective-permute-start(bf16[1024,256]{1,0:T(8,128)(2,1)S(1)} %get-tuple-element.2), channel_id=1, source_target_pairs={{0,4},{4,8},{8,12},{12,16},{16,20},{20,24},{24,28},{1,5},{5,9},{9,... | collective-permute-start | bytes 1572872 | tf_op jit(solution)/shard_map/ppermute | solution.py:15
  218.0 10.0 %collective-permute-done.5 = bf16[1024,256]{1,0:T(8,128)(2,1)S(1)} collective-permute-done((bf16[1024,256]{1,0:T(8,128)(2,1)S(1)}, bf16[1024,256]{1,0:T(8,128)(2,1)S(1)}, u32[]{:S(2)}, u32[]{:S(2)}) %collective-permute-start.5) | collective-permute-done | bytes 524320 | tf_op jit(solution)/shard_map/ppermute | solution.py:17
  228.0 11.4 %collective-permute-done.4 = bf16[1024,256]{1,0:T(8,128)(2,1)S(1)} collective-permute-done((bf16[1024,256]{1,0:T(8,128)(2,1)S(1)}, bf16[1024,256]{1,0:T(8,128)(2,1)S(1)}, u32[]{:S(2)}, u32[]{:S(2)}) %collective-permute-start.4) | collective-permute-done | bytes 524320 | tf_op jit(solution)/shard_map/ppermute | solution.py:15
  239.5 7.5 %gather_fusion.2 = bf16[2048,256]{1,0:T(8,128)(2,1)S(1)} fusion(bf16[3072,256]{1,0:T(8,128)(2,1)S(1)} %pad_maximum_fusion.1, s32[2048]{0:T(1024)S(1)} %get-tuple-element.8), kind=kCustom, calls=%fused_computation.2 | custom fusion | bytes 2105344 | tf_op jit(solution)/shard_map/gather | solution.py:40
  248.0 0.7 copy-done.1
  248.7 5.8 %fusion.14 = f32[256,2048]{1,0:T(8,128)S(1)} fusion(bf16[2048,256]{1,0:T(8,128)(2,1)S(1)} %multiply_convert_fusion, bf16[2048,2048]{1,0:T(8,128)(2,1)} %param.8), kind=kOutput, calls=%fused_computation.36 | convolution fusion | flops 2147483648 | bytes 11534336 | tf_op jit(solution)/shard_map/dot_general | solution.py:48
  254.5 118.0 %all-reduce.5.cloned.1.call-done = bf16[512,256]{1,0:T(8,128)(2,1)} async-done(((bf16[512,256]{1,0:T(8,128)(2,1)}), bf16[512,256]{1,0:T(8,128)(2,1)}) %all-reduce.5.cloned.1.call-update) | async-done | bytes 262160 | tf_op jit(solution)/shard_map/psum | solution.py:46
  372.5 1.7 fusion.4
  374.7 9.8 %scatter_custom_fusion.1 = bf16[3072,256]{1,0:T(8,128)(2,1)S(1)} fusion(s32[2048]{0:T(1024)S(1)} %get-tuple-element.9, bf16[2048,256]{1,0:T(8,128)(2,1)S(1)} %copy.10, bf16[]{:T(256)} %constant.10.clone.1), kind=kCustom, calls=%fused_computation.22 | custom fusion | bytes 1572866 | tf_op jit(solution)/shard_map/scatter | solution.py:54
  384.5 1.3 collective-permute-start.6
  385.8 4.6 %collective-permute-start.7 = (bf16[1024,256]{1,0:T(8,128)(2,1)S(1)}, bf16[1024,256]{1,0:T(8,128)(2,1)S(1)}, u32[]{:S(2)}, u32[]{:S(2)}) collective-permute-start(bf16[1024,256]{1,0:T(8,128)(2,1)S(1)} %get-tuple-element.5), channel_id=1, source_target_pairs={{0,4},{4,8},{8,12},{12,16},{16,20},{20,24},{24,28},{1,5},{5,9},{9,... | collective-permute-start | bytes 1572872 | tf_op jit(solution)/shard_map/ppermute | solution.py:27
  390.4 8.9 %collective-permute-done.6 = bf16[1024,256]{1,0:T(8,128)(2,1)S(1)} collective-permute-done((bf16[1024,256]{1,0:T(8,128)(2,1)S(1)}, bf16[1024,256]{1,0:T(8,128)(2,1)S(1)}, u32[]{:S(2)}, u32[]{:S(2)}) %collective-permute-start.6) | collective-permute-done | bytes 524320 | tf_op jit(solution)/shard_map/ppermute | solution.py:27
  399.3 11.1 %collective-permute-done.7 = bf16[1024,256]{1,0:T(8,128)(2,1)S(1)} collective-permute-done((bf16[1024,256]{1,0:T(8,128)(2,1)S(1)}, bf16[1024,256]{1,0:T(8,128)(2,1)S(1)}, u32[]{:S(2)}, u32[]{:S(2)}) %collective-permute-start.7) | collective-permute-done | bytes 524320 | tf_op jit(solution)/shard_map/ppermute | solution.py:27
  410.4 1.1 convert_add_fusion
  (28 shorter events, 4.1 us)
Async XLA Ops:
  7.2 165.2 %copy-start = (bf16[16,2048]{1,0:T(8,128)(2,1)S(1)}, bf16[16,2048]{1,0:T(8,128)(2,1)}, u32[]{:S(2)}) copy-start(bf16[16,2048]{1,0:T(8,128)(2,1)} %param.9) | copy-start | bytes 196612
  7.2 165.2 %all-reduce.3.cloned.1.call-start = ((), (), s32[]{:S(2)}) async-start(), calls=%async_computation | async-start | bytes 524288 | tf_op jit(solution)/shard_map/psum | solution.py:46
  8.5 16.8 %collective-permute-start.1 = (bf16[1024,256]{1,0:T(8,128)(2,1)S(1)}, bf16[1024,256]{1,0:T(8,128)(2,1)S(1)}, u32[]{:S(2)}, u32[]{:S(2)}) collective-permute-start(bf16[1024,256]{1,0:T(8,128)(2,1)S(1)} %convert_element_type.56), channel_id=1, source_target_pairs={{4,0},{8,4},{12,8},{16,12},{20,16},{24,20},{28,24},{5,1},{9,5},{13... | collective-permute-start | bytes 1572872 | tf_op jit(solution)/shard_map/ppermute | solution.py:17
  9.8 26.8 %collective-permute-start = (bf16[1024,256]{1,0:T(8,128)(2,1)S(1)}, bf16[1024,256]{1,0:T(8,128)(2,1)S(1)}, u32[]{:S(2)}, u32[]{:S(2)}) collective-permute-start(bf16[1024,256]{1,0:T(8,128)(2,1)S(1)} %convert_element_type.56), channel_id=1, source_target_pairs={{0,4},{4,8},{8,12},{12,16},{16,20},{20,24},{24,28},{1,5},{5,9},{9,... | collective-permute-start | bytes 1572872 | tf_op jit(solution)/shard_map/ppermute | solution.py:15
  36.8 7.5 %copy-start.3 = (f32[2048]{0:T(1024)S(1)}, f32[2048]{0:T(1024)}, u32[]{:S(2)}) copy-start(f32[2048]{0:T(1024)} %param.10) | copy-start | bytes 24580
  45.3 0.7 copy-start.2
  46.0 126.4 %copy-start.4 = (bf16[16,512]{1,0:T(8,128)(2,1)S(1)}, bf16[16,512]{1,0:T(8,128)(2,1)}, u32[]{:S(2)}) copy-start(bf16[16,512]{1,0:T(8,128)(2,1)} %param.11) | copy-start | bytes 49156
  46.0 326.5 %all-reduce.5.cloned.1.call-start = ((), (), s32[]{:S(2)}) async-start(), calls=%async_computation.1 | async-start | bytes 524288 | tf_op jit(solution)/shard_map/psum | solution.py:46
  184.5 14.8 %collective-permute-start.2 = (bf16[1024,256]{1,0:T(8,128)(2,1)S(1)}, bf16[1024,256]{1,0:T(8,128)(2,1)S(1)}, u32[]{:S(2)}, u32[]{:S(2)}) collective-permute-start(bf16[1024,256]{1,0:T(8,128)(2,1)S(1)} %get-tuple-element.6), channel_id=1, source_target_pairs={{4,0},{8,4},{12,8},{16,12},{20,16},{24,20},{28,24},{5,1},{9,5},{13... | collective-permute-start | bytes 1572872 | tf_op jit(solution)/shard_map/ppermute | solution.py:27
  185.8 24.6 %collective-permute-start.3 = (bf16[1024,256]{1,0:T(8,128)(2,1)S(1)}, bf16[1024,256]{1,0:T(8,128)(2,1)S(1)}, u32[]{:S(2)}, u32[]{:S(2)}) collective-permute-start(bf16[1024,256]{1,0:T(8,128)(2,1)S(1)} %get-tuple-element.7), channel_id=1, source_target_pairs={{0,4},{4,8},{8,12},{12,16},{16,20},{20,24},{24,28},{1,5},{5,9},{9,... | collective-permute-start | bytes 1572872 | tf_op jit(solution)/shard_map/ppermute | solution.py:27
  211.5 16.5 %collective-permute-start.5 = (bf16[1024,256]{1,0:T(8,128)(2,1)S(1)}, bf16[1024,256]{1,0:T(8,128)(2,1)S(1)}, u32[]{:S(2)}, u32[]{:S(2)}) collective-permute-start(bf16[1024,256]{1,0:T(8,128)(2,1)S(1)} %get-tuple-element.2), channel_id=1, source_target_pairs={{4,0},{8,4},{12,8},{16,12},{20,16},{24,20},{28,24},{5,1},{9,5},{13... | collective-permute-start | bytes 1572872 | tf_op jit(solution)/shard_map/ppermute | solution.py:17
  212.8 26.6 %collective-permute-start.4 = (bf16[1024,256]{1,0:T(8,128)(2,1)S(1)}, bf16[1024,256]{1,0:T(8,128)(2,1)S(1)}, u32[]{:S(2)}, u32[]{:S(2)}) collective-permute-start(bf16[1024,256]{1,0:T(8,128)(2,1)S(1)} %get-tuple-element.2), channel_id=1, source_target_pairs={{0,4},{4,8},{8,12},{12,16},{16,20},{20,24},{24,28},{1,5},{5,9},{9,... | collective-permute-start | bytes 1572872 | tf_op jit(solution)/shard_map/ppermute | solution.py:15
  248.0 0.7 copy-start.1
  384.5 14.8 %collective-permute-start.6 = (bf16[1024,256]{1,0:T(8,128)(2,1)S(1)}, bf16[1024,256]{1,0:T(8,128)(2,1)S(1)}, u32[]{:S(2)}, u32[]{:S(2)}) collective-permute-start(bf16[1024,256]{1,0:T(8,128)(2,1)S(1)} %get-tuple-element.4), channel_id=1, source_target_pairs={{4,0},{8,4},{12,8},{16,12},{20,16},{24,20},{28,24},{5,1},{9,5},{13... | collective-permute-start | bytes 1572872 | tf_op jit(solution)/shard_map/ppermute | solution.py:27
  385.8 24.6 %collective-permute-start.7 = (bf16[1024,256]{1,0:T(8,128)(2,1)S(1)}, bf16[1024,256]{1,0:T(8,128)(2,1)S(1)}, u32[]{:S(2)}, u32[]{:S(2)}) collective-permute-start(bf16[1024,256]{1,0:T(8,128)(2,1)S(1)} %get-tuple-element.5), channel_id=1, source_target_pairs={{0,4},{4,8},{8,12},{12,16},{16,20},{20,24},{24,28},{1,5},{5,9},{9,... | collective-permute-start | bytes 1572872 | tf_op jit(solution)/shard_map/ppermute | solution.py:27
Sparse Core Ops, SparseCore 0:
  46.1 126.2 all-reduce.2
  248.8 123.6 all-reduce.4

commit v2 on v0

--- a/solution.py
+++ b/solution.py
@@ -2,6 +2,8 @@
 import jax.numpy as jnp
 from jax import lax
 from jax.sharding import PartitionSpec as P
+
+AXES = ("sub", "grp")
 
 
 def with_halo(cells, sides, width):
@@ -27,12 +29,29 @@
     return lax.ppermute(shard, axis, pairs)
 
 
+def gather_all(block):
+    count = lax.axis_size("sub") * lax.axis_size("grp")
+    me = lax.axis_index("sub") * lax.axis_size("grp") + lax.axis_index("grp")
+    rows = block.shape[0]
+    held = lax.dynamic_update_slice_in_dim(
+        jnp.zeros((count * rows, block.shape[1]), block.dtype), block, me * rows, 0
+    )
+    span = 1
+    while span < count:
+        start = (me // span) * span
+        piece = lax.dynamic_slice_in_dim(held, start * rows, span * rows, 0)
+        got = lax.ppermute(piece, AXES, [(i, i ^ span) for i in range(count)])
+        held = lax.dynamic_update_slice_in_dim(held, got, (start ^ span) * rows, 0)
+        span *= 2
+    return held
+
+
+CHUNKS = 4
+
+
 def shards(resid, schur_inv, basis, scaling, coarse_inv, source_row, primal_idx):
     own_count = resid.shape[0]
     scale_column = scaling[:, None]
-
-    def add_all(portion):
-        return jnp.dot(coarse_inv, portion, preferred_element_type=jnp.float32)
 
     def precondition(vector_in):
         rounded = vector_in.astype(jnp.bfloat16)
@@ -40,7 +59,7 @@
         gathered = padded[source_row]
         scaled = (scale_column * gathered.astype(jnp.float32)).astype(jnp.bfloat16)
         primal = scaled[primal_idx]
-        coarse = add_all(lax.all_gather(primal, ("sub", "grp"), axis=0, tiled=True))
+        coarse = jnp.dot(coarse_inv, gather_all(primal), preferred_element_type=jnp.float32)
         coarse_rounded = coarse.astype(jnp.bfloat16)
         solved = jnp.dot(schur_inv, scaled, preferred_element_type=jnp.float32)
         solved = solved + lax.dot_general(
@@ -58,9 +77,13 @@
             + from_previous.astype(jnp.float32)
         )
 
-    first_apply = precondition(resid)
-    second_apply = precondition(first_apply)
-    return (first_apply, second_apply)
+    width = resid.shape[1] // CHUNKS
+    firsts, seconds = [], []
+    for c in range(CHUNKS):
+        first = precondition(resid[:, c * width : (c + 1) * width])
+        firsts.append(first)
+        seconds.append(precondition(first))
+    return (jnp.concatenate(firsts, axis=1), jnp.concatenate(seconds, axis=1))
 
 
 def solution(mesh):
@@ -68,14 +91,14 @@
         shards,
         mesh=mesh,
         in_specs=(
-            P(("sub", "grp"), None),
-            P(("sub", "grp"), None),
-            P(("sub", "grp"), None),
-            P(("sub", "grp")),
-            P(("sub", "grp"), None),
-            P(("sub", "grp")),
-            P(("sub", "grp")),
+            P(AXES, None),
+            P(AXES, None),
+            P(AXES, None),
+            P(AXES),
+            P(AXES, None),
+            P(AXES),
+            P(AXES),
         ),
-        out_specs=(P(("sub", "grp"), None), P(("sub", "grp"), None)),
+        out_specs=(P(AXES, None), P(AXES, None)),
         check_vma=False,
     )

time: 237 us -> 406 us (1.71); the launches traced: 236 us -> 398 us
  starting transfers between devices: 24.9 us -> 146 us
  local copies, waits for them, and re-layouts: 36.9 us -> 123 us
  blocking collectives: 78 us -> 0 us
  matrix products: 13 us -> 53.6 us
  waiting for transfers between devices: 76.8 us -> 54.7 us
  other arithmetic: 5.85 us -> 19.6 us
    all_gather x2 -> x0, blocking collectives: 78 us -> none  [precondition(): coarse = add_all(lax.all_gather(primal, ('sub', 'grp'), axis=0, tiled=True))]
    ppermute x0 -> x40, starting transfers between devices: none -> 46.1 us  [gather_all(): got = lax.ppermute(piece, AXES, [(i, i ^ span) for i in range(count)])]
    gather x2 -> x8, local copies, waits for them, and re-layouts: 15 us -> 54.9 us  [precondition(): gathered = padded[source_row]]
    dot_general x2 -> x8, matrix products: 11.5 us -> 49.7 us  [precondition(): solved = jnp.dot(schur_inv, scaled, preferred_element_type=jnp.float32)]
    ppermute x4 -> x16, starting transfers between devices: 11.7 us -> 46.2 us  [shifted(): return lax.ppermute(shard, axis, pairs)]
    ppermute x2 -> x8, starting transfers between devices: 10.6 us -> 43.2 us  [with_halo(): lax.ppermute(tail, axis, [(i, (i + 1) % count) for i in range(ends)])]
    scatter x2 -> x8, local copies, waits for them, and re-layouts: 19.6 us -> 48.8 us  [precondition(): jnp.zeros((3 * own_count, weighted.shape[1]), jnp.bfloat16).at[source_row]]
    ppermute x2 -> x8, waiting for transfers between devices: 18.7 us -> 4.3 us  [with_halo(): lax.ppermute(head, axis, [((i + 1) % count, i) for i in range(ends)])]
  transfers between devices with their start and end apart: 8 -> 72, of which waited for: 8 -> 21; matrix products, arithmetic and copies ran while one was open for 1% -> 41% of each run, Pallas kernels for 0% -> 0%
where the time goes in v2:
time: 406 us; the launch traced here: 398 us
  starting transfers between devices  146 us (36%)
  local copies, waits for them, and re-layouts  123 us (30%)
  waiting for transfers between devices  54.7 us (13%)
  matrix products  53.6 us (13%)
  other arithmetic  19.6 us (5%)
    gather x8, local copies, waits for them, and re-layouts, precondition(): gathered = padded[source_row]  54.9 us
    dot_general x8, matrix products, precondition(): solved = jnp.dot(schur_inv, scaled, preferred_element_type=jnp.float32)  49.7 us
    scatter x8, local copies, waits for them, and re-layouts, precondition(): jnp.zeros((3 * own_count, weighted.shape[1]), jnp.bfloat16).at[source_row]  48.8 us
    ppermute x16, starting transfers between devices, shifted(): return lax.ppermute(shard, axis, pairs)  46.2 us
    ppermute x40, starting transfers between devices, gather_all(): got = lax.ppermute(piece, AXES, [(i, i ^ span) for i in range(count)])  46.1 us
    ppermute x8, starting transfers between devices, with_halo(): lax.ppermute(tail, axis, [(i, (i + 1) % count) for i in range(ends)])  43.2 us
    ppermute x16, waiting for transfers between devices, shifted(): return lax.ppermute(shard, axis, pairs)  26.5 us
    ppermute x40, waiting for transfers between devices, gather_all(): got = lax.ppermute(piece, AXES, [(i, i ^ span) for i in range(count)])  12.2 us
  transfers between devices with their start and end apart: 72, of which 21 were waited for; matrix products, arithmetic and copies ran while one was open for 41% of the time, Pallas kernels for 0%

profile of v2, /device:TPU:0, one launch (start us, length us, event | category | flops | bytes accessed | tf_op | source)
XLA Modules:
  0.0 398.5 jit_solution(5761684331859210352)
XLA Ops:
  13.4 5.8 %collective-permute-done = bf16[1024,64]{1,0:T(8,128)(2,1)S(1)} collective-permute-done((bf16[1024,64]{1,0:T(8,128)(2,1)S(1)}, bf16[1024,64]{1,0:T(8,128)(2,1)S(1)}, u32[]{:S(2)}, u32[]{:S(2)}) %collective-permute-start) | collective-permute-done | bytes 131104 | tf_op jit(solution)/shard_map/ppermute | solution.py:17
  19.3 6.2 %gather_fusion = bf16[2048,64]{1,0:T(8,128)(2,1)S(1)} fusion(bf16[3072,64]{1,0:T(8,128)(2,1)S(1)} %pad_maximum_fusion.2, s32[2048]{0:T(1024)S(1)} %get-tuple-element.37), kind=kCustom, calls=%fused_computation | custom fusion | bytes 532480 | tf_op jit(solution)/shard_map/gather | solution.py:59
  44.4 6.2 %collective-permute-start.18 = (bf16[1024,64]{1,0:T(8,128)(2,1)S(1)}, bf16[1024,64]{1,0:T(8,128)(2,1)}, u32[]{:S(2)}, u32[]{:S(2)}) collective-permute-start(bf16[1024,64]{1,0:T(8,128)(2,1)S(1)} %get-tuple-element.28), channel_id=1, source_target_pairs={{0,4},{4,8},{8,12},{12,16},{16,20},{20,24},{24,28},{1,5},{5,9},{9,... | collective-permute-start | bytes 393224 | tf_op jit(solution)/shard_map/ppermute | solution.py:17
  51.9 5.5 %collective-permute-start.27 = (bf16[1024,64]{1,0:T(8,128)(2,1)S(1)}, bf16[1024,64]{1,0:T(8,128)(2,1)}, u32[]{:S(2)}, u32[]{:S(2)}) collective-permute-start(bf16[1024,64]{1,0:T(8,128)(2,1)S(1)} %get-tuple-element.27), channel_id=1, source_target_pairs={{0,4},{4,8},{8,12},{12,16},{16,20},{20,24},{24,28},{1,5},{5,9},{9,... | collective-permute-start | bytes 393224 | tf_op jit(solution)/shard_map/ppermute | solution.py:17
  57.4 5.5 %collective-permute-done.9 = bf16[1024,64]{1,0:T(8,128)(2,1)S(1)} collective-permute-done((bf16[1024,64]{1,0:T(8,128)(2,1)S(1)}, bf16[1024,64]{1,0:T(8,128)(2,1)S(1)}, u32[]{:S(2)}, u32[]{:S(2)}) %collective-permute-start.9) | collective-permute-done | bytes 131104 | tf_op jit(solution)/shard_map/ppermute | solution.py:17
  69.2 6.5 %fusion.23 = bf16[2048,64]{0,1:T(8,128)(2,1)S(1)} fusion(f32[64,2048]{1,0:T(8,128)S(1)} %fusion.24, bf16[2048,2048]{1,0:T(8,128)(2,1)} %param.8, f32[2048]{0:T(1024)S(1)} %copy-done.7, bf16[2048,64]{1,0:T(8,128)(2,1)S(1)} %gather_fusion), kind=kOutput, calls=%fused_computation.55 | convolution fusion | flops 537657344 | bytes 9445376 | tf_op jit(solution)/shard_map/dot_general | solution.py:64
  75.9 6.0 %scatter_custom_fusion = bf16[3072,64]{1,0:T(8,128)(2,1)S(1)} fusion(s32[2048]{0:T(1024)S(1)} %get-tuple-element.38, bf16[2048,64]{1,0:T(8,128)(2,1)S(1)} %copy.9, bf16[]{:T(256)} %constant.135.clone.1), kind=kCustom, calls=%fused_computation.112 | custom fusion | bytes 393218 | tf_op jit(solution)/shard_map/scatter | solution.py:70
  88.3 6.9 %collective-permute-done.8 = bf16[1024,64]{1,0:T(8,128)(2,1)S(1)} collective-permute-done((bf16[1024,64]{1,0:T(8,128)(2,1)S(1)}, bf16[1024,64]{1,0:T(8,128)(2,1)S(1)}, u32[]{:S(2)}, u32[]{:S(2)}) %collective-permute-start.8) | collective-permute-done | bytes 131104 | tf_op jit(solution)/shard_map/ppermute | solution.py:29
  97.4 5.9 %collective-permute-start.36 = (bf16[1024,64]{1,0:T(8,128)(2,1)S(1)}, bf16[1024,64]{1,0:T(8,128)(2,1)}, u32[]{:S(2)}, u32[]{:S(2)}) collective-permute-start(bf16[1024,64]{1,0:T(8,128)(2,1)S(1)} %get-tuple-element.2), channel_id=1, source_target_pairs={{0,4},{4,8},{8,12},{12,16},{16,20},{20,24},{24,28},{1,5},{5,9},{9,... | collective-permute-start | bytes 393224 | tf_op jit(solution)/shard_map/ppermute | solution.py:17
  104.5 6.2 %gather_fusion.2 = bf16[2048,64]{1,0:T(8,128)(2,1)S(1)} fusion(bf16[3072,64]{1,0:T(8,128)(2,1)S(1)} %pad_maximum_fusion.3, s32[2048]{0:T(1024)S(1)} %get-tuple-element.37), kind=kCustom, calls=%fused_computation.2 | custom fusion | bytes 532480 | tf_op jit(solution)/shard_map/gather | solution.py:59
  110.7 8.0 %gather_fusion.4 = bf16[2048,64]{1,0:T(8,128)(2,1)} fusion(bf16[3072,64]{1,0:T(8,128)(2,1)S(1)} %pad_maximum_fusion.4, s32[2048]{0:T(1024)S(1)} %get-tuple-element.37), kind=kCustom, calls=%fused_computation.4 | custom fusion | bytes 532480 | tf_op jit(solution)/shard_map/gather | solution.py:59
  118.7 8.0 %gather_fusion.6 = bf16[2048,64]{1,0:T(8,128)(2,1)} fusion(bf16[3072,64]{1,0:T(8,128)(2,1)S(1)} %pad_maximum_fusion.5, s32[2048]{0:T(1024)S(1)} %get-tuple-element.37), kind=kCustom, calls=%fused_computation.6 | custom fusion | bytes 532480 | tf_op jit(solution)/shard_map/gather | solution.py:59
  128.6 8.1 %gather_fusion.8 = bf16[2048,64]{1,0:T(8,128)(2,1)} fusion(bf16[3072,64]{1,0:T(8,128)(2,1)S(1)} %pad_maximum_fusion.6, s32[2048]{0:T(1024)S(1)} %get-tuple-element.37), kind=kCustom, calls=%fused_computation.8 | custom fusion | bytes 532480 | tf_op jit(solution)/shard_map/gather | solution.py:59
  164.9 6.1 %fusion.20 = bf16[2048,64]{0,1:T(8,128)(2,1)S(1)} fusion(f32[64,2048]{1,0:T(8,128)S(1)} %fusion.27, bf16[2048,64]{1,0:T(8,128)(2,1)S(1)} %get-tuple-element.33, bf16[2048,2048]{1,0:T(8,128)(2,1)} %param.8, f32[2048]{0:T(1024)S(1)} %copy-done.7), kind=kOutput, calls=%fused_computation.52 | convolution fusion | flops 537264128 | bytes 9445376 | tf_op jit(solution)/shard_map/dot_general | solution.py:64
  172.0 6.3 %scatter_custom_fusion.3 = bf16[3072,64]{1,0:T(8,128)(2,1)S(1)} fusion(s32[2048]{0:T(1024)S(1)} %get-tuple-element.38, bf16[2048,64]{1,0:T(8,128)(2,1)} %copy.12, bf16[]{:T(256)} %constant.135.clone.1), kind=kCustom, calls=%fused_computation.106 | custom fusion | bytes 393728 | tf_op jit(solution)/shard_map/scatter | solution.py:70
  185.0 6.1 %fusion.21 = bf16[2048,64]{0,1:T(8,128)(2,1)S(1)} fusion(f32[64,2048]{1,0:T(8,128)S(1)} %fusion.26, bf16[2048,64]{1,0:T(8,128)(2,1)S(1)} %get-tuple-element.32, bf16[2048,2048]{1,0:T(8,128)(2,1)} %param.8, f32[2048]{0:T(1024)S(1)} %copy-done.7), kind=kOutput, calls=%fused_computation.53 | convolution fusion | flops 537264128 | bytes 9445376 | tf_op jit(solution)/shard_map/dot_general | solution.py:64
  191.3 6.0 %scatter_custom_fusion.2 = bf16[3072,64]{1,0:T(8,128)(2,1)S(1)} fusion(s32[2048]{0:T(1024)S(1)} %get-tuple-element.38, bf16[2048,64]{1,0:T(8,128)(2,1)S(1)} %copy.11, bf16[]{:T(256)} %constant.135.clone.1), kind=kCustom, calls=%fused_computation.108 | custom fusion | bytes 393218 | tf_op jit(solution)/shard_map/scatter | solution.py:70
  204.7 6.8 %fusion.22 = bf16[2048,64]{0,1:T(8,128)(2,1)} fusion(f32[64,2048]{1,0:T(8,128)S(1)} %fusion.25, bf16[2048,64]{1,0:T(8,128)(2,1)S(1)} %get-tuple-element.31, bf16[2048,2048]{1,0:T(8,128)(2,1)} %param.8, f32[2048]{0:T(1024)S(1)} %copy-done.7), kind=kOutput, calls=%fused_computation.54 | convolution fusion | flops 537264128 | bytes 9445376 | tf_op jit(solution)/shard_map/dot_general | solution.py:64
  213.4 6.3 %scatter_custom_fusion.1 = bf16[3072,64]{1,0:T(8,128)(2,1)S(1)} fusion(s32[2048]{0:T(1024)S(1)} %get-tuple-element.38, bf16[2048,64]{1,0:T(8,128)(2,1)} %copy.10, bf16[]{:T(256)} %constant.135.clone.1), kind=kCustom, calls=%fused_computation.110 | custom fusion | bytes 393728 | tf_op jit(solution)/shard_map/scatter | solution.py:70
  226.8 6.1 %fusion.19 = bf16[2048,64]{0,1:T(8,128)(2,1)S(1)} fusion(f32[64,2048]{1,0:T(8,128)} %fusion.28, bf16[2048,64]{1,0:T(8,128)(2,1)S(1)} %get-tuple-element.30, bf16[2048,2048]{1,0:T(8,128)(2,1)} %param.8, f32[2048]{0:T(1024)S(1)} %copy-done.7), kind=kOutput, calls=%fused_computation.51 | convolution fusion | flops 537264128 | bytes 9445376 | tf_op jit(solution)/shard_map/dot_general | solution.py:64
  233.9 6.3 %scatter_custom_fusion.4 = bf16[3072,64]{1,0:T(8,128)(2,1)S(1)} fusion(s32[2048]{0:T(1024)S(1)} %get-tuple-element.38, bf16[2048,64]{1,0:T(8,128)(2,1)} %copy.13, bf16[]{:T(256)} %constant.135.clone.1), kind=kCustom, calls=%fused_computation.104 | custom fusion | bytes 393728 | tf_op jit(solution)/shard_map/scatter | solution.py:70
  254.5 5.7 %collective-permute-start.45 = (bf16[1024,64]{1,0:T(8,128)(2,1)S(1)}, bf16[1024,64]{1,0:T(8,128)(2,1)S(1)}, u32[]{:S(2)}, u32[]{:S(2)}) collective-permute-start(bf16[1024,64]{1,0:T(8,128)(2,1)S(1)} %get-tuple-element.4), channel_id=1, source_target_pairs={{0,4},{4,8},{8,12},{12,16},{16,20},{20,24},{24,28},{1,5},{5,9},{9,... | collective-permute-start | bytes 393224 | tf_op jit(solution)/shard_map/ppermute | solution.py:17
  262.7 12.1 %collective-permute-done.44 = bf16[1024,64]{1,0:T(8,128)(2,1)S(1)} collective-permute-done((bf16[1024,64]{1,0:T(8,128)(2,1)S(1)}, bf16[1024,64]{1,0:T(8,128)(2,1)S(1)}, u32[]{:S(2)}, u32[]{:S(2)}) %collective-permute-start.44) | collective-permute-done | bytes 131104 | tf_op jit(solution)/shard_map/ppermute | solution.py:29
  288.9 6.2 %gather_fusion.10 = bf16[2048,64]{1,0:T(8,128)(2,1)S(1)} fusion(bf16[3072,64]{1,0:T(8,128)(2,1)S(1)} %pad_maximum_fusion.7, s32[2048]{0:T(1024)S(1)} %get-tuple-element.37), kind=kCustom, calls=%fused_computation.10 | custom fusion | bytes 532480 | tf_op jit(solution)/shard_map/gather | solution.py:59
  295.1 6.2 %gather_fusion.12 = bf16[2048,64]{1,0:T(8,128)(2,1)S(1)} fusion(bf16[3072,64]{1,0:T(8,128)(2,1)S(1)} %pad_maximum_fusion.8, s32[2048]{0:T(1024)S(1)} %get-tuple-element.37), kind=kCustom, calls=%fused_computation.12 | custom fusion | bytes 532480 | tf_op jit(solution)/shard_map/gather | solution.py:59
  302.5 6.2 %gather_fusion.14 = bf16[2048,64]{1,0:T(8,128)(2,1)S(1)} fusion(bf16[3072,64]{1,0:T(8,128)(2,1)S(1)} %pad_maximum_fusion.9, s32[2048]{0:T(1024)S(1)} %get-tuple-element.37), kind=kCustom, calls=%fused_computation.14 | custom fusion | bytes 532480 | tf_op jit(solution)/shard_map/gather | solution.py:59
  331.6 6.1 %fusion.16 = bf16[2048,64]{0,1:T(8,128)(2,1)S(1)} fusion(f32[64,2048]{1,0:T(8,128)S(1)} %fusion.31, bf16[2048,64]{1,0:T(8,128)(2,1)S(1)} %get-tuple-element.36, bf16[2048,2048]{1,0:T(8,128)(2,1)} %param.8, f32[2048]{0:T(1024)S(1)} %copy-done.7), kind=kOutput, calls=%fused_computation.48 | convolution fusion | flops 537264128 | bytes 9445376 | tf_op jit(solution)/shard_map/dot_general | solution.py:64
  338.0 6.0 %scatter_custom_fusion.7 = bf16[3072,64]{1,0:T(8,128)(2,1)S(1)} fusion(s32[2048]{0:T(1024)S(1)} %get-tuple-element.38, bf16[2048,64]{1,0:T(8,128)(2,1)S(1)} %copy.16, bf16[]{:T(256)} %constant.135.clone.1), kind=kCustom, calls=%fused_computation.98 | custom fusion | bytes 393218 | tf_op jit(solution)/shard_map/scatter | solution.py:70
  351.1 6.1 %fusion.17 = bf16[2048,64]{0,1:T(8,128)(2,1)S(1)} fusion(f32[64,2048]{1,0:T(8,128)S(1)} %fusion.30, bf16[2048,64]{1,0:T(8,128)(2,1)S(1)} %get-tuple-element.35, bf16[2048,2048]{1,0:T(8,128)(2,1)} %param.8, f32[2048]{0:T(1024)S(1)} %copy-done.7), kind=kOutput, calls=%fused_computation.49 | convolution fusion | flops 537264128 | bytes 9445376 | tf_op jit(solution)/shard_map/dot_general | solution.py:64
  357.4 6.0 %scatter_custom_fusion.6 = bf16[3072,64]{1,0:T(8,128)(2,1)S(1)} fusion(s32[2048]{0:T(1024)S(1)} %get-tuple-element.38, bf16[2048,64]{1,0:T(8,128)(2,1)S(1)} %copy.15, bf16[]{:T(256)} %constant.135.clone.1), kind=kCustom, calls=%fused_computation.100 | custom fusion | bytes 393218 | tf_op jit(solution)/shard_map/scatter | solution.py:70
  371.4 6.1 %fusion.18 = bf16[2048,64]{0,1:T(8,128)(2,1)S(1)} fusion(f32[64,2048]{1,0:T(8,128)S(1)} %fusion.29, bf16[2048,64]{1,0:T(8,128)(2,1)S(1)} %get-tuple-element.34, bf16[2048,2048]{1,0:T(8,128)(2,1)} %param.8, f32[2048]{0:T(1024)S(1)} %copy-done.7), kind=kOutput, calls=%fused_computation.50 | convolution fusion | flops 537264128 | bytes 9445376 | tf_op jit(solution)/shard_map/dot_general | solution.py:64
  377.8 6.0 %scatter_custom_fusion.5 = bf16[3072,64]{1,0:T(8,128)(2,1)S(1)} fusion(s32[2048]{0:T(1024)S(1)} %get-tuple-element.38, bf16[2048,64]{1,0:T(8,128)(2,1)S(1)} %copy.14, bf16[]{:T(256)} %constant.135.clone.1), kind=kCustom, calls=%fused_computation.102 | custom fusion | bytes 393218 | tf_op jit(solution)/shard_map/scatter | solution.py:70
  (312 shorter events, 189.5 us)
Async XLA Ops:
  3.5 15.6 %collective-permute-start = (bf16[1024,64]{1,0:T(8,128)(2,1)S(1)}, bf16[1024,64]{1,0:T(8,128)(2,1)S(1)}, u32[]{:S(2)}, u32[]{:S(2)}) collective-permute-start(bf16[1024,64]{1,0:T(8,128)(2,1)S(1)} %get-tuple-element.26), channel_id=1, source_target_pairs={{0,4},{4,8},{8,12},{12,16},{16,20},{20,24},{24,28},{1,5},{5,9},{9,... | collective-permute-start | bytes 393224 | tf_op jit(solution)/shard_map/ppermute | solution.py:17
  35.6 15.0 %collective-permute-start.5 = (bf16[128,64]{1,0:T(8,128)(2,1)S(1)}, bf16[128,64]{1,0:T(8,128)(2,1)S(1)}, u32[]{:S(2)}, u32[]{:S(2)}) collective-permute-start(bf16[128,64]{1,0:T(8,128)(2,1)S(1)} %constant_dynamic-slice_fusion.36), channel_id=1, source_target_pairs={{0,8},{1,9},{2,10},{3,11},{4,12},{5,13},{6,14},{7,15},{8,0},{9,1},... | collective-permute-start | bytes 49160 | tf_op jit(solution)/shard_map/ppermute | solution.py:43
  37.3 14.7 %collective-permute-start.10 = (bf16[1024,64]{1,0:T(8,128)(2,1)S(1)}, bf16[1024,64]{1,0:T(8,128)(2,1)S(1)}, u32[]{:S(2)}, u32[]{:S(2)}) collective-permute-start(bf16[1024,64]{1,0:T(8,128)(2,1)S(1)} %get-tuple-element.29), channel_id=1, source_target_pairs={{4,0},{8,4},{12,8},{16,12},{20,16},{24,20},{28,24},{5,1},{9,5},{13... | collective-permute-start | bytes 393224 | tf_op jit(solution)/shard_map/ppermute | solution.py:19
  38.6 24.4 %collective-permute-start.9 = (bf16[1024,64]{1,0:T(8,128)(2,1)S(1)}, bf16[1024,64]{1,0:T(8,128)(2,1)S(1)}, u32[]{:S(2)}, u32[]{:S(2)}) collective-permute-start(bf16[1024,64]{1,0:T(8,128)(2,1)S(1)} %get-tuple-element.29), channel_id=1, source_target_pairs={{0,4},{4,8},{8,12},{12,16},{16,20},{20,24},{24,28},{1,5},{5,9},{9,... | collective-permute-start | bytes 393224 | tf_op jit(solution)/shard_map/ppermute | solution.py:17
  43.1 42.6 %collective-permute-start.19 = (bf16[1024,64]{1,0:T(8,128)(2,1)S(1)}, bf16[1024,64]{1,0:T(8,128)(2,1)}, u32[]{:S(2)}, u32[]{:S(2)}) collective-permute-start(bf16[1024,64]{1,0:T(8,128)(2,1)S(1)} %get-tuple-element.28), channel_id=1, source_target_pairs={{4,0},{8,4},{12,8},{16,12},{20,16},{24,20},{28,24},{5,1},{9,5},{13... | collective-permute-start | bytes 393224 | tf_op jit(solution)/shard_map/ppermute | solution.py:19
  44.4 42.7 %collective-permute-start.18 = (bf16[1024,64]{1,0:T(8,128)(2,1)S(1)}, bf16[1024,64]{1,0:T(8,128)(2,1)}, u32[]{:S(2)}, u32[]{:S(2)}) collective-permute-start(bf16[1024,64]{1,0:T(8,128)(2,1)S(1)} %get-tuple-element.28), channel_id=1, source_target_pairs={{0,4},{4,8},{8,12},{12,16},{16,20},{20,24},{24,28},{1,5},{5,9},{9,... | collective-permute-start | bytes 393224 | tf_op jit(solution)/shard_map/ppermute | solution.py:17
  50.6 52.7 %collective-permute-start.28 = (bf16[1024,64]{1,0:T(8,128)(2,1)S(1)}, bf16[1024,64]{1,0:T(8,128)(2,1)}, u32[]{:S(2)}, u32[]{:S(2)}) collective-permute-start(bf16[1024,64]{1,0:T(8,128)(2,1)S(1)} %get-tuple-element.27), channel_id=1, source_target_pairs={{4,0},{8,4},{12,8},{16,12},{20,16},{24,20},{28,24},{5,1},{9,5},{13... | collective-permute-start | bytes 393224 | tf_op jit(solution)/shard_map/ppermute | solution.py:19
  51.9 51.4 %collective-permute-start.27 = (bf16[1024,64]{1,0:T(8,128)(2,1)S(1)}, bf16[1024,64]{1,0:T(8,128)(2,1)}, u32[]{:S(2)}, u32[]{:S(2)}) collective-permute-start(bf16[1024,64]{1,0:T(8,128)(2,1)S(1)} %get-tuple-element.27), channel_id=1, source_target_pairs={{0,4},{4,8},{8,12},{12,16},{16,20},{20,24},{24,28},{1,5},{5,9},{9,... | collective-permute-start | bytes 393224 | tf_op jit(solution)/shard_map/ppermute | solution.py:17
  96.1 30.6 %collective-permute-start.37 = (bf16[1024,64]{1,0:T(8,128)(2,1)S(1)}, bf16[1024,64]{1,0:T(8,128)(2,1)S(1)}, u32[]{:S(2)}, u32[]{:S(2)}) collective-permute-start(bf16[1024,64]{1,0:T(8,128)(2,1)S(1)} %get-tuple-element.2), channel_id=1, source_target_pairs={{4,0},{8,4},{12,8},{16,12},{20,16},{24,20},{28,24},{5,1},{9,5},{13... | collective-permute-start | bytes 393224 | tf_op jit(solution)/shard_map/ppermute | solution.py:19
  97.4 30.0 %collective-permute-start.36 = (bf16[1024,64]{1,0:T(8,128)(2,1)S(1)}, bf16[1024,64]{1,0:T(8,128)(2,1)}, u32[]{:S(2)}, u32[]{:S(2)}) collective-permute-start(bf16[1024,64]{1,0:T(8,128)(2,1)S(1)} %get-tuple-element.2), channel_id=1, source_target_pairs={{0,4},{4,8},{8,12},{12,16},{16,20},{20,24},{24,28},{1,5},{5,9},{9,... | collective-permute-start | bytes 393224 | tf_op jit(solution)/shard_map/ppermute | solution.py:17
  158.4 26.1 %collective-permute-start.24 = (bf16[256,64]{1,0:T(8,128)(2,1)S(1)}, bf16[256,64]{1,0:T(8,128)(2,1)S(1)}, u32[]{:S(2)}, u32[]{:S(2)}) collective-permute-start(bf16[256,64]{1,0:T(8,128)(2,1)S(1)} %constant_dynamic-slice_fusion.25), channel_id=1, source_target_pairs={{0,16},{1,17},{2,18},{3,19},{4,20},{5,21},{6,22},{7,23},{8,24},{9,... | collective-permute-start | bytes 98312 | tf_op jit(solution)/shard_map/ppermute | solution.py:43
  160.0 43.4 %collective-permute-start.15 = (bf16[256,64]{1,0:T(8,128)(2,1)}, bf16[256,64]{1,0:T(8,128)(2,1)}, u32[]{:S(2)}, u32[]{:S(2)}) collective-permute-start(bf16[256,64]{1,0:T(8,128)(2,1)} %constant_dynamic-slice_fusion.30), channel_id=1, source_target_pairs={{0,16},{1,17},{2,18},{3,19},{4,20},{5,21},{6,22},{7,23},{8,24},{9,... | collective-permute-start | bytes 98312 | tf_op jit(solution)/shard_map/ppermute | solution.py:43
  162.7 60.8 %collective-permute-start.42 = (bf16[256,64]{1,0:T(8,128)(2,1)}, bf16[256,64]{1,0:T(8,128)(2,1)}, u32[]{:S(2)}, u32[]{:S(2)}) collective-permute-start(bf16[256,64]{1,0:T(8,128)(2,1)} %constant_dynamic-slice_fusion.15), channel_id=1, source_target_pairs={{0,16},{1,17},{2,18},{3,19},{4,20},{5,21},{6,22},{7,23},{8,24},{9,... | collective-permute-start | bytes 98312 | tf_op jit(solution)/shard_map/ppermute | solution.py:43
  179.1 75.4 %collective-permute-start.35 = (bf16[1024,64]{1,0:T(8,128)(2,1)}, bf16[1024,64]{1,0:T(8,128)(2,1)}, u32[]{:S(2)}, u32[]{:S(2)}) collective-permute-start(bf16[1024,64]{1,0:T(8,128)(2,1)} %get-tuple-element.25), channel_id=1, source_target_pairs={{0,4},{4,8},{8,12},{12,16},{16,20},{20,24},{24,28},{1,5},{5,9},{9,... | collective-permute-start | bytes 393224 | tf_op jit(solution)/shard_map/ppermute | solution.py:29
  182.9 77.4 %collective-permute-start.34 = (bf16[1024,64]{1,0:T(8,128)(2,1)}, bf16[1024,64]{1,0:T(8,128)(2,1)}, u32[]{:S(2)}, u32[]{:S(2)}) collective-permute-start(bf16[1024,64]{1,0:T(8,128)(2,1)} %get-tuple-element.24), channel_id=1, source_target_pairs={{4,0},{8,4},{12,8},{16,12},{20,16},{24,20},{28,24},{5,1},{9,5},{13... | collective-permute-start | bytes 393224 | tf_op jit(solution)/shard_map/ppermute | solution.py:29
  198.1 49.8 %collective-permute-start.26 = (bf16[1024,64]{1,0:T(8,128)(2,1)}, bf16[1024,64]{1,0:T(8,128)(2,1)}, u32[]{:S(2)}, u32[]{:S(2)}) collective-permute-start(bf16[1024,64]{1,0:T(8,128)(2,1)} %get-tuple-element.23), channel_id=1, source_target_pairs={{0,4},{4,8},{8,12},{12,16},{16,20},{20,24},{24,28},{1,5},{5,9},{9,... | collective-permute-start | bytes 393224 | tf_op jit(solution)/shard_map/ppermute | solution.py:29
  220.5 19.7 %collective-permute-start.17 = (bf16[1024,64]{1,0:T(8,128)(2,1)}, bf16[1024,64]{1,0:T(8,128)(2,1)}, u32[]{:S(2)}, u32[]{:S(2)}) collective-permute-start(bf16[1024,64]{1,0:T(8,128)(2,1)} %get-tuple-element.21), channel_id=1, source_target_pairs={{0,4},{4,8},{8,12},{12,16},{16,20},{20,24},{24,28},{1,5},{5,9},{9,... | collective-permute-start | bytes 393224 | tf_op jit(solution)/shard_map/ppermute | solution.py:29
  223.4 18.1 %collective-permute-start.16 = (bf16[1024,64]{1,0:T(8,128)(2,1)}, bf16[1024,64]{1,0:T(8,128)(2,1)}, u32[]{:S(2)}, u32[]{:S(2)}) collective-permute-start(bf16[1024,64]{1,0:T(8,128)(2,1)} %get-tuple-element.20), channel_id=1, source_target_pairs={{4,0},{8,4},{12,8},{16,12},{20,16},{24,20},{28,24},{5,1},{9,5},{13... | collective-permute-start | bytes 393224 | tf_op jit(solution)/shard_map/ppermute | solution.py:29
  241.6 33.2 %collective-permute-start.44 = (bf16[1024,64]{1,0:T(8,128)(2,1)S(1)}, bf16[1024,64]{1,0:T(8,128)(2,1)S(1)}, u32[]{:S(2)}, u32[]{:S(2)}) collective-permute-start(bf16[1024,64]{1,0:T(8,128)(2,1)S(1)} %get-tuple-element.11), channel_id=1, source_target_pairs={{0,4},{4,8},{8,12},{12,16},{16,20},{20,24},{24,28},{1,5},{5,9},{9,... | collective-permute-start | bytes 393224 | tf_op jit(solution)/shard_map/ppermute | solution.py:29
  247.9 31.2 %collective-permute-start.43 = (bf16[1024,64]{1,0:T(8,128)(2,1)S(1)}, bf16[1024,64]{1,0:T(8,128)(2,1)S(1)}, u32[]{:S(2)}, u32[]{:S(2)}) collective-permute-start(bf16[1024,64]{1,0:T(8,128)(2,1)S(1)} %get-tuple-element.10), channel_id=1, source_target_pairs={{4,0},{8,4},{12,8},{16,12},{20,16},{24,20},{28,24},{5,1},{9,5},{13... | collective-permute-start | bytes 393224 | tf_op jit(solution)/shard_map/ppermute | solution.py:29
  252.1 30.7 %collective-permute-start.46 = (bf16[1024,64]{1,0:T(8,128)(2,1)S(1)}, bf16[1024,64]{1,0:T(8,128)(2,1)S(1)}, u32[]{:S(2)}, u32[]{:S(2)}) collective-permute-start(bf16[1024,64]{1,0:T(8,128)(2,1)S(1)} %get-tuple-element.4), channel_id=1, source_target_pairs={{4,0},{8,4},{12,8},{16,12},{20,16},{24,20},{28,24},{5,1},{9,5},{13... | collective-permute-start | bytes 393224 | tf_op jit(solution)/shard_map/ppermute | solution.py:19
  254.5 33.8 %collective-permute-start.45 = (bf16[1024,64]{1,0:T(8,128)(2,1)S(1)}, bf16[1024,64]{1,0:T(8,128)(2,1)S(1)}, u32[]{:S(2)}, u32[]{:S(2)}) collective-permute-start(bf16[1024,64]{1,0:T(8,128)(2,1)S(1)} %get-tuple-element.4), channel_id=1, source_target_pairs={{0,4},{4,8},{8,12},{12,16},{16,20},{20,24},{24,28},{1,5},{5,9},{9,... | collective-permute-start | bytes 393224 | tf_op jit(solution)/shard_map/ppermute | solution.py:17
  260.2 28.2 %collective-permute-start.55 = (bf16[1024,64]{1,0:T(8,128)(2,1)S(1)}, bf16[1024,64]{1,0:T(8,128)(2,1)S(1)}, u32[]{:S(2)}, u32[]{:S(2)}) collective-permute-start(bf16[1024,64]{1,0:T(8,128)(2,1)S(1)} %get-tuple-element.6), channel_id=1, source_target_pairs={{4,0},{8,4},{12,8},{16,12},{20,16},{24,20},{28,24},{5,1},{9,5},{13... | collective-permute-start | bytes 393224 | tf_op jit(solution)/shard_map/ppermute | solution.py:19
  274.7 14.0 %collective-permute-start.54 = (bf16[1024,64]{1,0:T(8,128)(2,1)S(1)}, bf16[1024,64]{1,0:T(8,128)(2,1)S(1)}, u32[]{:S(2)}, u32[]{:S(2)}) collective-permute-start(bf16[1024,64]{1,0:T(8,128)(2,1)S(1)} %get-tuple-element.6), channel_id=1, source_target_pairs={{0,4},{4,8},{8,12},{12,16},{16,20},{20,24},{24,28},{1,5},{5,9},{9,... | collective-permute-start | bytes 393224 | tf_op jit(solution)/shard_map/ppermute | solution.py:17
  279.2 22.2 %collective-permute-start.64 = (bf16[1024,64]{1,0:T(8,128)(2,1)S(1)}, bf16[1024,64]{1,0:T(8,128)(2,1)}, u32[]{:S(2)}, u32[]{:S(2)}) collective-permute-start(bf16[1024,64]{1,0:T(8,128)(2,1)S(1)} %get-tuple-element.8), channel_id=1, source_target_pairs={{4,0},{8,4},{12,8},{16,12},{20,16},{24,20},{28,24},{5,1},{9,5},{13... | collective-permute-start | bytes 393224 | tf_op jit(solution)/shard_map/ppermute | solution.py:19
  282.8 18.5 %collective-permute-start.63 = (bf16[1024,64]{1,0:T(8,128)(2,1)S(1)}, bf16[1024,64]{1,0:T(8,128)(2,1)}, u32[]{:S(2)}, u32[]{:S(2)}) collective-permute-start(bf16[1024,64]{1,0:T(8,128)(2,1)S(1)} %get-tuple-element.8), channel_id=1, source_target_pairs={{0,4},{4,8},{8,12},{12,16},{16,20},{20,24},{24,28},{1,5},{5,9},{9,... | collective-permute-start | bytes 393224 | tf_op jit(solution)/shard_map/ppermute | solution.py:17
  326.0 24.6 %collective-permute-start.60 = (bf16[256,64]{1,0:T(8,128)(2,1)S(1)}, bf16[256,64]{1,0:T(8,128)(2,1)S(1)}, u32[]{:S(2)}, u32[]{:S(2)}) collective-permute-start(bf16[256,64]{1,0:T(8,128)(2,1)S(1)} %constant_dynamic-slice_fusion.5), channel_id=1, source_target_pairs={{0,16},{1,17},{2,18},{3,19},{4,20},{5,21},{6,22},{7,23},{8,24},{9,... | collective-permute-start | bytes 98312 | tf_op jit(solution)/shard_map/ppermute | solution.py:43
  327.7 43.3 %collective-permute-start.51 = (bf16[256,64]{1,0:T(8,128)(2,1)S(1)}, bf16[256,64]{1,0:T(8,128)(2,1)S(1)}, u32[]{:S(2)}, u32[]{:S(2)}) collective-permute-start(bf16[256,64]{1,0:T(8,128)(2,1)S(1)} %constant_dynamic-slice_fusion.10), channel_id=1, source_target_pairs={{0,16},{1,17},{2,18},{3,19},{4,20},{5,21},{6,22},{7,23},{8,24},{9,... | collective-permute-start | bytes 98312 | tf_op jit(solution)/shard_map/ppermute | solution.py:43
  344.8 43.6 %collective-permute-start.71 = (bf16[1024,64]{1,0:T(8,128)(2,1)}, bf16[1024,64]{1,0:T(8,128)(2,1)}, u32[]{:S(2)}, u32[]{:S(2)}) collective-permute-start(bf16[1024,64]{1,0:T(8,128)(2,1)} %get-tuple-element.17), channel_id=1, source_target_pairs={{0,4},{4,8},{8,12},{12,16},{16,20},{20,24},{24,28},{1,5},{5,9},{9,... | collective-permute-start | bytes 393224 | tf_op jit(solution)/shard_map/ppermute | solution.py:29
  349.4 40.3 %collective-permute-start.70 = (bf16[1024,64]{1,0:T(8,128)(2,1)}, bf16[1024,64]{1,0:T(8,128)(2,1)}, u32[]{:S(2)}, u32[]{:S(2)}) collective-permute-start(bf16[1024,64]{1,0:T(8,128)(2,1)} %get-tuple-element.16), channel_id=1, source_target_pairs={{4,0},{8,4},{12,8},{16,12},{20,16},{24,20},{28,24},{5,1},{9,5},{13... | collective-permute-start | bytes 393224 | tf_op jit(solution)/shard_map/ppermute | solution.py:29
  364.3 26.6 %collective-permute-start.62 = (bf16[1024,64]{1,0:T(8,128)(2,1)}, bf16[1024,64]{1,0:T(8,128)(2,1)}, u32[]{:S(2)}, u32[]{:S(2)}) collective-permute-start(bf16[1024,64]{1,0:T(8,128)(2,1)} %get-tuple-element.15), channel_id=1, source_target_pairs={{0,4},{4,8},{8,12},{12,16},{16,20},{20,24},{24,28},{1,5},{5,9},{9,... | collective-permute-start | bytes 393224 | tf_op jit(solution)/shard_map/ppermute | solution.py:29
  369.5 21.3 %collective-permute-start.61 = (bf16[1024,64]{1,0:T(8,128)(2,1)}, bf16[1024,64]{1,0:T(8,128)(2,1)}, u32[]{:S(2)}, u32[]{:S(2)}) collective-permute-start(bf16[1024,64]{1,0:T(8,128)(2,1)} %get-tuple-element.14), channel_id=1, source_target_pairs={{4,0},{8,4},{12,8},{16,12},{20,16},{24,20},{28,24},{5,1},{9,5},{13... | collective-permute-start | bytes 393224 | tf_op jit(solution)/shard_map/ppermute | solution.py:29
  (51 other events, 412.0 us)

commit v3 on v2

--- a/solution.py
+++ b/solution.py
@@ -46,20 +46,40 @@
     return held
 
 
-CHUNKS = 4
-
-
 def shards(resid, schur_inv, basis, scaling, coarse_inv, source_row, primal_idx):
     own_count = resid.shape[0]
     scale_column = scaling[:, None]
 
+    primal_source = source_row[primal_idx]
+    region = primal_source // own_count
+    offset = primal_source % own_count
+    primal_scale = scaling[primal_idx]
+    asks_previous = jnp.stack([jnp.where(region == 0, offset, 0).astype(jnp.float32), primal_scale])
+    asks_next = jnp.stack([jnp.where(region == 2, offset, 0).astype(jnp.float32), primal_scale])
+    asked_by_next = shifted(asks_previous, "sub", -1)
+    asked_by_previous = shifted(asks_next, "sub", 1)
+    own_offset = jnp.where(region == 1, offset, 0)
+
+    def primal_rows(rounded, rows, scale):
+        return (scale[:, None] * rounded[rows].astype(jnp.float32)).astype(jnp.bfloat16)
+
     def precondition(vector_in):
         rounded = vector_in.astype(jnp.bfloat16)
+        for_next = primal_rows(rounded, asked_by_next[0].astype(jnp.int32), asked_by_next[1])
+        for_previous = primal_rows(rounded, asked_by_previous[0].astype(jnp.int32), asked_by_previous[1])
+        from_previous_owner = shifted(for_next, "sub", 1)
+        from_next_owner = shifted(for_previous, "sub", -1)
+        mine = primal_rows(rounded, own_offset, primal_scale)
+        primal = jnp.where(
+            (region == 1)[:, None], mine,
+            jnp.where((region == 0)[:, None], from_previous_owner, from_next_owner),
+        )
+        primal_all = gather_all(primal)
+
         padded = with_halo(rounded, (("sub", 0),), own_count)
         gathered = padded[source_row]
         scaled = (scale_column * gathered.astype(jnp.float32)).astype(jnp.bfloat16)
-        primal = scaled[primal_idx]
-        coarse = jnp.dot(coarse_inv, gather_all(primal), preferred_element_type=jnp.float32)
+        coarse = jnp.dot(coarse_inv, primal_all, preferred_element_type=jnp.float32)
         coarse_rounded = coarse.astype(jnp.bfloat16)
         solved = jnp.dot(schur_inv, scaled, preferred_element_type=jnp.float32)
         solved = solved + lax.dot_general(
@@ -77,13 +97,9 @@
             + from_previous.astype(jnp.float32)
         )
 
-    width = resid.shape[1] // CHUNKS
-    firsts, seconds = [], []
-    for c in range(CHUNKS):
-        first = precondition(resid[:, c * width : (c + 1) * width])
-        firsts.append(first)
-        seconds.append(precondition(first))
-    return (jnp.concatenate(firsts, axis=1), jnp.concatenate(seconds, axis=1))
+    first_apply = precondition(resid)
+    second_apply = precondition(first_apply)
+    return (first_apply, second_apply)
 
 
 def solution(mesh):

time: 406 us -> 221 us (0.54); the launches traced: 398 us -> 220 us
  starting transfers between devices: 146 us -> 52.2 us
  local copies, waits for them, and re-layouts: 123 us -> 42.2 us
  waiting for transfers between devices: 54.7 us -> 100 us
  matrix products: 53.6 us -> 19.7 us
  other arithmetic: 19.6 us -> 5.09 us
    gather x8 -> x2, local copies, waits for them, and re-layouts: 54.9 us -> 15 us  [precondition(): gathered = padded[source_row]]
    ppermute x40 -> x10, starting transfers between devices: 46.1 us -> 10.2 us  [gather_all(): got = lax.ppermute(piece, AXES, [(i, i ^ span) for i in range(count)])]
    dot_general x8 -> x2, matrix products: 49.7 us -> 15 us  [precondition(): solved = jnp.dot(schur_inv, scaled, preferred_element_type=jnp.float32)]
    ppermute x8 -> x2, starting transfers between devices: 43.2 us -> 9.34 us  [with_halo(): lax.ppermute(tail, axis, [(i, (i + 1) % count) for i in range(ends)])]
    scatter x8 -> x2, local copies, waits for them, and re-layouts: 48.8 us -> 19.6 us  [precondition(): jnp.zeros((3 * own_count, weighted.shape[1]), jnp.bfloat16).at[source_row]]
    ppermute x16 -> x10, waiting for transfers between devices: 26.5 us -> 53 us  [shifted(): return lax.ppermute(shard, axis, pairs)]
    ppermute x40 -> x10, waiting for transfers between devices: 12.2 us -> 37.7 us  [gather_all(): got = lax.ppermute(piece, AXES, [(i, i ^ span) for i in range(count)])]
    ppermute x16 -> x10, starting transfers between devices: 46.2 us -> 30.1 us  [shifted(): return lax.ppermute(shard, axis, pairs)]
  transfers between devices with their start and end apart: 72 -> 24, of which waited for: 21 -> 17; matrix products, arithmetic and copies ran while one was open for 41% -> 1% of each run, Pallas kernels for 0% -> 0%
where the time goes in v3:
time: 221 us; the launch traced here: 220 us
  waiting for transfers between devices  100 us (45%)
  starting transfers between devices  52.2 us (24%)
  local copies, waits for them, and re-layouts  42.2 us (19%)
  matrix products  19.7 us (9%)
  other arithmetic  5.09 us (2%)
    ppermute x10, waiting for transfers between devices, shifted(): return lax.ppermute(shard, axis, pairs)  53 us
    ppermute x10, waiting for transfers between devices, gather_all(): got = lax.ppermute(piece, AXES, [(i, i ^ span) for i in range(count)])  37.7 us
    ppermute x10, starting transfers between devices, shifted(): return lax.ppermute(shard, axis, pairs)  30.1 us
    scatter x2, local copies, waits for them, and re-layouts, precondition(): jnp.zeros((3 * own_count, weighted.shape[1]), jnp.bfloat16).at[source_row]  19.6 us
    dot_general x2, matrix products, precondition(): solved = jnp.dot(schur_inv, scaled, preferred_element_type=jnp.float32)  15 us
    gather x2, local copies, waits for them, and re-layouts, precondition(): gathered = padded[source_row]  15 us
    ppermute x10, starting transfers between devices, gather_all(): got = lax.ppermute(piece, AXES, [(i, i ^ span) for i in range(count)])  10.2 us
    ppermute x2, waiting for transfers between devices, with_halo(): lax.ppermute(tail, axis, [(i, (i + 1) % count) for i in range(ends)])  9.43 us
  transfers between devices with their start and end apart: 24, of which 17 were waited for; matrix products, arithmetic and copies ran while one was open for 1% of the time, Pallas kernels for 0%

profile of v3, /device:TPU:0, one launch (start us, length us, event | category | flops | bytes accessed | tf_op | source)
XLA Modules:
  0.0 220.4 jit_solution(16675655806531301136)
XLA Ops:
  4.1 4.8 %collective-permute-start.4 = (f32[2,16]{1,0:T(2,128)S(1)}, f32[2,16]{1,0:T(2,128)S(1)}, u32[]{:S(2)}, u32[]{:S(2)}) collective-permute-start(f32[2,16]{1,0:T(2,128)S(1)} %get-tuple-element.12), channel_id=1, source_target_pairs={{0,4},{4,8},{8,12},{12,16},{16,20},{20,24},{24,28},{1,5},{5,9},{9,... | collective-permute-start | bytes 392 | tf_op jit(solution)/shard_map/ppermute | solution.py:29
  11.6 2.8 %collective-permute-done.2 = f32[2,16]{1,0:T(2,128)S(1)} collective-permute-done((f32[2,16]{1,0:T(2,128)S(1)}, f32[2,16]{1,0:T(2,128)S(1)}, u32[]{:S(2)}, u32[]{:S(2)}) %collective-permute-start.2) | collective-permute-done | bytes 160 | tf_op jit(solution)/shard_map/ppermute | solution.py:29
  15.7 4.3 %collective-permute-start.3 = (bf16[16,256]{1,0:T(8,128)(2,1)S(1)}, bf16[16,256]{1,0:T(8,128)(2,1)S(1)}, u32[]{:S(2)}, u32[]{:S(2)}) collective-permute-start(bf16[16,256]{1,0:T(8,128)(2,1)S(1)} %multiply_convert_fusion.8), channel_id=1, source_target_pairs={{0,4},{4,8},{8,12},{12,16},{16,20},{20,24},{24,28},{1,5},{5,9},{9,... | collective-permute-start | bytes 24584 | tf_op jit(solution)/shard_map/ppermute | solution.py:29
  22.1 3.6 %collective-permute-done.5 = bf16[16,256]{1,0:T(8,128)(2,1)S(1)} collective-permute-done((bf16[16,256]{1,0:T(8,128)(2,1)S(1)}, bf16[16,256]{1,0:T(8,128)(2,1)S(1)}, u32[]{:S(2)}, u32[]{:S(2)}) %collective-permute-start.5) | collective-permute-done | bytes 8224 | tf_op jit(solution)/shard_map/ppermute | solution.py:29
  28.5 2.2 %collective-permute-done.7 = bf16[32,256]{1,0:T(8,128)(2,1)S(1)} collective-permute-done((bf16[32,256]{1,0:T(8,128)(2,1)S(1)}, bf16[32,256]{1,0:T(8,128)(2,1)S(1)}, u32[]{:S(2)}, u32[]{:S(2)}) %collective-permute-start.7) | collective-permute-done | bytes 16416 | tf_op jit(solution)/shard_map/ppermute | solution.py:43
  32.3 2.4 %collective-permute-done.8 = bf16[64,256]{1,0:T(8,128)(2,1)S(1)} collective-permute-done((bf16[64,256]{1,0:T(8,128)(2,1)S(1)}, bf16[64,256]{1,0:T(8,128)(2,1)S(1)}, u32[]{:S(2)}, u32[]{:S(2)}) %collective-permute-start.8) | collective-permute-done | bytes 32800 | tf_op jit(solution)/shard_map/ppermute | solution.py:43
  34.7 1.6 collective-permute-start.9
  37.6 4.6 %collective-permute-start = (bf16[1024,256]{1,0:T(8,128)(2,1)S(1)}, bf16[1024,256]{1,0:T(8,128)(2,1)S(1)}, u32[]{:S(2)}, u32[]{:S(2)}) collective-permute-start(bf16[1024,256]{1,0:T(8,128)(2,1)S(1)} %convert_element_type.140), channel_id=1, source_target_pairs={{0,4},{4,8},{8,12},{12,16},{16,20},{20,24},{24,28},{1,5},{5,9},{9,... | collective-permute-start | bytes 1572872 | tf_op jit(solution)/shard_map/ppermute | solution.py:17
  43.4 12.7 %collective-permute-done.10 = bf16[256,256]{1,0:T(8,128)(2,1)S(1)} collective-permute-done((bf16[256,256]{1,0:T(8,128)(2,1)S(1)}, bf16[256,256]{1,0:T(8,128)(2,1)S(1)}, u32[]{:S(2)}, u32[]{:S(2)}) %collective-permute-start.10) | collective-permute-done | bytes 131104 | tf_op jit(solution)/shard_map/ppermute | solution.py:43
  56.1 4.6 %collective-permute-done = bf16[1024,256]{1,0:T(8,128)(2,1)S(1)} collective-permute-done((bf16[1024,256]{1,0:T(8,128)(2,1)S(1)}, bf16[1024,256]{1,0:T(8,128)(2,1)S(1)}, u32[]{:S(2)}, u32[]{:S(2)}) %collective-permute-start) | collective-permute-done | bytes 524320 | tf_op jit(solution)/shard_map/ppermute | solution.py:17
  60.9 7.5 %gather_fusion = bf16[2048,256]{1,0:T(8,128)(2,1)S(1)} fusion(bf16[3072,256]{1,0:T(8,128)(2,1)S(1)} %pad_maximum_fusion, s32[2048]{0:T(1024)S(1)} %get-tuple-element.10), kind=kCustom, calls=%fused_computation | custom fusion | bytes 2105344 | tf_op jit(solution)/shard_map/gather | solution.py:80
  68.4 7.5 %fusion.6 = f32[256,2048]{1,0:T(8,128)} fusion(bf16[2048,2048]{1,0:T(8,128)(2,1)} %param.8, bf16[2048,256]{1,0:T(8,128)(2,1)S(1)} %gather_fusion, f32[2048]{0:T(1024)S(1)} %copy-done.1), kind=kOutput, calls=%fused_computation.26 | convolution fusion | flops 2149056512 | bytes 11542528 | tf_op jit(solution)/shard_map/dot_general | solution.py:84
  76.0 2.3 %fusion.5 = bf16[2048,256]{0,1:T(8,128)(2,1)S(1)} fusion(f32[256,2048]{1,0:T(8,128)} %fusion.6, bf16[16,2048]{1,0:T(8,128)(2,1)S(1)} %copy-done, bf16[512,256]{1,0:T(8,128)(2,1)S(1)} %constant_dynamic-update-slice_fusion.5, bf16[16,512]{1,0:T(8,128)(2,1)S(1)} %copy-done.3, f32[2048]{0:T(1024)S(1)} %copy-done.1), kind=kOutput, calls=%fused_computation.19 | convolution fusion | flops 22548480 | bytes 3497984 | tf_op jit(solution)/shard_map/dot_general | solution.py:85
  78.8 9.8 %scatter_custom_fusion = bf16[3072,256]{1,0:T(8,128)(2,1)S(1)} fusion(s32[2048]{0:T(1024)S(1)} %get-tuple-element.11, bf16[2048,256]{1,0:T(8,128)(2,1)S(1)} %copy.11, bf16[]{:T(256)} %constant.102.clone.1), kind=kCustom, calls=%fused_computation.34 | custom fusion | bytes 1572866 | tf_op jit(solution)/shard_map/scatter | solution.py:90
  90.0 5.0 %collective-permute-start.12 = (bf16[1024,256]{1,0:T(8,128)(2,1)S(1)}, bf16[1024,256]{1,0:T(8,128)(2,1)S(1)}, u32[]{:S(2)}, u32[]{:S(2)}) collective-permute-start(bf16[1024,256]{1,0:T(8,128)(2,1)S(1)} %get-tuple-element.9), channel_id=1, source_target_pairs={{0,4},{4,8},{8,12},{12,16},{16,20},{20,24},{24,28},{1,5},{5,9},{9,... | collective-permute-start | bytes 1572872 | tf_op jit(solution)/shard_map/ppermute | solution.py:29
  95.0 10.1 %collective-permute-done.11 = bf16[1024,256]{1,0:T(8,128)(2,1)S(1)} collective-permute-done((bf16[1024,256]{1,0:T(8,128)(2,1)S(1)}, bf16[1024,256]{1,0:T(8,128)(2,1)S(1)}, u32[]{:S(2)}, u32[]{:S(2)}) %collective-permute-start.11) | collective-permute-done | bytes 524320 | tf_op jit(solution)/shard_map/ppermute | solution.py:29
  105.2 11.4 %collective-permute-done.12 = bf16[1024,256]{1,0:T(8,128)(2,1)S(1)} collective-permute-done((bf16[1024,256]{1,0:T(8,128)(2,1)S(1)}, bf16[1024,256]{1,0:T(8,128)(2,1)S(1)}, u32[]{:S(2)}, u32[]{:S(2)}) %collective-permute-start.12) | collective-permute-done | bytes 524320 | tf_op jit(solution)/shard_map/ppermute | solution.py:29
  119.1 4.4 %collective-permute-start.15 = (bf16[16,256]{1,0:T(8,128)(2,1)S(1)}, bf16[16,256]{1,0:T(8,128)(2,1)S(1)}, u32[]{:S(2)}, u32[]{:S(2)}) collective-permute-start(bf16[16,256]{1,0:T(8,128)(2,1)S(1)} %multiply_convert_fusion.5), channel_id=1, source_target_pairs={{0,4},{4,8},{8,12},{12,16},{16,20},{20,24},{24,28},{1,5},{5,9},{9,... | collective-permute-start | bytes 24584 | tf_op jit(solution)/shard_map/ppermute | solution.py:29
  125.4 3.6 %collective-permute-done.16 = bf16[16,256]{1,0:T(8,128)(2,1)S(1)} collective-permute-done((bf16[16,256]{1,0:T(8,128)(2,1)S(1)}, bf16[16,256]{1,0:T(8,128)(2,1)S(1)}, u32[]{:S(2)}, u32[]{:S(2)}) %collective-permute-start.16) | collective-permute-done | bytes 8224 | tf_op jit(solution)/shard_map/ppermute | solution.py:29
  130.3 1.5 collective-permute-start.18
  131.9 2.2 collective-permute-done.18
  135.0 3.0 %collective-permute-done.19 = bf16[64,256]{1,0:T(8,128)(2,1)S(1)} collective-permute-done((bf16[64,256]{1,0:T(8,128)(2,1)S(1)}, bf16[64,256]{1,0:T(8,128)(2,1)S(1)}, u32[]{:S(2)}, u32[]{:S(2)}) %collective-permute-start.19) | collective-permute-done | bytes 32800 | tf_op jit(solution)/shard_map/ppermute | solution.py:43
  139.8 4.8 %collective-permute-start.13 = (bf16[1024,256]{1,0:T(8,128)(2,1)S(1)}, bf16[1024,256]{1,0:T(8,128)(2,1)S(1)}, u32[]{:S(2)}, u32[]{:S(2)}) collective-permute-start(bf16[1024,256]{1,0:T(8,128)(2,1)S(1)} %get-tuple-element.2), channel_id=1, source_target_pairs={{0,4},{4,8},{8,12},{12,16},{16,20},{20,24},{24,28},{1,5},{5,9},{9,... | collective-permute-start | bytes 1572872 | tf_op jit(solution)/shard_map/ppermute | solution.py:17
  146.1 12.8 %collective-permute-done.21 = bf16[256,256]{1,0:T(8,128)(2,1)S(1)} collective-permute-done((bf16[256,256]{1,0:T(8,128)(2,1)S(1)}, bf16[256,256]{1,0:T(8,128)(2,1)S(1)}, u32[]{:S(2)}, u32[]{:S(2)}) %collective-permute-start.21) | collective-permute-done | bytes 131104 | tf_op jit(solution)/shard_map/ppermute | solution.py:43
  158.9 4.8 %collective-permute-done.13 = bf16[1024,256]{1,0:T(8,128)(2,1)S(1)} collective-permute-done((bf16[1024,256]{1,0:T(8,128)(2,1)S(1)}, bf16[1024,256]{1,0:T(8,128)(2,1)S(1)}, u32[]{:S(2)}, u32[]{:S(2)}) %collective-permute-start.13) | collective-permute-done | bytes 524320 | tf_op jit(solution)/shard_map/ppermute | solution.py:17
  163.8 7.5 %gather_fusion.6 = bf16[2048,256]{1,0:T(8,128)(2,1)S(1)} fusion(bf16[3072,256]{1,0:T(8,128)(2,1)S(1)} %pad_maximum_fusion.1, s32[2048]{0:T(1024)S(1)} %get-tuple-element.10), kind=kCustom, calls=%fused_computation.6 | custom fusion | bytes 2105344 | tf_op jit(solution)/shard_map/gather | solution.py:80
  171.3 7.5 %fusion.7 = f32[256,2048]{1,0:T(8,128)} fusion(bf16[2048,2048]{1,0:T(8,128)(2,1)} %param.8, bf16[2048,256]{1,0:T(8,128)(2,1)S(1)} %gather_fusion.6, f32[2048]{0:T(1024)S(1)} %copy-done.1), kind=kOutput, calls=%fused_computation.27 | convolution fusion | flops 2149056512 | bytes 11542528 | tf_op jit(solution)/shard_map/dot_general | solution.py:84
  178.8 2.3 %fusion.4 = bf16[2048,256]{0,1:T(8,128)(2,1)S(1)} fusion(f32[256,2048]{1,0:T(8,128)} %fusion.7, bf16[16,2048]{1,0:T(8,128)(2,1)S(1)} %copy-done, bf16[512,256]{1,0:T(8,128)(2,1)S(1)} %constant_dynamic-update-slice_fusion, bf16[16,512]{1,0:T(8,128)(2,1)S(1)} %copy-done.3, f32[2048]{0:T(1024)S(1)} %copy-done.1), kind=kOutput, calls=%fused_computation.18 | convolution fusion | flops 22548480 | bytes 3497984 | tf_op jit(solution)/shard_map/dot_general | solution.py:85
  181.6 9.8 %scatter_custom_fusion.1 = bf16[3072,256]{1,0:T(8,128)(2,1)S(1)} fusion(s32[2048]{0:T(1024)S(1)} %get-tuple-element.11, bf16[2048,256]{1,0:T(8,128)(2,1)S(1)} %copy.12, bf16[]{:T(256)} %constant.102.clone.1), kind=kCustom, calls=%fused_computation.32 | custom fusion | bytes 1572866 | tf_op jit(solution)/shard_map/scatter | solution.py:90
  192.8 5.0 %collective-permute-start.23 = (bf16[1024,256]{1,0:T(8,128)(2,1)S(1)}, bf16[1024,256]{1,0:T(8,128)(2,1)S(1)}, u32[]{:S(2)}, u32[]{:S(2)}) collective-permute-start(bf16[1024,256]{1,0:T(8,128)(2,1)S(1)} %get-tuple-element.7), channel_id=1, source_target_pairs={{0,4},{4,8},{8,12},{12,16},{16,20},{20,24},{24,28},{1,5},{5,9},{9,... | collective-permute-start | bytes 1572872 | tf_op jit(solution)/shard_map/ppermute | solution.py:29
  197.9 10.0 %collective-permute-done.22 = bf16[1024,256]{1,0:T(8,128)(2,1)S(1)} collective-permute-done((bf16[1024,256]{1,0:T(8,128)(2,1)S(1)}, bf16[1024,256]{1,0:T(8,128)(2,1)S(1)}, u32[]{:S(2)}, u32[]{:S(2)}) %collective-permute-start.22) | collective-permute-done | bytes 524320 | tf_op jit(solution)/shard_map/ppermute | solution.py:29
  207.9 11.4 %collective-permute-done.23 = bf16[1024,256]{1,0:T(8,128)(2,1)S(1)} collective-permute-done((bf16[1024,256]{1,0:T(8,128)(2,1)S(1)}, bf16[1024,256]{1,0:T(8,128)(2,1)S(1)}, u32[]{:S(2)}, u32[]{:S(2)}) %collective-permute-start.23) | collective-permute-done | bytes 524320 | tf_op jit(solution)/shard_map/ppermute | solution.py:29
  (91 shorter events, 31.1 us)
Async XLA Ops:
  0.6 75.3 %copy-start = (bf16[16,2048]{1,0:T(8,128)(2,1)S(1)}, bf16[16,2048]{1,0:T(8,128)(2,1)}, u32[]{:S(2)}) copy-start(bf16[16,2048]{1,0:T(8,128)(2,1)} %param.9) | copy-start | bytes 196612
  0.6 42.7 %copy-start.2 = (s32[2048]{0:T(1024)S(1)}, s32[2048]{0:T(1024)}, u32[]{:S(2)}) copy-start(s32[2048]{0:T(1024)} %param.12) | copy-start | bytes 24580
  4.1 7.5 %collective-permute-start.4 = (f32[2,16]{1,0:T(2,128)S(1)}, f32[2,16]{1,0:T(2,128)S(1)}, u32[]{:S(2)}, u32[]{:S(2)}) collective-permute-start(f32[2,16]{1,0:T(2,128)S(1)} %get-tuple-element.12), channel_id=1, source_target_pairs={{0,4},{4,8},{8,12},{12,16},{16,20},{20,24},{24,28},{1,5},{5,9},{9,... | collective-permute-start | bytes 392 | tf_op jit(solution)/shard_map/ppermute | solution.py:29
  9.0 5.5 %collective-permute-start.2 = (f32[2,16]{1,0:T(2,128)S(1)}, f32[2,16]{1,0:T(2,128)S(1)}, u32[]{:S(2)}, u32[]{:S(2)}) collective-permute-start(f32[2,16]{1,0:T(2,128)S(1)} %get-tuple-element.13), channel_id=1, source_target_pairs={{4,0},{8,4},{12,8},{16,12},{20,16},{24,20},{28,24},{5,1},{9,5},{13... | collective-permute-start | bytes 392 | tf_op jit(solution)/shard_map/ppermute | solution.py:29
  15.7 6.3 %collective-permute-start.3 = (bf16[16,256]{1,0:T(8,128)(2,1)S(1)}, bf16[16,256]{1,0:T(8,128)(2,1)S(1)}, u32[]{:S(2)}, u32[]{:S(2)}) collective-permute-start(bf16[16,256]{1,0:T(8,128)(2,1)S(1)} %multiply_convert_fusion.8), channel_id=1, source_target_pairs={{0,4},{4,8},{8,12},{12,16},{16,20},{20,24},{24,28},{1,5},{5,9},{9,... | collective-permute-start | bytes 24584 | tf_op jit(solution)/shard_map/ppermute | solution.py:29
  20.2 5.5 %collective-permute-start.5 = (bf16[16,256]{1,0:T(8,128)(2,1)S(1)}, bf16[16,256]{1,0:T(8,128)(2,1)S(1)}, u32[]{:S(2)}, u32[]{:S(2)}) collective-permute-start(bf16[16,256]{1,0:T(8,128)(2,1)S(1)} %multiply_convert_fusion.7), channel_id=1, source_target_pairs={{4,0},{8,4},{12,8},{16,12},{20,16},{24,20},{28,24},{5,1},{9,5},{13... | collective-permute-start | bytes 24584 | tf_op jit(solution)/shard_map/ppermute | solution.py:29
  25.8 1.2 collective-permute-start.6
  27.0 3.7 %collective-permute-start.7 = (bf16[32,256]{1,0:T(8,128)(2,1)S(1)}, bf16[32,256]{1,0:T(8,128)(2,1)S(1)}, u32[]{:S(2)}, u32[]{:S(2)}) collective-permute-start(bf16[32,256]{1,0:T(8,128)(2,1)S(1)} %constant_dynamic-slice_fusion.8), channel_id=1, source_target_pairs={{0,2},{1,3},{2,0},{3,1},{4,6},{5,7},{6,4},{7,5},{8,10},{9,11},{10,... | collective-permute-start | bytes 49160 | tf_op jit(solution)/shard_map/ppermute | solution.py:43
  30.8 3.9 %collective-permute-start.8 = (bf16[64,256]{1,0:T(8,128)(2,1)S(1)}, bf16[64,256]{1,0:T(8,128)(2,1)S(1)}, u32[]{:S(2)}, u32[]{:S(2)}) collective-permute-start(bf16[64,256]{1,0:T(8,128)(2,1)S(1)} %constant_dynamic-slice_fusion.7), channel_id=1, source_target_pairs={{0,4},{1,5},{2,6},{3,7},{4,0},{5,1},{6,2},{7,3},{8,12},{9,13},{10,... | collective-permute-start | bytes 98312 | tf_op jit(solution)/shard_map/ppermute | solution.py:43
  34.7 7.6 %collective-permute-start.9 = (bf16[128,256]{1,0:T(8,128)(2,1)S(1)}, bf16[128,256]{1,0:T(8,128)(2,1)S(1)}, u32[]{:S(2)}, u32[]{:S(2)}) collective-permute-start(bf16[128,256]{1,0:T(8,128)(2,1)S(1)} %constant_dynamic-slice_fusion.6), channel_id=1, source_target_pairs={{0,8},{1,9},{2,10},{3,11},{4,12},{5,13},{6,14},{7,15},{8,0},{9,1},... | collective-permute-start | bytes 196616 | tf_op jit(solution)/shard_map/ppermute | solution.py:43
  36.3 19.8 %collective-permute-start.1 = (bf16[1024,256]{1,0:T(8,128)(2,1)S(1)}, bf16[1024,256]{1,0:T(8,128)(2,1)S(1)}, u32[]{:S(2)}, u32[]{:S(2)}) collective-permute-start(bf16[1024,256]{1,0:T(8,128)(2,1)S(1)} %convert_element_type.140), channel_id=1, source_target_pairs={{4,0},{8,4},{12,8},{16,12},{20,16},{24,20},{28,24},{5,1},{9,5},{13... | collective-permute-start | bytes 1572872 | tf_op jit(solution)/shard_map/ppermute | solution.py:19
  37.6 23.2 %collective-permute-start = (bf16[1024,256]{1,0:T(8,128)(2,1)S(1)}, bf16[1024,256]{1,0:T(8,128)(2,1)S(1)}, u32[]{:S(2)}, u32[]{:S(2)}) collective-permute-start(bf16[1024,256]{1,0:T(8,128)(2,1)S(1)} %convert_element_type.140), channel_id=1, source_target_pairs={{0,4},{4,8},{8,12},{12,16},{16,20},{20,24},{24,28},{1,5},{5,9},{9,... | collective-permute-start | bytes 1572872 | tf_op jit(solution)/shard_map/ppermute | solution.py:17
  42.3 13.8 %collective-permute-start.10 = (bf16[256,256]{1,0:T(8,128)(2,1)S(1)}, bf16[256,256]{1,0:T(8,128)(2,1)S(1)}, u32[]{:S(2)}, u32[]{:S(2)}) collective-permute-start(bf16[256,256]{1,0:T(8,128)(2,1)S(1)} %constant_dynamic-slice_fusion.5), channel_id=1, source_target_pairs={{0,16},{1,17},{2,18},{3,19},{4,20},{5,21},{6,22},{7,23},{8,24},{9,... | collective-permute-start | bytes 393224 | tf_op jit(solution)/shard_map/ppermute | solution.py:43
  60.9 7.5 %copy-start.1 = (f32[2048]{0:T(1024)S(1)}, f32[2048]{0:T(1024)}, u32[]{:S(2)}) copy-start(f32[2048]{0:T(1024)} %param.10) | copy-start | bytes 24580
  68.4 7.5 %copy-start.3 = (bf16[16,512]{1,0:T(8,128)(2,1)S(1)}, bf16[16,512]{1,0:T(8,128)(2,1)}, u32[]{:S(2)}) copy-start(bf16[16,512]{1,0:T(8,128)(2,1)} %param.11) | copy-start | bytes 49156
  88.7 16.5 %collective-permute-start.11 = (bf16[1024,256]{1,0:T(8,128)(2,1)S(1)}, bf16[1024,256]{1,0:T(8,128)(2,1)S(1)}, u32[]{:S(2)}, u32[]{:S(2)}) collective-permute-start(bf16[1024,256]{1,0:T(8,128)(2,1)S(1)} %get-tuple-element.8), channel_id=1, source_target_pairs={{4,0},{8,4},{12,8},{16,12},{20,16},{24,20},{28,24},{5,1},{9,5},{13... | collective-permute-start | bytes 1572872 | tf_op jit(solution)/shard_map/ppermute | solution.py:29
  90.0 26.6 %collective-permute-start.12 = (bf16[1024,256]{1,0:T(8,128)(2,1)S(1)}, bf16[1024,256]{1,0:T(8,128)(2,1)S(1)}, u32[]{:S(2)}, u32[]{:S(2)}) collective-permute-start(bf16[1024,256]{1,0:T(8,128)(2,1)S(1)} %get-tuple-element.9), channel_id=1, source_target_pairs={{0,4},{4,8},{8,12},{12,16},{16,20},{20,24},{24,28},{1,5},{5,9},{9,... | collective-permute-start | bytes 1572872 | tf_op jit(solution)/shard_map/ppermute | solution.py:29
  119.1 6.3 %collective-permute-start.15 = (bf16[16,256]{1,0:T(8,128)(2,1)S(1)}, bf16[16,256]{1,0:T(8,128)(2,1)S(1)}, u32[]{:S(2)}, u32[]{:S(2)}) collective-permute-start(bf16[16,256]{1,0:T(8,128)(2,1)S(1)} %multiply_convert_fusion.5), channel_id=1, source_target_pairs={{0,4},{4,8},{8,12},{12,16},{16,20},{20,24},{24,28},{1,5},{5,9},{9,... | collective-permute-start | bytes 24584 | tf_op jit(solution)/shard_map/ppermute | solution.py:29
  123.5 5.5 %collective-permute-start.16 = (bf16[16,256]{1,0:T(8,128)(2,1)S(1)}, bf16[16,256]{1,0:T(8,128)(2,1)S(1)}, u32[]{:S(2)}, u32[]{:S(2)}) collective-permute-start(bf16[16,256]{1,0:T(8,128)(2,1)S(1)} %multiply_convert_fusion.4), channel_id=1, source_target_pairs={{4,0},{8,4},{12,8},{16,12},{20,16},{24,20},{28,24},{5,1},{9,5},{13... | collective-permute-start | bytes 24584 | tf_op jit(solution)/shard_map/ppermute | solution.py:29
  129.1 1.2 collective-permute-start.17
  130.3 3.7 %collective-permute-start.18 = (bf16[32,256]{1,0:T(8,128)(2,1)S(1)}, bf16[32,256]{1,0:T(8,128)(2,1)S(1)}, u32[]{:S(2)}, u32[]{:S(2)}) collective-permute-start(bf16[32,256]{1,0:T(8,128)(2,1)S(1)} %constant_dynamic-slice_fusion.3), channel_id=1, source_target_pairs={{0,2},{1,3},{2,0},{3,1},{4,6},{5,7},{6,4},{7,5},{8,10},{9,11},{10,... | collective-permute-start | bytes 49160 | tf_op jit(solution)/shard_map/ppermute | solution.py:43
  134.1 3.9 %collective-permute-start.19 = (bf16[64,256]{1,0:T(8,128)(2,1)S(1)}, bf16[64,256]{1,0:T(8,128)(2,1)S(1)}, u32[]{:S(2)}, u32[]{:S(2)}) collective-permute-start(bf16[64,256]{1,0:T(8,128)(2,1)S(1)} %constant_dynamic-slice_fusion.2), channel_id=1, source_target_pairs={{0,4},{1,5},{2,6},{3,7},{4,0},{5,1},{6,2},{7,3},{8,12},{9,13},{10,... | collective-permute-start | bytes 98312 | tf_op jit(solution)/shard_map/ppermute | solution.py:43
  138.0 6.6 %collective-permute-start.20 = (bf16[128,256]{1,0:T(8,128)(2,1)S(1)}, bf16[128,256]{1,0:T(8,128)(2,1)S(1)}, u32[]{:S(2)}, u32[]{:S(2)}) collective-permute-start(bf16[128,256]{1,0:T(8,128)(2,1)S(1)} %constant_dynamic-slice_fusion.1), channel_id=1, source_target_pairs={{0,8},{1,9},{2,10},{3,11},{4,12},{5,13},{6,14},{7,15},{8,0},{9,1},... | collective-permute-start | bytes 196616 | tf_op jit(solution)/shard_map/ppermute | solution.py:43
  138.5 20.3 %collective-permute-start.14 = (bf16[1024,256]{1,0:T(8,128)(2,1)S(1)}, bf16[1024,256]{1,0:T(8,128)(2,1)S(1)}, u32[]{:S(2)}, u32[]{:S(2)}) collective-permute-start(bf16[1024,256]{1,0:T(8,128)(2,1)S(1)} %get-tuple-element.2), channel_id=1, source_target_pairs={{4,0},{8,4},{12,8},{16,12},{20,16},{24,20},{28,24},{5,1},{9,5},{13... | collective-permute-start | bytes 1572872 | tf_op jit(solution)/shard_map/ppermute | solution.py:19
  139.8 23.8 %collective-permute-start.13 = (bf16[1024,256]{1,0:T(8,128)(2,1)S(1)}, bf16[1024,256]{1,0:T(8,128)(2,1)S(1)}, u32[]{:S(2)}, u32[]{:S(2)}) collective-permute-start(bf16[1024,256]{1,0:T(8,128)(2,1)S(1)} %get-tuple-element.2), channel_id=1, source_target_pairs={{0,4},{4,8},{8,12},{12,16},{16,20},{20,24},{24,28},{1,5},{5,9},{9,... | collective-permute-start | bytes 1572872 | tf_op jit(solution)/shard_map/ppermute | solution.py:17
  144.6 14.2 %collective-permute-start.21 = (bf16[256,256]{1,0:T(8,128)(2,1)S(1)}, bf16[256,256]{1,0:T(8,128)(2,1)S(1)}, u32[]{:S(2)}, u32[]{:S(2)}) collective-permute-start(bf16[256,256]{1,0:T(8,128)(2,1)S(1)} %constant_dynamic-slice_fusion), channel_id=1, source_target_pairs={{0,16},{1,17},{2,18},{3,19},{4,20},{5,21},{6,22},{7,23},{8,24},{9,... | collective-permute-start | bytes 393224 | tf_op jit(solution)/shard_map/ppermute | solution.py:43
  191.5 16.4 %collective-permute-start.22 = (bf16[1024,256]{1,0:T(8,128)(2,1)S(1)}, bf16[1024,256]{1,0:T(8,128)(2,1)S(1)}, u32[]{:S(2)}, u32[]{:S(2)}) collective-permute-start(bf16[1024,256]{1,0:T(8,128)(2,1)S(1)} %get-tuple-element.6), channel_id=1, source_target_pairs={{4,0},{8,4},{12,8},{16,12},{20,16},{24,20},{28,24},{5,1},{9,5},{13... | collective-permute-start | bytes 1572872 | tf_op jit(solution)/shard_map/ppermute | solution.py:29
  192.8 26.4 %collective-permute-start.23 = (bf16[1024,256]{1,0:T(8,128)(2,1)S(1)}, bf16[1024,256]{1,0:T(8,128)(2,1)S(1)}, u32[]{:S(2)}, u32[]{:S(2)}) collective-permute-start(bf16[1024,256]{1,0:T(8,128)(2,1)S(1)} %get-tuple-element.7), channel_id=1, source_target_pairs={{0,4},{4,8},{8,12},{12,16},{16,20},{20,24},{24,28},{1,5},{5,9},{9,... | collective-permute-start | bytes 1572872 | tf_op jit(solution)/shard_map/ppermute | solution.py:29

commit v4 on v2

--- a/solution.py
+++ b/solution.py
@@ -46,22 +46,23 @@
     return held
 
 
-CHUNKS = 4
-
-
 def shards(resid, schur_inv, basis, scaling, coarse_inv, source_row, primal_idx):
     own_count = resid.shape[0]
     scale_column = scaling[:, None]
+    primal_source = source_row[primal_idx]
+    primal_scale = scaling[primal_idx][:, None]
 
     def precondition(vector_in):
         rounded = vector_in.astype(jnp.bfloat16)
         padded = with_halo(rounded, (("sub", 0),), own_count)
+        primal = (primal_scale * padded[primal_source].astype(jnp.float32)).astype(jnp.bfloat16)
+        primal_all = gather_all(primal)
         gathered = padded[source_row]
         scaled = (scale_column * gathered.astype(jnp.float32)).astype(jnp.bfloat16)
-        primal = scaled[primal_idx]
-        coarse = jnp.dot(coarse_inv, gather_all(primal), preferred_element_type=jnp.float32)
+        solved = jnp.dot(schur_inv, scaled, preferred_element_type=jnp.float32)
+        solved = lax.optimization_barrier(solved)
+        coarse = jnp.dot(coarse_inv, primal_all, preferred_element_type=jnp.float32)
         coarse_rounded = coarse.astype(jnp.bfloat16)
-        solved = jnp.dot(schur_inv, scaled, preferred_element_type=jnp.float32)
         solved = solved + lax.dot_general(
             basis, coarse_rounded, (((0,), (0,)), ((), ())), preferred_element_type=jnp.float32
         )
@@ -77,13 +78,9 @@
             + from_previous.astype(jnp.float32)
         )
 
-    width = resid.shape[1] // CHUNKS
-    firsts, seconds = [], []
-    for c in range(CHUNKS):
-        first = precondition(resid[:, c * width : (c + 1) * width])
-        firsts.append(first)
-        seconds.append(precondition(first))
-    return (jnp.concatenate(firsts, axis=1), jnp.concatenate(seconds, axis=1))
+    first_apply = precondition(resid)
+    second_apply = precondition(first_apply)
+    return (first_apply, second_apply)
 
 
 def solution(mesh):

time: 406 us -> 186 us (0.46); the launches traced: 398 us -> 186 us
  starting transfers between devices: 146 us -> 38.9 us
  local copies, waits for them, and re-layouts: 123 us -> 40.4 us
  matrix products: 53.6 us -> 12.9 us
  waiting for transfers between devices: 54.7 us -> 87.6 us
  other arithmetic: 19.6 us -> 4.72 us
    gather x8 -> x4, local copies, waits for them, and re-layouts: 54.9 us -> 16.3 us  [precondition(): gathered = padded[source_row]]
    dot_general x8 -> x2, matrix products: 49.7 us -> 11.5 us  [precondition(): solved = jnp.dot(schur_inv, scaled, preferred_element_type=jnp.float32)]
    ppermute x16 -> x4, starting transfers between devices: 46.2 us -> 11.8 us  [shifted(): return lax.ppermute(shard, axis, pairs)]
    ppermute x8 -> x2, starting transfers between devices: 43.2 us -> 10.7 us  [with_halo(): lax.ppermute(tail, axis, [(i, (i + 1) % count) for i in range(ends)])]
    ppermute x40 -> x10, starting transfers between devices: 46.1 us -> 13.8 us  [gather_all(): got = lax.ppermute(piece, AXES, [(i, i ^ span) for i in range(count)])]
    scatter x8 -> x2, local copies, waits for them, and re-layouts: 48.8 us -> 19.6 us  [precondition(): jnp.zeros((3 * own_count, weighted.shape[1]), jnp.bfloat16).at[source_row]]
    ppermute x8 -> x2, waiting for transfers between devices: 4.3 us -> 17.2 us  [with_halo(): lax.ppermute(head, axis, [((i + 1) % count, i) for i in range(ends)])]
    ppermute x8 -> x2, waiting for transfers between devices: 11.7 us -> 22.8 us  [with_halo(): lax.ppermute(tail, axis, [(i, (i + 1) % count) for i in range(ends)])]
  transfers between devices with their start and end apart: 72 -> 18, of which waited for: 21 -> 15; matrix products, arithmetic and copies ran while one was open for 41% -> 16% of each run, Pallas kernels for 0% -> 0%
where the time goes in v4:
time: 186 us
  waiting for transfers between devices  87.6 us (47%)
  local copies, waits for them, and re-layouts  40.4 us (22%)
  starting transfers between devices  38.9 us (21%)
  matrix products  12.9 us (7%)
  other arithmetic  4.72 us (3%)
    ppermute x4, waiting for transfers between devices, shifted(): return lax.ppermute(shard, axis, pairs)  35.9 us
    ppermute x2, waiting for transfers between devices, with_halo(): lax.ppermute(tail, axis, [(i, (i + 1) % count) for i in range(ends)])  22.8 us
    scatter x2, local copies, waits for them, and re-layouts, precondition(): jnp.zeros((3 * own_count, weighted.shape[1]), jnp.bfloat16).at[source_row]  19.6 us
    ppermute x2, waiting for transfers between devices, with_halo(): lax.ppermute(head, axis, [((i + 1) % count, i) for i in range(ends)])  17.2 us
    gather x4, local copies, waits for them, and re-layouts, precondition(): gathered = padded[source_row]  16.3 us
    ppermute x10, starting transfers between devices, gather_all(): got = lax.ppermute(piece, AXES, [(i, i ^ span) for i in range(count)])  13.8 us
    ppermute x10, waiting for transfers between devices, gather_all(): got = lax.ppermute(piece, AXES, [(i, i ^ span) for i in range(count)])  11.8 us
    ppermute x4, starting transfers between devices, shifted(): return lax.ppermute(shard, axis, pairs)  11.8 us
  transfers between devices with their start and end apart: 18, of which 15 were waited for; matrix products, arithmetic and copies ran while one was open for 16% of the time, Pallas kernels for 0%

profile of v4, /device:TPU:0, one launch (start us, length us, event | category | flops | bytes accessed | tf_op | source)
XLA Modules:
  0.0 185.6 jit_solution(14988413243228633612)
XLA Ops:
  0.7 1.3 convert_element_type.62
  3.3 5.5 %collective-permute-start = (bf16[1024,256]{1,0:T(8,128)(2,1)S(1)}, bf16[1024,256]{1,0:T(8,128)(2,1)S(1)}, u32[]{:S(2)}, u32[]{:S(2)}) collective-permute-start(bf16[1024,256]{1,0:T(8,128)(2,1)S(1)} %convert_element_type.62), channel_id=1, source_target_pairs={{0,4},{4,8},{8,12},{12,16},{16,20},{20,24},{24,28},{1,5},{5,9},{9,... | collective-permute-start | bytes 1572872 | tf_op jit(solution)/shard_map/ppermute | solution.py:17
  9.5 1.4 gather_fusion.1
  11.5 7.2 %collective-permute-done.1 = bf16[1024,256]{1,0:T(8,128)(2,1)S(1)} collective-permute-done((bf16[1024,256]{1,0:T(8,128)(2,1)S(1)}, bf16[1024,256]{1,0:T(8,128)(2,1)S(1)}, u32[]{:S(2)}, u32[]{:S(2)}) %collective-permute-start.1) | collective-permute-done | bytes 524320 | tf_op jit(solution)/shard_map/ppermute | solution.py:19
  18.7 11.4 %collective-permute-done = bf16[1024,256]{1,0:T(8,128)(2,1)S(1)} collective-permute-done((bf16[1024,256]{1,0:T(8,128)(2,1)S(1)}, bf16[1024,256]{1,0:T(8,128)(2,1)S(1)}, u32[]{:S(2)}, u32[]{:S(2)}) %collective-permute-start) | collective-permute-done | bytes 524320 | tf_op jit(solution)/shard_map/ppermute | solution.py:17
  32.1 1.5 collective-permute-start.3
  33.7 2.2 %collective-permute-done.3 = bf16[32,256]{1,0:T(8,128)(2,1)S(1)} collective-permute-done((bf16[32,256]{1,0:T(8,128)(2,1)S(1)}, bf16[32,256]{1,0:T(8,128)(2,1)S(1)}, u32[]{:S(2)}, u32[]{:S(2)}) %collective-permute-start.3) | collective-permute-done | bytes 16416 | tf_op jit(solution)/shard_map/ppermute | solution.py:43
  35.9 2.5 %collective-permute-start.4 = (bf16[64,256]{1,0:T(8,128)(2,1)S(1)}, bf16[64,256]{1,0:T(8,128)(2,1)S(1)}, u32[]{:S(2)}, u32[]{:S(2)}) collective-permute-start(bf16[64,256]{1,0:T(8,128)(2,1)S(1)} %constant_dynamic-slice_fusion.7), channel_id=1, source_target_pairs={{0,4},{1,5},{2,6},{3,7},{4,0},{5,1},{6,2},{7,3},{8,12},{9,13},{10,... | collective-permute-start | bytes 98312 | tf_op jit(solution)/shard_map/ppermute | solution.py:43
  38.4 1.9 %collective-permute-done.4 = bf16[64,256]{1,0:T(8,128)(2,1)S(1)} collective-permute-done((bf16[64,256]{1,0:T(8,128)(2,1)S(1)}, bf16[64,256]{1,0:T(8,128)(2,1)S(1)}, u32[]{:S(2)}, u32[]{:S(2)}) %collective-permute-start.4) | collective-permute-done | bytes 32800 | tf_op jit(solution)/shard_map/ppermute | solution.py:43
  40.3 1.6 collective-permute-start.5
  41.9 7.5 %gather_fusion = bf16[2048,256]{1,0:T(8,128)(2,1)S(1)} fusion(bf16[3072,256]{1,0:T(8,128)(2,1)S(1)} %pad_maximum_fusion, s32[2048]{0:T(1024)S(1)} %get-tuple-element.8), kind=kCustom, calls=%fused_computation | custom fusion | bytes 2105344 | tf_op jit(solution)/shard_map/gather | solution.py:60
  50.1 2.3 %collective-permute-start.6 = (bf16[256,256]{1,0:T(8,128)(2,1)S(1)}, bf16[256,256]{1,0:T(8,128)(2,1)S(1)}, u32[]{:S(2)}, u32[]{:S(2)}) collective-permute-start(bf16[256,256]{1,0:T(8,128)(2,1)S(1)} %constant_dynamic-slice_fusion.5), channel_id=1, source_target_pairs={{0,16},{1,17},{2,18},{3,19},{4,20},{5,21},{6,22},{7,23},{8,24},{9,... | collective-permute-start | bytes 393224 | tf_op jit(solution)/shard_map/ppermute | solution.py:43
  52.4 5.7 %convolution_bitcast_fusion.3 = f32[2048,256]{0,1:T(8,128)S(1)} fusion(bf16[2048,2048]{1,0:T(8,128)(2,1)} %param.8, bf16[2048,256]{0,1:T(8,128)(2,1)S(1)} %copy.11, f32[2048]{0:T(1024)S(1)} %copy-done.1), kind=kOutput, calls=%fused_computation.15 | convolution fusion | flops 2149056512 | bytes 11542528 | tf_op jit(solution)/shard_map/dot_general | solution.py:62
  59.5 9.8 %scatter_custom_fusion = bf16[3072,256]{1,0:T(8,128)(2,1)S(1)} fusion(s32[2048]{0:T(1024)S(1)} %get-tuple-element.9, bf16[2048,256]{1,0:T(8,128)(2,1)S(1)} %copy.12, bf16[]{:T(256)} %constant.76.clone.1), kind=kCustom, calls=%fused_computation.30 | custom fusion | bytes 1572866 | tf_op jit(solution)/shard_map/scatter | solution.py:71
  69.4 1.3 collective-permute-start.7
  70.7 4.6 %collective-permute-start.8 = (bf16[1024,256]{1,0:T(8,128)(2,1)S(1)}, bf16[1024,256]{1,0:T(8,128)(2,1)S(1)}, u32[]{:S(2)}, u32[]{:S(2)}) collective-permute-start(bf16[1024,256]{1,0:T(8,128)(2,1)S(1)} %get-tuple-element.7), channel_id=1, source_target_pairs={{0,4},{4,8},{8,12},{12,16},{16,20},{20,24},{24,28},{1,5},{5,9},{9,... | collective-permute-start | bytes 1572872 | tf_op jit(solution)/shard_map/ppermute | solution.py:29
  75.3 7.1 %collective-permute-done.7 = bf16[1024,256]{1,0:T(8,128)(2,1)S(1)} collective-permute-done((bf16[1024,256]{1,0:T(8,128)(2,1)S(1)}, bf16[1024,256]{1,0:T(8,128)(2,1)S(1)}, u32[]{:S(2)}, u32[]{:S(2)}) %collective-permute-start.7) | collective-permute-done | bytes 524320 | tf_op jit(solution)/shard_map/ppermute | solution.py:29
  82.4 10.8 %collective-permute-done.8 = bf16[1024,256]{1,0:T(8,128)(2,1)S(1)} collective-permute-done((bf16[1024,256]{1,0:T(8,128)(2,1)S(1)}, bf16[1024,256]{1,0:T(8,128)(2,1)S(1)}, u32[]{:S(2)}, u32[]{:S(2)}) %collective-permute-start.8) | collective-permute-done | bytes 524320 | tf_op jit(solution)/shard_map/ppermute | solution.py:29
  95.7 5.2 %collective-permute-start.9 = (bf16[1024,256]{1,0:T(8,128)(2,1)S(1)}, bf16[1024,256]{1,0:T(8,128)(2,1)S(1)}, u32[]{:S(2)}, u32[]{:S(2)}) collective-permute-start(bf16[1024,256]{1,0:T(8,128)(2,1)S(1)} %get-tuple-element.2), channel_id=1, source_target_pairs={{0,4},{4,8},{8,12},{12,16},{16,20},{20,24},{24,28},{1,5},{5,9},{9,... | collective-permute-start | bytes 1572872 | tf_op jit(solution)/shard_map/ppermute | solution.py:17
  100.9 10.0 %collective-permute-done.10 = bf16[1024,256]{1,0:T(8,128)(2,1)S(1)} collective-permute-done((bf16[1024,256]{1,0:T(8,128)(2,1)S(1)}, bf16[1024,256]{1,0:T(8,128)(2,1)S(1)}, u32[]{:S(2)}, u32[]{:S(2)}) %collective-permute-start.10) | collective-permute-done | bytes 524320 | tf_op jit(solution)/shard_map/ppermute | solution.py:19
  110.9 11.4 %collective-permute-done.9 = bf16[1024,256]{1,0:T(8,128)(2,1)S(1)} collective-permute-done((bf16[1024,256]{1,0:T(8,128)(2,1)S(1)}, bf16[1024,256]{1,0:T(8,128)(2,1)S(1)}, u32[]{:S(2)}, u32[]{:S(2)}) %collective-permute-start.9) | collective-permute-done | bytes 524320 | tf_op jit(solution)/shard_map/ppermute | solution.py:17
  124.3 1.5 collective-permute-start.12
  125.8 2.2 %collective-permute-done.12 = bf16[32,256]{1,0:T(8,128)(2,1)S(1)} collective-permute-done((bf16[32,256]{1,0:T(8,128)(2,1)S(1)}, bf16[32,256]{1,0:T(8,128)(2,1)S(1)}, u32[]{:S(2)}, u32[]{:S(2)}) %collective-permute-start.12) | collective-permute-done | bytes 16416 | tf_op jit(solution)/shard_map/ppermute | solution.py:43
  128.0 2.5 %collective-permute-start.13 = (bf16[64,256]{1,0:T(8,128)(2,1)S(1)}, bf16[64,256]{1,0:T(8,128)(2,1)S(1)}, u32[]{:S(2)}, u32[]{:S(2)}) collective-permute-start(bf16[64,256]{1,0:T(8,128)(2,1)S(1)} %constant_dynamic-slice_fusion.2), channel_id=1, source_target_pairs={{0,4},{1,5},{2,6},{3,7},{4,0},{5,1},{6,2},{7,3},{8,12},{9,13},{10,... | collective-permute-start | bytes 98312 | tf_op jit(solution)/shard_map/ppermute | solution.py:43
  130.5 1.9 %collective-permute-done.13 = bf16[64,256]{1,0:T(8,128)(2,1)S(1)} collective-permute-done((bf16[64,256]{1,0:T(8,128)(2,1)S(1)}, bf16[64,256]{1,0:T(8,128)(2,1)S(1)}, u32[]{:S(2)}, u32[]{:S(2)}) %collective-permute-start.13) | collective-permute-done | bytes 32800 | tf_op jit(solution)/shard_map/ppermute | solution.py:43
  132.4 1.7 collective-permute-start.14
  134.2 7.5 %gather_fusion.4 = bf16[2048,256]{1,0:T(8,128)(2,1)S(1)} fusion(bf16[3072,256]{1,0:T(8,128)(2,1)S(1)} %pad_maximum_fusion.1, s32[2048]{0:T(1024)S(1)} %get-tuple-element.8), kind=kCustom, calls=%fused_computation.4 | custom fusion | bytes 2105344 | tf_op jit(solution)/shard_map/gather | solution.py:60
  142.5 5.7 %convolution_bitcast_fusion.1 = f32[2048,256]{0,1:T(8,128)S(1)} fusion(bf16[2048,2048]{1,0:T(8,128)(2,1)} %param.8, bf16[2048,256]{0,1:T(8,128)(2,1)S(1)} %copy.13, f32[2048]{0:T(1024)S(1)} %copy-done.1), kind=kOutput, calls=%fused_computation.11 | convolution fusion | flops 2149056512 | bytes 11542528 | tf_op jit(solution)/shard_map/dot_general | solution.py:62
  150.8 9.8 %scatter_custom_fusion.1 = bf16[3072,256]{1,0:T(8,128)(2,1)S(1)} fusion(s32[2048]{0:T(1024)S(1)} %get-tuple-element.9, bf16[2048,256]{1,0:T(8,128)(2,1)S(1)} %copy.14, bf16[]{:T(256)} %constant.76.clone.1), kind=kCustom, calls=%fused_computation.28 | custom fusion | bytes 1572866 | tf_op jit(solution)/shard_map/scatter | solution.py:71
  161.9 4.6 %collective-permute-start.17 = (bf16[1024,256]{1,0:T(8,128)(2,1)S(1)}, bf16[1024,256]{1,0:T(8,128)(2,1)S(1)}, u32[]{:S(2)}, u32[]{:S(2)}) collective-permute-start(bf16[1024,256]{1,0:T(8,128)(2,1)S(1)} %get-tuple-element.5), channel_id=1, source_target_pairs={{0,4},{4,8},{8,12},{12,16},{16,20},{20,24},{24,28},{1,5},{5,9},{9,... | collective-permute-start | bytes 1572872 | tf_op jit(solution)/shard_map/ppermute | solution.py:29
  166.5 6.5 %collective-permute-done.16 = bf16[1024,256]{1,0:T(8,128)(2,1)S(1)} collective-permute-done((bf16[1024,256]{1,0:T(8,128)(2,1)S(1)}, bf16[1024,256]{1,0:T(8,128)(2,1)S(1)}, u32[]{:S(2)}, u32[]{:S(2)}) %collective-permute-start.16) | collective-permute-done | bytes 524320 | tf_op jit(solution)/shard_map/ppermute | solution.py:29
  173.1 11.4 %collective-permute-done.17 = bf16[1024,256]{1,0:T(8,128)(2,1)S(1)} collective-permute-done((bf16[1024,256]{1,0:T(8,128)(2,1)S(1)}, bf16[1024,256]{1,0:T(8,128)(2,1)S(1)}, u32[]{:S(2)}, u32[]{:S(2)}) %collective-permute-start.17) | collective-permute-done | bytes 524320 | tf_op jit(solution)/shard_map/ppermute | solution.py:29
  (64 shorter events, 17.0 us)
Async XLA Ops:
  0.6 57.6 %copy-start = (bf16[16,2048]{1,0:T(8,128)(2,1)S(1)}, bf16[16,2048]{1,0:T(8,128)(2,1)}, u32[]{:S(2)}) copy-start(bf16[16,2048]{1,0:T(8,128)(2,1)} %param.9) | copy-start | bytes 196612
  0.6 10.2 %copy-start.2 = (s32[2048]{0:T(1024)S(1)}, s32[2048]{0:T(1024)}, u32[]{:S(2)}) copy-start(s32[2048]{0:T(1024)} %param.12) | copy-start | bytes 24580
  2.0 16.8 %collective-permute-start.1 = (bf16[1024,256]{1,0:T(8,128)(2,1)S(1)}, bf16[1024,256]{1,0:T(8,128)(2,1)S(1)}, u32[]{:S(2)}, u32[]{:S(2)}) collective-permute-start(bf16[1024,256]{1,0:T(8,128)(2,1)S(1)} %convert_element_type.62), channel_id=1, source_target_pairs={{4,0},{8,4},{12,8},{16,12},{20,16},{24,20},{28,24},{5,1},{9,5},{13... | collective-permute-start | bytes 1572872 | tf_op jit(solution)/shard_map/ppermute | solution.py:19
  3.3 26.8 %collective-permute-start = (bf16[1024,256]{1,0:T(8,128)(2,1)S(1)}, bf16[1024,256]{1,0:T(8,128)(2,1)S(1)}, u32[]{:S(2)}, u32[]{:S(2)}) collective-permute-start(bf16[1024,256]{1,0:T(8,128)(2,1)S(1)} %convert_element_type.62), channel_id=1, source_target_pairs={{0,4},{4,8},{8,12},{12,16},{16,20},{20,24},{24,28},{1,5},{5,9},{9,... | collective-permute-start | bytes 1572872 | tf_op jit(solution)/shard_map/ppermute | solution.py:17
  30.9 1.2 collective-permute-start.2
  32.1 3.7 %collective-permute-start.3 = (bf16[32,256]{1,0:T(8,128)(2,1)S(1)}, bf16[32,256]{1,0:T(8,128)(2,1)S(1)}, u32[]{:S(2)}, u32[]{:S(2)}) collective-permute-start(bf16[32,256]{1,0:T(8,128)(2,1)S(1)} %constant_dynamic-slice_fusion.8), channel_id=1, source_target_pairs={{0,2},{1,3},{2,0},{3,1},{4,6},{5,7},{6,4},{7,5},{8,10},{9,11},{10,... | collective-permute-start | bytes 49160 | tf_op jit(solution)/shard_map/ppermute | solution.py:43
  35.9 4.4 %collective-permute-start.4 = (bf16[64,256]{1,0:T(8,128)(2,1)S(1)}, bf16[64,256]{1,0:T(8,128)(2,1)S(1)}, u32[]{:S(2)}, u32[]{:S(2)}) collective-permute-start(bf16[64,256]{1,0:T(8,128)(2,1)S(1)} %constant_dynamic-slice_fusion.7), channel_id=1, source_target_pairs={{0,4},{1,5},{2,6},{3,7},{4,0},{5,1},{6,2},{7,3},{8,12},{9,13},{10,... | collective-permute-start | bytes 98312 | tf_op jit(solution)/shard_map/ppermute | solution.py:43
  40.3 9.8 %collective-permute-start.5 = (bf16[128,256]{1,0:T(8,128)(2,1)S(1)}, bf16[128,256]{1,0:T(8,128)(2,1)S(1)}, u32[]{:S(2)}, u32[]{:S(2)}) collective-permute-start(bf16[128,256]{1,0:T(8,128)(2,1)S(1)} %constant_dynamic-slice_fusion.6), channel_id=1, source_target_pairs={{0,8},{1,9},{2,10},{3,11},{4,12},{5,13},{6,14},{7,15},{8,0},{9,1},... | collective-permute-start | bytes 196616 | tf_op jit(solution)/shard_map/ppermute | solution.py:43
  49.4 3.0 %copy-start.1 = (f32[2048]{0:T(1024)S(1)}, f32[2048]{0:T(1024)}, u32[]{:S(2)}) copy-start(f32[2048]{0:T(1024)} %param.10) | copy-start | bytes 24580
  50.1 8.1 %copy-start.3 = (bf16[16,512]{1,0:T(8,128)(2,1)S(1)}, bf16[16,512]{1,0:T(8,128)(2,1)}, u32[]{:S(2)}) copy-start(bf16[16,512]{1,0:T(8,128)(2,1)} %param.11) | copy-start | bytes 49156
  50.1 8.0 %collective-permute-start.6 = (bf16[256,256]{1,0:T(8,128)(2,1)S(1)}, bf16[256,256]{1,0:T(8,128)(2,1)S(1)}, u32[]{:S(2)}, u32[]{:S(2)}) collective-permute-start(bf16[256,256]{1,0:T(8,128)(2,1)S(1)} %constant_dynamic-slice_fusion.5), channel_id=1, source_target_pairs={{0,16},{1,17},{2,18},{3,19},{4,20},{5,21},{6,22},{7,23},{8,24},{9,... | collective-permute-start | bytes 393224 | tf_op jit(solution)/shard_map/ppermute | solution.py:43
  69.4 13.0 %collective-permute-start.7 = (bf16[1024,256]{1,0:T(8,128)(2,1)S(1)}, bf16[1024,256]{1,0:T(8,128)(2,1)S(1)}, u32[]{:S(2)}, u32[]{:S(2)}) collective-permute-start(bf16[1024,256]{1,0:T(8,128)(2,1)S(1)} %get-tuple-element.6), channel_id=1, source_target_pairs={{4,0},{8,4},{12,8},{16,12},{20,16},{24,20},{28,24},{5,1},{9,5},{13... | collective-permute-start | bytes 1572872 | tf_op jit(solution)/shard_map/ppermute | solution.py:29
  70.7 22.5 %collective-permute-start.8 = (bf16[1024,256]{1,0:T(8,128)(2,1)S(1)}, bf16[1024,256]{1,0:T(8,128)(2,1)S(1)}, u32[]{:S(2)}, u32[]{:S(2)}) collective-permute-start(bf16[1024,256]{1,0:T(8,128)(2,1)S(1)} %get-tuple-element.7), channel_id=1, source_target_pairs={{0,4},{4,8},{8,12},{12,16},{16,20},{20,24},{24,28},{1,5},{5,9},{9,... | collective-permute-start | bytes 1572872 | tf_op jit(solution)/shard_map/ppermute | solution.py:29
  94.4 16.5 %collective-permute-start.10 = (bf16[1024,256]{1,0:T(8,128)(2,1)S(1)}, bf16[1024,256]{1,0:T(8,128)(2,1)S(1)}, u32[]{:S(2)}, u32[]{:S(2)}) collective-permute-start(bf16[1024,256]{1,0:T(8,128)(2,1)S(1)} %get-tuple-element.2), channel_id=1, source_target_pairs={{4,0},{8,4},{12,8},{16,12},{20,16},{24,20},{28,24},{5,1},{9,5},{13... | collective-permute-start | bytes 1572872 | tf_op jit(solution)/shard_map/ppermute | solution.py:19
  95.7 26.6 %collective-permute-start.9 = (bf16[1024,256]{1,0:T(8,128)(2,1)S(1)}, bf16[1024,256]{1,0:T(8,128)(2,1)S(1)}, u32[]{:S(2)}, u32[]{:S(2)}) collective-permute-start(bf16[1024,256]{1,0:T(8,128)(2,1)S(1)} %get-tuple-element.2), channel_id=1, source_target_pairs={{0,4},{4,8},{8,12},{12,16},{16,20},{20,24},{24,28},{1,5},{5,9},{9,... | collective-permute-start | bytes 1572872 | tf_op jit(solution)/shard_map/ppermute | solution.py:17
  123.1 1.2 collective-permute-start.11
  124.3 3.7 %collective-permute-start.12 = (bf16[32,256]{1,0:T(8,128)(2,1)S(1)}, bf16[32,256]{1,0:T(8,128)(2,1)S(1)}, u32[]{:S(2)}, u32[]{:S(2)}) collective-permute-start(bf16[32,256]{1,0:T(8,128)(2,1)S(1)} %constant_dynamic-slice_fusion.3), channel_id=1, source_target_pairs={{0,2},{1,3},{2,0},{3,1},{4,6},{5,7},{6,4},{7,5},{8,10},{9,11},{10,... | collective-permute-start | bytes 49160 | tf_op jit(solution)/shard_map/ppermute | solution.py:43
  128.0 4.4 %collective-permute-start.13 = (bf16[64,256]{1,0:T(8,128)(2,1)S(1)}, bf16[64,256]{1,0:T(8,128)(2,1)S(1)}, u32[]{:S(2)}, u32[]{:S(2)}) collective-permute-start(bf16[64,256]{1,0:T(8,128)(2,1)S(1)} %constant_dynamic-slice_fusion.2), channel_id=1, source_target_pairs={{0,4},{1,5},{2,6},{3,7},{4,0},{5,1},{6,2},{7,3},{8,12},{9,13},{10,... | collective-permute-start | bytes 98312 | tf_op jit(solution)/shard_map/ppermute | solution.py:43
  132.4 9.9 %collective-permute-start.14 = (bf16[128,256]{1,0:T(8,128)(2,1)S(1)}, bf16[128,256]{1,0:T(8,128)(2,1)S(1)}, u32[]{:S(2)}, u32[]{:S(2)}) collective-permute-start(bf16[128,256]{1,0:T(8,128)(2,1)S(1)} %constant_dynamic-slice_fusion.1), channel_id=1, source_target_pairs={{0,8},{1,9},{2,10},{3,11},{4,12},{5,13},{6,14},{7,15},{8,0},{9,1},... | collective-permute-start | bytes 196616 | tf_op jit(solution)/shard_map/ppermute | solution.py:43
  142.4 7.1 %collective-permute-start.15 = (bf16[256,256]{1,0:T(8,128)(2,1)S(1)}, bf16[256,256]{1,0:T(8,128)(2,1)S(1)}, u32[]{:S(2)}, u32[]{:S(2)}) collective-permute-start(bf16[256,256]{1,0:T(8,128)(2,1)S(1)} %constant_dynamic-slice_fusion), channel_id=1, source_target_pairs={{0,16},{1,17},{2,18},{3,19},{4,20},{5,21},{6,22},{7,23},{8,24},{9,... | collective-permute-start | bytes 393224 | tf_op jit(solution)/shard_map/ppermute | solution.py:43
  160.6 12.4 %collective-permute-start.16 = (bf16[1024,256]{1,0:T(8,128)(2,1)S(1)}, bf16[1024,256]{1,0:T(8,128)(2,1)S(1)}, u32[]{:S(2)}, u32[]{:S(2)}) collective-permute-start(bf16[1024,256]{1,0:T(8,128)(2,1)S(1)} %get-tuple-element.4), channel_id=1, source_target_pairs={{4,0},{8,4},{12,8},{16,12},{20,16},{24,20},{28,24},{5,1},{9,5},{13... | collective-permute-start | bytes 1572872 | tf_op jit(solution)/shard_map/ppermute | solution.py:29
  161.9 22.5 %collective-permute-start.17 = (bf16[1024,256]{1,0:T(8,128)(2,1)S(1)}, bf16[1024,256]{1,0:T(8,128)(2,1)S(1)}, u32[]{:S(2)}, u32[]{:S(2)}) collective-permute-start(bf16[1024,256]{1,0:T(8,128)(2,1)S(1)} %get-tuple-element.5), channel_id=1, source_target_pairs={{0,4},{4,8},{8,12},{12,16},{16,20},{20,24},{24,28},{1,5},{5,9},{9,... | collective-permute-start | bytes 1572872 | tf_op jit(solution)/shard_map/ppermute | solution.py:29

commit v5 on v4

--- a/solution.py
+++ b/solution.py
@@ -52,13 +52,27 @@
     primal_source = source_row[primal_idx]
     primal_scale = scaling[primal_idx][:, None]
 
+    picks = [
+        (source_row[:, None] == (region * own_count + jnp.arange(own_count))[None, :]).astype(jnp.bfloat16)
+        for region in range(3)
+    ]
+    places = [
+        ((region * own_count + jnp.arange(own_count))[:, None] == source_row[None, :]).astype(jnp.bfloat16)
+        for region in range(3)
+    ]
+
+    def select(matrix, rows):
+        return jnp.dot(matrix, rows, preferred_element_type=jnp.float32)
+
     def precondition(vector_in):
         rounded = vector_in.astype(jnp.bfloat16)
         padded = with_halo(rounded, (("sub", 0),), own_count)
+        before = padded[:own_count]
+        after = padded[2 * own_count :]
         primal = (primal_scale * padded[primal_source].astype(jnp.float32)).astype(jnp.bfloat16)
         primal_all = gather_all(primal)
-        gathered = padded[source_row]
-        scaled = (scale_column * gathered.astype(jnp.float32)).astype(jnp.bfloat16)
+        gathered = select(picks[1], rounded) + select(picks[0], before) + select(picks[2], after)
+        scaled = (scale_column * gathered).astype(jnp.bfloat16)
         solved = jnp.dot(schur_inv, scaled, preferred_element_type=jnp.float32)
         solved = lax.optimization_barrier(solved)
         coarse = jnp.dot(coarse_inv, primal_all, preferred_element_type=jnp.float32)
@@ -67,13 +81,13 @@
             basis, coarse_rounded, (((0,), (0,)), ((), ())), preferred_element_type=jnp.float32
         )
         weighted = (scale_column * solved).astype(jnp.bfloat16)
-        spread = (
-            jnp.zeros((3 * own_count, weighted.shape[1]), jnp.bfloat16).at[source_row].set(weighted)
-        )
-        from_next = shifted(spread[:own_count], "sub", -1)
-        from_previous = shifted(spread[2 * own_count :], "sub", 1)
+        to_previous = select(places[0], weighted).astype(jnp.bfloat16)
+        to_next = select(places[2], weighted).astype(jnp.bfloat16)
+        from_next = shifted(to_previous, "sub", -1)
+        from_previous = shifted(to_next, "sub", 1)
+        kept = select(places[1], weighted).astype(jnp.bfloat16)
         return (
-            spread[own_count : 2 * own_count].astype(jnp.float32)
+            kept.astype(jnp.float32)
             + from_next.astype(jnp.float32)
             + from_previous.astype(jnp.float32)
         )

time: 186 us -> 172 us (0.925)
  local copies, waits for them, and re-layouts: 40.4 us -> 3.43 us
  matrix products: 12.9 us -> 41.9 us
  waiting for transfers between devices: 87.6 us -> 83.8 us
  other arithmetic: 4.72 us -> 2.36 us
    dot_general x0 -> x10, matrix products: none -> 23.1 us  [select(): return jnp.dot(matrix, rows, preferred_element_type=jnp.float32)]
    scatter x2 -> x0, local copies, waits for them, and re-layouts: 19.6 us -> none  [precondition(): jnp.zeros((3 * own_count, weighted.shape[1]), jnp.bfloat16).at[source_row]]
    gather x4 -> x0, local copies, waits for them, and re-layouts: 16.3 us -> none  [precondition(): gathered = padded[source_row]]
    dot_general x2, matrix products: 11.5 us -> 17.4 us  [precondition(): solved = jnp.dot(schur_inv, scaled, preferred_element_type=jnp.float32)]
    ppermute x10, waiting for transfers between devices: 11.8 us -> 7.41 us  [gather_all(): got = lax.ppermute(piece, AXES, [(i, i ^ span) for i in range(count)])]
  transfers between devices with their start and end apart: 18 -> 18, of which waited for: 15 -> 12; matrix products, arithmetic and copies ran while one was open for 16% -> 19% of each run, Pallas kernels for 0% -> 0%
where the time goes in v5:
time: 172 us; the launch traced here: 171 us
  waiting for transfers between devices  83.8 us (49%)
  matrix products  41.9 us (24%)
  starting transfers between devices  38.8 us (23%)
  local copies, waits for them, and re-layouts  3.43 us (2%)
  other arithmetic  2.36 us (1%)
    ppermute x4, waiting for transfers between devices, shifted(): return lax.ppermute(shard, axis, pairs)  36.2 us
    dot_general x10, matrix products, select(): return jnp.dot(matrix, rows, preferred_element_type=jnp.float32)  23.1 us
    ppermute x2, waiting for transfers between devices, with_halo(): lax.ppermute(tail, axis, [(i, (i + 1) % count) for i in range(ends)])  22.8 us
    ppermute x2, waiting for transfers between devices, with_halo(): lax.ppermute(head, axis, [((i + 1) % count, i) for i in range(ends)])  17.4 us
    dot_general x2, matrix products, precondition(): solved = jnp.dot(schur_inv, scaled, preferred_element_type=jnp.float32)  17.4 us
    ppermute x10, starting transfers between devices, gather_all(): got = lax.ppermute(piece, AXES, [(i, i ^ span) for i in range(count)])  13.7 us
    ppermute x4, starting transfers between devices, shifted(): return lax.ppermute(shard, axis, pairs)  11.9 us
    ppermute x2, starting transfers between devices, with_halo(): lax.ppermute(tail, axis, [(i, (i + 1) % count) for i in range(ends)])  10.5 us
  transfers between devices with their start and end apart: 18, of which 12 were waited for; matrix products, arithmetic and copies ran while one was open for 19% of the time, Pallas kernels for 0%

profile of v5, /device:TPU:0, one launch (start us, length us, event | category | flops | bytes accessed | tf_op | source)
XLA Modules:
  0.0 171.1 jit_solution(5767908734237549445)
XLA Ops:
  3.3 5.5 %collective-permute-start = (bf16[1024,256]{1,0:T(8,128)(2,1)S(1)}, bf16[1024,256]{1,0:T(8,128)(2,1)S(1)}, u32[]{:S(2)}, u32[]{:S(2)}) collective-permute-start(bf16[1024,256]{1,0:T(8,128)(2,1)S(1)} %convert_element_type.80), channel_id=1, source_target_pairs={{0,4},{4,8},{8,12},{12,16},{16,20},{20,24},{24,28},{1,5},{5,9},{9,... | collective-permute-start | bytes 1572872 | tf_op jit(solution)/shard_map/ppermute | solution.py:17
  9.5 1.4 gather_fusion
  11.5 7.2 %collective-permute-done.1 = bf16[1024,256]{1,0:T(8,128)(2,1)S(1)} collective-permute-done((bf16[1024,256]{1,0:T(8,128)(2,1)S(1)}, bf16[1024,256]{1,0:T(8,128)(2,1)S(1)}, u32[]{:S(2)}, u32[]{:S(2)}) %collective-permute-start.1) | collective-permute-done | bytes 524320 | tf_op jit(solution)/shard_map/ppermute | solution.py:19
  18.7 11.4 %collective-permute-done = bf16[1024,256]{1,0:T(8,128)(2,1)S(1)} collective-permute-done((bf16[1024,256]{1,0:T(8,128)(2,1)S(1)}, bf16[1024,256]{1,0:T(8,128)(2,1)S(1)}, u32[]{:S(2)}, u32[]{:S(2)}) %collective-permute-start) | collective-permute-done | bytes 524320 | tf_op jit(solution)/shard_map/ppermute | solution.py:17
  32.1 1.5 collective-permute-start.3
  33.7 3.1 %fusion.10 = f32[2048,256]{0,1:T(8,128)} fusion(bf16[1024,256]{1,0:T(8,128)(2,1)S(1)} %convert_element_type.80, s32[1024]{0:T(1024)S(1)} %iota_add_fusion.1, s32[2048]{0:T(1024)S(1)} %copy-done.2), kind=kOutput, calls=%fused_computation.14 | convolution fusion | flops 1075838976 | bytes 2633728 | tf_op jit(solution)/shard_map/dot_general | solution.py:65
  36.7 2.5 %collective-permute-start.4 = (bf16[64,256]{1,0:T(8,128)(2,1)S(1)}, bf16[64,256]{1,0:T(8,128)(2,1)S(1)}, u32[]{:S(2)}, u32[]{:S(2)}) collective-permute-start(bf16[64,256]{1,0:T(8,128)(2,1)S(1)} %constant_dynamic-slice_fusion.7), channel_id=1, source_target_pairs={{0,4},{1,5},{2,6},{3,7},{4,0},{5,1},{6,2},{7,3},{8,12},{9,13},{10,... | collective-permute-start | bytes 98312 | tf_op jit(solution)/shard_map/ppermute | solution.py:43
  39.3 1.9 %collective-permute-done.4 = bf16[64,256]{1,0:T(8,128)(2,1)S(1)} collective-permute-done((bf16[64,256]{1,0:T(8,128)(2,1)S(1)}, bf16[64,256]{1,0:T(8,128)(2,1)S(1)}, u32[]{:S(2)}, u32[]{:S(2)}) %collective-permute-start.4) | collective-permute-done | bytes 32800 | tf_op jit(solution)/shard_map/ppermute | solution.py:43
  41.2 1.6 collective-permute-start.5
  42.9 3.0 %fusion.6 = f32[2048,256]{0,1:T(8,128)} fusion(bf16[1024,256]{1,0:T(8,128)(2,1)S(1)} %collective-permute-done.1, s32[1024]{0:T(1024)S(1)} %iota_add_fusion, s32[2048]{0:T(1024)S(1)} %copy-done.2), kind=kOutput, calls=%fused_computation.10 | convolution fusion | flops 1075838976 | bytes 2633728 | tf_op jit(solution)/shard_map/dot_general | solution.py:65
  45.9 2.3 %collective-permute-start.6 = (bf16[256,256]{1,0:T(8,128)(2,1)S(1)}, bf16[256,256]{1,0:T(8,128)(2,1)S(1)}, u32[]{:S(2)}, u32[]{:S(2)}) collective-permute-start(bf16[256,256]{1,0:T(8,128)(2,1)S(1)} %constant_dynamic-slice_fusion.5), channel_id=1, source_target_pairs={{0,16},{1,17},{2,18},{3,19},{4,20},{5,21},{6,22},{7,23},{8,24},{9,... | collective-permute-start | bytes 393224 | tf_op jit(solution)/shard_map/ppermute | solution.py:43
  48.2 8.8 %convolution_bitcast_fusion.3 = f32[2048,256]{0,1:T(8,128)S(1)} fusion(bf16[2048,2048]{1,0:T(8,128)(2,1)} %param.8, f32[2048,256]{0,1:T(8,128)} %fusion.6, f32[2048,256]{0,1:T(8,128)} %fusion.10, bf16[1024,256]{1,0:T(8,128)(2,1)S(1)} %collective-permute-done, s32[2048]{0:T(1024)S(1)} %copy-done.2, f32[2048]{0:T(1024)S(1)} %copy-done.1), kind=kOutput, calls=%fused_computation.53 | convolution fusion | flops 3225419776 | bytes 15220736 | tf_op jit(solution)/shard_map/dot_general | solution.py:76
  59.2 1.5 fusion.62
  62.0 4.8 %collective-permute-start.8 = (bf16[1024,256]{1,0:T(8,128)(2,1)S(1)}, bf16[1024,256]{1,0:T(8,128)(2,1)S(1)}, u32[]{:S(2)}, u32[]{:S(2)}) collective-permute-start(bf16[1024,256]{1,0:T(8,128)(2,1)S(1)} %fusion.76), channel_id=1, source_target_pairs={{0,4},{4,8},{8,12},{12,16},{16,20},{20,24},{24,28},{1,5},{5,9},{9,... | collective-permute-start | bytes 1572872 | tf_op jit(solution)/shard_map/ppermute | solution.py:29
  66.8 7.8 %collective-permute-done.7 = bf16[1024,256]{1,0:T(8,128)(2,1)S(1)} collective-permute-done((bf16[1024,256]{1,0:T(8,128)(2,1)S(1)}, bf16[1024,256]{1,0:T(8,128)(2,1)S(1)}, u32[]{:S(2)}, u32[]{:S(2)}) %collective-permute-start.7) | collective-permute-done | bytes 524320 | tf_op jit(solution)/shard_map/ppermute | solution.py:29
  74.6 10.8 %collective-permute-done.8 = bf16[1024,256]{1,0:T(8,128)(2,1)S(1)} collective-permute-done((bf16[1024,256]{1,0:T(8,128)(2,1)S(1)}, bf16[1024,256]{1,0:T(8,128)(2,1)S(1)}, u32[]{:S(2)}, u32[]{:S(2)}) %collective-permute-start.8) | collective-permute-done | bytes 524320 | tf_op jit(solution)/shard_map/ppermute | solution.py:29
  85.4 2.4 %fusion.87 = (bf16[1024,256]{1,0:T(8,128)(2,1)S(1)}, f32[1024,256]{1,0:T(8,128)}) fusion(bf16[1024,256]{1,0:T(8,128)(2,1)S(1)} %collective-permute-done.8, bf16[1024,256]{1,0:T(8,128)(2,1)S(1)} %collective-permute-done.7, bf16[2048,256]{0,1:T(8,128)(2,1)S(1)} %fusion.56, s32[2048]{0:T(1024)S(1)} %copy-done.2, s32[1024]{0:T(1024)S(1)} %iota_add_fusion.1), kind=kOutput, calls=%fused_computation.109 | convolution fusion | flops 1077673984 | bytes 3682304 | tf_op jit(solution)/shard_map/dot_general | solution.py:65
  89.1 5.0 %collective-permute-start.9 = (bf16[1024,256]{1,0:T(8,128)(2,1)S(1)}, bf16[1024,256]{1,0:T(8,128)(2,1)S(1)}, u32[]{:S(2)}, u32[]{:S(2)}) collective-permute-start(bf16[1024,256]{1,0:T(8,128)(2,1)S(1)} %get-tuple-element.2), channel_id=1, source_target_pairs={{0,4},{4,8},{8,12},{12,16},{16,20},{20,24},{24,28},{1,5},{5,9},{9,... | collective-permute-start | bytes 1572872 | tf_op jit(solution)/shard_map/ppermute | solution.py:17
  94.2 10.1 %collective-permute-done.10 = bf16[1024,256]{1,0:T(8,128)(2,1)S(1)} collective-permute-done((bf16[1024,256]{1,0:T(8,128)(2,1)S(1)}, bf16[1024,256]{1,0:T(8,128)(2,1)S(1)}, u32[]{:S(2)}, u32[]{:S(2)}) %collective-permute-start.10) | collective-permute-done | bytes 524320 | tf_op jit(solution)/shard_map/ppermute | solution.py:19
  104.3 11.4 %collective-permute-done.9 = bf16[1024,256]{1,0:T(8,128)(2,1)S(1)} collective-permute-done((bf16[1024,256]{1,0:T(8,128)(2,1)S(1)}, bf16[1024,256]{1,0:T(8,128)(2,1)S(1)}, u32[]{:S(2)}, u32[]{:S(2)}) %collective-permute-start.9) | collective-permute-done | bytes 524320 | tf_op jit(solution)/shard_map/ppermute | solution.py:17
  118.2 3.2 %collective-permute-done.12 = bf16[32,256]{1,0:T(8,128)(2,1)S(1)} collective-permute-done((bf16[32,256]{1,0:T(8,128)(2,1)S(1)}, bf16[32,256]{1,0:T(8,128)(2,1)S(1)}, u32[]{:S(2)}, u32[]{:S(2)}) %collective-permute-start.12) | collective-permute-done | bytes 16416 | tf_op jit(solution)/shard_map/ppermute | solution.py:43
  121.4 2.5 %collective-permute-start.13 = (bf16[64,256]{1,0:T(8,128)(2,1)S(1)}, bf16[64,256]{1,0:T(8,128)(2,1)S(1)}, u32[]{:S(2)}, u32[]{:S(2)}) collective-permute-start(bf16[64,256]{1,0:T(8,128)(2,1)S(1)} %constant_dynamic-slice_fusion.2), channel_id=1, source_target_pairs={{0,4},{1,5},{2,6},{3,7},{4,0},{5,1},{6,2},{7,3},{8,12},{9,13},{10,... | collective-permute-start | bytes 98312 | tf_op jit(solution)/shard_map/ppermute | solution.py:43
  123.9 3.0 %fusion.4 = f32[2048,256]{0,1:T(8,128)} fusion(bf16[1024,256]{1,0:T(8,128)(2,1)S(1)} %collective-permute-done.10, s32[1024]{0:T(1024)S(1)} %iota_add_fusion, s32[2048]{0:T(1024)S(1)} %copy-done.2), kind=kOutput, calls=%fused_computation.8 | convolution fusion | flops 1075838976 | bytes 2633728 | tf_op jit(solution)/shard_map/dot_general | solution.py:65
  127.0 1.8 %collective-permute-start.14 = (bf16[128,256]{1,0:T(8,128)(2,1)S(1)}, bf16[128,256]{1,0:T(8,128)(2,1)S(1)}, u32[]{:S(2)}, u32[]{:S(2)}) collective-permute-start(bf16[128,256]{1,0:T(8,128)(2,1)S(1)} %constant_dynamic-slice_fusion.1), channel_id=1, source_target_pairs={{0,8},{1,9},{2,10},{3,11},{4,12},{5,13},{6,14},{7,15},{8,0},{9,1},... | collective-permute-start | bytes 196616 | tf_op jit(solution)/shard_map/ppermute | solution.py:43
  128.8 3.3 %fusion.18 = f32[2048,256]{0,1:T(8,128)} fusion(bf16[1024,256]{1,0:T(8,128)(2,1)S(1)} %collective-permute-done.9, s32[2048]{0:T(1024)S(1)} %copy-done.2), kind=kOutput, calls=%fused_computation.24 | convolution fusion | flops 1075838976 | bytes 2629632 | tf_op jit(solution)/shard_map/dot_general | solution.py:65
  133.0 8.6 %convolution_bitcast_fusion.1 = f32[2048,256]{0,1:T(8,128)S(1)} fusion(bf16[2048,2048]{1,0:T(8,128)(2,1)} %param.8, f32[2048,256]{0,1:T(8,128)} %fusion.4, f32[2048,256]{0,1:T(8,128)} %fusion.18, bf16[1024,256]{1,0:T(8,128)(2,1)S(1)} %copy-done.4, s32[1024]{0:T(1024)S(1)} %iota_add_fusion.1, s32[2048]{0:T(1024)S(1)} %copy-done.2, f32[2048]{0:T(1024)S(1)} %copy-done.1), kind=kOutput, calls=%fused_computation.49 | convolution fusion | flops 3225419776 | bytes 15224832 | tf_op jit(solution)/shard_map/dot_general | solution.py:76
  142.4 1.4 fusion.79
  143.7 1.5 fusion.63
  146.6 4.6 %collective-permute-start.17 = (bf16[1024,256]{1,0:T(8,128)(2,1)S(1)}, bf16[1024,256]{1,0:T(8,128)(2,1)S(1)}, u32[]{:S(2)}, u32[]{:S(2)}) collective-permute-start(bf16[1024,256]{1,0:T(8,128)(2,1)S(1)} %fusion.79), channel_id=1, source_target_pairs={{0,4},{4,8},{8,12},{12,16},{16,20},{20,24},{24,28},{1,5},{5,9},{9,... | collective-permute-start | bytes 1572872 | tf_op jit(solution)/shard_map/ppermute | solution.py:29
  151.2 7.5 %collective-permute-done.16 = bf16[1024,256]{1,0:T(8,128)(2,1)S(1)} collective-permute-done((bf16[1024,256]{1,0:T(8,128)(2,1)S(1)}, bf16[1024,256]{1,0:T(8,128)(2,1)S(1)}, u32[]{:S(2)}, u32[]{:S(2)}) %collective-permute-start.16) | collective-permute-done | bytes 524320 | tf_op jit(solution)/shard_map/ppermute | solution.py:29
  158.6 10.1 %collective-permute-done.17 = bf16[1024,256]{1,0:T(8,128)(2,1)S(1)} collective-permute-done((bf16[1024,256]{1,0:T(8,128)(2,1)S(1)}, bf16[1024,256]{1,0:T(8,128)(2,1)S(1)}, u32[]{:S(2)}, u32[]{:S(2)}) %collective-permute-start.17) | collective-permute-done | bytes 524320 | tf_op jit(solution)/shard_map/ppermute | solution.py:29
  168.7 2.4 %convert_add_fusion = f32[1024,256]{1,0:T(8,128)} fusion(bf16[1024,256]{1,0:T(8,128)(2,1)S(1)} %collective-permute-done.17, bf16[1024,256]{1,0:T(8,128)(2,1)S(1)} %collective-permute-done.16, bf16[2048,256]{0,1:T(8,128)(2,1)S(1)} %fusion.57, s32[2048]{0:T(1024)S(1)} %copy-done.2, s32[1024]{0:T(1024)S(1)} %iota_add_fusion.1), kind=kOutput, calls=%fused_computation.76 | convolution fusion | flops 1077411840 | bytes 3158016 | tf_op jit(solution)/shard_map/dot_general | solution.py:65
  (67 shorter events, 16.1 us)
Async XLA Ops:
  0.6 56.5 %copy-start = (bf16[16,2048]{1,0:T(8,128)(2,1)S(1)}, bf16[16,2048]{1,0:T(8,128)(2,1)}, u32[]{:S(2)}) copy-start(bf16[16,2048]{1,0:T(8,128)(2,1)} %param.9) | copy-start | bytes 196612
  0.6 10.2 %copy-start.2 = (s32[2048]{0:T(1024)S(1)}, s32[2048]{0:T(1024)}, u32[]{:S(2)}) copy-start(s32[2048]{0:T(1024)} %param.12) | copy-start | bytes 24580
  2.0 16.8 %collective-permute-start.1 = (bf16[1024,256]{1,0:T(8,128)(2,1)S(1)}, bf16[1024,256]{1,0:T(8,128)(2,1)S(1)}, u32[]{:S(2)}, u32[]{:S(2)}) collective-permute-start(bf16[1024,256]{1,0:T(8,128)(2,1)S(1)} %convert_element_type.80), channel_id=1, source_target_pairs={{4,0},{8,4},{12,8},{16,12},{20,16},{24,20},{28,24},{5,1},{9,5},{13... | collective-permute-start | bytes 1572872 | tf_op jit(solution)/shard_map/ppermute | solution.py:19
  3.3 26.8 %collective-permute-start = (bf16[1024,256]{1,0:T(8,128)(2,1)S(1)}, bf16[1024,256]{1,0:T(8,128)(2,1)S(1)}, u32[]{:S(2)}, u32[]{:S(2)}) collective-permute-start(bf16[1024,256]{1,0:T(8,128)(2,1)S(1)} %convert_element_type.80), channel_id=1, source_target_pairs={{0,4},{4,8},{8,12},{12,16},{16,20},{20,24},{24,28},{1,5},{5,9},{9,... | collective-permute-start | bytes 1572872 | tf_op jit(solution)/shard_map/ppermute | solution.py:17
  30.9 1.2 collective-permute-start.2
  32.1 4.6 %collective-permute-start.3 = (bf16[32,256]{1,0:T(8,128)(2,1)S(1)}, bf16[32,256]{1,0:T(8,128)(2,1)S(1)}, u32[]{:S(2)}, u32[]{:S(2)}) collective-permute-start(bf16[32,256]{1,0:T(8,128)(2,1)S(1)} %constant_dynamic-slice_fusion.8), channel_id=1, source_target_pairs={{0,2},{1,3},{2,0},{3,1},{4,6},{5,7},{6,4},{7,5},{8,10},{9,11},{10,... | collective-permute-start | bytes 49160 | tf_op jit(solution)/shard_map/ppermute | solution.py:43
  36.7 4.4 %collective-permute-start.4 = (bf16[64,256]{1,0:T(8,128)(2,1)S(1)}, bf16[64,256]{1,0:T(8,128)(2,1)S(1)}, u32[]{:S(2)}, u32[]{:S(2)}) collective-permute-start(bf16[64,256]{1,0:T(8,128)(2,1)S(1)} %constant_dynamic-slice_fusion.7), channel_id=1, source_target_pairs={{0,4},{1,5},{2,6},{3,7},{4,0},{5,1},{6,2},{7,3},{8,12},{9,13},{10,... | collective-permute-start | bytes 98312 | tf_op jit(solution)/shard_map/ppermute | solution.py:43
  41.2 7.1 %copy-start.1 = (f32[2048]{0:T(1024)S(1)}, f32[2048]{0:T(1024)}, u32[]{:S(2)}) copy-start(f32[2048]{0:T(1024)} %param.10) | copy-start | bytes 24580
  41.2 4.7 %collective-permute-start.5 = (bf16[128,256]{1,0:T(8,128)(2,1)S(1)}, bf16[128,256]{1,0:T(8,128)(2,1)S(1)}, u32[]{:S(2)}, u32[]{:S(2)}) collective-permute-start(bf16[128,256]{1,0:T(8,128)(2,1)S(1)} %constant_dynamic-slice_fusion.6), channel_id=1, source_target_pairs={{0,8},{1,9},{2,10},{3,11},{4,12},{5,13},{6,14},{7,15},{8,0},{9,1},... | collective-permute-start | bytes 196616 | tf_op jit(solution)/shard_map/ppermute | solution.py:43
  45.9 11.2 %copy-start.5 = (bf16[16,512]{1,0:T(8,128)(2,1)S(1)}, bf16[16,512]{1,0:T(8,128)(2,1)}, u32[]{:S(2)}) copy-start(bf16[16,512]{1,0:T(8,128)(2,1)} %param.11) | copy-start | bytes 49156
  45.9 11.1 %collective-permute-start.6 = (bf16[256,256]{1,0:T(8,128)(2,1)S(1)}, bf16[256,256]{1,0:T(8,128)(2,1)S(1)}, u32[]{:S(2)}, u32[]{:S(2)}) collective-permute-start(bf16[256,256]{1,0:T(8,128)(2,1)S(1)} %constant_dynamic-slice_fusion.5), channel_id=1, source_target_pairs={{0,16},{1,17},{2,18},{3,19},{4,20},{5,21},{6,22},{7,23},{8,24},{9,... | collective-permute-start | bytes 393224 | tf_op jit(solution)/shard_map/ppermute | solution.py:43
  60.7 13.9 %collective-permute-start.7 = (bf16[1024,256]{1,0:T(8,128)(2,1)S(1)}, bf16[1024,256]{1,0:T(8,128)(2,1)S(1)}, u32[]{:S(2)}, u32[]{:S(2)}) collective-permute-start(bf16[1024,256]{1,0:T(8,128)(2,1)S(1)} %fusion.62), channel_id=1, source_target_pairs={{4,0},{8,4},{12,8},{16,12},{20,16},{24,20},{28,24},{5,1},{9,5},{13... | collective-permute-start | bytes 1572872 | tf_op jit(solution)/shard_map/ppermute | solution.py:29
  62.0 23.4 %collective-permute-start.8 = (bf16[1024,256]{1,0:T(8,128)(2,1)S(1)}, bf16[1024,256]{1,0:T(8,128)(2,1)S(1)}, u32[]{:S(2)}, u32[]{:S(2)}) collective-permute-start(bf16[1024,256]{1,0:T(8,128)(2,1)S(1)} %fusion.76), channel_id=1, source_target_pairs={{0,4},{4,8},{8,12},{12,16},{16,20},{20,24},{24,28},{1,5},{5,9},{9,... | collective-permute-start | bytes 1572872 | tf_op jit(solution)/shard_map/ppermute | solution.py:29
  87.8 39.2 %copy-start.3 = (bf16[1024,256]{1,0:T(8,128)(2,1)}, bf16[1024,256]{1,0:T(8,128)(2,1)S(1)}, u32[]{:S(2)}) copy-start(bf16[1024,256]{1,0:T(8,128)(2,1)S(1)} %get-tuple-element.2) | copy-start | bytes 1572868
  87.8 16.5 %collective-permute-start.10 = (bf16[1024,256]{1,0:T(8,128)(2,1)S(1)}, bf16[1024,256]{1,0:T(8,128)(2,1)S(1)}, u32[]{:S(2)}, u32[]{:S(2)}) collective-permute-start(bf16[1024,256]{1,0:T(8,128)(2,1)S(1)} %get-tuple-element.2), channel_id=1, source_target_pairs={{4,0},{8,4},{12,8},{16,12},{20,16},{24,20},{28,24},{5,1},{9,5},{13... | collective-permute-start | bytes 1572872 | tf_op jit(solution)/shard_map/ppermute | solution.py:19
  89.1 26.6 %collective-permute-start.9 = (bf16[1024,256]{1,0:T(8,128)(2,1)S(1)}, bf16[1024,256]{1,0:T(8,128)(2,1)S(1)}, u32[]{:S(2)}, u32[]{:S(2)}) collective-permute-start(bf16[1024,256]{1,0:T(8,128)(2,1)S(1)} %get-tuple-element.2), channel_id=1, source_target_pairs={{0,4},{4,8},{8,12},{12,16},{16,20},{20,24},{24,28},{1,5},{5,9},{9,... | collective-permute-start | bytes 1572872 | tf_op jit(solution)/shard_map/ppermute | solution.py:17
  116.5 1.2 collective-permute-start.11
  117.7 3.7 %collective-permute-start.12 = (bf16[32,256]{1,0:T(8,128)(2,1)S(1)}, bf16[32,256]{1,0:T(8,128)(2,1)S(1)}, u32[]{:S(2)}, u32[]{:S(2)}) collective-permute-start(bf16[32,256]{1,0:T(8,128)(2,1)S(1)} %constant_dynamic-slice_fusion.3), channel_id=1, source_target_pairs={{0,2},{1,3},{2,0},{3,1},{4,6},{5,7},{6,4},{7,5},{8,10},{9,11},{10,... | collective-permute-start | bytes 49160 | tf_op jit(solution)/shard_map/ppermute | solution.py:43
  121.4 5.5 %collective-permute-start.13 = (bf16[64,256]{1,0:T(8,128)(2,1)S(1)}, bf16[64,256]{1,0:T(8,128)(2,1)S(1)}, u32[]{:S(2)}, u32[]{:S(2)}) collective-permute-start(bf16[64,256]{1,0:T(8,128)(2,1)S(1)} %constant_dynamic-slice_fusion.2), channel_id=1, source_target_pairs={{0,4},{1,5},{2,6},{3,7},{4,0},{5,1},{6,2},{7,3},{8,12},{9,13},{10,... | collective-permute-start | bytes 98312 | tf_op jit(solution)/shard_map/ppermute | solution.py:43
  127.0 6.0 %copy-start.4 = (bf16[1024,256]{1,0:T(8,128)(2,1)S(1)}, bf16[1024,256]{1,0:T(8,128)(2,1)}, u32[]{:S(2)}) copy-start(bf16[1024,256]{1,0:T(8,128)(2,1)} %copy-done.3) | copy-start | bytes 1572868
  127.0 5.1 %collective-permute-start.14 = (bf16[128,256]{1,0:T(8,128)(2,1)S(1)}, bf16[128,256]{1,0:T(8,128)(2,1)S(1)}, u32[]{:S(2)}, u32[]{:S(2)}) collective-permute-start(bf16[128,256]{1,0:T(8,128)(2,1)S(1)} %constant_dynamic-slice_fusion.1), channel_id=1, source_target_pairs={{0,8},{1,9},{2,10},{3,11},{4,12},{5,13},{6,14},{7,15},{8,0},{9,1},... | collective-permute-start | bytes 196616 | tf_op jit(solution)/shard_map/ppermute | solution.py:43
  132.1 9.5 %collective-permute-start.15 = (bf16[256,256]{1,0:T(8,128)(2,1)S(1)}, bf16[256,256]{1,0:T(8,128)(2,1)S(1)}, u32[]{:S(2)}, u32[]{:S(2)}) collective-permute-start(bf16[256,256]{1,0:T(8,128)(2,1)S(1)} %constant_dynamic-slice_fusion), channel_id=1, source_target_pairs={{0,16},{1,17},{2,18},{3,19},{4,20},{5,21},{6,22},{7,23},{8,24},{9,... | collective-permute-start | bytes 393224 | tf_op jit(solution)/shard_map/ppermute | solution.py:43
  145.3 13.4 %collective-permute-start.16 = (bf16[1024,256]{1,0:T(8,128)(2,1)S(1)}, bf16[1024,256]{1,0:T(8,128)(2,1)S(1)}, u32[]{:S(2)}, u32[]{:S(2)}) collective-permute-start(bf16[1024,256]{1,0:T(8,128)(2,1)S(1)} %fusion.63), channel_id=1, source_target_pairs={{4,0},{8,4},{12,8},{16,12},{20,16},{24,20},{28,24},{5,1},{9,5},{13... | collective-permute-start | bytes 1572872 | tf_op jit(solution)/shard_map/ppermute | solution.py:29
  146.6 22.2 %collective-permute-start.17 = (bf16[1024,256]{1,0:T(8,128)(2,1)S(1)}, bf16[1024,256]{1,0:T(8,128)(2,1)S(1)}, u32[]{:S(2)}, u32[]{:S(2)}) collective-permute-start(bf16[1024,256]{1,0:T(8,128)(2,1)S(1)} %fusion.79), channel_id=1, source_target_pairs={{0,4},{4,8},{8,12},{12,16},{16,20},{20,24},{24,28},{1,5},{5,9},{9,... | collective-permute-start | bytes 1572872 | tf_op jit(solution)/shard_map/ppermute | solution.py:29

commit v6 on v5

--- a/solution.py
+++ b/solution.py
@@ -70,7 +70,10 @@
         before = padded[:own_count]
         after = padded[2 * own_count :]
         primal = (primal_scale * padded[primal_source].astype(jnp.float32)).astype(jnp.bfloat16)
-        primal_all = gather_all(primal)
+        count = lax.axis_size("sub") * lax.axis_size("grp")
+        primal_all = lax.all_to_all(
+            jnp.broadcast_to(primal[None], (count,) + primal.shape), AXES, 0, 0, tiled=False
+        ).reshape(-1, primal.shape[1])
         gathered = select(picks[1], rounded) + select(picks[0], before) + select(picks[2], after)
         scaled = (scale_column * gathered).astype(jnp.bfloat16)
         solved = jnp.dot(schur_inv, scaled, preferred_element_type=jnp.float32)

time: 172 us -> 166 us (0.965)
  waiting for transfers between devices: 83.8 us -> 79.7 us
  starting transfers between devices: 38.8 us -> 36.4 us
    ppermute x10 -> x0, starting transfers between devices: 13.7 us -> none  [gather_all(): got = lax.ppermute(piece, AXES, [(i, i ^ span) for i in range(count)])]
    all_to_all x0 -> x2, starting transfers between devices: none -> 11.4 us  [precondition(): lax.all_to_all(jnp.broadcast_to(primal[None], (count,) + primal.shape), A...]
    ppermute x10 -> x0, waiting for transfers between devices: 7.41 us -> none  [gather_all(): got = lax.ppermute(piece, AXES, [(i, i ^ span) for i in range(count)])]
    ppermute x4, waiting for transfers between devices: 36.2 us -> 42.6 us  [shifted(): return lax.ppermute(shard, axis, pairs)]
    ppermute x2, waiting for transfers between devices: 17.4 us -> 14.3 us  [with_halo(): lax.ppermute(head, axis, [((i + 1) % count, i) for i in range(ends)])]
  transfers between devices with their start and end apart: 18 -> 10, of which waited for: 12 -> 8; matrix products, arithmetic and copies ran while one was open for 19% -> 20% of each run, Pallas kernels for 0% -> 0%
where the time goes in v6:
time: 166 us
  waiting for transfers between devices  79.7 us (48%)
  matrix products  41.9 us (25%)
  starting transfers between devices  36.4 us (22%)
  local copies, waits for them, and re-layouts  4.69 us (3%)
  other arithmetic  2.35 us (1%)
    ppermute x4, waiting for transfers between devices, shifted(): return lax.ppermute(shard, axis, pairs)  42.6 us
    dot_general x10, matrix products, select(): return jnp.dot(matrix, rows, preferred_element_type=jnp.float32)  22.9 us
    ppermute x2, waiting for transfers between devices, with_halo(): lax.ppermute(tail, axis, [(i, (i + 1) % count) for i in range(ends)])  22.8 us
    dot_general x2, matrix products, precondition(): solved = jnp.dot(schur_inv, scaled, preferred_element_type=jnp.float32)  17.5 us
    ppermute x2, waiting for transfers between devices, with_halo(): lax.ppermute(head, axis, [((i + 1) % count, i) for i in range(ends)])  14.3 us
    ppermute x4, starting transfers between devices, shifted(): return lax.ppermute(shard, axis, pairs)  11.9 us
    all_to_all x2, starting transfers between devices, precondition(): lax.all_to_all(jnp.broadcast_to(primal[None], (count,) + primal.shape), A...  11.4 us
    ppermute x2, starting transfers between devices, with_halo(): lax.ppermute(tail, axis, [(i, (i + 1) % count) for i in range(ends)])  10.6 us
  transfers between devices with their start and end apart: 10, of which 8 were waited for; matrix products, arithmetic and copies ran while one was open for 20% of the time, Pallas kernels for 0%

profile of v6, /device:TPU:0, one launch (start us, length us, event | category | flops | bytes accessed | tf_op | source)
XLA Modules:
  0.0 166.0 jit_solution(3633725895394886618)
XLA Ops:
  0.7 1.3 convert_element_type.96
  2.0 1.3 collective-permute-start.1
  3.3 5.5 %collective-permute-start = (bf16[1024,256]{1,0:T(8,128)(2,1)S(1)}, bf16[1024,256]{1,0:T(8,128)(2,1)S(1)}, u32[]{:S(2)}, u32[]{:S(2)}) collective-permute-start(bf16[1024,256]{1,0:T(8,128)(2,1)S(1)} %convert_element_type.96), channel_id=1, source_target_pairs={{0,4},{4,8},{8,12},{12,16},{16,20},{20,24},{24,28},{1,5},{5,9},{9,... | collective-permute-start | bytes 1572872 | tf_op jit(solution)/shard_map/ppermute | solution.py:17
  9.5 1.4 gather_fusion
  11.5 3.0 %fusion.10 = f32[2048,256]{0,1:T(8,128)} fusion(bf16[1024,256]{1,0:T(8,128)(2,1)S(1)} %convert_element_type.96, s32[1024]{0:T(1024)S(1)} %iota_add_fusion.1, s32[2048]{0:T(1024)S(1)} %copy-done.2), kind=kOutput, calls=%fused_computation.14 | convolution fusion | flops 1075838976 | bytes 2633728 | tf_op jit(solution)/shard_map/dot_general | solution.py:65
  14.5 4.2 %collective-permute-done.1 = bf16[1024,256]{1,0:T(8,128)(2,1)S(1)} collective-permute-done((bf16[1024,256]{1,0:T(8,128)(2,1)S(1)}, bf16[1024,256]{1,0:T(8,128)(2,1)S(1)}, u32[]{:S(2)}, u32[]{:S(2)}) %collective-permute-start.1) | collective-permute-done | bytes 524320 | tf_op jit(solution)/shard_map/ppermute | solution.py:19
  18.7 11.4 %collective-permute-done = bf16[1024,256]{1,0:T(8,128)(2,1)S(1)} collective-permute-done((bf16[1024,256]{1,0:T(8,128)(2,1)S(1)}, bf16[1024,256]{1,0:T(8,128)(2,1)S(1)}, u32[]{:S(2)}, u32[]{:S(2)}) %collective-permute-start) | collective-permute-done | bytes 524320 | tf_op jit(solution)/shard_map/ppermute | solution.py:17
  31.6 5.8 %all-to-all-start = ((bf16[32,16,256]{2,1,0:T(8,128)(2,1)}), bf16[32,16,256]{2,1,0:T(8,128)(2,1)S(1)}, u32[]{:S(2)}, u32[]{:S(2)}) async-start(bf16[32,16,256]{2,1,0:T(8,128)(2,1)} %broadcast_in_dim.7), calls=%async_computation | async-start | bytes 524288 | tf_op jit(solution)/shard_map/all_to_all | solution.py:74
  37.5 3.0 %fusion.6 = f32[2048,256]{0,1:T(8,128)} fusion(bf16[1024,256]{1,0:T(8,128)(2,1)S(1)} %collective-permute-done.1, s32[1024]{0:T(1024)S(1)} %iota_add_fusion, s32[2048]{0:T(1024)S(1)} %copy-done.2), kind=kOutput, calls=%fused_computation.10 | convolution fusion | flops 1075838976 | bytes 2633728 | tf_op jit(solution)/shard_map/dot_general | solution.py:65
  40.5 9.0 %convolution_bitcast_fusion.3 = f32[2048,256]{0,1:T(8,128)S(1)} fusion(bf16[2048,2048]{1,0:T(8,128)(2,1)} %param.8, f32[2048,256]{0,1:T(8,128)} %fusion.6, f32[2048,256]{0,1:T(8,128)} %fusion.10, bf16[1024,256]{1,0:T(8,128)(2,1)} %copy-done.5, s32[2048]{0:T(1024)S(1)} %copy-done.2, f32[2048]{0:T(1024)S(1)} %copy-done.1), kind=kOutput, calls=%fused_computation.53 | convolution fusion | flops 3225419776 | bytes 15220736 | tf_op jit(solution)/shard_map/dot_general | solution.py:79
  50.2 1.4 fusion.76
  51.6 1.5 fusion.62
  53.1 1.3 collective-permute-start.2
  54.4 4.8 %collective-permute-start.3 = (bf16[1024,256]{1,0:T(8,128)(2,1)S(1)}, bf16[1024,256]{1,0:T(8,128)(2,1)S(1)}, u32[]{:S(2)}, u32[]{:S(2)}) collective-permute-start(bf16[1024,256]{1,0:T(8,128)(2,1)S(1)} %fusion.76), channel_id=1, source_target_pairs={{0,4},{4,8},{8,12},{12,16},{16,20},{20,24},{24,28},{1,5},{5,9},{9,... | collective-permute-start | bytes 1572872 | tf_op jit(solution)/shard_map/ppermute | solution.py:29
  59.2 9.9 %collective-permute-done.2 = bf16[1024,256]{1,0:T(8,128)(2,1)S(1)} collective-permute-done((bf16[1024,256]{1,0:T(8,128)(2,1)S(1)}, bf16[1024,256]{1,0:T(8,128)(2,1)S(1)}, u32[]{:S(2)}, u32[]{:S(2)}) %collective-permute-start.2) | collective-permute-done | bytes 524320 | tf_op jit(solution)/shard_map/ppermute | solution.py:29
  69.1 11.3 %collective-permute-done.3 = bf16[1024,256]{1,0:T(8,128)(2,1)S(1)} collective-permute-done((bf16[1024,256]{1,0:T(8,128)(2,1)S(1)}, bf16[1024,256]{1,0:T(8,128)(2,1)S(1)}, u32[]{:S(2)}, u32[]{:S(2)}) %collective-permute-start.3) | collective-permute-done | bytes 524320 | tf_op jit(solution)/shard_map/ppermute | solution.py:29
  80.4 2.4 %fusion.85 = (bf16[1024,256]{1,0:T(8,128)(2,1)S(1)}, f32[1024,256]{1,0:T(8,128)}) fusion(bf16[1024,256]{1,0:T(8,128)(2,1)S(1)} %collective-permute-done.3, bf16[1024,256]{1,0:T(8,128)(2,1)S(1)} %collective-permute-done.2, bf16[2048,256]{0,1:T(8,128)(2,1)S(1)} %fusion.56, s32[2048]{0:T(1024)S(1)} %copy-done.2, s32[1024]{0:T(1024)S(1)} %iota_add_fusion.1), kind=kOutput, calls=%fused_computation.87 | convolution fusion | flops 1077673984 | bytes 3682304 | tf_op jit(solution)/shard_map/dot_general | solution.py:65
  82.9 1.3 collective-permute-start.5
  84.1 5.0 %collective-permute-start.4 = (bf16[1024,256]{1,0:T(8,128)(2,1)S(1)}, bf16[1024,256]{1,0:T(8,128)(2,1)S(1)}, u32[]{:S(2)}, u32[]{:S(2)}) collective-permute-start(bf16[1024,256]{1,0:T(8,128)(2,1)S(1)} %get-tuple-element.2), channel_id=1, source_target_pairs={{0,4},{4,8},{8,12},{12,16},{16,20},{20,24},{24,28},{1,5},{5,9},{9,... | collective-permute-start | bytes 1572872 | tf_op jit(solution)/shard_map/ppermute | solution.py:17
  89.2 10.1 %collective-permute-done.5 = bf16[1024,256]{1,0:T(8,128)(2,1)S(1)} collective-permute-done((bf16[1024,256]{1,0:T(8,128)(2,1)S(1)}, bf16[1024,256]{1,0:T(8,128)(2,1)S(1)}, u32[]{:S(2)}, u32[]{:S(2)}) %collective-permute-start.5) | collective-permute-done | bytes 524320 | tf_op jit(solution)/shard_map/ppermute | solution.py:19
  99.3 11.4 %collective-permute-done.4 = bf16[1024,256]{1,0:T(8,128)(2,1)S(1)} collective-permute-done((bf16[1024,256]{1,0:T(8,128)(2,1)S(1)}, bf16[1024,256]{1,0:T(8,128)(2,1)S(1)}, u32[]{:S(2)}, u32[]{:S(2)}) %collective-permute-start.4) | collective-permute-done | bytes 524320 | tf_op jit(solution)/shard_map/ppermute | solution.py:17
  112.2 5.6 %all-to-all-start.1 = ((bf16[32,16,256]{2,1,0:T(8,128)(2,1)}), bf16[32,16,256]{2,1,0:T(8,128)(2,1)S(1)}, u32[]{:S(2)}, u32[]{:S(2)}) async-start(bf16[32,16,256]{2,1,0:T(8,128)(2,1)} %broadcast_in_dim.8), calls=%async_computation.1 | async-start | bytes 524288 | tf_op jit(solution)/shard_map/all_to_all | solution.py:74
  117.8 3.3 %fusion.18 = f32[2048,256]{0,1:T(8,128)} fusion(bf16[1024,256]{1,0:T(8,128)(2,1)S(1)} %collective-permute-done.4, s32[2048]{0:T(1024)S(1)} %copy-done.2), kind=kOutput, calls=%fused_computation.24 | convolution fusion | flops 1075838976 | bytes 2629632 | tf_op jit(solution)/shard_map/dot_general | solution.py:65
  121.1 3.0 %fusion.4 = f32[2048,256]{0,1:T(8,128)} fusion(bf16[1024,256]{1,0:T(8,128)(2,1)S(1)} %collective-permute-done.5, s32[1024]{0:T(1024)S(1)} %iota_add_fusion, s32[2048]{0:T(1024)S(1)} %copy-done.2), kind=kOutput, calls=%fused_computation.8 | convolution fusion | flops 1075838976 | bytes 2633728 | tf_op jit(solution)/shard_map/dot_general | solution.py:65
  124.1 8.6 %convolution_bitcast_fusion.1 = f32[2048,256]{0,1:T(8,128)S(1)} fusion(bf16[2048,2048]{1,0:T(8,128)(2,1)} %param.8, f32[2048,256]{0,1:T(8,128)} %fusion.4, f32[2048,256]{0,1:T(8,128)} %fusion.18, bf16[1024,256]{1,0:T(8,128)(2,1)S(1)} %copy-done.4, s32[1024]{0:T(1024)S(1)} %iota_add_fusion.1, s32[2048]{0:T(1024)S(1)} %copy-done.2, f32[2048]{0:T(1024)S(1)} %copy-done.1), kind=kOutput, calls=%fused_computation.49 | convolution fusion | flops 3225419776 | bytes 15224832 | tf_op jit(solution)/shard_map/dot_general | solution.py:79
  133.4 1.4 fusion.79
  134.8 1.5 fusion.63
  136.3 1.3 collective-permute-start.6
  137.6 4.6 %collective-permute-start.7 = (bf16[1024,256]{1,0:T(8,128)(2,1)S(1)}, bf16[1024,256]{1,0:T(8,128)(2,1)S(1)}, u32[]{:S(2)}, u32[]{:S(2)}) collective-permute-start(bf16[1024,256]{1,0:T(8,128)(2,1)S(1)} %fusion.79), channel_id=1, source_target_pairs={{0,4},{4,8},{8,12},{12,16},{16,20},{20,24},{24,28},{1,5},{5,9},{9,... | collective-permute-start | bytes 1572872 | tf_op jit(solution)/shard_map/ppermute | solution.py:29
  142.2 10.1 %collective-permute-done.6 = bf16[1024,256]{1,0:T(8,128)(2,1)S(1)} collective-permute-done((bf16[1024,256]{1,0:T(8,128)(2,1)S(1)}, bf16[1024,256]{1,0:T(8,128)(2,1)S(1)}, u32[]{:S(2)}, u32[]{:S(2)}) %collective-permute-start.6) | collective-permute-done | bytes 524320 | tf_op jit(solution)/shard_map/ppermute | solution.py:29
  152.3 11.3 %collective-permute-done.7 = bf16[1024,256]{1,0:T(8,128)(2,1)S(1)} collective-permute-done((bf16[1024,256]{1,0:T(8,128)(2,1)S(1)}, bf16[1024,256]{1,0:T(8,128)(2,1)S(1)}, u32[]{:S(2)}, u32[]{:S(2)}) %collective-permute-start.7) | collective-permute-done | bytes 524320 | tf_op jit(solution)/shard_map/ppermute | solution.py:29
  163.6 2.4 %convert_add_fusion = f32[1024,256]{1,0:T(8,128)} fusion(bf16[1024,256]{1,0:T(8,128)(2,1)S(1)} %collective-permute-done.7, bf16[1024,256]{1,0:T(8,128)(2,1)S(1)} %collective-permute-done.6, bf16[2048,256]{0,1:T(8,128)(2,1)S(1)} %fusion.57, s32[2048]{0:T(1024)S(1)} %copy-done.2, s32[1024]{0:T(1024)S(1)} %iota_add_fusion.1), kind=kOutput, calls=%fused_computation.76 | convolution fusion | flops 1077411840 | bytes 3158016 | tf_op jit(solution)/shard_map/dot_general | solution.py:65
  (33 shorter events, 5.8 us)
Async XLA Ops:
  0.6 48.9 %copy-start = (bf16[16,2048]{1,0:T(8,128)(2,1)S(1)}, bf16[16,2048]{1,0:T(8,128)(2,1)}, u32[]{:S(2)}) copy-start(bf16[16,2048]{1,0:T(8,128)(2,1)} %param.9) | copy-start | bytes 196612
  0.6 10.2 %copy-start.2 = (s32[2048]{0:T(1024)S(1)}, s32[2048]{0:T(1024)}, u32[]{:S(2)}) copy-start(s32[2048]{0:T(1024)} %param.12) | copy-start | bytes 24580
  2.0 16.8 %collective-permute-start.1 = (bf16[1024,256]{1,0:T(8,128)(2,1)S(1)}, bf16[1024,256]{1,0:T(8,128)(2,1)S(1)}, u32[]{:S(2)}, u32[]{:S(2)}) collective-permute-start(bf16[1024,256]{1,0:T(8,128)(2,1)S(1)} %convert_element_type.96), channel_id=1, source_target_pairs={{4,0},{8,4},{12,8},{16,12},{20,16},{24,20},{28,24},{5,1},{9,5},{13... | collective-permute-start | bytes 1572872 | tf_op jit(solution)/shard_map/ppermute | solution.py:19
  3.3 26.8 %collective-permute-start = (bf16[1024,256]{1,0:T(8,128)(2,1)S(1)}, bf16[1024,256]{1,0:T(8,128)(2,1)S(1)}, u32[]{:S(2)}, u32[]{:S(2)}) collective-permute-start(bf16[1024,256]{1,0:T(8,128)(2,1)S(1)} %convert_element_type.96), channel_id=1, source_target_pairs={{0,4},{4,8},{8,12},{12,16},{16,20},{20,24},{24,28},{1,5},{5,9},{9,... | collective-permute-start | bytes 1572872 | tf_op jit(solution)/shard_map/ppermute | solution.py:17
  30.1 7.3 %copy-start.5 = (bf16[1024,256]{1,0:T(8,128)(2,1)}, bf16[1024,256]{1,0:T(8,128)(2,1)S(1)}, u32[]{:S(2)}) copy-start(bf16[1024,256]{1,0:T(8,128)(2,1)S(1)} %collective-permute-done) | copy-start | bytes 1572868
  31.6 17.9 %all-to-all-start = ((bf16[32,16,256]{2,1,0:T(8,128)(2,1)}), bf16[32,16,256]{2,1,0:T(8,128)(2,1)S(1)}, u32[]{:S(2)}, u32[]{:S(2)}) async-start(bf16[32,16,256]{2,1,0:T(8,128)(2,1)} %broadcast_in_dim.7), calls=%async_computation | async-start | bytes 524288 | tf_op jit(solution)/shard_map/all_to_all | solution.py:74
  37.5 3.0 %copy-start.1 = (f32[2048]{0:T(1024)S(1)}, f32[2048]{0:T(1024)}, u32[]{:S(2)}) copy-start(f32[2048]{0:T(1024)} %param.10) | copy-start | bytes 24580
  40.5 9.0 %copy-start.6 = (bf16[16,512]{1,0:T(8,128)(2,1)S(1)}, bf16[16,512]{1,0:T(8,128)(2,1)}, u32[]{:S(2)}) copy-start(bf16[16,512]{1,0:T(8,128)(2,1)} %param.11) | copy-start | bytes 49156
  53.1 16.0 %collective-permute-start.2 = (bf16[1024,256]{1,0:T(8,128)(2,1)S(1)}, bf16[1024,256]{1,0:T(8,128)(2,1)S(1)}, u32[]{:S(2)}, u32[]{:S(2)}) collective-permute-start(bf16[1024,256]{1,0:T(8,128)(2,1)S(1)} %fusion.62), channel_id=1, source_target_pairs={{4,0},{8,4},{12,8},{16,12},{20,16},{24,20},{28,24},{5,1},{9,5},{13... | collective-permute-start | bytes 1572872 | tf_op jit(solution)/shard_map/ppermute | solution.py:29
  54.4 26.0 %collective-permute-start.3 = (bf16[1024,256]{1,0:T(8,128)(2,1)S(1)}, bf16[1024,256]{1,0:T(8,128)(2,1)S(1)}, u32[]{:S(2)}, u32[]{:S(2)}) collective-permute-start(bf16[1024,256]{1,0:T(8,128)(2,1)S(1)} %fusion.76), channel_id=1, source_target_pairs={{0,4},{4,8},{8,12},{12,16},{16,20},{20,24},{24,28},{1,5},{5,9},{9,... | collective-permute-start | bytes 1572872 | tf_op jit(solution)/shard_map/ppermute | solution.py:29
  82.9 27.9 %copy-start.3 = (bf16[1024,256]{1,0:T(8,128)(2,1)}, bf16[1024,256]{1,0:T(8,128)(2,1)S(1)}, u32[]{:S(2)}) copy-start(bf16[1024,256]{1,0:T(8,128)(2,1)S(1)} %get-tuple-element.2) | copy-start | bytes 1572868
  82.9 16.5 %collective-permute-start.5 = (bf16[1024,256]{1,0:T(8,128)(2,1)S(1)}, bf16[1024,256]{1,0:T(8,128)(2,1)S(1)}, u32[]{:S(2)}, u32[]{:S(2)}) collective-permute-start(bf16[1024,256]{1,0:T(8,128)(2,1)S(1)} %get-tuple-element.2), channel_id=1, source_target_pairs={{4,0},{8,4},{12,8},{16,12},{20,16},{24,20},{28,24},{5,1},{9,5},{13... | collective-permute-start | bytes 1572872 | tf_op jit(solution)/shard_map/ppermute | solution.py:19
  84.1 26.6 %collective-permute-start.4 = (bf16[1024,256]{1,0:T(8,128)(2,1)S(1)}, bf16[1024,256]{1,0:T(8,128)(2,1)S(1)}, u32[]{:S(2)}, u32[]{:S(2)}) collective-permute-start(bf16[1024,256]{1,0:T(8,128)(2,1)S(1)} %get-tuple-element.2), channel_id=1, source_target_pairs={{0,4},{4,8},{8,12},{12,16},{16,20},{20,24},{24,28},{1,5},{5,9},{9,... | collective-permute-start | bytes 1572872 | tf_op jit(solution)/shard_map/ppermute | solution.py:17
  112.2 20.5 %all-to-all-start.1 = ((bf16[32,16,256]{2,1,0:T(8,128)(2,1)}), bf16[32,16,256]{2,1,0:T(8,128)(2,1)S(1)}, u32[]{:S(2)}, u32[]{:S(2)}) async-start(bf16[32,16,256]{2,1,0:T(8,128)(2,1)} %broadcast_in_dim.8), calls=%async_computation.1 | async-start | bytes 524288 | tf_op jit(solution)/shard_map/all_to_all | solution.py:74
  121.1 3.0 %copy-start.4 = (bf16[1024,256]{1,0:T(8,128)(2,1)S(1)}, bf16[1024,256]{1,0:T(8,128)(2,1)}, u32[]{:S(2)}) copy-start(bf16[1024,256]{1,0:T(8,128)(2,1)} %copy-done.3) | copy-start | bytes 1572868
  136.3 16.0 %collective-permute-start.6 = (bf16[1024,256]{1,0:T(8,128)(2,1)S(1)}, bf16[1024,256]{1,0:T(8,128)(2,1)S(1)}, u32[]{:S(2)}, u32[]{:S(2)}) collective-permute-start(bf16[1024,256]{1,0:T(8,128)(2,1)S(1)} %fusion.63), channel_id=1, source_target_pairs={{4,0},{8,4},{12,8},{16,12},{20,16},{24,20},{28,24},{5,1},{9,5},{13... | collective-permute-start | bytes 1572872 | tf_op jit(solution)/shard_map/ppermute | solution.py:29
  137.6 26.0 %collective-permute-start.7 = (bf16[1024,256]{1,0:T(8,128)(2,1)S(1)}, bf16[1024,256]{1,0:T(8,128)(2,1)S(1)}, u32[]{:S(2)}, u32[]{:S(2)}) collective-permute-start(bf16[1024,256]{1,0:T(8,128)(2,1)S(1)} %fusion.79), channel_id=1, source_target_pairs={{0,4},{4,8},{8,12},{12,16},{16,20},{20,24},{24,28},{1,5},{5,9},{9,... | collective-permute-start | bytes 1572872 | tf_op jit(solution)/shard_map/ppermute | solution.py:29

commit v7 on v6

--- a/solution.py
+++ b/solution.py
@@ -52,14 +52,10 @@
     primal_source = source_row[primal_idx]
     primal_scale = scaling[primal_idx][:, None]
 
-    picks = [
-        (source_row[:, None] == (region * own_count + jnp.arange(own_count))[None, :]).astype(jnp.bfloat16)
-        for region in range(3)
-    ]
-    places = [
-        ((region * own_count + jnp.arange(own_count))[:, None] == source_row[None, :]).astype(jnp.bfloat16)
-        for region in range(3)
-    ]
+    padded_rows = jnp.arange(3 * own_count)
+    pick = (source_row[:, None] == padded_rows[None, :]).astype(jnp.bfloat16)
+    place = (padded_rows[:, None] == source_row[None, :]).astype(jnp.bfloat16)
+    pick, place = lax.optimization_barrier((pick, place))
 
     def select(matrix, rows):
         return jnp.dot(matrix, rows, preferred_element_type=jnp.float32)
@@ -67,14 +63,12 @@
     def precondition(vector_in):
         rounded = vector_in.astype(jnp.bfloat16)
         padded = with_halo(rounded, (("sub", 0),), own_count)
-        before = padded[:own_count]
-        after = padded[2 * own_count :]
         primal = (primal_scale * padded[primal_source].astype(jnp.float32)).astype(jnp.bfloat16)
         count = lax.axis_size("sub") * lax.axis_size("grp")
         primal_all = lax.all_to_all(
             jnp.broadcast_to(primal[None], (count,) + primal.shape), AXES, 0, 0, tiled=False
         ).reshape(-1, primal.shape[1])
-        gathered = select(picks[1], rounded) + select(picks[0], before) + select(picks[2], after)
+        gathered = select(pick, padded)
         scaled = (scale_column * gathered).astype(jnp.bfloat16)
         solved = jnp.dot(schur_inv, scaled, preferred_element_type=jnp.float32)
         solved = lax.optimization_barrier(solved)
@@ -84,11 +78,11 @@
             basis, coarse_rounded, (((0,), (0,)), ((), ())), preferred_element_type=jnp.float32
         )
         weighted = (scale_column * solved).astype(jnp.bfloat16)
-        to_previous = select(places[0], weighted).astype(jnp.bfloat16)
-        to_next = select(places[2], weighted).astype(jnp.bfloat16)
+        to_previous = select(place[:own_count], weighted).astype(jnp.bfloat16)
+        to_next = select(place[2 * own_count :], weighted).astype(jnp.bfloat16)
         from_next = shifted(to_previous, "sub", -1)
         from_previous = shifted(to_next, "sub", 1)
-        kept = select(places[1], weighted).astype(jnp.bfloat16)
+        kept = lax.optimization_barrier(select(place[own_count : 2 * own_count], weighted).astype(jnp.bfloat16))
         return (
             kept.astype(jnp.float32)
             + from_next.astype(jnp.float32)

time: 166 us -> 171 us (1.030)
  other arithmetic: 2.35 us -> 27 us
  waiting for transfers between devices: 79.7 us -> 61.2 us
  matrix products: 41.9 us -> 39.2 us
    convert_element_type x0 -> x2, other arithmetic: none -> 21.9 us  [the longest x1 11.1 us: shards(): place = (padded_rows[:, None] == source_row[None, :]).astype(jnp.bfloat16)]
    ppermute x2, waiting for transfers between devices: 22.8 us -> 11.3 us  [with_halo(): lax.ppermute(tail, axis, [(i, (i + 1) % count) for i in range(ends)])]
    dot_general x10 -> x6, matrix products: 22.9 us -> 17.2 us  [select(): return jnp.dot(matrix, rows, preferred_element_type=jnp.float32)]
    ppermute x2, waiting for transfers between devices: 14.3 us -> 10.2 us  [with_halo(): lax.ppermute(head, axis, [((i + 1) % count, i) for i in range(ends)])]
    ppermute x4, waiting for transfers between devices: 42.6 us -> 39.4 us  [shifted(): return lax.ppermute(shard, axis, pairs)]
    dot_general x2, matrix products: 17.5 us -> 20.5 us  [precondition(): solved = jnp.dot(schur_inv, scaled, preferred_element_type=jnp.float32)]
  transfers between devices with their start and end apart: 10 -> 10, of which waited for: 8 -> 8; matrix products, arithmetic and copies ran while one was open for 20% -> 27% of each run, Pallas kernels for 0% -> 0%
where the time goes in v7:
time: 171 us; the launch traced here: 170 us
  waiting for transfers between devices  61.2 us (36%)
  matrix products  39.2 us (23%)
  starting transfers between devices  37.1 us (22%)
  other arithmetic  27 us (16%)
  local copies, waits for them, and re-layouts  4.8 us (3%)
    ppermute x4, waiting for transfers between devices, shifted(): return lax.ppermute(shard, axis, pairs)  39.4 us
    dot_general x2, matrix products, precondition(): solved = jnp.dot(schur_inv, scaled, preferred_element_type=jnp.float32)  20.5 us
    dot_general x6, matrix products, select(): return jnp.dot(matrix, rows, preferred_element_type=jnp.float32)  17.2 us
    all_to_all x2, starting transfers between devices, precondition(): lax.all_to_all(jnp.broadcast_to(primal[None], (count,) + primal.shape), A...  12.2 us
    ppermute x4, starting transfers between devices, shifted(): return lax.ppermute(shard, axis, pairs)  11.7 us
    ppermute x2, waiting for transfers between devices, with_halo(): lax.ppermute(tail, axis, [(i, (i + 1) % count) for i in range(ends)])  11.3 us
    convert_element_type x1, other arithmetic, shards(): place = (padded_rows[:, None] == source_row[None, :]).astype(jnp.bfloat16)  11.1 us
    convert_element_type x1, other arithmetic, shards(): pick = (source_row[:, None] == padded_rows[None, :]).astype(jnp.bfloat16)  10.8 us
  transfers between devices with their start and end apart: 10, of which 8 were waited for; matrix products, arithmetic and copies ran while one was open for 27% of the time, Pallas kernels for 0%

profile of v7, /device:TPU:0, one launch (start us, length us, event | category | flops | bytes accessed | tf_op | source)
XLA Modules:
  0.0 170.1 jit_solution(4705825794925521311)
XLA Ops:
  0.6 1.3 convert_element_type.98
  2.0 1.3 collective-permute-start.1
  3.3 5.5 %collective-permute-start = (bf16[1024,256]{1,0:T(8,128)(2,1)S(1)}, bf16[1024,256]{1,0:T(8,128)(2,1)S(1)}, u32[]{:S(2)}, u32[]{:S(2)}) collective-permute-start(bf16[1024,256]{1,0:T(8,128)(2,1)S(1)} %convert_element_type.98), channel_id=1, source_target_pairs={{0,4},{4,8},{8,12},{12,16},{16,20},{20,24},{24,28},{1,5},{5,9},{9,... | collective-permute-start | bytes 1572872 | tf_op jit(solution)/shard_map/ppermute | solution.py:17
  8.8 10.8 %fusion = bf16[2048,3072]{1,0:T(8,128)(2,1)} fusion(s32[2048]{0:T(1024)} %param.12), kind=kLoop, calls=%fused_computation.6 | loop fusion | flops 12582912 | bytes 12591104 | tf_op jit(solution)/shard_map/convert_element_type | solution.py:56
  19.6 11.1 %fusion.1 = bf16[3072,2048]{1,0:T(8,128)(2,1)} fusion(s32[2048]{0:T(1024)S(1)} %copy-done.2), kind=kLoop, calls=%fused_computation.7 | loop fusion | flops 12582912 | bytes 12591104 | tf_op jit(solution)/shard_map/convert_element_type | solution.py:57
  33.6 6.4 %all-to-all-start = ((bf16[32,16,256]{2,1,0:T(8,128)(2,1)}), bf16[32,16,256]{2,1,0:T(8,128)(2,1)S(1)}, u32[]{:S(2)}, u32[]{:S(2)}) async-start(bf16[32,16,256]{2,1,0:T(8,128)(2,1)} %broadcast_in_dim.7), calls=%async_computation | async-start | bytes 524288 | tf_op jit(solution)/shard_map/all_to_all | solution.py:68
  40.0 10.2 %convolution_bitcast_fusion.3 = f32[2048,256]{0,1:T(8,128)S(1)} fusion(bf16[2048,2048]{1,0:T(8,128)(2,1)} %param.8, bf16[2048,3072]{1,0:T(8,128)(2,1)} %fusion, f32[2048]{0:T(1024)S(1)} %copy-done.1, bf16[1024,256]{1,0:T(8,128)(2,1)S(1)} %collective-permute-done.1, bf16[1024,256]{1,0:T(8,128)(2,1)S(1)} %convert_element_type.98, bf16[1024,256]{1,0:T(8,128)(2,1)} %copy-done.3), kind=kOutput, calls=%fused_computation.27 | convolution fusion | flops 5374476288 | bytes 24649728 | tf_op jit(solution)/shard_map/dot_general | solution.py:73
  51.2 3.6 %fusion.34 = bf16[1024,256]{1,0:T(8,128)(2,1)S(1)} fusion(bf16[2048,256]{0,1:T(8,128)(2,1)S(1)} %fusion.18, bf16[3072,2048]{1,0:T(8,128)(2,1)} %fusion.1), kind=kOutput, calls=%fused_computation.40 | convolution fusion | flops 1074003968 | bytes 5767168 | tf_op jit(solution)/shard_map/dot_general | solution.py:61
  54.8 3.6 %fusion.28 = bf16[1024,256]{1,0:T(8,128)(2,1)S(1)} fusion(bf16[2048,256]{0,1:T(8,128)(2,1)S(1)} %fusion.18, bf16[3072,2048]{1,0:T(8,128)(2,1)} %fusion.1), kind=kOutput, calls=%fused_computation.38 | convolution fusion | flops 1074003968 | bytes 5767168 | tf_op jit(solution)/shard_map/dot_general | solution.py:61
  58.5 1.3 collective-permute-start.2
  59.8 4.6 %collective-permute-start.3 = (bf16[1024,256]{1,0:T(8,128)(2,1)S(1)}, bf16[1024,256]{1,0:T(8,128)(2,1)S(1)}, u32[]{:S(2)}, u32[]{:S(2)}) collective-permute-start(bf16[1024,256]{1,0:T(8,128)(2,1)S(1)} %fusion.34), channel_id=1, source_target_pairs={{0,4},{4,8},{8,12},{12,16},{16,20},{20,24},{24,28},{1,5},{5,9},{9,... | collective-permute-start | bytes 1572872 | tf_op jit(solution)/shard_map/ppermute | solution.py:29
  64.4 1.4 fusion.22
  65.8 8.3 %collective-permute-done.2 = bf16[1024,256]{1,0:T(8,128)(2,1)S(1)} collective-permute-done((bf16[1024,256]{1,0:T(8,128)(2,1)S(1)}, bf16[1024,256]{1,0:T(8,128)(2,1)S(1)}, u32[]{:S(2)}, u32[]{:S(2)}) %collective-permute-start.2) | collective-permute-done | bytes 524320 | tf_op jit(solution)/shard_map/ppermute | solution.py:29
  74.1 11.3 %collective-permute-done.3 = bf16[1024,256]{1,0:T(8,128)(2,1)S(1)} collective-permute-done((bf16[1024,256]{1,0:T(8,128)(2,1)S(1)}, bf16[1024,256]{1,0:T(8,128)(2,1)S(1)}, u32[]{:S(2)}, u32[]{:S(2)}) %collective-permute-start.3) | collective-permute-done | bytes 524320 | tf_op jit(solution)/shard_map/ppermute | solution.py:29
  85.4 1.2 fusion.43
  86.6 1.3 collective-permute-start.5
  87.8 5.0 %collective-permute-start.4 = (bf16[1024,256]{1,0:T(8,128)(2,1)S(1)}, bf16[1024,256]{1,0:T(8,128)(2,1)S(1)}, u32[]{:S(2)}, u32[]{:S(2)}) collective-permute-start(bf16[1024,256]{1,0:T(8,128)(2,1)S(1)} %get-tuple-element.6), channel_id=1, source_target_pairs={{0,4},{4,8},{8,12},{12,16},{16,20},{20,24},{24,28},{1,5},{5,9},{9,... | collective-permute-start | bytes 1572872 | tf_op jit(solution)/shard_map/ppermute | solution.py:17
  92.9 10.2 %collective-permute-done.5 = bf16[1024,256]{1,0:T(8,128)(2,1)} collective-permute-done((bf16[1024,256]{1,0:T(8,128)(2,1)S(1)}, bf16[1024,256]{1,0:T(8,128)(2,1)}, u32[]{:S(2)}, u32[]{:S(2)}) %collective-permute-start.5) | collective-permute-done | bytes 524320 | tf_op jit(solution)/shard_map/ppermute | solution.py:19
  103.1 11.3 %collective-permute-done.4 = bf16[1024,256]{1,0:T(8,128)(2,1)S(1)} collective-permute-done((bf16[1024,256]{1,0:T(8,128)(2,1)S(1)}, bf16[1024,256]{1,0:T(8,128)(2,1)S(1)}, u32[]{:S(2)}, u32[]{:S(2)}) %collective-permute-start.4) | collective-permute-done | bytes 524320 | tf_op jit(solution)/shard_map/ppermute | solution.py:17
  114.4 0.8 copy-done.4
  115.2 1.1 pad_maximum_fusion.1
  117.0 0.7 broadcast_in_dim.8
  117.8 5.8 %all-to-all-start.1 = ((bf16[32,16,256]{2,1,0:T(8,128)(2,1)}), bf16[32,16,256]{2,1,0:T(8,128)(2,1)S(1)}, u32[]{:S(2)}, u32[]{:S(2)}) async-start(bf16[32,16,256]{2,1,0:T(8,128)(2,1)} %broadcast_in_dim.8), calls=%async_computation.1 | async-start | bytes 524288 | tf_op jit(solution)/shard_map/all_to_all | solution.py:68
  123.6 10.3 %convolution_bitcast_fusion.1 = f32[2048,256]{0,1:T(8,128)S(1)} fusion(bf16[2048,2048]{1,0:T(8,128)(2,1)} %param.8, bf16[2048,3072]{1,0:T(8,128)(2,1)} %fusion, f32[2048]{0:T(1024)S(1)} %copy-done.1, bf16[1024,256]{1,0:T(8,128)(2,1)} %collective-permute-done.5, bf16[1024,256]{1,0:T(8,128)(2,1)S(1)} %get-tuple-element.6, bf16[1024,256]{1,0:T(8,128)(2,1)} %copy-done.4), kind=kOutput, calls=%fused_computation.23 | convolution fusion | flops 5374476288 | bytes 24649728 | tf_op jit(solution)/shard_map/dot_general | solution.py:73
  134.7 3.6 %fusion.37 = bf16[1024,256]{1,0:T(8,128)(2,1)S(1)} fusion(bf16[2048,256]{0,1:T(8,128)(2,1)S(1)} %fusion.19, bf16[3072,2048]{1,0:T(8,128)(2,1)} %fusion.1), kind=kOutput, calls=%fused_computation.41 | convolution fusion | flops 1074003968 | bytes 5767168 | tf_op jit(solution)/shard_map/dot_general | solution.py:61
  138.3 3.6 %fusion.31 = bf16[1024,256]{1,0:T(8,128)(2,1)S(1)} fusion(bf16[2048,256]{0,1:T(8,128)(2,1)S(1)} %fusion.19, bf16[3072,2048]{1,0:T(8,128)(2,1)} %fusion.1), kind=kOutput, calls=%fused_computation.39 | convolution fusion | flops 1074003968 | bytes 5767168 | tf_op jit(solution)/shard_map/dot_general | solution.py:61
  142.0 1.3 collective-permute-start.6
  143.3 4.6 %collective-permute-start.7 = (bf16[1024,256]{1,0:T(8,128)(2,1)S(1)}, bf16[1024,256]{1,0:T(8,128)(2,1)S(1)}, u32[]{:S(2)}, u32[]{:S(2)}) collective-permute-start(bf16[1024,256]{1,0:T(8,128)(2,1)S(1)} %fusion.37), channel_id=1, source_target_pairs={{0,4},{4,8},{8,12},{12,16},{16,20},{20,24},{24,28},{1,5},{5,9},{9,... | collective-permute-start | bytes 1572872 | tf_op jit(solution)/shard_map/ppermute | solution.py:29
  147.9 1.4 fusion.25
  149.3 8.4 %collective-permute-done.6 = bf16[1024,256]{1,0:T(8,128)(2,1)S(1)} collective-permute-done((bf16[1024,256]{1,0:T(8,128)(2,1)S(1)}, bf16[1024,256]{1,0:T(8,128)(2,1)S(1)}, u32[]{:S(2)}, u32[]{:S(2)}) %collective-permute-start.6) | collective-permute-done | bytes 524320 | tf_op jit(solution)/shard_map/ppermute | solution.py:29
  157.7 11.3 %collective-permute-done.7 = bf16[1024,256]{1,0:T(8,128)(2,1)S(1)} collective-permute-done((bf16[1024,256]{1,0:T(8,128)(2,1)S(1)}, bf16[1024,256]{1,0:T(8,128)(2,1)S(1)}, u32[]{:S(2)}, u32[]{:S(2)}) %collective-permute-start.7) | collective-permute-done | bytes 524320 | tf_op jit(solution)/shard_map/ppermute | solution.py:29
  169.0 1.1 convert_add_fusion
  (45 shorter events, 5.3 us)
Async XLA Ops:
  0.6 49.8 %copy-start = (bf16[16,2048]{1,0:T(8,128)(2,1)S(1)}, bf16[16,2048]{1,0:T(8,128)(2,1)}, u32[]{:S(2)}) copy-start(bf16[16,2048]{1,0:T(8,128)(2,1)} %param.9) | copy-start | bytes 196612
  2.0 17.7 %copy-start.2 = (s32[2048]{0:T(1024)S(1)}, s32[2048]{0:T(1024)}, u32[]{:S(2)}) copy-start(s32[2048]{0:T(1024)} %param.12) | copy-start | bytes 24580
  2.0 30.1 %collective-permute-start.1 = (bf16[1024,256]{1,0:T(8,128)(2,1)S(1)}, bf16[1024,256]{1,0:T(8,128)(2,1)S(1)}, u32[]{:S(2)}, u32[]{:S(2)}) collective-permute-start(bf16[1024,256]{1,0:T(8,128)(2,1)S(1)} %convert_element_type.98), channel_id=1, source_target_pairs={{4,0},{8,4},{12,8},{16,12},{20,16},{24,20},{28,24},{5,1},{9,5},{13... | collective-permute-start | bytes 1572872 | tf_op jit(solution)/shard_map/ppermute | solution.py:19
  3.3 28.8 %collective-permute-start = (bf16[1024,256]{1,0:T(8,128)(2,1)S(1)}, bf16[1024,256]{1,0:T(8,128)(2,1)S(1)}, u32[]{:S(2)}, u32[]{:S(2)}) collective-permute-start(bf16[1024,256]{1,0:T(8,128)(2,1)S(1)} %convert_element_type.98), channel_id=1, source_target_pairs={{0,4},{4,8},{8,12},{12,16},{16,20},{20,24},{24,28},{1,5},{5,9},{9,... | collective-permute-start | bytes 1572872 | tf_op jit(solution)/shard_map/ppermute | solution.py:17
  19.6 11.1 %copy-start.6 = (s32[16]{0:T(128)S(1)}, s32[16]{0:T(128)}, u32[]{:S(2)}) copy-start(s32[16]{0:T(128)} %param.13) | copy-start | bytes 196
  19.6 11.8 %copy-start.1 = (f32[2048]{0:T(1024)S(1)}, f32[2048]{0:T(1024)}, u32[]{:S(2)}) copy-start(f32[2048]{0:T(1024)} %param.10) | copy-start | bytes 24580
  32.1 1.5 copy-start.3
  33.6 16.8 %all-to-all-start = ((bf16[32,16,256]{2,1,0:T(8,128)(2,1)}), bf16[32,16,256]{2,1,0:T(8,128)(2,1)S(1)}, u32[]{:S(2)}, u32[]{:S(2)}) async-start(bf16[32,16,256]{2,1,0:T(8,128)(2,1)} %broadcast_in_dim.7), calls=%async_computation | async-start | bytes 524288 | tf_op jit(solution)/shard_map/all_to_all | solution.py:68
  40.0 10.4 %copy-start.5 = (bf16[16,512]{1,0:T(8,128)(2,1)S(1)}, bf16[16,512]{1,0:T(8,128)(2,1)}, u32[]{:S(2)}) copy-start(bf16[16,512]{1,0:T(8,128)(2,1)} %param.11) | copy-start | bytes 49156
  51.2 13.2 %slice-start = ((s8[12582912]{0:T(1024)(128)(4,1)}), s8[4194304]{0:T(1024)(128)(4,1)S(1)}, s32[]{:S(2)}) async-start(s8[12582912]{0:T(1024)(128)(4,1)} %bitcast.42), calls=%async_computation.2 | async-start | bytes 8388608
  51.2 13.2 %slice-start.1 = ((s8[12582912]{0:T(1024)(128)(4,1)}), s8[4194304]{0:T(1024)(128)(4,1)S(1)}, s32[]{:S(2)}) async-start(s8[12582912]{0:T(1024)(128)(4,1)} %bitcast.42), calls=%async_computation.3 | async-start | bytes 8388608
  54.8 9.6 %slice-start.2 = ((s8[12582912]{0:T(1024)(128)(4,1)}), s8[4194304]{0:T(1024)(128)(4,1)S(1)}, s32[]{:S(2)}) async-start(s8[12582912]{0:T(1024)(128)(4,1)} %bitcast.42), calls=%async_computation.4 | async-start | bytes 8388608
  58.5 15.6 %collective-permute-start.2 = (bf16[1024,256]{1,0:T(8,128)(2,1)S(1)}, bf16[1024,256]{1,0:T(8,128)(2,1)S(1)}, u32[]{:S(2)}, u32[]{:S(2)}) collective-permute-start(bf16[1024,256]{1,0:T(8,128)(2,1)S(1)} %fusion.28), channel_id=1, source_target_pairs={{4,0},{8,4},{12,8},{16,12},{20,16},{24,20},{28,24},{5,1},{9,5},{13... | collective-permute-start | bytes 1572872 | tf_op jit(solution)/shard_map/ppermute | solution.py:29
  59.8 25.6 %collective-permute-start.3 = (bf16[1024,256]{1,0:T(8,128)(2,1)S(1)}, bf16[1024,256]{1,0:T(8,128)(2,1)S(1)}, u32[]{:S(2)}, u32[]{:S(2)}) collective-permute-start(bf16[1024,256]{1,0:T(8,128)(2,1)S(1)} %fusion.34), channel_id=1, source_target_pairs={{0,4},{4,8},{8,12},{12,16},{16,20},{20,24},{24,28},{1,5},{5,9},{9,... | collective-permute-start | bytes 1572872 | tf_op jit(solution)/shard_map/ppermute | solution.py:29
  86.6 16.6 %collective-permute-start.5 = (bf16[1024,256]{1,0:T(8,128)(2,1)S(1)}, bf16[1024,256]{1,0:T(8,128)(2,1)}, u32[]{:S(2)}, u32[]{:S(2)}) collective-permute-start(bf16[1024,256]{1,0:T(8,128)(2,1)S(1)} %get-tuple-element.6), channel_id=1, source_target_pairs={{4,0},{8,4},{12,8},{16,12},{20,16},{24,20},{28,24},{5,1},{9,5},{13... | collective-permute-start | bytes 1572872 | tf_op jit(solution)/shard_map/ppermute | solution.py:19
  87.8 26.6 %collective-permute-start.4 = (bf16[1024,256]{1,0:T(8,128)(2,1)S(1)}, bf16[1024,256]{1,0:T(8,128)(2,1)S(1)}, u32[]{:S(2)}, u32[]{:S(2)}) collective-permute-start(bf16[1024,256]{1,0:T(8,128)(2,1)S(1)} %get-tuple-element.6), channel_id=1, source_target_pairs={{0,4},{4,8},{8,12},{12,16},{16,20},{20,24},{24,28},{1,5},{5,9},{9,... | collective-permute-start | bytes 1572872 | tf_op jit(solution)/shard_map/ppermute | solution.py:17
  114.4 0.8 copy-start.4
  117.8 16.2 %all-to-all-start.1 = ((bf16[32,16,256]{2,1,0:T(8,128)(2,1)}), bf16[32,16,256]{2,1,0:T(8,128)(2,1)S(1)}, u32[]{:S(2)}, u32[]{:S(2)}) async-start(bf16[32,16,256]{2,1,0:T(8,128)(2,1)} %broadcast_in_dim.8), calls=%async_computation.1 | async-start | bytes 524288 | tf_op jit(solution)/shard_map/all_to_all | solution.py:68
  134.7 13.2 %slice-start.3 = ((s8[12582912]{0:T(1024)(128)(4,1)}), s8[4194304]{0:T(1024)(128)(4,1)S(1)}, s32[]{:S(2)}) async-start(s8[12582912]{0:T(1024)(128)(4,1)} %bitcast.44), calls=%async_computation.5 | async-start | bytes 8388608
  134.7 13.2 %slice-start.4 = ((s8[12582912]{0:T(1024)(128)(4,1)}), s8[4194304]{0:T(1024)(128)(4,1)S(1)}, s32[]{:S(2)}) async-start(s8[12582912]{0:T(1024)(128)(4,1)} %bitcast.44), calls=%async_computation.6 | async-start | bytes 8388608
  138.3 9.6 %slice-start.5 = ((s8[12582912]{0:T(1024)(128)(4,1)}), s8[4194304]{0:T(1024)(128)(4,1)S(1)}, s32[]{:S(2)}) async-start(s8[12582912]{0:T(1024)(128)(4,1)} %bitcast.44), calls=%async_computation.7 | async-start | bytes 8388608
  142.0 15.7 %collective-permute-start.6 = (bf16[1024,256]{1,0:T(8,128)(2,1)S(1)}, bf16[1024,256]{1,0:T(8,128)(2,1)S(1)}, u32[]{:S(2)}, u32[]{:S(2)}) collective-permute-start(bf16[1024,256]{1,0:T(8,128)(2,1)S(1)} %fusion.31), channel_id=1, source_target_pairs={{4,0},{8,4},{12,8},{16,12},{20,16},{24,20},{28,24},{5,1},{9,5},{13... | collective-permute-start | bytes 1572872 | tf_op jit(solution)/shard_map/ppermute | solution.py:29
  143.3 25.7 %collective-permute-start.7 = (bf16[1024,256]{1,0:T(8,128)(2,1)S(1)}, bf16[1024,256]{1,0:T(8,128)(2,1)S(1)}, u32[]{:S(2)}, u32[]{:S(2)}) collective-permute-start(bf16[1024,256]{1,0:T(8,128)(2,1)S(1)} %fusion.37), channel_id=1, source_target_pairs={{0,4},{4,8},{8,12},{12,16},{16,20},{20,24},{24,28},{1,5},{5,9},{9,... | collective-permute-start | bytes 1572872 | tf_op jit(solution)/shard_map/ppermute | solution.py:29

commit v8 on v6

--- a/solution.py
+++ b/solution.py
@@ -52,10 +52,10 @@
     primal_source = source_row[primal_idx]
     primal_scale = scaling[primal_idx][:, None]
 
-    picks = [
-        (source_row[:, None] == (region * own_count + jnp.arange(own_count))[None, :]).astype(jnp.bfloat16)
-        for region in range(3)
-    ]
+    padded_rows = jnp.arange(3 * own_count)
+    pick = (source_row[:, None] == padded_rows[None, :]).astype(jnp.bfloat16)
+    spread_inv = jnp.dot(schur_inv, pick, preferred_element_type=jnp.float32).astype(jnp.bfloat16)
+    spread_scale = jnp.zeros((3 * own_count,), jnp.float32).at[source_row].set(scaling)[:, None]
     places = [
         ((region * own_count + jnp.arange(own_count))[:, None] == source_row[None, :]).astype(jnp.bfloat16)
         for region in range(3)
@@ -67,16 +67,13 @@
     def precondition(vector_in):
         rounded = vector_in.astype(jnp.bfloat16)
         padded = with_halo(rounded, (("sub", 0),), own_count)
-        before = padded[:own_count]
-        after = padded[2 * own_count :]
         primal = (primal_scale * padded[primal_source].astype(jnp.float32)).astype(jnp.bfloat16)
         count = lax.axis_size("sub") * lax.axis_size("grp")
         primal_all = lax.all_to_all(
             jnp.broadcast_to(primal[None], (count,) + primal.shape), AXES, 0, 0, tiled=False
         ).reshape(-1, primal.shape[1])
-        gathered = select(picks[1], rounded) + select(picks[0], before) + select(picks[2], after)
-        scaled = (scale_column * gathered).astype(jnp.bfloat16)
-        solved = jnp.dot(schur_inv, scaled, preferred_element_type=jnp.float32)
+        scaled = (spread_scale * padded.astype(jnp.float32)).astype(jnp.bfloat16)
+        solved = jnp.dot(spread_inv, scaled, preferred_element_type=jnp.float32)
         solved = lax.optimization_barrier(solved)
         coarse = jnp.dot(coarse_inv, primal_all, preferred_element_type=jnp.float32)
         coarse_rounded = coarse.astype(jnp.bfloat16)

time: 166 us -> 185 us (1.11)
  matrix products: 41.9 us -> 65.5 us
  waiting for transfers between devices: 79.7 us -> 64.6 us
  local copies, waits for them, and re-layouts: 4.69 us -> 12 us
  other arithmetic: 2.35 us -> 6.25 us
    dot_general x2 -> x3, matrix products: 17.5 us -> 53.7 us  [the longest x1 33.4 us: shards(): jnp.dot(schur_inv, pick, preferred_element_type=jnp.float32)]
    dot_general x10 -> x6, matrix products: 22.9 us -> 10.3 us  [select(): return jnp.dot(matrix, rows, preferred_element_type=jnp.float32)]
    ppermute x2, waiting for transfers between devices: 22.8 us -> 11.8 us  [with_halo(): lax.ppermute(tail, axis, [(i, (i + 1) % count) for i in range(ends)])]
    scatter x0 -> x1, local copies, waits for them, and re-layouts: none -> 8.06 us  [shards(): jnp.zeros((3 * own_count,), jnp.float32).at[source_row].set(scaling)]
    ppermute x2, waiting for transfers between devices: 14.3 us -> 9.44 us  [with_halo(): lax.ppermute(head, axis, [((i + 1) % count, i) for i in range(ends)])]
    convert_element_type x0 -> x2, other arithmetic: none -> 3.86 us  [precondition(): weighted = (scale_column * solved).astype(jnp.bfloat16)]
    ppermute x4, starting transfers between devices: 11.9 us -> 9.06 us  [shifted(): return lax.ppermute(shard, axis, pairs)]
  transfers between devices with their start and end apart: 10 -> 10, of which waited for: 8 -> 6; matrix products, arithmetic and copies ran while one was open for 20% -> 35% of each run, Pallas kernels for 0% -> 0%
where the time goes in v8:
time: 185 us; the launch traced here: 184 us
  matrix products  65.5 us (35%)
  waiting for transfers between devices  64.6 us (35%)
  starting transfers between devices  34.7 us (19%)
  local copies, waits for them, and re-layouts  12 us (6%)
  other arithmetic  6.25 us (3%)
    ppermute x4, waiting for transfers between devices, shifted(): return lax.ppermute(shard, axis, pairs)  42.7 us
    dot_general x1, matrix products, shards(): jnp.dot(schur_inv, pick, preferred_element_type=jnp.float32)  33.4 us
    dot_general x2, matrix products, precondition(): solved = jnp.dot(spread_inv, scaled, preferred_element_type=jnp.float32)  20.2 us
    all_to_all x2, starting transfers between devices, precondition(): lax.all_to_all(jnp.broadcast_to(primal[None], (count,) + primal.shape), A...  12.5 us
    ppermute x2, waiting for transfers between devices, with_halo(): lax.ppermute(tail, axis, [(i, (i + 1) % count) for i in range(ends)])  11.8 us
    ppermute x2, starting transfers between devices, with_halo(): lax.ppermute(tail, axis, [(i, (i + 1) % count) for i in range(ends)])  10.5 us
    dot_general x6, matrix products, select(): return jnp.dot(matrix, rows, preferred_element_type=jnp.float32)  10.3 us
    ppermute x2, waiting for transfers between devices, with_halo(): lax.ppermute(head, axis, [((i + 1) % count, i) for i in range(ends)])  9.44 us
  transfers between devices with their start and end apart: 10, of which 6 were waited for; matrix products, arithmetic and copies ran while one was open for 35% of the time, Pallas kernels for 0%

profile of v8, /device:TPU:0, one launch (start us, length us, event | category | flops | bytes accessed | tf_op | source)
XLA Modules:
  0.0 184.0 jit_solution(10578353826992715493)
XLA Ops:
  0.6 1.3 convert_element_type.105
  2.0 1.3 collective-permute-start.1
  3.3 5.5 %collective-permute-start = (bf16[1024,256]{1,0:T(8,128)(2,1)S(1)}, bf16[1024,256]{1,0:T(8,128)(2,1)S(1)}, u32[]{:S(2)}, u32[]{:S(2)}) collective-permute-start(bf16[1024,256]{1,0:T(8,128)(2,1)S(1)} %convert_element_type.105), channel_id=1, source_target_pairs={{0,4},{4,8},{8,12},{12,16},{16,20},{20,24},{24,28},{1,5},{5,9},{9,... | collective-permute-start | bytes 1572872 | tf_op jit(solution)/shard_map/ppermute | solution.py:17
  8.8 0.7 compare_select_fusion
  9.5 33.4 %fusion.4 = bf16[3072,2048]{1,0:T(8,128)(2,1)} fusion(bf16[2048,2048]{1,0:T(8,128)(2,1)} %param.8, s32[2048]{0:T(1024)} %param.12), kind=kOutput, calls=%fused_computation.9 | convolution fusion | flops 25788678144 | bytes 20979712 | tf_op jit(solution)/shard_map/dot_general | solution.py:57
  44.3 8.1 %scatter_custom_fusion = f32[3072]{0:T(1024)S(1)} fusion(s32[2048]{0:T(1024)S(1)} %compare_select_fusion, f32[2048]{0:T(1024)S(1)} %copy-done.1, f32[]{:T(128)} %constant.6.clone.1), kind=kCustom, calls=%fused_computation.58 | custom fusion | bytes 12292 | tf_op jit(solution)/shard_map/scatter | solution.py:58
  53.2 0.7 broadcast_in_dim.13
  53.9 6.4 %all-to-all-start = ((bf16[32,16,256]{2,1,0:T(8,128)(2,1)}), bf16[32,16,256]{2,1,0:T(8,128)(2,1)S(1)}, u32[]{:S(2)}, u32[]{:S(2)}) async-start(bf16[32,16,256]{2,1,0:T(8,128)(2,1)} %broadcast_in_dim.13), calls=%async_computation | async-start | bytes 524288 | tf_op jit(solution)/shard_map/all_to_all | solution.py:72
  60.3 10.1 %fusion.27 = f32[2048,256]{1,0:T(8,128)} fusion(bf16[3072,2048]{1,0:T(8,128)(2,1)} %fusion.4, f32[3072]{0:T(1024)S(1)} %scatter_custom_fusion, bf16[1024,256]{1,0:T(8,128)(2,1)S(1)} %collective-permute-done.1, bf16[1024,256]{1,0:T(8,128)(2,1)S(1)} %convert_element_type.105, bf16[1024,256]{1,0:T(8,128)(2,1)S(1)} %collective-permute-done), kind=kOutput, calls=%fused_computation.37 | convolution fusion | flops 3227516928 | bytes 16265216 | tf_op jit(solution)/shard_map/dot_general | solution.py:76
  70.7 0.8 convolution_bitcast_fusion.1
  71.5 1.9 %multiply_convert_fusion.3 = bf16[2048,256]{1,0:T(8,128)(2,1)S(1)} fusion(f32[2048,256]{1,0:T(8,128)} %fusion.27, f32[2048,256]{1,0:T(8,128)S(1)} %convolution_bitcast_fusion.1, f32[2048]{0:T(1024)S(1)} %copy-done.1), kind=kLoop, calls=%fused_computation.36 | loop fusion | flops 1572864 | bytes 5251072 | tf_op jit(solution)/shard_map/convert_element_type | solution.py:83
  73.4 1.5 fusion.31
  74.9 1.3 fusion.45
  76.2 3.2 %collective-permute-start.3 = (bf16[1024,256]{1,0:T(8,128)(2,1)S(1)}, bf16[1024,256]{1,0:T(8,128)(2,1)S(1)}, u32[]{:S(2)}, u32[]{:S(2)}) collective-permute-start(bf16[1024,256]{1,0:T(8,128)(2,1)S(1)} %fusion.45), channel_id=1, source_target_pairs={{0,4},{4,8},{8,12},{12,16},{16,20},{20,24},{24,28},{1,5},{5,9},{9,... | collective-permute-start | bytes 1572872 | tf_op jit(solution)/shard_map/ppermute | solution.py:29
  79.5 1.3 collective-permute-start.2
  80.8 21.4 %collective-permute-done.3 = bf16[1024,256]{1,0:T(8,128)(2,1)S(1)} collective-permute-done((bf16[1024,256]{1,0:T(8,128)(2,1)S(1)}, bf16[1024,256]{1,0:T(8,128)(2,1)S(1)}, u32[]{:S(2)}, u32[]{:S(2)}) %collective-permute-start.3) | collective-permute-done | bytes 524320 | tf_op jit(solution)/shard_map/ppermute | solution.py:29
  102.2 2.4 %fusion.54 = (bf16[1024,256]{1,0:T(8,128)(2,1)S(1)}, f32[1024,256]{1,0:T(8,128)}) fusion(bf16[1024,256]{1,0:T(8,128)(2,1)S(1)} %collective-permute-done.3, bf16[1024,256]{1,0:T(8,128)(2,1)S(1)} %collective-permute-done.2, bf16[2048,256]{1,0:T(8,128)(2,1)S(1)} %multiply_convert_fusion.3, s32[2048]{0:T(1024)S(1)} %copy-done.2, s32[1024]{0:T(1024)S(1)} %iota_add_fusion.1), kind=kOutput, calls=%fused_computation.67 | convolution fusion | flops 1077673984 | bytes 3682304 | tf_op jit(solution)/shard_map/dot_general | solution.py:65
  104.6 1.3 collective-permute-start.5
  105.9 5.0 %collective-permute-start.4 = (bf16[1024,256]{1,0:T(8,128)(2,1)S(1)}, bf16[1024,256]{1,0:T(8,128)(2,1)S(1)}, u32[]{:S(2)}, u32[]{:S(2)}) collective-permute-start(bf16[1024,256]{1,0:T(8,128)(2,1)S(1)} %get-tuple-element.2), channel_id=1, source_target_pairs={{0,4},{4,8},{8,12},{12,16},{16,20},{20,24},{24,28},{1,5},{5,9},{9,... | collective-permute-start | bytes 1572872 | tf_op jit(solution)/shard_map/ppermute | solution.py:17
  110.9 9.4 %collective-permute-done.5 = bf16[1024,256]{1,0:T(8,128)(2,1)S(1)} collective-permute-done((bf16[1024,256]{1,0:T(8,128)(2,1)S(1)}, bf16[1024,256]{1,0:T(8,128)(2,1)S(1)}, u32[]{:S(2)}, u32[]{:S(2)}) %collective-permute-start.5) | collective-permute-done | bytes 524320 | tf_op jit(solution)/shard_map/ppermute | solution.py:19
  120.3 11.8 %collective-permute-done.4 = bf16[1024,256]{1,0:T(8,128)(2,1)S(1)} collective-permute-done((bf16[1024,256]{1,0:T(8,128)(2,1)S(1)}, bf16[1024,256]{1,0:T(8,128)(2,1)S(1)}, u32[]{:S(2)}, u32[]{:S(2)}) %collective-permute-start.4) | collective-permute-done | bytes 524320 | tf_op jit(solution)/shard_map/ppermute | solution.py:17
  132.9 0.7 broadcast_in_dim.14
  133.7 6.1 %all-to-all-start.1 = ((bf16[32,16,256]{2,1,0:T(8,128)(2,1)}), bf16[32,16,256]{2,1,0:T(8,128)(2,1)S(1)}, u32[]{:S(2)}, u32[]{:S(2)}) async-start(bf16[32,16,256]{2,1,0:T(8,128)(2,1)} %broadcast_in_dim.14), calls=%async_computation.1 | async-start | bytes 524288 | tf_op jit(solution)/shard_map/all_to_all | solution.py:72
  139.8 10.1 %fusion.28 = f32[2048,256]{1,0:T(8,128)} fusion(bf16[3072,2048]{1,0:T(8,128)(2,1)} %fusion.4, f32[3072]{0:T(1024)S(1)} %scatter_custom_fusion, bf16[1024,256]{1,0:T(8,128)(2,1)S(1)} %collective-permute-done.5, bf16[1024,256]{1,0:T(8,128)(2,1)S(1)} %get-tuple-element.2, bf16[1024,256]{1,0:T(8,128)(2,1)S(1)} %collective-permute-done.4), kind=kOutput, calls=%fused_computation.38 | convolution fusion | flops 3227516928 | bytes 16265216 | tf_op jit(solution)/shard_map/dot_general | solution.py:76
  150.2 0.8 convolution_bitcast_fusion
  150.9 1.9 %multiply_convert_fusion.2 = bf16[2048,256]{1,0:T(8,128)(2,1)S(1)} fusion(f32[2048,256]{1,0:T(8,128)} %fusion.28, f32[2048,256]{1,0:T(8,128)S(1)} %convolution_bitcast_fusion, f32[2048]{0:T(1024)S(1)} %copy-done.1), kind=kLoop, calls=%fused_computation.35 | loop fusion | flops 1572864 | bytes 5251072 | tf_op jit(solution)/shard_map/convert_element_type | solution.py:83
  152.9 1.3 fusion.48
  154.2 1.5 fusion.32
  155.7 3.2 %collective-permute-start.7 = (bf16[1024,256]{1,0:T(8,128)(2,1)S(1)}, bf16[1024,256]{1,0:T(8,128)(2,1)S(1)}, u32[]{:S(2)}, u32[]{:S(2)}) collective-permute-start(bf16[1024,256]{1,0:T(8,128)(2,1)S(1)} %fusion.48), channel_id=1, source_target_pairs={{0,4},{4,8},{8,12},{12,16},{16,20},{20,24},{24,28},{1,5},{5,9},{9,... | collective-permute-start | bytes 1572872 | tf_op jit(solution)/shard_map/ppermute | solution.py:29
  158.9 1.3 collective-permute-start.6
  160.2 21.4 %collective-permute-done.7 = bf16[1024,256]{1,0:T(8,128)(2,1)S(1)} collective-permute-done((bf16[1024,256]{1,0:T(8,128)(2,1)S(1)}, bf16[1024,256]{1,0:T(8,128)(2,1)S(1)}, u32[]{:S(2)}, u32[]{:S(2)}) %collective-permute-start.7) | collective-permute-done | bytes 524320 | tf_op jit(solution)/shard_map/ppermute | solution.py:29
  181.6 2.4 %convert_add_fusion = f32[1024,256]{1,0:T(8,128)} fusion(bf16[1024,256]{1,0:T(8,128)(2,1)S(1)} %collective-permute-done.7, bf16[1024,256]{1,0:T(8,128)(2,1)S(1)} %collective-permute-done.6, bf16[2048,256]{1,0:T(8,128)(2,1)S(1)} %multiply_convert_fusion.2, s32[2048]{0:T(1024)S(1)} %copy-done.2, s32[1024]{0:T(1024)S(1)} %iota_add_fusion.1), kind=kOutput, calls=%fused_computation.53 | convolution fusion | flops 1077411840 | bytes 3158016 | tf_op jit(solution)/shard_map/dot_general | solution.py:65
  (30 shorter events, 3.5 us)
Async XLA Ops:
  0.6 70.1 %copy-start = (bf16[16,2048]{1,0:T(8,128)(2,1)S(1)}, bf16[16,2048]{1,0:T(8,128)(2,1)}, u32[]{:S(2)}) copy-start(bf16[16,2048]{1,0:T(8,128)(2,1)} %param.9) | copy-start | bytes 196612
  2.0 50.4 %collective-permute-start.1 = (bf16[1024,256]{1,0:T(8,128)(2,1)S(1)}, bf16[1024,256]{1,0:T(8,128)(2,1)S(1)}, u32[]{:S(2)}, u32[]{:S(2)}) collective-permute-start(bf16[1024,256]{1,0:T(8,128)(2,1)S(1)} %convert_element_type.105), channel_id=1, source_target_pairs={{4,0},{8,4},{12,8},{16,12},{20,16},{24,20},{28,24},{5,1},{9,5},{13... | collective-permute-start | bytes 1572872 | tf_op jit(solution)/shard_map/ppermute | solution.py:19
  3.3 49.1 %collective-permute-start = (bf16[1024,256]{1,0:T(8,128)(2,1)S(1)}, bf16[1024,256]{1,0:T(8,128)(2,1)S(1)}, u32[]{:S(2)}, u32[]{:S(2)}) collective-permute-start(bf16[1024,256]{1,0:T(8,128)(2,1)S(1)} %convert_element_type.105), channel_id=1, source_target_pairs={{0,4},{4,8},{8,12},{12,16},{16,20},{20,24},{24,28},{1,5},{5,9},{9,... | collective-permute-start | bytes 1572872 | tf_op jit(solution)/shard_map/ppermute | solution.py:17
  9.5 33.5 %copy-start.4 = (s32[16]{0:T(128)S(1)}, s32[16]{0:T(128)}, u32[]{:S(2)}) copy-start(s32[16]{0:T(128)} %param.13) | copy-start | bytes 196
  9.5 33.5 %copy-start.2 = (s32[2048]{0:T(1024)S(1)}, s32[2048]{0:T(1024)}, u32[]{:S(2)}) copy-start(s32[2048]{0:T(1024)} %param.12) | copy-start | bytes 24580
  9.5 34.1 %copy-start.1 = (f32[2048]{0:T(1024)S(1)}, f32[2048]{0:T(1024)}, u32[]{:S(2)}) copy-start(f32[2048]{0:T(1024)} %param.10) | copy-start | bytes 24580
  53.9 16.8 %all-to-all-start = ((bf16[32,16,256]{2,1,0:T(8,128)(2,1)}), bf16[32,16,256]{2,1,0:T(8,128)(2,1)S(1)}, u32[]{:S(2)}, u32[]{:S(2)}) async-start(bf16[32,16,256]{2,1,0:T(8,128)(2,1)} %broadcast_in_dim.13), calls=%async_computation | async-start | bytes 524288 | tf_op jit(solution)/shard_map/all_to_all | solution.py:72
  60.3 10.4 %copy-start.3 = (bf16[16,512]{1,0:T(8,128)(2,1)S(1)}, bf16[16,512]{1,0:T(8,128)(2,1)}, u32[]{:S(2)}) copy-start(bf16[16,512]{1,0:T(8,128)(2,1)} %param.11) | copy-start | bytes 49156
  76.2 25.9 %collective-permute-start.3 = (bf16[1024,256]{1,0:T(8,128)(2,1)S(1)}, bf16[1024,256]{1,0:T(8,128)(2,1)S(1)}, u32[]{:S(2)}, u32[]{:S(2)}) collective-permute-start(bf16[1024,256]{1,0:T(8,128)(2,1)S(1)} %fusion.45), channel_id=1, source_target_pairs={{0,4},{4,8},{8,12},{12,16},{16,20},{20,24},{24,28},{1,5},{5,9},{9,... | collective-permute-start | bytes 1572872 | tf_op jit(solution)/shard_map/ppermute | solution.py:29
  79.5 22.7 %collective-permute-start.2 = (bf16[1024,256]{1,0:T(8,128)(2,1)S(1)}, bf16[1024,256]{1,0:T(8,128)(2,1)S(1)}, u32[]{:S(2)}, u32[]{:S(2)}) collective-permute-start(bf16[1024,256]{1,0:T(8,128)(2,1)S(1)} %fusion.31), channel_id=1, source_target_pairs={{4,0},{8,4},{12,8},{16,12},{20,16},{24,20},{28,24},{5,1},{9,5},{13... | collective-permute-start | bytes 1572872 | tf_op jit(solution)/shard_map/ppermute | solution.py:29
  104.6 15.8 %collective-permute-start.5 = (bf16[1024,256]{1,0:T(8,128)(2,1)S(1)}, bf16[1024,256]{1,0:T(8,128)(2,1)S(1)}, u32[]{:S(2)}, u32[]{:S(2)}) collective-permute-start(bf16[1024,256]{1,0:T(8,128)(2,1)S(1)} %get-tuple-element.2), channel_id=1, source_target_pairs={{4,0},{8,4},{12,8},{16,12},{20,16},{24,20},{28,24},{5,1},{9,5},{13... | collective-permute-start | bytes 1572872 | tf_op jit(solution)/shard_map/ppermute | solution.py:19
  105.9 26.3 %collective-permute-start.4 = (bf16[1024,256]{1,0:T(8,128)(2,1)S(1)}, bf16[1024,256]{1,0:T(8,128)(2,1)S(1)}, u32[]{:S(2)}, u32[]{:S(2)}) collective-permute-start(bf16[1024,256]{1,0:T(8,128)(2,1)S(1)} %get-tuple-element.2), channel_id=1, source_target_pairs={{0,4},{4,8},{8,12},{12,16},{16,20},{20,24},{24,28},{1,5},{5,9},{9,... | collective-permute-start | bytes 1572872 | tf_op jit(solution)/shard_map/ppermute | solution.py:17
  133.7 16.5 %all-to-all-start.1 = ((bf16[32,16,256]{2,1,0:T(8,128)(2,1)}), bf16[32,16,256]{2,1,0:T(8,128)(2,1)S(1)}, u32[]{:S(2)}, u32[]{:S(2)}) async-start(bf16[32,16,256]{2,1,0:T(8,128)(2,1)} %broadcast_in_dim.14), calls=%async_computation.1 | async-start | bytes 524288 | tf_op jit(solution)/shard_map/all_to_all | solution.py:72
  155.7 25.9 %collective-permute-start.7 = (bf16[1024,256]{1,0:T(8,128)(2,1)S(1)}, bf16[1024,256]{1,0:T(8,128)(2,1)S(1)}, u32[]{:S(2)}, u32[]{:S(2)}) collective-permute-start(bf16[1024,256]{1,0:T(8,128)(2,1)S(1)} %fusion.48), channel_id=1, source_target_pairs={{0,4},{4,8},{8,12},{12,16},{16,20},{20,24},{24,28},{1,5},{5,9},{9,... | collective-permute-start | bytes 1572872 | tf_op jit(solution)/shard_map/ppermute | solution.py:29
  158.9 22.7 %collective-permute-start.6 = (bf16[1024,256]{1,0:T(8,128)(2,1)S(1)}, bf16[1024,256]{1,0:T(8,128)(2,1)S(1)}, u32[]{:S(2)}, u32[]{:S(2)}) collective-permute-start(bf16[1024,256]{1,0:T(8,128)(2,1)S(1)} %fusion.32), channel_id=1, source_target_pairs={{4,0},{8,4},{12,8},{16,12},{20,16},{24,20},{28,24},{5,1},{9,5},{13... | collective-permute-start | bytes 1572872 | tf_op jit(solution)/shard_map/ppermute | solution.py:29

commit v9 on v8

--- a/solution.py
+++ b/solution.py
@@ -1,6 +1,8 @@
 import jax
 import jax.numpy as jnp
 from jax import lax
+from jax.experimental import pallas as pl
+from jax.experimental.pallas import tpu as pltpu
 from jax.sharding import PartitionSpec as P
 
 AXES = ("sub", "grp")
@@ -46,16 +48,53 @@
     return held
 
 
+def _solve_kernel(rows_ref, padded_ref, scale_ref, block_ref, out_ref, gathered_ref, scaled_ref):
+    @pl.when(pl.program_id(0) == 0)
+    def _():
+        def body(l, carry):
+            gathered_ref[pl.ds(l, 1), :] = padded_ref[pl.ds(rows_ref[l], 1), :]
+            return carry
+
+        lax.fori_loop(0, gathered_ref.shape[0], body, 0, unroll=8)
+        scaled_ref[...] = (scale_ref[...] * gathered_ref[...]).astype(jnp.bfloat16)
+
+    out_ref[...] = jnp.dot(block_ref[...], scaled_ref[...], preferred_element_type=jnp.float32)
+
+
+def gather_solve(factor, padded, rows, scale_column, block=256):
+    size, width = factor.shape[0], padded.shape[1]
+    return pl.pallas_call(
+        _solve_kernel,
+        out_shape=jax.ShapeDtypeStruct((size, width), jnp.float32),
+        grid_spec=pltpu.PrefetchScalarGridSpec(
+            num_scalar_prefetch=1,
+            grid=(size // block,),
+            in_specs=[
+                pl.BlockSpec(padded.shape, lambda i, r: (0, 0)),
+                pl.BlockSpec(scale_column.shape, lambda i, r: (0, 0)),
+                pl.BlockSpec((block, factor.shape[1]), lambda i, r: (i, 0)),
+            ],
+            out_specs=pl.BlockSpec((block, width), lambda i, r: (i, 0)),
+            scratch_shapes=[
+                pltpu.VMEM((factor.shape[1], width), jnp.float32),
+                pltpu.VMEM((factor.shape[1], width), jnp.bfloat16),
+            ],
+        ),
+        compiler_params=pltpu.CompilerParams(dimension_semantics=("arbitrary",)),
+        cost_estimate=pl.CostEstimate(
+            flops=2 * size * factor.shape[1] * width,
+            bytes_accessed=factor.size * 2 + padded.size * 4 + size * width * 4,
+            transcendentals=0,
+        ),
+    )(rows, padded, scale_column, factor)
+
+
 def shards(resid, schur_inv, basis, scaling, coarse_inv, source_row, primal_idx):
     own_count = resid.shape[0]
     scale_column = scaling[:, None]
     primal_source = source_row[primal_idx]
     primal_scale = scaling[primal_idx][:, None]
 
-    padded_rows = jnp.arange(3 * own_count)
-    pick = (source_row[:, None] == padded_rows[None, :]).astype(jnp.bfloat16)
-    spread_inv = jnp.dot(schur_inv, pick, preferred_element_type=jnp.float32).astype(jnp.bfloat16)
-    spread_scale = jnp.zeros((3 * own_count,), jnp.float32).at[source_row].set(scaling)[:, None]
     places = [
         ((region * own_count + jnp.arange(own_count))[:, None] == source_row[None, :]).astype(jnp.bfloat16)
         for region in range(3)
@@ -66,15 +105,13 @@
 
     def precondition(vector_in):
         rounded = vector_in.astype(jnp.bfloat16)
-        padded = with_halo(rounded, (("sub", 0),), own_count)
-        primal = (primal_scale * padded[primal_source].astype(jnp.float32)).astype(jnp.bfloat16)
+        padded = with_halo(rounded, (("sub", 0),), own_count).astype(jnp.float32)
+        primal = (primal_scale * padded[primal_source]).astype(jnp.bfloat16)
         count = lax.axis_size("sub") * lax.axis_size("grp")
         primal_all = lax.all_to_all(
             jnp.broadcast_to(primal[None], (count,) + primal.shape), AXES, 0, 0, tiled=False
         ).reshape(-1, primal.shape[1])
-        scaled = (spread_scale * padded.astype(jnp.float32)).astype(jnp.bfloat16)
-        solved = jnp.dot(spread_inv, scaled, preferred_element_type=jnp.float32)
-        solved = lax.optimization_barrier(solved)
+        solved = gather_solve(schur_inv, padded, source_row, scale_column)
         coarse = jnp.dot(coarse_inv, primal_all, preferred_element_type=jnp.float32)
         coarse_rounded = coarse.astype(jnp.bfloat16)
         solved = solved + lax.dot_general(
@@ -85,7 +122,7 @@
         to_next = select(places[2], weighted).astype(jnp.bfloat16)
         from_next = shifted(to_previous, "sub", -1)
         from_previous = shifted(to_next, "sub", 1)
-        kept = select(places[1], weighted).astype(jnp.bfloat16)
+        kept = lax.optimization_barrier(select(places[1], weighted).astype(jnp.bfloat16))
         return (
             kept.astype(jnp.float32)
             + from_next.astype(jnp.float32)

time: 185 us -> 184 us (level)
  matrix products: 65.5 us -> 12.4 us
  Pallas kernels: 0 us -> 37 us
  waiting for transfers between devices: 64.6 us -> 78.4 us
  local copies, waits for them, and re-layouts: 12 us -> 7.49 us
  other arithmetic: 6.25 us -> 10.4 us
    dot_general x3 -> x0, matrix products: 53.7 us -> none  [the longest x1 33.4 us: shards(): jnp.dot(schur_inv, pick, preferred_element_type=jnp.float32)]
    pallas_call x0 -> x2, Pallas kernels: none -> 37 us  [gather_solve(): pl.pallas_call(_solve_kernel, out_shape=jax.ShapeDtypeStruct((size, width...]
    ppermute x2, waiting for transfers between devices: 11.8 us -> 22.4 us  [with_halo(): lax.ppermute(tail, axis, [(i, (i + 1) % count) for i in range(ends)])]
    scatter x1 -> x0, local copies, waits for them, and re-layouts: 8.06 us -> none  [shards(): jnp.zeros((3 * own_count,), jnp.float32).at[source_row].set(scaling)]
    ppermute x2, waiting for transfers between devices: 9.44 us -> 15.9 us  [with_halo(): lax.ppermute(head, axis, [((i + 1) % count, i) for i in range(ends)])]
    dot_general x2, matrix products: 1.52 us -> 4.19 us  [precondition(): lax.dot_general(basis, coarse_rounded, (((0,), (0,)), ((), ())), preferre...]
    ppermute x4, waiting for transfers between devices: 42.7 us -> 40.1 us  [shifted(): return lax.ppermute(shard, axis, pairs)]
    dot_general x6, matrix products: 10.3 us -> 8.24 us  [select(): return jnp.dot(matrix, rows, preferred_element_type=jnp.float32)]
  transfers between devices with their start and end apart: 10 -> 10, of which waited for: 6 -> 6; matrix products, arithmetic and copies ran while one was open for 35% -> 4% of each run, Pallas kernels for 0% -> 20%
where the time goes in v9:
time: 184 us; the launch traced here: 182 us
  waiting for transfers between devices  78.4 us (43%)
  Pallas kernels  37 us (20%)
  starting transfers between devices  35.7 us (19%)
  matrix products  12.4 us (7%)
  other arithmetic  10.4 us (6%)
  local copies, waits for them, and re-layouts  7.49 us (4%)
    ppermute x4, waiting for transfers between devices, shifted(): return lax.ppermute(shard, axis, pairs)  40.1 us
    pallas_call x2, Pallas kernels, gather_solve(): pl.pallas_call(_solve_kernel, out_shape=jax.ShapeDtypeStruct((size, width...  37 us
    ppermute x2, waiting for transfers between devices, with_halo(): lax.ppermute(tail, axis, [(i, (i + 1) % count) for i in range(ends)])  22.4 us
    ppermute x2, waiting for transfers between devices, with_halo(): lax.ppermute(head, axis, [((i + 1) % count, i) for i in range(ends)])  15.9 us
    all_to_all x2, starting transfers between devices, precondition(): lax.all_to_all(jnp.broadcast_to(primal[None], (count,) + primal.shape), A...  12 us
    ppermute x2, starting transfers between devices, with_halo(): lax.ppermute(tail, axis, [(i, (i + 1) % count) for i in range(ends)])  11.3 us
    ppermute x4, starting transfers between devices, shifted(): return lax.ppermute(shard, axis, pairs)  9.82 us
    dot_general x6, matrix products, select(): return jnp.dot(matrix, rows, preferred_element_type=jnp.float32)  8.24 us
  transfers between devices with their start and end apart: 10, of which 6 were waited for; matrix products, arithmetic and copies ran while one was open for 4% of the time, Pallas kernels for 20%

profile of v9, /device:TPU:0, one launch (start us, length us, event | category | flops | bytes accessed | tf_op | source)
XLA Modules:
  0.0 182.4 jit_solution(14402502387086218684)
XLA Ops:
  0.7 1.3 convert_element_type.79
  2.0 1.3 collective-permute-start.1
  3.3 6.3 %collective-permute-start = (bf16[1024,256]{1,0:T(8,128)(2,1)S(1)}, bf16[1024,256]{1,0:T(8,128)(2,1)}, u32[]{:S(2)}, u32[]{:S(2)}) collective-permute-start(bf16[1024,256]{1,0:T(8,128)(2,1)S(1)} %convert_element_type.79), channel_id=1, source_target_pairs={{0,4},{4,8},{8,12},{12,16},{16,20},{20,24},{24,28},{1,5},{5,9},{9,... | collective-permute-start | bytes 1572872 | tf_op jit(solution)/shard_map/ppermute | solution.py:19
  10.2 1.4 gather_fusion.1
  12.3 6.5 %collective-permute-done.1 = bf16[1024,256]{1,0:T(8,128)(2,1)S(1)} collective-permute-done((bf16[1024,256]{1,0:T(8,128)(2,1)S(1)}, bf16[1024,256]{1,0:T(8,128)(2,1)S(1)}, u32[]{:S(2)}, u32[]{:S(2)}) %collective-permute-start.1) | collective-permute-done | bytes 524320 | tf_op jit(solution)/shard_map/ppermute | solution.py:21
  19.5 10.6 %collective-permute-done = bf16[1024,256]{1,0:T(8,128)(2,1)} collective-permute-done((bf16[1024,256]{1,0:T(8,128)(2,1)S(1)}, bf16[1024,256]{1,0:T(8,128)(2,1)}, u32[]{:S(2)}, u32[]{:S(2)}) %collective-permute-start) | collective-permute-done | bytes 524320 | tf_op jit(solution)/shard_map/ppermute | solution.py:19
  30.1 1.6 maximum_convert_fusion.padded_ref
  33.5 5.9 %all-to-all-start = ((bf16[32,16,256]{2,1,0:T(8,128)(2,1)}), bf16[32,16,256]{2,1,0:T(8,128)(2,1)S(1)}, u32[]{:S(2)}, u32[]{:S(2)}) async-start(bf16[32,16,256]{2,1,0:T(8,128)(2,1)} %broadcast_in_dim.10), calls=%async_computation | async-start | bytes 524288 | tf_op jit(solution)/shard_map/all_to_all | solution.py:111
  39.4 1.3 copy.11.scale_ref
  40.8 18.6 %shard_map.86 = f32[2048,256]{1,0:T(8,128)} custom-call(s32[2048]{0:T(1024)} %rows_ref.3, f32[3072,256]{1,0:T(8,128)} %copy-done.5, f32[2048,1]{1,0:T(8,128)} %copy.11.scale_ref, bf16[2048,2048]{1,0:T(8,128)(2,1)} %block_ref.3), custom_call_target="tpu_custom_call" | custom-call | flops 2147483648 | bytes 13631488 | tf_op jit(solution)/shard_map/pallas_call | solution.py:66
  59.4 2.1 %convolution_bitcast_fusion.1 = f32[2048,256]{1,0:T(8,128)} fusion(bf16[16,2048]{1,0:T(8,128)(2,1)S(1)} %copy-done, bf16[512,256]{1,0:T(8,128)(2,1)S(1)} %bitcast.24, bf16[16,512]{1,0:T(8,128)(2,1)S(1)} %copy-done.10), kind=kOutput, calls=%fused_computation.26 | convolution fusion | flops 20975616 | bytes 2441216 | tf_op jit(solution)/shard_map/dot_general | solution.py:117
  61.5 2.0 %multiply_convert_fusion.1 = bf16[2048,256]{1,0:T(8,128)(2,1)S(1)} fusion(f32[2048,256]{1,0:T(8,128)S(1)} %copy-done.7, f32[2048,256]{1,0:T(8,128)} %convolution_bitcast_fusion.1, f32[2048]{0:T(1024)S(1)} %copy-done.1), kind=kLoop, calls=%fused_computation.28 | loop fusion | flops 1572864 | bytes 5251072 | tf_op jit(solution)/shard_map/convert_element_type | solution.py:120
  63.5 1.5 fusion.20
  65.0 1.3 fusion.28
  66.3 3.7 %collective-permute-start.3 = (bf16[1024,256]{1,0:T(8,128)(2,1)S(1)}, bf16[1024,256]{1,0:T(8,128)(2,1)S(1)}, u32[]{:S(2)}, u32[]{:S(2)}) collective-permute-start(bf16[1024,256]{1,0:T(8,128)(2,1)S(1)} %fusion.28), channel_id=1, source_target_pairs={{0,4},{4,8},{8,12},{12,16},{16,20},{20,24},{24,28},{1,5},{5,9},{9,... | collective-permute-start | bytes 1572872 | tf_op jit(solution)/shard_map/ppermute | solution.py:31
  70.0 1.3 collective-permute-start.2
  71.3 1.3 fusion.22
  72.7 20.0 %collective-permute-done.3 = bf16[1024,256]{1,0:T(8,128)(2,1)S(1)} collective-permute-done((bf16[1024,256]{1,0:T(8,128)(2,1)S(1)}, bf16[1024,256]{1,0:T(8,128)(2,1)S(1)}, u32[]{:S(2)}, u32[]{:S(2)}) %collective-permute-start.3) | collective-permute-done | bytes 524320 | tf_op jit(solution)/shard_map/ppermute | solution.py:31
  93.9 1.3 collective-permute-start.5
  95.2 5.0 %collective-permute-start.4 = (bf16[1024,256]{1,0:T(8,128)(2,1)S(1)}, bf16[1024,256]{1,0:T(8,128)(2,1)S(1)}, u32[]{:S(2)}, u32[]{:S(2)}) collective-permute-start(bf16[1024,256]{1,0:T(8,128)(2,1)S(1)} %get-tuple-element.2), channel_id=1, source_target_pairs={{0,4},{4,8},{8,12},{12,16},{16,20},{20,24},{24,28},{1,5},{5,9},{9,... | collective-permute-start | bytes 1572872 | tf_op jit(solution)/shard_map/ppermute | solution.py:19
  100.3 9.4 %collective-permute-done.5 = bf16[1024,256]{1,0:T(8,128)(2,1)S(1)} collective-permute-done((bf16[1024,256]{1,0:T(8,128)(2,1)S(1)}, bf16[1024,256]{1,0:T(8,128)(2,1)S(1)}, u32[]{:S(2)}, u32[]{:S(2)}) %collective-permute-start.5) | collective-permute-done | bytes 524320 | tf_op jit(solution)/shard_map/ppermute | solution.py:21
  109.7 11.8 %collective-permute-done.4 = bf16[1024,256]{1,0:T(8,128)(2,1)S(1)} collective-permute-done((bf16[1024,256]{1,0:T(8,128)(2,1)S(1)}, bf16[1024,256]{1,0:T(8,128)(2,1)S(1)}, u32[]{:S(2)}, u32[]{:S(2)}) %collective-permute-start.4) | collective-permute-done | bytes 524320 | tf_op jit(solution)/shard_map/ppermute | solution.py:19
  123.5 6.1 %all-to-all-start.1 = ((bf16[32,16,256]{2,1,0:T(8,128)(2,1)}), bf16[32,16,256]{2,1,0:T(8,128)(2,1)S(1)}, u32[]{:S(2)}, u32[]{:S(2)}) async-start(bf16[32,16,256]{2,1,0:T(8,128)(2,1)} %broadcast_in_dim.11), calls=%async_computation.1 | async-start | bytes 524288 | tf_op jit(solution)/shard_map/all_to_all | solution.py:111
  129.6 18.4 %shard_map.87 = f32[2048,256]{1,0:T(8,128)} custom-call(s32[2048]{0:T(1024)} %rows_ref.3, f32[3072,256]{1,0:T(8,128)} %copy-done.4, f32[2048,1]{1,0:T(8,128)} %copy.11.scale_ref, bf16[2048,2048]{1,0:T(8,128)(2,1)} %block_ref.3), custom_call_target="tpu_custom_call" | custom-call | flops 2147483648 | bytes 13631488 | tf_op jit(solution)/shard_map/pallas_call | solution.py:66
  148.0 2.1 %convolution_bitcast_fusion = f32[2048,256]{1,0:T(8,128)} fusion(bf16[16,2048]{1,0:T(8,128)(2,1)S(1)} %copy-done, bf16[512,256]{1,0:T(8,128)(2,1)S(1)} %bitcast.25, bf16[16,512]{1,0:T(8,128)(2,1)S(1)} %copy-done.10), kind=kOutput, calls=%fused_computation.25 | convolution fusion | flops 20975616 | bytes 2441216 | tf_op jit(solution)/shard_map/dot_general | solution.py:117
  150.1 2.0 %multiply_convert_fusion = bf16[2048,256]{1,0:T(8,128)(2,1)S(1)} fusion(f32[2048,256]{1,0:T(8,128)S(1)} %copy-done.6, f32[2048,256]{1,0:T(8,128)} %convolution_bitcast_fusion, f32[2048]{0:T(1024)S(1)} %copy-done.1), kind=kLoop, calls=%fused_computation.27 | loop fusion | flops 1572864 | bytes 5251072 | tf_op jit(solution)/shard_map/convert_element_type | solution.py:120
  152.2 1.3 fusion.31
  153.5 1.5 fusion.21
  155.0 3.5 %collective-permute-start.7 = (bf16[1024,256]{1,0:T(8,128)(2,1)S(1)}, bf16[1024,256]{1,0:T(8,128)(2,1)S(1)}, u32[]{:S(2)}, u32[]{:S(2)}) collective-permute-start(bf16[1024,256]{1,0:T(8,128)(2,1)S(1)} %fusion.31), channel_id=1, source_target_pairs={{0,4},{4,8},{8,12},{12,16},{16,20},{20,24},{24,28},{1,5},{5,9},{9,... | collective-permute-start | bytes 1572872 | tf_op jit(solution)/shard_map/ppermute | solution.py:31
  158.5 1.3 collective-permute-start.6
  159.8 1.3 fusion.25
  161.2 20.1 %collective-permute-done.7 = bf16[1024,256]{1,0:T(8,128)(2,1)S(1)} collective-permute-done((bf16[1024,256]{1,0:T(8,128)(2,1)S(1)}, bf16[1024,256]{1,0:T(8,128)(2,1)S(1)}, u32[]{:S(2)}, u32[]{:S(2)}) %collective-permute-start.7) | collective-permute-done | bytes 524320 | tf_op jit(solution)/shard_map/ppermute | solution.py:31
  (42 shorter events, 8.2 us)
Async XLA Ops:
  0.6 58.7 %copy-start = (bf16[16,2048]{1,0:T(8,128)(2,1)S(1)}, bf16[16,2048]{1,0:T(8,128)(2,1)}, u32[]{:S(2)}) copy-start(bf16[16,2048]{1,0:T(8,128)(2,1)} %param.9) | copy-start | bytes 196612
  0.6 10.9 %copy-start.1 = (f32[2048]{0:T(1024)S(1)}, f32[2048]{0:T(1024)}, u32[]{:S(2)}) copy-start(f32[2048]{0:T(1024)} %param.10) | copy-start | bytes 24580
  2.0 16.8 %copy-start.8 = (bf16[1024,256]{1,0:T(8,128)(2,1)}, bf16[1024,256]{1,0:T(8,128)(2,1)S(1)}, u32[]{:S(2)}) copy-start(bf16[1024,256]{1,0:T(8,128)(2,1)S(1)} %convert_element_type.79) | copy-start | bytes 1572868
  2.0 16.8 %collective-permute-start.1 = (bf16[1024,256]{1,0:T(8,128)(2,1)S(1)}, bf16[1024,256]{1,0:T(8,128)(2,1)S(1)}, u32[]{:S(2)}, u32[]{:S(2)}) collective-permute-start(bf16[1024,256]{1,0:T(8,128)(2,1)S(1)} %convert_element_type.79), channel_id=1, source_target_pairs={{4,0},{8,4},{12,8},{16,12},{20,16},{24,20},{28,24},{5,1},{9,5},{13... | collective-permute-start | bytes 1572872 | tf_op jit(solution)/shard_map/ppermute | solution.py:21
  3.3 26.8 %collective-permute-start = (bf16[1024,256]{1,0:T(8,128)(2,1)S(1)}, bf16[1024,256]{1,0:T(8,128)(2,1)}, u32[]{:S(2)}, u32[]{:S(2)}) collective-permute-start(bf16[1024,256]{1,0:T(8,128)(2,1)S(1)} %convert_element_type.79), channel_id=1, source_target_pairs={{0,4},{4,8},{8,12},{12,16},{16,20},{20,24},{24,28},{1,5},{5,9},{9,... | collective-permute-start | bytes 1572872 | tf_op jit(solution)/shard_map/ppermute | solution.py:19
  18.8 0.8 copy-start.9
  31.7 9.0 %copy-start.5 = (f32[3072,256]{1,0:T(8,128)}, f32[3072,256]{1,0:T(8,128)S(1)}, u32[]{:S(2)}) copy-start(f32[3072,256]{1,0:T(8,128)S(1)} %maximum_convert_fusion.padded_ref) | copy-start | bytes 9437188
  33.5 25.9 %all-to-all-start = ((bf16[32,16,256]{2,1,0:T(8,128)(2,1)}), bf16[32,16,256]{2,1,0:T(8,128)(2,1)S(1)}, u32[]{:S(2)}, u32[]{:S(2)}) async-start(bf16[32,16,256]{2,1,0:T(8,128)(2,1)} %broadcast_in_dim.10), calls=%async_computation | async-start | bytes 524288 | tf_op jit(solution)/shard_map/all_to_all | solution.py:111
  40.8 18.6 %copy-start.10 = (bf16[16,512]{1,0:T(8,128)(2,1)S(1)}, bf16[16,512]{1,0:T(8,128)(2,1)}, u32[]{:S(2)}) copy-start(bf16[16,512]{1,0:T(8,128)(2,1)} %param.11) | copy-start | bytes 49156
  59.3 2.1 %copy-start.7 = (f32[2048,256]{1,0:T(8,128)S(1)}, f32[2048,256]{1,0:T(8,128)}, u32[]{:S(2)}) copy-start(f32[2048,256]{1,0:T(8,128)} %shard_map.86) | copy-start | bytes 6291460
  61.5 2.0 %copy-start.2 = (s32[2048]{0:T(1024)S(1)}, s32[2048]{0:T(1024)}, u32[]{:S(2)}) copy-start(s32[2048]{0:T(1024)} %rows_ref.3) | copy-start | bytes 24580
  66.3 26.4 %collective-permute-start.3 = (bf16[1024,256]{1,0:T(8,128)(2,1)S(1)}, bf16[1024,256]{1,0:T(8,128)(2,1)S(1)}, u32[]{:S(2)}, u32[]{:S(2)}) collective-permute-start(bf16[1024,256]{1,0:T(8,128)(2,1)S(1)} %fusion.28), channel_id=1, source_target_pairs={{0,4},{4,8},{8,12},{12,16},{16,20},{20,24},{24,28},{1,5},{5,9},{9,... | collective-permute-start | bytes 1572872 | tf_op jit(solution)/shard_map/ppermute | solution.py:31
  70.0 22.7 %collective-permute-start.2 = (bf16[1024,256]{1,0:T(8,128)(2,1)S(1)}, bf16[1024,256]{1,0:T(8,128)(2,1)S(1)}, u32[]{:S(2)}, u32[]{:S(2)}) collective-permute-start(bf16[1024,256]{1,0:T(8,128)(2,1)S(1)} %fusion.20), channel_id=1, source_target_pairs={{4,0},{8,4},{12,8},{16,12},{20,16},{24,20},{28,24},{5,1},{9,5},{13... | collective-permute-start | bytes 1572872 | tf_op jit(solution)/shard_map/ppermute | solution.py:31
  93.9 15.8 %collective-permute-start.5 = (bf16[1024,256]{1,0:T(8,128)(2,1)S(1)}, bf16[1024,256]{1,0:T(8,128)(2,1)S(1)}, u32[]{:S(2)}, u32[]{:S(2)}) collective-permute-start(bf16[1024,256]{1,0:T(8,128)(2,1)S(1)} %get-tuple-element.2), channel_id=1, source_target_pairs={{4,0},{8,4},{12,8},{16,12},{20,16},{24,20},{28,24},{5,1},{9,5},{13... | collective-permute-start | bytes 1572872 | tf_op jit(solution)/shard_map/ppermute | solution.py:21
  95.2 26.3 %collective-permute-start.4 = (bf16[1024,256]{1,0:T(8,128)(2,1)S(1)}, bf16[1024,256]{1,0:T(8,128)(2,1)S(1)}, u32[]{:S(2)}, u32[]{:S(2)}) collective-permute-start(bf16[1024,256]{1,0:T(8,128)(2,1)S(1)} %get-tuple-element.2), channel_id=1, source_target_pairs={{0,4},{4,8},{8,12},{12,16},{16,20},{20,24},{24,28},{1,5},{5,9},{9,... | collective-permute-start | bytes 1572872 | tf_op jit(solution)/shard_map/ppermute | solution.py:19
  121.8 7.8 %copy-start.4 = (f32[3072,256]{1,0:T(8,128)}, f32[3072,256]{1,0:T(8,128)S(1)}, u32[]{:S(2)}) copy-start(f32[3072,256]{1,0:T(8,128)S(1)} %maximum_convert_fusion.1.padded_ref) | copy-start | bytes 9437188
  123.5 24.6 %all-to-all-start.1 = ((bf16[32,16,256]{2,1,0:T(8,128)(2,1)}), bf16[32,16,256]{2,1,0:T(8,128)(2,1)S(1)}, u32[]{:S(2)}, u32[]{:S(2)}) async-start(bf16[32,16,256]{2,1,0:T(8,128)(2,1)} %broadcast_in_dim.11), calls=%async_computation.1 | async-start | bytes 524288 | tf_op jit(solution)/shard_map/all_to_all | solution.py:111
  148.0 2.1 %copy-start.6 = (f32[2048,256]{1,0:T(8,128)S(1)}, f32[2048,256]{1,0:T(8,128)}, u32[]{:S(2)}) copy-start(f32[2048,256]{1,0:T(8,128)} %shard_map.87) | copy-start | bytes 6291460
  150.1 2.0 %copy-start.3 = (s32[2048]{0:T(1024)S(1)}, s32[2048]{0:T(1024)}, u32[]{:S(2)}) copy-start(s32[2048]{0:T(1024)} %rows_ref.3) | copy-start | bytes 24580
  155.0 26.2 %collective-permute-start.7 = (bf16[1024,256]{1,0:T(8,128)(2,1)S(1)}, bf16[1024,256]{1,0:T(8,128)(2,1)S(1)}, u32[]{:S(2)}, u32[]{:S(2)}) collective-permute-start(bf16[1024,256]{1,0:T(8,128)(2,1)S(1)} %fusion.31), channel_id=1, source_target_pairs={{0,4},{4,8},{8,12},{12,16},{16,20},{20,24},{24,28},{1,5},{5,9},{9,... | collective-permute-start | bytes 1572872 | tf_op jit(solution)/shard_map/ppermute | solution.py:31
  158.5 22.7 %collective-permute-start.6 = (bf16[1024,256]{1,0:T(8,128)(2,1)S(1)}, bf16[1024,256]{1,0:T(8,128)(2,1)S(1)}, u32[]{:S(2)}, u32[]{:S(2)}) collective-permute-start(bf16[1024,256]{1,0:T(8,128)(2,1)S(1)} %fusion.21), channel_id=1, source_target_pairs={{4,0},{8,4},{12,8},{16,12},{20,16},{24,20},{28,24},{5,1},{9,5},{13... | collective-permute-start | bytes 1572872 | tf_op jit(solution)/shard_map/ppermute | solution.py:31

commit v10 on v6

--- a/solution.py
+++ b/solution.py
@@ -88,7 +88,7 @@
         to_next = select(places[2], weighted).astype(jnp.bfloat16)
         from_next = shifted(to_previous, "sub", -1)
         from_previous = shifted(to_next, "sub", 1)
-        kept = select(places[1], weighted).astype(jnp.bfloat16)
+        kept = lax.optimization_barrier(select(places[1], weighted).astype(jnp.bfloat16))
         return (
             kept.astype(jnp.float32)
             + from_next.astype(jnp.float32)

time: 166 us -> 164 us (0.988)
  waiting for transfers between devices: 79.7 us -> 76.9 us
  other arithmetic: 2.35 us -> 4.65 us
  matrix products: 41.9 us -> 39.9 us
    ppermute x4, waiting for transfers between devices: 42.6 us -> 39.9 us  [shifted(): return lax.ppermute(shard, axis, pairs)]
    dot_general x10, matrix products: 22.9 us -> 21.1 us  [select(): return jnp.dot(matrix, rows, preferred_element_type=jnp.float32)]
  transfers between devices with their start and end apart: 10 -> 10, of which waited for: 8 -> 8; matrix products, arithmetic and copies ran while one was open for 20% -> 22% of each run, Pallas kernels for 0% -> 0%
where the time goes in v10:
time: 164 us; the launch traced here: 163 us
  waiting for transfers between devices  76.9 us (47%)
  matrix products  39.9 us (24%)
  starting transfers between devices  36.5 us (22%)
  local copies, waits for them, and re-layouts  4.66 us (3%)
  other arithmetic  4.65 us (3%)
    ppermute x4, waiting for transfers between devices, shifted(): return lax.ppermute(shard, axis, pairs)  39.9 us
    ppermute x2, waiting for transfers between devices, with_halo(): lax.ppermute(tail, axis, [(i, (i + 1) % count) for i in range(ends)])  22.8 us
    dot_general x10, matrix products, select(): return jnp.dot(matrix, rows, preferred_element_type=jnp.float32)  21.1 us
    dot_general x2, matrix products, precondition(): solved = jnp.dot(schur_inv, scaled, preferred_element_type=jnp.float32)  17.4 us
    ppermute x2, waiting for transfers between devices, with_halo(): lax.ppermute(head, axis, [((i + 1) % count, i) for i in range(ends)])  14.3 us
    ppermute x4, starting transfers between devices, shifted(): return lax.ppermute(shard, axis, pairs)  11.9 us
    all_to_all x2, starting transfers between devices, precondition(): lax.all_to_all(jnp.broadcast_to(primal[None], (count,) + primal.shape), A...  11.4 us
    ppermute x2, starting transfers between devices, with_halo(): lax.ppermute(tail, axis, [(i, (i + 1) % count) for i in range(ends)])  10.6 us
  transfers between devices with their start and end apart: 10, of which 8 were waited for; matrix products, arithmetic and copies ran while one was open for 22% of the time, Pallas kernels for 0%

profile of v10, /device:TPU:0, one launch (start us, length us, event | category | flops | bytes accessed | tf_op | source)
XLA Modules:
  0.0 163.4 jit_solution(17853987965046464955)
XLA Ops:
  0.7 1.3 convert_element_type.96
  2.0 1.3 collective-permute-start.1
  3.3 5.5 %collective-permute-start = (bf16[1024,256]{1,0:T(8,128)(2,1)S(1)}, bf16[1024,256]{1,0:T(8,128)(2,1)S(1)}, u32[]{:S(2)}, u32[]{:S(2)}) collective-permute-start(bf16[1024,256]{1,0:T(8,128)(2,1)S(1)} %convert_element_type.96), channel_id=1, source_target_pairs={{0,4},{4,8},{8,12},{12,16},{16,20},{20,24},{24,28},{1,5},{5,9},{9,... | collective-permute-start | bytes 1572872 | tf_op jit(solution)/shard_map/ppermute | solution.py:17
  9.5 1.4 gather_fusion
  11.5 3.1 %fusion.10 = f32[2048,256]{0,1:T(8,128)} fusion(bf16[1024,256]{1,0:T(8,128)(2,1)S(1)} %convert_element_type.96, s32[1024]{0:T(1024)S(1)} %iota_add_fusion.1, s32[2048]{0:T(1024)S(1)} %copy-done.2), kind=kOutput, calls=%fused_computation.14 | convolution fusion | flops 1075838976 | bytes 2633728 | tf_op jit(solution)/shard_map/dot_general | solution.py:65
  14.6 4.1 %collective-permute-done.1 = bf16[1024,256]{1,0:T(8,128)(2,1)S(1)} collective-permute-done((bf16[1024,256]{1,0:T(8,128)(2,1)S(1)}, bf16[1024,256]{1,0:T(8,128)(2,1)S(1)}, u32[]{:S(2)}, u32[]{:S(2)}) %collective-permute-start.1) | collective-permute-done | bytes 524320 | tf_op jit(solution)/shard_map/ppermute | solution.py:19
  18.7 11.4 %collective-permute-done = bf16[1024,256]{1,0:T(8,128)(2,1)S(1)} collective-permute-done((bf16[1024,256]{1,0:T(8,128)(2,1)S(1)}, bf16[1024,256]{1,0:T(8,128)(2,1)S(1)}, u32[]{:S(2)}, u32[]{:S(2)}) %collective-permute-start) | collective-permute-done | bytes 524320 | tf_op jit(solution)/shard_map/ppermute | solution.py:17
  31.6 5.8 %all-to-all-start = ((bf16[32,16,256]{2,1,0:T(8,128)(2,1)}), bf16[32,16,256]{2,1,0:T(8,128)(2,1)S(1)}, u32[]{:S(2)}, u32[]{:S(2)}) async-start(bf16[32,16,256]{2,1,0:T(8,128)(2,1)} %broadcast_in_dim.7), calls=%async_computation | async-start | bytes 524288 | tf_op jit(solution)/shard_map/all_to_all | solution.py:74
  37.5 3.1 %fusion.6 = f32[2048,256]{0,1:T(8,128)} fusion(bf16[1024,256]{1,0:T(8,128)(2,1)S(1)} %collective-permute-done.1, s32[1024]{0:T(1024)S(1)} %iota_add_fusion, s32[2048]{0:T(1024)S(1)} %copy-done.2), kind=kOutput, calls=%fused_computation.10 | convolution fusion | flops 1075838976 | bytes 2633728 | tf_op jit(solution)/shard_map/dot_general | solution.py:65
  40.5 8.8 %convolution_bitcast_fusion.3 = f32[2048,256]{0,1:T(8,128)S(1)} fusion(bf16[2048,2048]{1,0:T(8,128)(2,1)} %param.8, f32[2048,256]{0,1:T(8,128)} %fusion.6, f32[2048,256]{0,1:T(8,128)} %fusion.10, bf16[1024,256]{1,0:T(8,128)(2,1)S(1)} %collective-permute-done, s32[2048]{0:T(1024)S(1)} %copy-done.2, f32[2048]{0:T(1024)S(1)} %copy-done.1), kind=kOutput, calls=%fused_computation.53 | convolution fusion | flops 3225419776 | bytes 15220736 | tf_op jit(solution)/shard_map/dot_general | solution.py:79
  50.1 1.4 fusion.70
  51.5 1.5 fusion.62
  53.0 1.3 collective-permute-start.2
  54.3 4.8 %collective-permute-start.3 = (bf16[1024,256]{1,0:T(8,128)(2,1)S(1)}, bf16[1024,256]{1,0:T(8,128)(2,1)S(1)}, u32[]{:S(2)}, u32[]{:S(2)}) collective-permute-start(bf16[1024,256]{1,0:T(8,128)(2,1)S(1)} %fusion.70), channel_id=1, source_target_pairs={{0,4},{4,8},{8,12},{12,16},{16,20},{20,24},{24,28},{1,5},{5,9},{9,... | collective-permute-start | bytes 1572872 | tf_op jit(solution)/shard_map/ppermute | solution.py:29
  59.1 1.4 fusion.64
  60.4 8.5 %collective-permute-done.2 = bf16[1024,256]{1,0:T(8,128)(2,1)S(1)} collective-permute-done((bf16[1024,256]{1,0:T(8,128)(2,1)S(1)}, bf16[1024,256]{1,0:T(8,128)(2,1)S(1)}, u32[]{:S(2)}, u32[]{:S(2)}) %collective-permute-start.2) | collective-permute-done | bytes 524320 | tf_op jit(solution)/shard_map/ppermute | solution.py:29
  69.0 11.3 %collective-permute-done.3 = bf16[1024,256]{1,0:T(8,128)(2,1)S(1)} collective-permute-done((bf16[1024,256]{1,0:T(8,128)(2,1)S(1)}, bf16[1024,256]{1,0:T(8,128)(2,1)S(1)}, u32[]{:S(2)}, u32[]{:S(2)}) %collective-permute-start.3) | collective-permute-done | bytes 524320 | tf_op jit(solution)/shard_map/ppermute | solution.py:29
  81.5 1.3 collective-permute-start.5
  82.7 5.0 %collective-permute-start.4 = (bf16[1024,256]{1,0:T(8,128)(2,1)S(1)}, bf16[1024,256]{1,0:T(8,128)(2,1)S(1)}, u32[]{:S(2)}, u32[]{:S(2)}) collective-permute-start(bf16[1024,256]{1,0:T(8,128)(2,1)S(1)} %get-tuple-element.2), channel_id=1, source_target_pairs={{0,4},{4,8},{8,12},{12,16},{16,20},{20,24},{24,28},{1,5},{5,9},{9,... | collective-permute-start | bytes 1572872 | tf_op jit(solution)/shard_map/ppermute | solution.py:17
  87.8 10.1 %collective-permute-done.5 = bf16[1024,256]{1,0:T(8,128)(2,1)S(1)} collective-permute-done((bf16[1024,256]{1,0:T(8,128)(2,1)S(1)}, bf16[1024,256]{1,0:T(8,128)(2,1)S(1)}, u32[]{:S(2)}, u32[]{:S(2)}) %collective-permute-start.5) | collective-permute-done | bytes 524320 | tf_op jit(solution)/shard_map/ppermute | solution.py:19
  97.9 11.4 %collective-permute-done.4 = bf16[1024,256]{1,0:T(8,128)(2,1)S(1)} collective-permute-done((bf16[1024,256]{1,0:T(8,128)(2,1)S(1)}, bf16[1024,256]{1,0:T(8,128)(2,1)S(1)}, u32[]{:S(2)}, u32[]{:S(2)}) %collective-permute-start.4) | collective-permute-done | bytes 524320 | tf_op jit(solution)/shard_map/ppermute | solution.py:17
  110.8 5.6 %all-to-all-start.1 = ((bf16[32,16,256]{2,1,0:T(8,128)(2,1)}), bf16[32,16,256]{2,1,0:T(8,128)(2,1)S(1)}, u32[]{:S(2)}, u32[]{:S(2)}) async-start(bf16[32,16,256]{2,1,0:T(8,128)(2,1)} %broadcast_in_dim.8), calls=%async_computation.1 | async-start | bytes 524288 | tf_op jit(solution)/shard_map/all_to_all | solution.py:74
  116.4 3.3 %fusion.18 = f32[2048,256]{0,1:T(8,128)} fusion(bf16[1024,256]{1,0:T(8,128)(2,1)S(1)} %collective-permute-done.4, s32[2048]{0:T(1024)S(1)} %copy-done.2), kind=kOutput, calls=%fused_computation.24 | convolution fusion | flops 1075838976 | bytes 2629632 | tf_op jit(solution)/shard_map/dot_general | solution.py:65
  119.7 3.1 %fusion.4 = f32[2048,256]{0,1:T(8,128)} fusion(bf16[1024,256]{1,0:T(8,128)(2,1)S(1)} %collective-permute-done.5, s32[1024]{0:T(1024)S(1)} %iota_add_fusion, s32[2048]{0:T(1024)S(1)} %copy-done.2), kind=kOutput, calls=%fused_computation.8 | convolution fusion | flops 1075838976 | bytes 2633728 | tf_op jit(solution)/shard_map/dot_general | solution.py:65
  122.8 8.6 %convolution_bitcast_fusion.1 = f32[2048,256]{0,1:T(8,128)S(1)} fusion(bf16[2048,2048]{1,0:T(8,128)(2,1)} %param.8, f32[2048,256]{0,1:T(8,128)} %fusion.4, f32[2048,256]{0,1:T(8,128)} %fusion.18, bf16[1024,256]{1,0:T(8,128)(2,1)S(1)} %get-tuple-element.2, s32[1024]{0:T(1024)S(1)} %iota_add_fusion.1, s32[2048]{0:T(1024)S(1)} %copy-done.2, f32[2048]{0:T(1024)S(1)} %copy-done.1), kind=kOutput, calls=%fused_computation.49 | convolution fusion | flops 3225419776 | bytes 15224832 | tf_op jit(solution)/shard_map/dot_general | solution.py:79
  132.1 1.4 fusion.73
  133.5 1.5 fusion.63
  135.0 1.3 collective-permute-start.6
  136.3 4.6 %collective-permute-start.7 = (bf16[1024,256]{1,0:T(8,128)(2,1)S(1)}, bf16[1024,256]{1,0:T(8,128)(2,1)S(1)}, u32[]{:S(2)}, u32[]{:S(2)}) collective-permute-start(bf16[1024,256]{1,0:T(8,128)(2,1)S(1)} %fusion.73), channel_id=1, source_target_pairs={{0,4},{4,8},{8,12},{12,16},{16,20},{20,24},{24,28},{1,5},{5,9},{9,... | collective-permute-start | bytes 1572872 | tf_op jit(solution)/shard_map/ppermute | solution.py:29
  140.9 1.4 fusion.67
  142.3 8.7 %collective-permute-done.6 = bf16[1024,256]{1,0:T(8,128)(2,1)S(1)} collective-permute-done((bf16[1024,256]{1,0:T(8,128)(2,1)S(1)}, bf16[1024,256]{1,0:T(8,128)(2,1)S(1)}, u32[]{:S(2)}, u32[]{:S(2)}) %collective-permute-start.6) | collective-permute-done | bytes 524320 | tf_op jit(solution)/shard_map/ppermute | solution.py:29
  151.0 11.3 %collective-permute-done.7 = bf16[1024,256]{1,0:T(8,128)(2,1)S(1)} collective-permute-done((bf16[1024,256]{1,0:T(8,128)(2,1)S(1)}, bf16[1024,256]{1,0:T(8,128)(2,1)S(1)}, u32[]{:S(2)}, u32[]{:S(2)}) %collective-permute-start.7) | collective-permute-done | bytes 524320 | tf_op jit(solution)/shard_map/ppermute | solution.py:29
  (29 shorter events, 8.1 us)
Async XLA Ops:
  0.6 48.7 %copy-start = (bf16[16,2048]{1,0:T(8,128)(2,1)S(1)}, bf16[16,2048]{1,0:T(8,128)(2,1)}, u32[]{:S(2)}) copy-start(bf16[16,2048]{1,0:T(8,128)(2,1)} %param.9) | copy-start | bytes 196612
  0.6 10.2 %copy-start.2 = (s32[2048]{0:T(1024)S(1)}, s32[2048]{0:T(1024)}, u32[]{:S(2)}) copy-start(s32[2048]{0:T(1024)} %param.12) | copy-start | bytes 24580
  2.0 16.8 %collective-permute-start.1 = (bf16[1024,256]{1,0:T(8,128)(2,1)S(1)}, bf16[1024,256]{1,0:T(8,128)(2,1)S(1)}, u32[]{:S(2)}, u32[]{:S(2)}) collective-permute-start(bf16[1024,256]{1,0:T(8,128)(2,1)S(1)} %convert_element_type.96), channel_id=1, source_target_pairs={{4,0},{8,4},{12,8},{16,12},{20,16},{24,20},{28,24},{5,1},{9,5},{13... | collective-permute-start | bytes 1572872 | tf_op jit(solution)/shard_map/ppermute | solution.py:19
  3.3 26.8 %collective-permute-start = (bf16[1024,256]{1,0:T(8,128)(2,1)S(1)}, bf16[1024,256]{1,0:T(8,128)(2,1)S(1)}, u32[]{:S(2)}, u32[]{:S(2)}) collective-permute-start(bf16[1024,256]{1,0:T(8,128)(2,1)S(1)} %convert_element_type.96), channel_id=1, source_target_pairs={{0,4},{4,8},{8,12},{12,16},{16,20},{20,24},{24,28},{1,5},{5,9},{9,... | collective-permute-start | bytes 1572872 | tf_op jit(solution)/shard_map/ppermute | solution.py:17
  31.6 17.7 %all-to-all-start = ((bf16[32,16,256]{2,1,0:T(8,128)(2,1)}), bf16[32,16,256]{2,1,0:T(8,128)(2,1)S(1)}, u32[]{:S(2)}, u32[]{:S(2)}) async-start(bf16[32,16,256]{2,1,0:T(8,128)(2,1)} %broadcast_in_dim.7), calls=%async_computation | async-start | bytes 524288 | tf_op jit(solution)/shard_map/all_to_all | solution.py:74
  37.5 3.1 %copy-start.1 = (f32[2048]{0:T(1024)S(1)}, f32[2048]{0:T(1024)}, u32[]{:S(2)}) copy-start(f32[2048]{0:T(1024)} %param.10) | copy-start | bytes 24580
  40.5 8.8 %copy-start.3 = (bf16[16,512]{1,0:T(8,128)(2,1)S(1)}, bf16[16,512]{1,0:T(8,128)(2,1)}, u32[]{:S(2)}) copy-start(bf16[16,512]{1,0:T(8,128)(2,1)} %param.11) | copy-start | bytes 49156
  53.0 16.0 %collective-permute-start.2 = (bf16[1024,256]{1,0:T(8,128)(2,1)S(1)}, bf16[1024,256]{1,0:T(8,128)(2,1)S(1)}, u32[]{:S(2)}, u32[]{:S(2)}) collective-permute-start(bf16[1024,256]{1,0:T(8,128)(2,1)S(1)} %fusion.62), channel_id=1, source_target_pairs={{4,0},{8,4},{12,8},{16,12},{20,16},{24,20},{28,24},{5,1},{9,5},{13... | collective-permute-start | bytes 1572872 | tf_op jit(solution)/shard_map/ppermute | solution.py:29
  54.3 26.0 %collective-permute-start.3 = (bf16[1024,256]{1,0:T(8,128)(2,1)S(1)}, bf16[1024,256]{1,0:T(8,128)(2,1)S(1)}, u32[]{:S(2)}, u32[]{:S(2)}) collective-permute-start(bf16[1024,256]{1,0:T(8,128)(2,1)S(1)} %fusion.70), channel_id=1, source_target_pairs={{0,4},{4,8},{8,12},{12,16},{16,20},{20,24},{24,28},{1,5},{5,9},{9,... | collective-permute-start | bytes 1572872 | tf_op jit(solution)/shard_map/ppermute | solution.py:29
  81.5 16.5 %collective-permute-start.5 = (bf16[1024,256]{1,0:T(8,128)(2,1)S(1)}, bf16[1024,256]{1,0:T(8,128)(2,1)S(1)}, u32[]{:S(2)}, u32[]{:S(2)}) collective-permute-start(bf16[1024,256]{1,0:T(8,128)(2,1)S(1)} %get-tuple-element.2), channel_id=1, source_target_pairs={{4,0},{8,4},{12,8},{16,12},{20,16},{24,20},{28,24},{5,1},{9,5},{13... | collective-permute-start | bytes 1572872 | tf_op jit(solution)/shard_map/ppermute | solution.py:19
  82.7 26.6 %collective-permute-start.4 = (bf16[1024,256]{1,0:T(8,128)(2,1)S(1)}, bf16[1024,256]{1,0:T(8,128)(2,1)S(1)}, u32[]{:S(2)}, u32[]{:S(2)}) collective-permute-start(bf16[1024,256]{1,0:T(8,128)(2,1)S(1)} %get-tuple-element.2), channel_id=1, source_target_pairs={{0,4},{4,8},{8,12},{12,16},{16,20},{20,24},{24,28},{1,5},{5,9},{9,... | collective-permute-start | bytes 1572872 | tf_op jit(solution)/shard_map/ppermute | solution.py:17
  110.8 20.6 %all-to-all-start.1 = ((bf16[32,16,256]{2,1,0:T(8,128)(2,1)}), bf16[32,16,256]{2,1,0:T(8,128)(2,1)S(1)}, u32[]{:S(2)}, u32[]{:S(2)}) async-start(bf16[32,16,256]{2,1,0:T(8,128)(2,1)} %broadcast_in_dim.8), calls=%async_computation.1 | async-start | bytes 524288 | tf_op jit(solution)/shard_map/all_to_all | solution.py:74
  135.0 16.0 %collective-permute-start.6 = (bf16[1024,256]{1,0:T(8,128)(2,1)S(1)}, bf16[1024,256]{1,0:T(8,128)(2,1)S(1)}, u32[]{:S(2)}, u32[]{:S(2)}) collective-permute-start(bf16[1024,256]{1,0:T(8,128)(2,1)S(1)} %fusion.63), channel_id=1, source_target_pairs={{4,0},{8,4},{12,8},{16,12},{20,16},{24,20},{28,24},{5,1},{9,5},{13... | collective-permute-start | bytes 1572872 | tf_op jit(solution)/shard_map/ppermute | solution.py:29
  136.3 26.0 %collective-permute-start.7 = (bf16[1024,256]{1,0:T(8,128)(2,1)S(1)}, bf16[1024,256]{1,0:T(8,128)(2,1)S(1)}, u32[]{:S(2)}, u32[]{:S(2)}) collective-permute-start(bf16[1024,256]{1,0:T(8,128)(2,1)S(1)} %fusion.73), channel_id=1, source_target_pairs={{0,4},{4,8},{8,12},{12,16},{16,20},{20,24},{24,28},{1,5},{5,9},{9,... | collective-permute-start | bytes 1572872 | tf_op jit(solution)/shard_map/ppermute | solution.py:29

commit v11 on v10

--- a/solution.py
+++ b/solution.py
@@ -74,7 +74,8 @@
         primal_all = lax.all_to_all(
             jnp.broadcast_to(primal[None], (count,) + primal.shape), AXES, 0, 0, tiled=False
         ).reshape(-1, primal.shape[1])
-        gathered = select(picks[1], rounded) + select(picks[0], before) + select(picks[2], after)
+        gathered_own = lax.optimization_barrier(select(picks[1], rounded))
+        gathered = gathered_own + select(picks[0], before) + select(picks[2], after)
         scaled = (scale_column * gathered).astype(jnp.bfloat16)
         solved = jnp.dot(schur_inv, scaled, preferred_element_type=jnp.float32)
         solved = lax.optimization_barrier(solved)

time: 164 us -> 161 us (0.982)
  waiting for transfers between devices: 76.9 us -> 73.8 us
    ppermute x2, waiting for transfers between devices: 14.3 us -> 11.1 us  [with_halo(): lax.ppermute(head, axis, [((i + 1) % count, i) for i in range(ends)])]
where the time goes in v11:
time: 161 us; the launch traced here: 160 us
  waiting for transfers between devices  73.8 us (46%)
  matrix products  40.6 us (25%)
  starting transfers between devices  36.4 us (23%)
  other arithmetic  4.64 us (3%)
  local copies, waits for them, and re-layouts  3.96 us (2%)
    ppermute x4, waiting for transfers between devices, shifted(): return lax.ppermute(shard, axis, pairs)  39.9 us
    ppermute x2, waiting for transfers between devices, with_halo(): lax.ppermute(tail, axis, [(i, (i + 1) % count) for i in range(ends)])  22.8 us
    dot_general x10, matrix products, select(): return jnp.dot(matrix, rows, preferred_element_type=jnp.float32)  21.6 us
    dot_general x2, matrix products, precondition(): solved = jnp.dot(schur_inv, scaled, preferred_element_type=jnp.float32)  17.6 us
    ppermute x4, starting transfers between devices, shifted(): return lax.ppermute(shard, axis, pairs)  11.9 us
    all_to_all x2, starting transfers between devices, precondition(): lax.all_to_all(jnp.broadcast_to(primal[None], (count,) + primal.shape), A...  11.4 us
    ppermute x2, waiting for transfers between devices, with_halo(): lax.ppermute(head, axis, [((i + 1) % count, i) for i in range(ends)])  11.1 us
    ppermute x2, starting transfers between devices, with_halo(): lax.ppermute(tail, axis, [(i, (i + 1) % count) for i in range(ends)])  10.6 us
  transfers between devices with their start and end apart: 10, of which 8 were waited for; matrix products, arithmetic and copies ran while one was open for 22% of the time, Pallas kernels for 0%

profile of v11, /device:TPU:0, one launch (start us, length us, event | category | flops | bytes accessed | tf_op | source)
XLA Modules:
  0.0 160.3 jit_solution(6009484375036210818)
XLA Ops:
  0.6 1.3 convert_element_type.96
  2.0 1.3 collective-permute-start.1
  3.3 5.5 %collective-permute-start = (bf16[1024,256]{1,0:T(8,128)(2,1)S(1)}, bf16[1024,256]{1,0:T(8,128)(2,1)S(1)}, u32[]{:S(2)}, u32[]{:S(2)}) collective-permute-start(bf16[1024,256]{1,0:T(8,128)(2,1)S(1)} %convert_element_type.96), channel_id=1, source_target_pairs={{0,4},{4,8},{8,12},{12,16},{16,20},{20,24},{24,28},{1,5},{5,9},{9,... | collective-permute-start | bytes 1572872 | tf_op jit(solution)/shard_map/ppermute | solution.py:17
  9.4 3.8 %fusion.10 = f32[2048,256]{0,1:T(8,128)} fusion(bf16[1024,256]{1,0:T(8,128)(2,1)S(1)} %convert_element_type.96, s32[1024]{0:T(1024)S(1)} %iota_add_fusion.1, s32[2048]{0:T(1024)} %param.12), kind=kOutput, calls=%fused_computation.14 | convolution fusion | flops 1075838976 | bytes 2633728 | tf_op jit(solution)/shard_map/dot_general | solution.py:65
  14.6 4.1 %collective-permute-done.1 = bf16[1024,256]{1,0:T(8,128)(2,1)S(1)} collective-permute-done((bf16[1024,256]{1,0:T(8,128)(2,1)S(1)}, bf16[1024,256]{1,0:T(8,128)(2,1)S(1)}, u32[]{:S(2)}, u32[]{:S(2)}) %collective-permute-start.1) | collective-permute-done | bytes 524320 | tf_op jit(solution)/shard_map/ppermute | solution.py:19
  18.7 11.4 %collective-permute-done = bf16[1024,256]{1,0:T(8,128)(2,1)S(1)} collective-permute-done((bf16[1024,256]{1,0:T(8,128)(2,1)S(1)}, bf16[1024,256]{1,0:T(8,128)(2,1)S(1)}, u32[]{:S(2)}, u32[]{:S(2)}) %collective-permute-start) | collective-permute-done | bytes 524320 | tf_op jit(solution)/shard_map/ppermute | solution.py:17
  31.6 5.8 %all-to-all-start = ((bf16[32,16,256]{2,1,0:T(8,128)(2,1)}), bf16[32,16,256]{2,1,0:T(8,128)(2,1)S(1)}, u32[]{:S(2)}, u32[]{:S(2)}) async-start(bf16[32,16,256]{2,1,0:T(8,128)(2,1)} %broadcast_in_dim.7), calls=%async_computation | async-start | bytes 524288 | tf_op jit(solution)/shard_map/all_to_all | solution.py:74
  37.4 3.1 %fusion.6 = f32[2048,256]{0,1:T(8,128)} fusion(bf16[1024,256]{1,0:T(8,128)(2,1)S(1)} %collective-permute-done.1, s32[1024]{0:T(1024)S(1)} %iota_add_fusion, s32[2048]{0:T(1024)S(1)} %copy-done.2), kind=kOutput, calls=%fused_computation.10 | convolution fusion | flops 1075838976 | bytes 2633728 | tf_op jit(solution)/shard_map/dot_general | solution.py:65
  40.5 8.8 %convolution_bitcast_fusion.3 = f32[2048,256]{0,1:T(8,128)S(1)} fusion(bf16[2048,2048]{1,0:T(8,128)(2,1)} %param.8, f32[2048,256]{0,1:T(8,128)} %fusion.6, f32[2048,256]{0,1:T(8,128)} %fusion.10, bf16[1024,256]{1,0:T(8,128)(2,1)S(1)} %collective-permute-done, s32[2048]{0:T(1024)S(1)} %copy-done.2, f32[2048]{0:T(1024)S(1)} %copy-done.1), kind=kOutput, calls=%fused_computation.53 | convolution fusion | flops 3225419776 | bytes 15220736 | tf_op jit(solution)/shard_map/dot_general | solution.py:80
  50.1 1.3 fusion.58
  51.4 1.5 fusion.50
  53.0 1.3 collective-permute-start.2
  54.3 4.8 %collective-permute-start.3 = (bf16[1024,256]{1,0:T(8,128)(2,1)S(1)}, bf16[1024,256]{1,0:T(8,128)(2,1)S(1)}, u32[]{:S(2)}, u32[]{:S(2)}) collective-permute-start(bf16[1024,256]{1,0:T(8,128)(2,1)S(1)} %fusion.58), channel_id=1, source_target_pairs={{0,4},{4,8},{8,12},{12,16},{16,20},{20,24},{24,28},{1,5},{5,9},{9,... | collective-permute-start | bytes 1572872 | tf_op jit(solution)/shard_map/ppermute | solution.py:29
  59.1 1.3 fusion.52
  60.4 8.6 %collective-permute-done.2 = bf16[1024,256]{1,0:T(8,128)(2,1)S(1)} collective-permute-done((bf16[1024,256]{1,0:T(8,128)(2,1)S(1)}, bf16[1024,256]{1,0:T(8,128)(2,1)S(1)}, u32[]{:S(2)}, u32[]{:S(2)}) %collective-permute-start.2) | collective-permute-done | bytes 524320 | tf_op jit(solution)/shard_map/ppermute | solution.py:29
  69.0 11.3 %collective-permute-done.3 = bf16[1024,256]{1,0:T(8,128)(2,1)S(1)} collective-permute-done((bf16[1024,256]{1,0:T(8,128)(2,1)S(1)}, bf16[1024,256]{1,0:T(8,128)(2,1)S(1)}, u32[]{:S(2)}, u32[]{:S(2)}) %collective-permute-start.3) | collective-permute-done | bytes 524320 | tf_op jit(solution)/shard_map/ppermute | solution.py:29
  80.3 1.2 fusion.66
  81.4 1.3 collective-permute-start.5
  82.7 5.0 %collective-permute-start.4 = (bf16[1024,256]{1,0:T(8,128)(2,1)S(1)}, bf16[1024,256]{1,0:T(8,128)(2,1)S(1)}, u32[]{:S(2)}, u32[]{:S(2)}) collective-permute-start(bf16[1024,256]{1,0:T(8,128)(2,1)S(1)} %get-tuple-element.2), channel_id=1, source_target_pairs={{0,4},{4,8},{8,12},{12,16},{16,20},{20,24},{24,28},{1,5},{5,9},{9,... | collective-permute-start | bytes 1572872 | tf_op jit(solution)/shard_map/ppermute | solution.py:17
  87.8 3.1 %fusion.8 = f32[2048,256]{0,1:T(8,128)} fusion(bf16[1024,256]{1,0:T(8,128)(2,1)S(1)} %get-tuple-element.2, s32[1024]{0:T(1024)S(1)} %iota_add_fusion.1, s32[2048]{0:T(1024)S(1)} %copy-done.2), kind=kOutput, calls=%fused_computation.12 | convolution fusion | flops 1075838976 | bytes 2633728 | tf_op jit(solution)/shard_map/dot_general | solution.py:65
  90.9 7.0 %collective-permute-done.5 = bf16[1024,256]{1,0:T(8,128)(2,1)S(1)} collective-permute-done((bf16[1024,256]{1,0:T(8,128)(2,1)S(1)}, bf16[1024,256]{1,0:T(8,128)(2,1)S(1)}, u32[]{:S(2)}, u32[]{:S(2)}) %collective-permute-start.5) | collective-permute-done | bytes 524320 | tf_op jit(solution)/shard_map/ppermute | solution.py:19
  97.9 11.4 %collective-permute-done.4 = bf16[1024,256]{1,0:T(8,128)(2,1)S(1)} collective-permute-done((bf16[1024,256]{1,0:T(8,128)(2,1)S(1)}, bf16[1024,256]{1,0:T(8,128)(2,1)S(1)}, u32[]{:S(2)}, u32[]{:S(2)}) %collective-permute-start.4) | collective-permute-done | bytes 524320 | tf_op jit(solution)/shard_map/ppermute | solution.py:17
  110.8 5.6 %all-to-all-start.1 = ((bf16[32,16,256]{2,1,0:T(8,128)(2,1)}), bf16[32,16,256]{2,1,0:T(8,128)(2,1)S(1)}, u32[]{:S(2)}, u32[]{:S(2)}) async-start(bf16[32,16,256]{2,1,0:T(8,128)(2,1)} %broadcast_in_dim.8), calls=%async_computation.1 | async-start | bytes 524288 | tf_op jit(solution)/shard_map/all_to_all | solution.py:74
  116.4 3.1 %fusion.4 = f32[2048,256]{0,1:T(8,128)} fusion(bf16[1024,256]{1,0:T(8,128)(2,1)S(1)} %collective-permute-done.5, s32[1024]{0:T(1024)S(1)} %iota_add_fusion, s32[2048]{0:T(1024)S(1)} %copy-done.2), kind=kOutput, calls=%fused_computation.8 | convolution fusion | flops 1075838976 | bytes 2633728 | tf_op jit(solution)/shard_map/dot_general | solution.py:65
  119.4 8.8 %convolution_bitcast_fusion.1 = f32[2048,256]{0,1:T(8,128)S(1)} fusion(bf16[2048,2048]{1,0:T(8,128)(2,1)} %param.8, f32[2048,256]{0,1:T(8,128)} %fusion.4, f32[2048,256]{0,1:T(8,128)} %fusion.8, f32[2048]{0:T(1024)S(1)} %copy-done.1, bf16[1024,256]{1,0:T(8,128)(2,1)S(1)} %collective-permute-done.4, s32[2048]{0:T(1024)S(1)} %copy-done.2), kind=kOutput, calls=%fused_computation.49 | convolution fusion | flops 3225419776 | bytes 15220736 | tf_op jit(solution)/shard_map/dot_general | solution.py:80
  129.0 1.4 fusion.61
  130.3 1.5 fusion.51
  131.9 1.3 collective-permute-start.6
  133.2 4.6 %collective-permute-start.7 = (bf16[1024,256]{1,0:T(8,128)(2,1)S(1)}, bf16[1024,256]{1,0:T(8,128)(2,1)S(1)}, u32[]{:S(2)}, u32[]{:S(2)}) collective-permute-start(bf16[1024,256]{1,0:T(8,128)(2,1)S(1)} %fusion.61), channel_id=1, source_target_pairs={{0,4},{4,8},{8,12},{12,16},{16,20},{20,24},{24,28},{1,5},{5,9},{9,... | collective-permute-start | bytes 1572872 | tf_op jit(solution)/shard_map/ppermute | solution.py:29
  137.8 1.4 fusion.55
  139.1 8.7 %collective-permute-done.6 = bf16[1024,256]{1,0:T(8,128)(2,1)S(1)} collective-permute-done((bf16[1024,256]{1,0:T(8,128)(2,1)S(1)}, bf16[1024,256]{1,0:T(8,128)(2,1)S(1)}, u32[]{:S(2)}, u32[]{:S(2)}) %collective-permute-start.6) | collective-permute-done | bytes 524320 | tf_op jit(solution)/shard_map/ppermute | solution.py:29
  147.9 11.3 %collective-permute-done.7 = bf16[1024,256]{1,0:T(8,128)(2,1)S(1)} collective-permute-done((bf16[1024,256]{1,0:T(8,128)(2,1)S(1)}, bf16[1024,256]{1,0:T(8,128)(2,1)S(1)}, u32[]{:S(2)}, u32[]{:S(2)}) %collective-permute-start.7) | collective-permute-done | bytes 524320 | tf_op jit(solution)/shard_map/ppermute | solution.py:29
  (29 shorter events, 7.6 us)
Async XLA Ops:
  0.6 48.7 %copy-start = (bf16[16,2048]{1,0:T(8,128)(2,1)S(1)}, bf16[16,2048]{1,0:T(8,128)(2,1)}, u32[]{:S(2)}) copy-start(bf16[16,2048]{1,0:T(8,128)(2,1)} %param.9) | copy-start | bytes 196612
  2.0 16.8 %collective-permute-start.1 = (bf16[1024,256]{1,0:T(8,128)(2,1)S(1)}, bf16[1024,256]{1,0:T(8,128)(2,1)S(1)}, u32[]{:S(2)}, u32[]{:S(2)}) collective-permute-start(bf16[1024,256]{1,0:T(8,128)(2,1)S(1)} %convert_element_type.96), channel_id=1, source_target_pairs={{4,0},{8,4},{12,8},{16,12},{20,16},{24,20},{28,24},{5,1},{9,5},{13... | collective-permute-start | bytes 1572872 | tf_op jit(solution)/shard_map/ppermute | solution.py:19
  3.3 26.8 %collective-permute-start = (bf16[1024,256]{1,0:T(8,128)(2,1)S(1)}, bf16[1024,256]{1,0:T(8,128)(2,1)S(1)}, u32[]{:S(2)}, u32[]{:S(2)}) collective-permute-start(bf16[1024,256]{1,0:T(8,128)(2,1)S(1)} %convert_element_type.96), channel_id=1, source_target_pairs={{0,4},{4,8},{8,12},{12,16},{16,20},{20,24},{24,28},{1,5},{5,9},{9,... | collective-permute-start | bytes 1572872 | tf_op jit(solution)/shard_map/ppermute | solution.py:17
  9.4 3.8 %copy-start.2 = (s32[2048]{0:T(1024)S(1)}, s32[2048]{0:T(1024)}, u32[]{:S(2)}) copy-start(s32[2048]{0:T(1024)} %param.12) | copy-start | bytes 24580
  9.4 4.5 %copy-start.1 = (f32[2048]{0:T(1024)S(1)}, f32[2048]{0:T(1024)}, u32[]{:S(2)}) copy-start(f32[2048]{0:T(1024)} %param.10) | copy-start | bytes 24580
  31.6 17.7 %all-to-all-start = ((bf16[32,16,256]{2,1,0:T(8,128)(2,1)}), bf16[32,16,256]{2,1,0:T(8,128)(2,1)S(1)}, u32[]{:S(2)}, u32[]{:S(2)}) async-start(bf16[32,16,256]{2,1,0:T(8,128)(2,1)} %broadcast_in_dim.7), calls=%async_computation | async-start | bytes 524288 | tf_op jit(solution)/shard_map/all_to_all | solution.py:74
  40.5 8.8 %copy-start.3 = (bf16[16,512]{1,0:T(8,128)(2,1)S(1)}, bf16[16,512]{1,0:T(8,128)(2,1)}, u32[]{:S(2)}) copy-start(bf16[16,512]{1,0:T(8,128)(2,1)} %param.11) | copy-start | bytes 49156
  53.0 16.0 %collective-permute-start.2 = (bf16[1024,256]{1,0:T(8,128)(2,1)S(1)}, bf16[1024,256]{1,0:T(8,128)(2,1)S(1)}, u32[]{:S(2)}, u32[]{:S(2)}) collective-permute-start(bf16[1024,256]{1,0:T(8,128)(2,1)S(1)} %fusion.50), channel_id=1, source_target_pairs={{4,0},{8,4},{12,8},{16,12},{20,16},{24,20},{28,24},{5,1},{9,5},{13... | collective-permute-start | bytes 1572872 | tf_op jit(solution)/shard_map/ppermute | solution.py:29
  54.3 26.0 %collective-permute-start.3 = (bf16[1024,256]{1,0:T(8,128)(2,1)S(1)}, bf16[1024,256]{1,0:T(8,128)(2,1)S(1)}, u32[]{:S(2)}, u32[]{:S(2)}) collective-permute-start(bf16[1024,256]{1,0:T(8,128)(2,1)S(1)} %fusion.58), channel_id=1, source_target_pairs={{0,4},{4,8},{8,12},{12,16},{16,20},{20,24},{24,28},{1,5},{5,9},{9,... | collective-permute-start | bytes 1572872 | tf_op jit(solution)/shard_map/ppermute | solution.py:29
  81.4 16.5 %collective-permute-start.5 = (bf16[1024,256]{1,0:T(8,128)(2,1)S(1)}, bf16[1024,256]{1,0:T(8,128)(2,1)S(1)}, u32[]{:S(2)}, u32[]{:S(2)}) collective-permute-start(bf16[1024,256]{1,0:T(8,128)(2,1)S(1)} %get-tuple-element.2), channel_id=1, source_target_pairs={{4,0},{8,4},{12,8},{16,12},{20,16},{24,20},{28,24},{5,1},{9,5},{13... | collective-permute-start | bytes 1572872 | tf_op jit(solution)/shard_map/ppermute | solution.py:19
  82.7 26.6 %collective-permute-start.4 = (bf16[1024,256]{1,0:T(8,128)(2,1)S(1)}, bf16[1024,256]{1,0:T(8,128)(2,1)S(1)}, u32[]{:S(2)}, u32[]{:S(2)}) collective-permute-start(bf16[1024,256]{1,0:T(8,128)(2,1)S(1)} %get-tuple-element.2), channel_id=1, source_target_pairs={{0,4},{4,8},{8,12},{12,16},{16,20},{20,24},{24,28},{1,5},{5,9},{9,... | collective-permute-start | bytes 1572872 | tf_op jit(solution)/shard_map/ppermute | solution.py:17
  110.8 17.5 %all-to-all-start.1 = ((bf16[32,16,256]{2,1,0:T(8,128)(2,1)}), bf16[32,16,256]{2,1,0:T(8,128)(2,1)S(1)}, u32[]{:S(2)}, u32[]{:S(2)}) async-start(bf16[32,16,256]{2,1,0:T(8,128)(2,1)} %broadcast_in_dim.8), calls=%async_computation.1 | async-start | bytes 524288 | tf_op jit(solution)/shard_map/all_to_all | solution.py:74
  131.9 16.0 %collective-permute-start.6 = (bf16[1024,256]{1,0:T(8,128)(2,1)S(1)}, bf16[1024,256]{1,0:T(8,128)(2,1)S(1)}, u32[]{:S(2)}, u32[]{:S(2)}) collective-permute-start(bf16[1024,256]{1,0:T(8,128)(2,1)S(1)} %fusion.51), channel_id=1, source_target_pairs={{4,0},{8,4},{12,8},{16,12},{20,16},{24,20},{28,24},{5,1},{9,5},{13... | collective-permute-start | bytes 1572872 | tf_op jit(solution)/shard_map/ppermute | solution.py:29
  133.2 26.0 %collective-permute-start.7 = (bf16[1024,256]{1,0:T(8,128)(2,1)S(1)}, bf16[1024,256]{1,0:T(8,128)(2,1)S(1)}, u32[]{:S(2)}, u32[]{:S(2)}) collective-permute-start(bf16[1024,256]{1,0:T(8,128)(2,1)S(1)} %fusion.61), channel_id=1, source_target_pairs={{0,4},{4,8},{8,12},{12,16},{16,20},{20,24},{24,28},{1,5},{5,9},{9,... | collective-permute-start | bytes 1572872 | tf_op jit(solution)/shard_map/ppermute | solution.py:29

commit v12 on v11

--- a/solution.py
+++ b/solution.py
@@ -1,6 +1,8 @@
 import jax
 import jax.numpy as jnp
 from jax import lax
+from jax.experimental import pallas as pl
+from jax.experimental.pallas import tpu as pltpu
 from jax.sharding import PartitionSpec as P
 
 AXES = ("sub", "grp")
@@ -46,6 +48,29 @@
     return held
 
 
+def _product_kernel(block_ref, rows_ref, out_ref):
+    out_ref[...] = jnp.dot(block_ref[...], rows_ref[...], preferred_element_type=jnp.float32)
+
+
+def factor_product(factor, rows, block=256):
+    size, width = factor.shape[0], rows.shape[1]
+    return pl.pallas_call(
+        _product_kernel,
+        out_shape=jax.ShapeDtypeStruct((size, width), jnp.float32),
+        grid=(size // block,),
+        in_specs=[
+            pl.BlockSpec((block, factor.shape[1]), lambda i: (i, 0)),
+            pl.BlockSpec(rows.shape, lambda i: (0, 0)),
+        ],
+        out_specs=pl.BlockSpec((block, width), lambda i: (i, 0)),
+        cost_estimate=pl.CostEstimate(
+            flops=2 * size * factor.shape[1] * width,
+            bytes_accessed=factor.size * 2 + rows.size * 2 + size * width * 4,
+            transcendentals=0,
+        ),
+    )(factor, rows)
+
+
 def shards(resid, schur_inv, basis, scaling, coarse_inv, source_row, primal_idx):
     own_count = resid.shape[0]
     scale_column = scaling[:, None]
@@ -77,8 +102,7 @@
         gathered_own = lax.optimization_barrier(select(picks[1], rounded))
         gathered = gathered_own + select(picks[0], before) + select(picks[2], after)
         scaled = (scale_column * gathered).astype(jnp.bfloat16)
-        solved = jnp.dot(schur_inv, scaled, preferred_element_type=jnp.float32)
-        solved = lax.optimization_barrier(solved)
+        solved = factor_product(schur_inv, scaled)
         coarse = jnp.dot(coarse_inv, primal_all, preferred_element_type=jnp.float32)
         coarse_rounded = coarse.astype(jnp.bfloat16)
         solved = solved + lax.dot_general(

time: 161 us -> 168 us (1.043)
  Pallas kernels: 0 us -> 17.7 us
  matrix products: 40.6 us -> 24.1 us
  other arithmetic: 4.64 us -> 8.59 us
    pallas_call x0 -> x2, Pallas kernels: none -> 17.7 us  [factor_product(): pl.pallas_call(_product_kernel, out_shape=jax.ShapeDtypeStruct((size, wid...]
    dot_general x2 -> x0, matrix products: 17.6 us -> none  [precondition(): solved = jnp.dot(schur_inv, scaled, preferred_element_type=jnp.float32)]
    convert_element_type x0 -> x2, other arithmetic: none -> 3.86 us  [precondition(): weighted = (scale_column * solved).astype(jnp.bfloat16)]
    dot_general x10 -> x12, matrix products: 21.6 us -> 22.6 us  [select(): return jnp.dot(matrix, rows, preferred_element_type=jnp.float32)]
  transfers between devices with their start and end apart: 10 -> 10, of which waited for: 8 -> 8; matrix products, arithmetic and copies ran while one was open for 22% -> 11% of each run, Pallas kernels for 0% -> 11%
where the time goes in v12:
time: 168 us; the launch traced here: 167 us
  waiting for transfers between devices  74.9 us (45%)
  starting transfers between devices  36.5 us (22%)
  matrix products  24.1 us (14%)
  Pallas kernels  17.7 us (11%)
  other arithmetic  8.59 us (5%)
  local copies, waits for them, and re-layouts  4.1 us (2%)
    ppermute x4, waiting for transfers between devices, shifted(): return lax.ppermute(shard, axis, pairs)  40 us
    ppermute x2, waiting for transfers between devices, with_halo(): lax.ppermute(tail, axis, [(i, (i + 1) % count) for i in range(ends)])  22.8 us
    dot_general x12, matrix products, select(): return jnp.dot(matrix, rows, preferred_element_type=jnp.float32)  22.6 us
    pallas_call x2, Pallas kernels, factor_product(): pl.pallas_call(_product_kernel, out_shape=jax.ShapeDtypeStruct((size, wid...  17.7 us
    ppermute x2, waiting for transfers between devices, with_halo(): lax.ppermute(head, axis, [((i + 1) % count, i) for i in range(ends)])  12.1 us
    ppermute x4, starting transfers between devices, shifted(): return lax.ppermute(shard, axis, pairs)  11.7 us
    all_to_all x2, starting transfers between devices, precondition(): lax.all_to_all(jnp.broadcast_to(primal[None], (count,) + primal.shape), A...  11.6 us
    ppermute x2, starting transfers between devices, with_halo(): lax.ppermute(tail, axis, [(i, (i + 1) % count) for i in range(ends)])  10.6 us
  transfers between devices with their start and end apart: 10, of which 8 were waited for; matrix products, arithmetic and copies ran while one was open for 11% of the time, Pallas kernels for 11%

profile of v12, /device:TPU:0, one launch (start us, length us, event | category | flops | bytes accessed | tf_op | source)
XLA Modules:
  0.0 166.7 jit_solution(12222268497627333705)
XLA Ops:
  0.6 1.3 convert_element_type.96
  3.3 5.5 %collective-permute-start = (bf16[1024,256]{1,0:T(8,128)(2,1)S(1)}, bf16[1024,256]{1,0:T(8,128)(2,1)S(1)}, u32[]{:S(2)}, u32[]{:S(2)}) collective-permute-start(bf16[1024,256]{1,0:T(8,128)(2,1)S(1)} %convert_element_type.96), channel_id=1, source_target_pairs={{0,4},{4,8},{8,12},{12,16},{16,20},{20,24},{24,28},{1,5},{5,9},{9,... | collective-permute-start | bytes 1572872 | tf_op jit(solution)/shard_map/ppermute | solution.py:19
  9.4 3.3 %fusion.10 = f32[2048,256]{1,0:T(8,128)} fusion(bf16[1024,256]{1,0:T(8,128)(2,1)S(1)} %convert_element_type.96, s32[1024]{0:T(1024)S(1)} %iota_add_fusion.1, s32[2048]{0:T(1024)} %param.12), kind=kOutput, calls=%fused_computation.14 | convolution fusion | flops 1075838976 | bytes 2633728 | tf_op jit(solution)/shard_map/dot_general | solution.py:90
  14.1 4.6 %collective-permute-done.1 = bf16[1024,256]{1,0:T(8,128)(2,1)S(1)} collective-permute-done((bf16[1024,256]{1,0:T(8,128)(2,1)S(1)}, bf16[1024,256]{1,0:T(8,128)(2,1)S(1)}, u32[]{:S(2)}, u32[]{:S(2)}) %collective-permute-start.1) | collective-permute-done | bytes 524320 | tf_op jit(solution)/shard_map/ppermute | solution.py:21
  18.7 11.4 %collective-permute-done = bf16[1024,256]{1,0:T(8,128)(2,1)S(1)} collective-permute-done((bf16[1024,256]{1,0:T(8,128)(2,1)S(1)}, bf16[1024,256]{1,0:T(8,128)(2,1)S(1)}, u32[]{:S(2)}, u32[]{:S(2)}) %collective-permute-start) | collective-permute-done | bytes 524320 | tf_op jit(solution)/shard_map/ppermute | solution.py:19
  31.6 5.8 %all-to-all-start = ((bf16[32,16,256]{2,1,0:T(8,128)(2,1)}), bf16[32,16,256]{2,1,0:T(8,128)(2,1)S(1)}, u32[]{:S(2)}, u32[]{:S(2)}) async-start(bf16[32,16,256]{2,1,0:T(8,128)(2,1)} %broadcast_in_dim.7), calls=%async_computation | async-start | bytes 524288 | tf_op jit(solution)/shard_map/all_to_all | solution.py:99
  37.4 1.4 fusion.6
  39.0 2.7 %fusion.43.rows_ref = bf16[2048,256]{1,0:T(8,128)(2,1)} fusion(f32[2048,256]{1,0:T(8,128)S(1)} %fusion.6, f32[2048,256]{1,0:T(8,128)S(1)} %copy-done.5, bf16[1024,256]{1,0:T(8,128)(2,1)S(1)} %collective-permute-done, s32[2048]{0:T(1024)S(1)} %copy-done.2, f32[2048]{0:T(1024)S(1)} %copy-done.1), kind=kOutput, calls=%fused_computation.51 | convolution fusion | flops 1077936128 | bytes 5783552 | tf_op jit(solution)/shard_map/dot_general | solution.py:90
  41.7 8.9 %shard_map.86 = f32[2048,256]{1,0:T(8,128)} custom-call(bf16[2048,2048]{1,0:T(8,128)(2,1)} %block_ref.3, bf16[2048,256]{1,0:T(8,128)(2,1)} %fusion.43.rows_ref), custom_call_target="tpu_custom_call" | custom-call | flops 2147483648 | bytes 11534336 | tf_op jit(solution)/shard_map/pallas_call | solution.py:57
  51.4 1.9 %multiply_convert_fusion.2 = bf16[2048,256]{1,0:T(8,128)(2,1)S(1)} fusion(f32[2048,256]{1,0:T(8,128)} %shard_map.86, f32[2048,256]{1,0:T(8,128)S(1)} %convolution_bitcast_fusion.1, f32[2048]{0:T(1024)S(1)} %copy-done.1), kind=kLoop, calls=%fused_computation.54 | loop fusion | flops 1572864 | bytes 5251072 | tf_op jit(solution)/shard_map/convert_element_type | solution.py:111
  53.3 1.3 fusion.52
  54.6 1.5 fusion.44
  56.1 1.3 collective-permute-start.2
  57.4 4.6 %collective-permute-start.3 = (bf16[1024,256]{1,0:T(8,128)(2,1)S(1)}, bf16[1024,256]{1,0:T(8,128)(2,1)S(1)}, u32[]{:S(2)}, u32[]{:S(2)}) collective-permute-start(bf16[1024,256]{1,0:T(8,128)(2,1)S(1)} %fusion.52), channel_id=1, source_target_pairs={{0,4},{4,8},{8,12},{12,16},{16,20},{20,24},{24,28},{1,5},{5,9},{9,... | collective-permute-start | bytes 1572872 | tf_op jit(solution)/shard_map/ppermute | solution.py:31
  62.0 1.3 fusion.46
  63.3 8.7 %collective-permute-done.2 = bf16[1024,256]{1,0:T(8,128)(2,1)S(1)} collective-permute-done((bf16[1024,256]{1,0:T(8,128)(2,1)S(1)}, bf16[1024,256]{1,0:T(8,128)(2,1)S(1)}, u32[]{:S(2)}, u32[]{:S(2)}) %collective-permute-start.2) | collective-permute-done | bytes 524320 | tf_op jit(solution)/shard_map/ppermute | solution.py:31
  72.1 11.3 %collective-permute-done.3 = bf16[1024,256]{1,0:T(8,128)(2,1)S(1)} collective-permute-done((bf16[1024,256]{1,0:T(8,128)(2,1)S(1)}, bf16[1024,256]{1,0:T(8,128)(2,1)S(1)}, u32[]{:S(2)}, u32[]{:S(2)}) %collective-permute-start.3) | collective-permute-done | bytes 524320 | tf_op jit(solution)/shard_map/ppermute | solution.py:31
  85.9 5.0 %collective-permute-start.4 = (bf16[1024,256]{1,0:T(8,128)(2,1)S(1)}, bf16[1024,256]{1,0:T(8,128)(2,1)S(1)}, u32[]{:S(2)}, u32[]{:S(2)}) collective-permute-start(bf16[1024,256]{1,0:T(8,128)(2,1)S(1)} %get-tuple-element.2), channel_id=1, source_target_pairs={{0,4},{4,8},{8,12},{12,16},{16,20},{20,24},{24,28},{1,5},{5,9},{9,... | collective-permute-start | bytes 1572872 | tf_op jit(solution)/shard_map/ppermute | solution.py:19
  91.0 2.6 %fusion.8 = f32[2048,256]{1,0:T(8,128)} fusion(bf16[1024,256]{1,0:T(8,128)(2,1)S(1)} %get-tuple-element.2, s32[1024]{0:T(1024)S(1)} %iota_add_fusion.1, s32[2048]{0:T(1024)S(1)} %copy-done.2), kind=kOutput, calls=%fused_computation.12 | convolution fusion | flops 1075838976 | bytes 2633728 | tf_op jit(solution)/shard_map/dot_general | solution.py:90
  93.6 7.5 %collective-permute-done.5 = bf16[1024,256]{1,0:T(8,128)(2,1)S(1)} collective-permute-done((bf16[1024,256]{1,0:T(8,128)(2,1)S(1)}, bf16[1024,256]{1,0:T(8,128)(2,1)S(1)}, u32[]{:S(2)}, u32[]{:S(2)}) %collective-permute-start.5) | collective-permute-done | bytes 524320 | tf_op jit(solution)/shard_map/ppermute | solution.py:21
  101.1 11.4 %collective-permute-done.4 = bf16[1024,256]{1,0:T(8,128)(2,1)S(1)} collective-permute-done((bf16[1024,256]{1,0:T(8,128)(2,1)S(1)}, bf16[1024,256]{1,0:T(8,128)(2,1)S(1)}, u32[]{:S(2)}, u32[]{:S(2)}) %collective-permute-start.4) | collective-permute-done | bytes 524320 | tf_op jit(solution)/shard_map/ppermute | solution.py:19
  114.0 5.8 %all-to-all-start.1 = ((bf16[32,16,256]{2,1,0:T(8,128)(2,1)}), bf16[32,16,256]{2,1,0:T(8,128)(2,1)S(1)}, u32[]{:S(2)}, u32[]{:S(2)}) async-start(bf16[32,16,256]{2,1,0:T(8,128)(2,1)} %broadcast_in_dim.8), calls=%async_computation.1 | async-start | bytes 524288 | tf_op jit(solution)/shard_map/all_to_all | solution.py:99
  119.8 1.7 %fusion.18 = f32[2048,256]{1,0:T(8,128)S(1)} fusion(bf16[1024,256]{1,0:T(8,128)(2,1)S(1)} %collective-permute-done.4, s32[2048]{0:T(1024)S(1)} %copy-done.2), kind=kOutput, calls=%fused_computation.24 | convolution fusion | flops 1075838976 | bytes 2629632 | tf_op jit(solution)/shard_map/dot_general | solution.py:90
  121.5 2.6 %multiply_convert_fusion.1.rows_ref = bf16[2048,256]{1,0:T(8,128)(2,1)} fusion(f32[2048,256]{1,0:T(8,128)S(1)} %copy-done.4, f32[2048,256]{1,0:T(8,128)S(1)} %fusion.18, f32[2048]{0:T(1024)S(1)} %copy-done.1, bf16[1024,256]{1,0:T(8,128)(2,1)S(1)} %collective-permute-done.5, s32[1024]{0:T(1024)S(1)} %iota_add_fusion, s32[2048]{0:T(1024)S(1)} %copy-done.2), kind=kOutput, calls=%fused_computation.53 | convolution fusion | flops 1077936128 | bytes 5787648 | tf_op jit(solution)/shard_map/dot_general | solution.py:90
  124.1 8.9 %shard_map.87 = f32[2048,256]{1,0:T(8,128)} custom-call(bf16[2048,2048]{1,0:T(8,128)(2,1)} %block_ref.3, bf16[2048,256]{1,0:T(8,128)(2,1)} %multiply_convert_fusion.1.rows_ref), custom_call_target="tpu_custom_call" | custom-call | flops 2147483648 | bytes 11534336 | tf_op jit(solution)/shard_map/pallas_call | solution.py:57
  133.7 1.9 %multiply_convert_fusion = bf16[2048,256]{1,0:T(8,128)(2,1)S(1)} fusion(f32[2048,256]{1,0:T(8,128)} %shard_map.87, f32[2048,256]{1,0:T(8,128)S(1)} %convolution_bitcast_fusion, f32[2048]{0:T(1024)S(1)} %copy-done.1), kind=kLoop, calls=%fused_computation.52 | loop fusion | flops 1572864 | bytes 5251072 | tf_op jit(solution)/shard_map/convert_element_type | solution.py:111
  135.7 1.3 fusion.55
  137.0 1.5 fusion.45
  139.8 4.6 %collective-permute-start.7 = (bf16[1024,256]{1,0:T(8,128)(2,1)S(1)}, bf16[1024,256]{1,0:T(8,128)(2,1)S(1)}, u32[]{:S(2)}, u32[]{:S(2)}) collective-permute-start(bf16[1024,256]{1,0:T(8,128)(2,1)S(1)} %fusion.55), channel_id=1, source_target_pairs={{0,4},{4,8},{8,12},{12,16},{16,20},{20,24},{24,28},{1,5},{5,9},{9,... | collective-permute-start | bytes 1572872 | tf_op jit(solution)/shard_map/ppermute | solution.py:31
  144.3 1.3 fusion.49
  145.7 8.6 %collective-permute-done.6 = bf16[1024,256]{1,0:T(8,128)(2,1)S(1)} collective-permute-done((bf16[1024,256]{1,0:T(8,128)(2,1)S(1)}, bf16[1024,256]{1,0:T(8,128)(2,1)S(1)}, u32[]{:S(2)}, u32[]{:S(2)}) %collective-permute-start.6) | collective-permute-done | bytes 524320 | tf_op jit(solution)/shard_map/ppermute | solution.py:31
  154.3 11.3 %collective-permute-done.7 = bf16[1024,256]{1,0:T(8,128)(2,1)S(1)} collective-permute-done((bf16[1024,256]{1,0:T(8,128)(2,1)S(1)}, bf16[1024,256]{1,0:T(8,128)(2,1)S(1)}, u32[]{:S(2)}, u32[]{:S(2)}) %collective-permute-start.7) | collective-permute-done | bytes 524320 | tf_op jit(solution)/shard_map/ppermute | solution.py:31
  (37 shorter events, 12.9 us)
Async XLA Ops:
  0.6 50.0 %copy-start = (bf16[16,2048]{1,0:T(8,128)(2,1)S(1)}, bf16[16,2048]{1,0:T(8,128)(2,1)}, u32[]{:S(2)}) copy-start(bf16[16,2048]{1,0:T(8,128)(2,1)} %param.9) | copy-start | bytes 196612
  2.0 16.8 %collective-permute-start.1 = (bf16[1024,256]{1,0:T(8,128)(2,1)S(1)}, bf16[1024,256]{1,0:T(8,128)(2,1)S(1)}, u32[]{:S(2)}, u32[]{:S(2)}) collective-permute-start(bf16[1024,256]{1,0:T(8,128)(2,1)S(1)} %convert_element_type.96), channel_id=1, source_target_pairs={{4,0},{8,4},{12,8},{16,12},{20,16},{24,20},{28,24},{5,1},{9,5},{13... | collective-permute-start | bytes 1572872 | tf_op jit(solution)/shard_map/ppermute | solution.py:21
  3.3 26.8 %collective-permute-start = (bf16[1024,256]{1,0:T(8,128)(2,1)S(1)}, bf16[1024,256]{1,0:T(8,128)(2,1)S(1)}, u32[]{:S(2)}, u32[]{:S(2)}) collective-permute-start(bf16[1024,256]{1,0:T(8,128)(2,1)S(1)} %convert_element_type.96), channel_id=1, source_target_pairs={{0,4},{4,8},{8,12},{12,16},{16,20},{20,24},{24,28},{1,5},{5,9},{9,... | collective-permute-start | bytes 1572872 | tf_op jit(solution)/shard_map/ppermute | solution.py:19
  9.4 3.3 %copy-start.2 = (s32[2048]{0:T(1024)S(1)}, s32[2048]{0:T(1024)}, u32[]{:S(2)}) copy-start(s32[2048]{0:T(1024)} %param.12) | copy-start | bytes 24580
  9.4 4.0 %copy-start.1 = (f32[2048]{0:T(1024)S(1)}, f32[2048]{0:T(1024)}, u32[]{:S(2)}) copy-start(f32[2048]{0:T(1024)} %param.10) | copy-start | bytes 24580
  31.6 19.0 %all-to-all-start = ((bf16[32,16,256]{2,1,0:T(8,128)(2,1)}), bf16[32,16,256]{2,1,0:T(8,128)(2,1)S(1)}, u32[]{:S(2)}, u32[]{:S(2)}) async-start(bf16[32,16,256]{2,1,0:T(8,128)(2,1)} %broadcast_in_dim.7), calls=%async_computation | async-start | bytes 524288 | tf_op jit(solution)/shard_map/all_to_all | solution.py:99
  37.4 1.6 copy-start.5
  41.7 8.9 %copy-start.3 = (bf16[16,512]{1,0:T(8,128)(2,1)S(1)}, bf16[16,512]{1,0:T(8,128)(2,1)}, u32[]{:S(2)}) copy-start(bf16[16,512]{1,0:T(8,128)(2,1)} %param.11) | copy-start | bytes 49156
  56.1 16.0 %collective-permute-start.2 = (bf16[1024,256]{1,0:T(8,128)(2,1)S(1)}, bf16[1024,256]{1,0:T(8,128)(2,1)S(1)}, u32[]{:S(2)}, u32[]{:S(2)}) collective-permute-start(bf16[1024,256]{1,0:T(8,128)(2,1)S(1)} %fusion.44), channel_id=1, source_target_pairs={{4,0},{8,4},{12,8},{16,12},{20,16},{24,20},{28,24},{5,1},{9,5},{13... | collective-permute-start | bytes 1572872 | tf_op jit(solution)/shard_map/ppermute | solution.py:31
  57.4 26.0 %collective-permute-start.3 = (bf16[1024,256]{1,0:T(8,128)(2,1)S(1)}, bf16[1024,256]{1,0:T(8,128)(2,1)S(1)}, u32[]{:S(2)}, u32[]{:S(2)}) collective-permute-start(bf16[1024,256]{1,0:T(8,128)(2,1)S(1)} %fusion.52), channel_id=1, source_target_pairs={{0,4},{4,8},{8,12},{12,16},{16,20},{20,24},{24,28},{1,5},{5,9},{9,... | collective-permute-start | bytes 1572872 | tf_op jit(solution)/shard_map/ppermute | solution.py:31
  84.6 16.5 %collective-permute-start.5 = (bf16[1024,256]{1,0:T(8,128)(2,1)S(1)}, bf16[1024,256]{1,0:T(8,128)(2,1)S(1)}, u32[]{:S(2)}, u32[]{:S(2)}) collective-permute-start(bf16[1024,256]{1,0:T(8,128)(2,1)S(1)} %get-tuple-element.2), channel_id=1, source_target_pairs={{4,0},{8,4},{12,8},{16,12},{20,16},{24,20},{28,24},{5,1},{9,5},{13... | collective-permute-start | bytes 1572872 | tf_op jit(solution)/shard_map/ppermute | solution.py:21
  85.9 26.6 %collective-permute-start.4 = (bf16[1024,256]{1,0:T(8,128)(2,1)S(1)}, bf16[1024,256]{1,0:T(8,128)(2,1)S(1)}, u32[]{:S(2)}, u32[]{:S(2)}) collective-permute-start(bf16[1024,256]{1,0:T(8,128)(2,1)S(1)} %get-tuple-element.2), channel_id=1, source_target_pairs={{0,4},{4,8},{8,12},{12,16},{16,20},{20,24},{24,28},{1,5},{5,9},{9,... | collective-permute-start | bytes 1572872 | tf_op jit(solution)/shard_map/ppermute | solution.py:19
  114.0 18.9 %all-to-all-start.1 = ((bf16[32,16,256]{2,1,0:T(8,128)(2,1)}), bf16[32,16,256]{2,1,0:T(8,128)(2,1)S(1)}, u32[]{:S(2)}, u32[]{:S(2)}) async-start(bf16[32,16,256]{2,1,0:T(8,128)(2,1)} %broadcast_in_dim.8), calls=%async_computation.1 | async-start | bytes 524288 | tf_op jit(solution)/shard_map/all_to_all | solution.py:99
  119.8 1.7 %copy-start.4 = (f32[2048,256]{1,0:T(8,128)S(1)}, f32[2048,256]{1,0:T(8,128)}, u32[]{:S(2)}) copy-start(f32[2048,256]{1,0:T(8,128)} %fusion.8) | copy-start | bytes 6291460
  138.5 15.8 %collective-permute-start.6 = (bf16[1024,256]{1,0:T(8,128)(2,1)S(1)}, bf16[1024,256]{1,0:T(8,128)(2,1)S(1)}, u32[]{:S(2)}, u32[]{:S(2)}) collective-permute-start(bf16[1024,256]{1,0:T(8,128)(2,1)S(1)} %fusion.45), channel_id=1, source_target_pairs={{4,0},{8,4},{12,8},{16,12},{20,16},{24,20},{28,24},{5,1},{9,5},{13... | collective-permute-start | bytes 1572872 | tf_op jit(solution)/shard_map/ppermute | solution.py:31
  139.8 25.8 %collective-permute-start.7 = (bf16[1024,256]{1,0:T(8,128)(2,1)S(1)}, bf16[1024,256]{1,0:T(8,128)(2,1)S(1)}, u32[]{:S(2)}, u32[]{:S(2)}) collective-permute-start(bf16[1024,256]{1,0:T(8,128)(2,1)S(1)} %fusion.55), channel_id=1, source_target_pairs={{0,4},{4,8},{8,12},{12,16},{16,20},{20,24},{24,28},{1,5},{5,9},{9,... | collective-permute-start | bytes 1572872 | tf_op jit(solution)/shard_map/ppermute | solution.py:31

commit v13 on v11

--- a/solution.py
+++ b/solution.py
@@ -66,16 +66,18 @@
 
     def precondition(vector_in):
         rounded = vector_in.astype(jnp.bfloat16)
-        padded = with_halo(rounded, (("sub", 0),), own_count)
-        before = padded[:own_count]
-        after = padded[2 * own_count :]
+        before = shifted(rounded, "sub", 1)
+        after = shifted(rounded, "sub", -1)
+        gathered_after = select(picks[2], after)
+        before, gathered_after = lax.optimization_barrier((before, gathered_after))
+        padded = jnp.concatenate([before, rounded, after], axis=0)
         primal = (primal_scale * padded[primal_source].astype(jnp.float32)).astype(jnp.bfloat16)
         count = lax.axis_size("sub") * lax.axis_size("grp")
         primal_all = lax.all_to_all(
             jnp.broadcast_to(primal[None], (count,) + primal.shape), AXES, 0, 0, tiled=False
         ).reshape(-1, primal.shape[1])
         gathered_own = lax.optimization_barrier(select(picks[1], rounded))
-        gathered = gathered_own + select(picks[0], before) + select(picks[2], after)
+        gathered = gathered_own + select(picks[0], before) + gathered_after
         scaled = (scale_column * gathered).astype(jnp.bfloat16)
         solved = jnp.dot(schur_inv, scaled, preferred_element_type=jnp.float32)
         solved = lax.optimization_barrier(solved)

time: 161 us -> 160 us (level)
  waiting for transfers between devices: 73.8 us -> 70.8 us
  starting transfers between devices: 36.4 us -> 38.7 us
    ppermute x4 -> x0, waiting for transfers between devices: 33.9 us -> none  [the longest x2 22.8 us: with_halo(): lax.ppermute(tail, axis, [(i, (i + 1) % count) for i in range(ends)])]
    ppermute x4 -> x8, waiting for transfers between devices: 39.9 us -> 66.5 us  [shifted(): return lax.ppermute(shard, axis, pairs)]
    ppermute x4 -> x0, starting transfers between devices: 13.1 us -> none  [the longest x2 10.6 us: with_halo(): lax.ppermute(tail, axis, [(i, (i + 1) % count) for i in range(ends)])]
    ppermute x4 -> x8, starting transfers between devices: 11.9 us -> 25 us  [shifted(): return lax.ppermute(shard, axis, pairs)]
    all_to_all x2, waiting for transfers between devices: 0.01 us -> 4.34 us  [precondition(): lax.all_to_all(jnp.broadcast_to(primal[None], (count,) + primal.shape), A...]
    dot_general x2, matrix products: 17.6 us -> 13.4 us  [precondition(): solved = jnp.dot(schur_inv, scaled, preferred_element_type=jnp.float32)]
    dot_general x10 -> x12, matrix products: 21.6 us -> 25.4 us  [select(): return jnp.dot(matrix, rows, preferred_element_type=jnp.float32)]
    all_to_all x2, starting transfers between devices: 11.4 us -> 13.7 us  [precondition(): lax.all_to_all(jnp.broadcast_to(primal[None], (count,) + primal.shape), A...]
  transfers between devices with their start and end apart: 10 -> 10, of which waited for: 8 -> 10; matrix products, arithmetic and copies ran while one was open for 22% -> 20% of each run, Pallas kernels for 0% -> 0%
where the time goes in v13:
time: 160 us; the launch traced here: 159 us
  waiting for transfers between devices  70.8 us (44%)
  matrix products  40.3 us (25%)
  starting transfers between devices  38.7 us (24%)
  other arithmetic  4.64 us (3%)
  local copies, waits for them, and re-layouts  3.96 us (2%)
    ppermute x8, waiting for transfers between devices, shifted(): return lax.ppermute(shard, axis, pairs)  66.5 us
    dot_general x12, matrix products, select(): return jnp.dot(matrix, rows, preferred_element_type=jnp.float32)  25.4 us
    ppermute x8, starting transfers between devices, shifted(): return lax.ppermute(shard, axis, pairs)  25 us
    all_to_all x2, starting transfers between devices, precondition(): lax.all_to_all(jnp.broadcast_to(primal[None], (count,) + primal.shape), A...  13.7 us
    dot_general x2, matrix products, precondition(): solved = jnp.dot(schur_inv, scaled, preferred_element_type=jnp.float32)  13.4 us
    all_to_all x2, waiting for transfers between devices, precondition(): lax.all_to_all(jnp.broadcast_to(primal[None], (count,) + primal.shape), A...  4.34 us
  transfers between devices with their start and end apart: 10, of which 10 were waited for; matrix products, arithmetic and copies ran while one was open for 20% of the time, Pallas kernels for 0%

profile of v13, /device:TPU:0, one launch (start us, length us, event | category | flops | bytes accessed | tf_op | source)
XLA Modules:
  0.0 159.3 jit_solution(16971606265093293710)
XLA Ops:
  0.6 1.3 convert_element_type.96
  2.0 1.3 collective-permute-start.1
  3.3 5.5 %collective-permute-start = (bf16[1024,256]{1,0:T(8,128)(2,1)S(1)}, bf16[1024,256]{1,0:T(8,128)(2,1)S(1)}, u32[]{:S(2)}, u32[]{:S(2)}) collective-permute-start(bf16[1024,256]{1,0:T(8,128)(2,1)S(1)} %convert_element_type.96), channel_id=1, source_target_pairs={{0,4},{4,8},{8,12},{12,16},{16,20},{20,24},{24,28},{1,5},{5,9},{9,... | collective-permute-start | bytes 1572872 | tf_op jit(solution)/shard_map/ppermute | solution.py:29
  9.4 3.3 %fusion.10 = f32[2048,256]{1,0:T(8,128)} fusion(bf16[1024,256]{1,0:T(8,128)(2,1)S(1)} %convert_element_type.96, s32[1024]{0:T(1024)S(1)} %iota_add_fusion.1, s32[2048]{0:T(1024)} %param.12), kind=kOutput, calls=%fused_computation.14 | convolution fusion | flops 1075838976 | bytes 2633728 | tf_op jit(solution)/shard_map/dot_general | solution.py:65
  14.1 4.6 %collective-permute-done.1 = bf16[1024,256]{1,0:T(8,128)(2,1)S(1)} collective-permute-done((bf16[1024,256]{1,0:T(8,128)(2,1)S(1)}, bf16[1024,256]{1,0:T(8,128)(2,1)S(1)}, u32[]{:S(2)}, u32[]{:S(2)}) %collective-permute-start.1) | collective-permute-done | bytes 524320 | tf_op jit(solution)/shard_map/ppermute | solution.py:29
  18.7 2.6 %fusion.6 = f32[2048,256]{1,0:T(8,128)} fusion(bf16[1024,256]{1,0:T(8,128)(2,1)S(1)} %collective-permute-done.1, s32[1024]{0:T(1024)S(1)} %iota_add_fusion, s32[2048]{0:T(1024)S(1)} %copy-done.2), kind=kOutput, calls=%fused_computation.10 | convolution fusion | flops 1075838976 | bytes 2633728 | tf_op jit(solution)/shard_map/dot_general | solution.py:65
  21.3 8.8 %collective-permute-done = bf16[1024,256]{1,0:T(8,128)(2,1)S(1)} collective-permute-done((bf16[1024,256]{1,0:T(8,128)(2,1)S(1)}, bf16[1024,256]{1,0:T(8,128)(2,1)S(1)}, u32[]{:S(2)}, u32[]{:S(2)}) %collective-permute-start) | collective-permute-done | bytes 524320 | tf_op jit(solution)/shard_map/ppermute | solution.py:29
  31.6 7.6 %all-to-all-start = ((bf16[32,16,256]{2,1,0:T(8,128)(2,1)}), bf16[32,16,256]{2,1,0:T(8,128)(2,1)S(1)}, u32[]{:S(2)}, u32[]{:S(2)}) async-start(bf16[32,16,256]{2,1,0:T(8,128)(2,1)} %broadcast_in_dim.7), calls=%async_computation | async-start | bytes 524288 | tf_op jit(solution)/shard_map/all_to_all | solution.py:76
  39.2 3.4 %fusion.49 = bf16[2048,256]{1,0:T(8,128)(2,1)S(1)} fusion(f32[2048,256]{1,0:T(8,128)} %fusion.6, f32[2048,256]{1,0:T(8,128)} %fusion.10, bf16[1024,256]{1,0:T(8,128)(2,1)S(1)} %collective-permute-done, s32[2048]{0:T(1024)S(1)} %copy-done.2, f32[2048]{0:T(1024)S(1)} %copy-done.1), kind=kOutput, calls=%fused_computation.59 | convolution fusion | flops 1077936128 | bytes 5783552 | tf_op jit(solution)/shard_map/dot_general | solution.py:65
  42.6 5.7 %convolution_bitcast_fusion.1 = f32[2048,256]{1,0:T(8,128)S(1)} fusion(bf16[2048,2048]{1,0:T(8,128)(2,1)} %param.8, bf16[2048,256]{1,0:T(8,128)(2,1)S(1)} %fusion.49), kind=kOutput, calls=%fused_computation.47 | convolution fusion | flops 2147483648 | bytes 11534336 | tf_op jit(solution)/shard_map/dot_general | solution.py:82
  48.4 1.4 all-to-all-done
  50.6 1.3 fusion.58
  51.9 1.5 fusion.50
  54.7 4.6 %collective-permute-start.3 = (bf16[1024,256]{1,0:T(8,128)(2,1)S(1)}, bf16[1024,256]{1,0:T(8,128)(2,1)S(1)}, u32[]{:S(2)}, u32[]{:S(2)}) collective-permute-start(bf16[1024,256]{1,0:T(8,128)(2,1)S(1)} %fusion.58), channel_id=1, source_target_pairs={{0,4},{4,8},{8,12},{12,16},{16,20},{20,24},{24,28},{1,5},{5,9},{9,... | collective-permute-start | bytes 1572872 | tf_op jit(solution)/shard_map/ppermute | solution.py:29
  59.3 1.3 fusion.52
  60.6 8.4 %collective-permute-done.2 = bf16[1024,256]{1,0:T(8,128)(2,1)S(1)} collective-permute-done((bf16[1024,256]{1,0:T(8,128)(2,1)S(1)}, bf16[1024,256]{1,0:T(8,128)(2,1)S(1)}, u32[]{:S(2)}, u32[]{:S(2)}) %collective-permute-start.2) | collective-permute-done | bytes 524320 | tf_op jit(solution)/shard_map/ppermute | solution.py:29
  69.0 10.3 %collective-permute-done.3 = bf16[1024,256]{1,0:T(8,128)(2,1)S(1)} collective-permute-done((bf16[1024,256]{1,0:T(8,128)(2,1)S(1)}, bf16[1024,256]{1,0:T(8,128)(2,1)S(1)}, u32[]{:S(2)}, u32[]{:S(2)}) %collective-permute-start.3) | collective-permute-done | bytes 524320 | tf_op jit(solution)/shard_map/ppermute | solution.py:29
  81.7 5.2 %collective-permute-start.4 = (bf16[1024,256]{1,0:T(8,128)(2,1)S(1)}, bf16[1024,256]{1,0:T(8,128)(2,1)S(1)}, u32[]{:S(2)}, u32[]{:S(2)}) collective-permute-start(bf16[1024,256]{1,0:T(8,128)(2,1)S(1)} %get-tuple-element.10), channel_id=1, source_target_pairs={{0,4},{4,8},{8,12},{12,16},{16,20},{20,24},{24,28},{1,5},{5,9},{9,... | collective-permute-start | bytes 1572872 | tf_op jit(solution)/shard_map/ppermute | solution.py:29
  87.0 2.6 %fusion.8 = f32[2048,256]{1,0:T(8,128)} fusion(bf16[1024,256]{1,0:T(8,128)(2,1)S(1)} %get-tuple-element.10, s32[1024]{0:T(1024)S(1)} %iota_add_fusion.1, s32[2048]{0:T(1024)S(1)} %copy-done.2), kind=kOutput, calls=%fused_computation.12 | convolution fusion | flops 1075838976 | bytes 2633728 | tf_op jit(solution)/shard_map/dot_general | solution.py:65
  89.6 7.3 %collective-permute-done.5 = bf16[1024,256]{1,0:T(8,128)(2,1)S(1)} collective-permute-done((bf16[1024,256]{1,0:T(8,128)(2,1)S(1)}, bf16[1024,256]{1,0:T(8,128)(2,1)S(1)}, u32[]{:S(2)}, u32[]{:S(2)}) %collective-permute-start.5) | collective-permute-done | bytes 524320 | tf_op jit(solution)/shard_map/ppermute | solution.py:29
  96.9 2.6 %fusion.4 = f32[2048,256]{1,0:T(8,128)} fusion(bf16[1024,256]{1,0:T(8,128)(2,1)S(1)} %collective-permute-done.5, s32[1024]{0:T(1024)S(1)} %iota_add_fusion, s32[2048]{0:T(1024)S(1)} %copy-done.2), kind=kOutput, calls=%fused_computation.8 | convolution fusion | flops 1075838976 | bytes 2633728 | tf_op jit(solution)/shard_map/dot_general | solution.py:65
  99.5 8.8 %collective-permute-done.4 = bf16[1024,256]{1,0:T(8,128)(2,1)S(1)} collective-permute-done((bf16[1024,256]{1,0:T(8,128)(2,1)S(1)}, bf16[1024,256]{1,0:T(8,128)(2,1)S(1)}, u32[]{:S(2)}, u32[]{:S(2)}) %collective-permute-start.4) | collective-permute-done | bytes 524320 | tf_op jit(solution)/shard_map/ppermute | solution.py:29
  108.3 2.7 %fusion.18 = f32[2048,256]{1,0:T(8,128)} fusion(bf16[1024,256]{1,0:T(8,128)(2,1)S(1)} %collective-permute-done.4, s32[2048]{0:T(1024)S(1)} %copy-done.2), kind=kOutput, calls=%fused_computation.24 | convolution fusion | flops 1075838976 | bytes 2629632 | tf_op jit(solution)/shard_map/dot_general | solution.py:65
  112.5 6.1 %all-to-all-start.1 = ((bf16[32,16,256]{2,1,0:T(8,128)(2,1)}), bf16[32,16,256]{2,1,0:T(8,128)(2,1)S(1)}, u32[]{:S(2)}, u32[]{:S(2)}) async-start(bf16[32,16,256]{2,1,0:T(8,128)(2,1)} %broadcast_in_dim.8), calls=%async_computation.1 | async-start | bytes 524288 | tf_op jit(solution)/shard_map/all_to_all | solution.py:76
  118.6 7.7 %convolution_bitcast_fusion = f32[2048,256]{1,0:T(8,128)S(1)} fusion(bf16[2048,2048]{1,0:T(8,128)(2,1)} %param.8, f32[2048,256]{1,0:T(8,128)} %fusion.4, f32[2048,256]{1,0:T(8,128)} %fusion.8, f32[2048,256]{1,0:T(8,128)} %fusion.18, f32[2048]{0:T(1024)S(1)} %copy-done.1), kind=kOutput, calls=%fused_computation.46 | convolution fusion | flops 2149580800 | bytes 16785408 | tf_op jit(solution)/shard_map/dot_general | solution.py:82
  126.2 2.9 %all-to-all-done.1 = bf16[32,16,256]{2,1,0:T(8,128)(2,1)S(1)} async-done(((bf16[32,16,256]{2,1,0:T(8,128)(2,1)}), bf16[32,16,256]{2,1,0:T(8,128)(2,1)S(1)}, u32[]{:S(2)}, u32[]{:S(2)}) %all-to-all-start.1) | async-done | bytes 262176 | tf_op jit(solution)/shard_map/all_to_all | solution.py:76
  129.9 1.3 fusion.61
  131.3 1.5 fusion.51
  134.0 4.6 %collective-permute-start.7 = (bf16[1024,256]{1,0:T(8,128)(2,1)S(1)}, bf16[1024,256]{1,0:T(8,128)(2,1)S(1)}, u32[]{:S(2)}, u32[]{:S(2)}) collective-permute-start(bf16[1024,256]{1,0:T(8,128)(2,1)S(1)} %fusion.61), channel_id=1, source_target_pairs={{0,4},{4,8},{8,12},{12,16},{16,20},{20,24},{24,28},{1,5},{5,9},{9,... | collective-permute-start | bytes 1572872 | tf_op jit(solution)/shard_map/ppermute | solution.py:29
  138.6 1.3 fusion.55
  140.0 8.4 %collective-permute-done.6 = bf16[1024,256]{1,0:T(8,128)(2,1)S(1)} collective-permute-done((bf16[1024,256]{1,0:T(8,128)(2,1)S(1)}, bf16[1024,256]{1,0:T(8,128)(2,1)S(1)}, u32[]{:S(2)}, u32[]{:S(2)}) %collective-permute-start.6) | collective-permute-done | bytes 524320 | tf_op jit(solution)/shard_map/ppermute | solution.py:29
  148.4 9.8 %collective-permute-done.7 = bf16[1024,256]{1,0:T(8,128)(2,1)S(1)} collective-permute-done((bf16[1024,256]{1,0:T(8,128)(2,1)S(1)}, bf16[1024,256]{1,0:T(8,128)(2,1)S(1)}, u32[]{:S(2)}, u32[]{:S(2)}) %collective-permute-start.7) | collective-permute-done | bytes 524320 | tf_op jit(solution)/shard_map/ppermute | solution.py:29
  (31 shorter events, 12.7 us)
Async XLA Ops:
  0.6 49.2 %copy-start = (bf16[16,2048]{1,0:T(8,128)(2,1)S(1)}, bf16[16,2048]{1,0:T(8,128)(2,1)}, u32[]{:S(2)}) copy-start(bf16[16,2048]{1,0:T(8,128)(2,1)} %param.9) | copy-start | bytes 196612
  2.0 16.8 %collective-permute-start.1 = (bf16[1024,256]{1,0:T(8,128)(2,1)S(1)}, bf16[1024,256]{1,0:T(8,128)(2,1)S(1)}, u32[]{:S(2)}, u32[]{:S(2)}) collective-permute-start(bf16[1024,256]{1,0:T(8,128)(2,1)S(1)} %convert_element_type.96), channel_id=1, source_target_pairs={{4,0},{8,4},{12,8},{16,12},{20,16},{24,20},{28,24},{5,1},{9,5},{13... | collective-permute-start | bytes 1572872 | tf_op jit(solution)/shard_map/ppermute | solution.py:29
  3.3 26.8 %collective-permute-start = (bf16[1024,256]{1,0:T(8,128)(2,1)S(1)}, bf16[1024,256]{1,0:T(8,128)(2,1)S(1)}, u32[]{:S(2)}, u32[]{:S(2)}) collective-permute-start(bf16[1024,256]{1,0:T(8,128)(2,1)S(1)} %convert_element_type.96), channel_id=1, source_target_pairs={{0,4},{4,8},{8,12},{12,16},{16,20},{20,24},{24,28},{1,5},{5,9},{9,... | collective-permute-start | bytes 1572872 | tf_op jit(solution)/shard_map/ppermute | solution.py:29
  9.4 3.4 %copy-start.2 = (s32[2048]{0:T(1024)S(1)}, s32[2048]{0:T(1024)}, u32[]{:S(2)}) copy-start(s32[2048]{0:T(1024)} %param.12) | copy-start | bytes 24580
  9.4 4.0 %copy-start.1 = (f32[2048]{0:T(1024)S(1)}, f32[2048]{0:T(1024)}, u32[]{:S(2)}) copy-start(f32[2048]{0:T(1024)} %param.10) | copy-start | bytes 24580
  31.6 18.2 %all-to-all-start = ((bf16[32,16,256]{2,1,0:T(8,128)(2,1)}), bf16[32,16,256]{2,1,0:T(8,128)(2,1)S(1)}, u32[]{:S(2)}, u32[]{:S(2)}) async-start(bf16[32,16,256]{2,1,0:T(8,128)(2,1)} %broadcast_in_dim.7), calls=%async_computation | async-start | bytes 524288 | tf_op jit(solution)/shard_map/all_to_all | solution.py:76
  42.6 7.2 %copy-start.3 = (bf16[16,512]{1,0:T(8,128)(2,1)S(1)}, bf16[16,512]{1,0:T(8,128)(2,1)}, u32[]{:S(2)}) copy-start(bf16[16,512]{1,0:T(8,128)(2,1)} %param.11) | copy-start | bytes 49156
  53.4 15.6 %collective-permute-start.2 = (bf16[1024,256]{1,0:T(8,128)(2,1)S(1)}, bf16[1024,256]{1,0:T(8,128)(2,1)S(1)}, u32[]{:S(2)}, u32[]{:S(2)}) collective-permute-start(bf16[1024,256]{1,0:T(8,128)(2,1)S(1)} %fusion.50), channel_id=1, source_target_pairs={{4,0},{8,4},{12,8},{16,12},{20,16},{24,20},{28,24},{5,1},{9,5},{13... | collective-permute-start | bytes 1572872 | tf_op jit(solution)/shard_map/ppermute | solution.py:29
  54.7 24.6 %collective-permute-start.3 = (bf16[1024,256]{1,0:T(8,128)(2,1)S(1)}, bf16[1024,256]{1,0:T(8,128)(2,1)S(1)}, u32[]{:S(2)}, u32[]{:S(2)}) collective-permute-start(bf16[1024,256]{1,0:T(8,128)(2,1)S(1)} %fusion.58), channel_id=1, source_target_pairs={{0,4},{4,8},{8,12},{12,16},{16,20},{20,24},{24,28},{1,5},{5,9},{9,... | collective-permute-start | bytes 1572872 | tf_op jit(solution)/shard_map/ppermute | solution.py:29
  80.4 16.5 %collective-permute-start.5 = (bf16[1024,256]{1,0:T(8,128)(2,1)S(1)}, bf16[1024,256]{1,0:T(8,128)(2,1)S(1)}, u32[]{:S(2)}, u32[]{:S(2)}) collective-permute-start(bf16[1024,256]{1,0:T(8,128)(2,1)S(1)} %get-tuple-element.10), channel_id=1, source_target_pairs={{4,0},{8,4},{12,8},{16,12},{20,16},{24,20},{28,24},{5,1},{9,5},{13... | collective-permute-start | bytes 1572872 | tf_op jit(solution)/shard_map/ppermute | solution.py:29
  81.7 26.6 %collective-permute-start.4 = (bf16[1024,256]{1,0:T(8,128)(2,1)S(1)}, bf16[1024,256]{1,0:T(8,128)(2,1)S(1)}, u32[]{:S(2)}, u32[]{:S(2)}) collective-permute-start(bf16[1024,256]{1,0:T(8,128)(2,1)S(1)} %get-tuple-element.10), channel_id=1, source_target_pairs={{0,4},{4,8},{8,12},{12,16},{16,20},{20,24},{24,28},{1,5},{5,9},{9,... | collective-permute-start | bytes 1572872 | tf_op jit(solution)/shard_map/ppermute | solution.py:29
  112.5 16.7 %all-to-all-start.1 = ((bf16[32,16,256]{2,1,0:T(8,128)(2,1)}), bf16[32,16,256]{2,1,0:T(8,128)(2,1)S(1)}, u32[]{:S(2)}, u32[]{:S(2)}) async-start(bf16[32,16,256]{2,1,0:T(8,128)(2,1)} %broadcast_in_dim.8), calls=%async_computation.1 | async-start | bytes 524288 | tf_op jit(solution)/shard_map/all_to_all | solution.py:76
  132.7 15.6 %collective-permute-start.6 = (bf16[1024,256]{1,0:T(8,128)(2,1)S(1)}, bf16[1024,256]{1,0:T(8,128)(2,1)S(1)}, u32[]{:S(2)}, u32[]{:S(2)}) collective-permute-start(bf16[1024,256]{1,0:T(8,128)(2,1)S(1)} %fusion.51), channel_id=1, source_target_pairs={{4,0},{8,4},{12,8},{16,12},{20,16},{24,20},{28,24},{5,1},{9,5},{13... | collective-permute-start | bytes 1572872 | tf_op jit(solution)/shard_map/ppermute | solution.py:29
  134.0 24.2 %collective-permute-start.7 = (bf16[1024,256]{1,0:T(8,128)(2,1)S(1)}, bf16[1024,256]{1,0:T(8,128)(2,1)S(1)}, u32[]{:S(2)}, u32[]{:S(2)}) collective-permute-start(bf16[1024,256]{1,0:T(8,128)(2,1)S(1)} %fusion.61), channel_id=1, source_target_pairs={{0,4},{4,8},{8,12},{12,16},{16,20},{20,24},{24,28},{1,5},{5,9},{9,... | collective-permute-start | bytes 1572872 | tf_op jit(solution)/shard_map/ppermute | solution.py:29

commit v14 on v13

--- a/solution.py
+++ b/solution.py
@@ -73,9 +73,9 @@
         padded = jnp.concatenate([before, rounded, after], axis=0)
         primal = (primal_scale * padded[primal_source].astype(jnp.float32)).astype(jnp.bfloat16)
         count = lax.axis_size("sub") * lax.axis_size("grp")
-        primal_all = lax.all_to_all(
-            jnp.broadcast_to(primal[None], (count,) + primal.shape), AXES, 0, 0, tiled=False
-        ).reshape(-1, primal.shape[1])
+        primal_copies = jnp.broadcast_to(primal[None], (count,) + primal.shape)
+        primal_all = lax.all_to_all(primal_copies, AXES, 0, 0, tiled=False).reshape(-1, primal.shape[1])
+        before, primal_copies = lax.optimization_barrier((before, primal_copies))
         gathered_own = lax.optimization_barrier(select(picks[1], rounded))
         gathered = gathered_own + select(picks[0], before) + gathered_after
         scaled = (scale_column * gathered).astype(jnp.bfloat16)

time: 160 us -> 157 us (0.981)
  matrix products: 40.3 us -> 37.4 us
    dot_general x2, matrix products: 13.4 us -> 11.8 us  [precondition(): solved = jnp.dot(schur_inv, scaled, preferred_element_type=jnp.float32)]
  transfers between devices with their start and end apart: 10 -> 10, of which waited for: 10 -> 10; matrix products, arithmetic and copies ran while one was open for 20% -> 21% of each run, Pallas kernels for 0% -> 0%
where the time goes in v14:
time: 157 us; the launch traced here: 156 us
  waiting for transfers between devices  70.4 us (45%)
  starting transfers between devices  38.7 us (25%)
  matrix products  37.4 us (24%)
  other arithmetic  4.64 us (3%)
  local copies, waits for them, and re-layouts  4.47 us (3%)
    ppermute x8, waiting for transfers between devices, shifted(): return lax.ppermute(shard, axis, pairs)  66.3 us
    ppermute x8, starting transfers between devices, shifted(): return lax.ppermute(shard, axis, pairs)  25 us
    dot_general x12, matrix products, select(): return jnp.dot(matrix, rows, preferred_element_type=jnp.float32)  24.1 us
    all_to_all x2, starting transfers between devices, precondition(): lax.all_to_all(primal_copies, AXES, 0, 0, tiled=False)  13.7 us
    dot_general x2, matrix products, precondition(): solved = jnp.dot(schur_inv, scaled, preferred_element_type=jnp.float32)  11.8 us
    all_to_all x2, waiting for transfers between devices, precondition(): lax.all_to_all(primal_copies, AXES, 0, 0, tiled=False)  4.05 us
  transfers between devices with their start and end apart: 10, of which 10 were waited for; matrix products, arithmetic and copies ran while one was open for 21% of the time, Pallas kernels for 0%

profile of v14, /device:TPU:0, one launch (start us, length us, event | category | flops | bytes accessed | tf_op | source)
XLA Modules:
  0.0 156.5 jit_solution(18347869612822686347)
XLA Ops:
  0.6 1.3 convert_element_type.96
  3.3 5.5 %collective-permute-start = (bf16[1024,256]{1,0:T(8,128)(2,1)S(1)}, bf16[1024,256]{1,0:T(8,128)(2,1)S(1)}, u32[]{:S(2)}, u32[]{:S(2)}) collective-permute-start(bf16[1024,256]{1,0:T(8,128)(2,1)S(1)} %convert_element_type.96), channel_id=1, source_target_pairs={{0,4},{4,8},{8,12},{12,16},{16,20},{20,24},{24,28},{1,5},{5,9},{9,... | collective-permute-start | bytes 1572872 | tf_op jit(solution)/shard_map/ppermute | solution.py:29
  9.4 3.3 %fusion.10 = f32[2048,256]{1,0:T(8,128)} fusion(bf16[1024,256]{1,0:T(8,128)(2,1)S(1)} %convert_element_type.96, s32[1024]{0:T(1024)S(1)} %iota_add_fusion.1, s32[2048]{0:T(1024)} %param.12), kind=kOutput, calls=%fused_computation.14 | convolution fusion | flops 1075838976 | bytes 2633728 | tf_op jit(solution)/shard_map/dot_general | solution.py:65
  14.1 4.6 %collective-permute-done.1 = bf16[1024,256]{1,0:T(8,128)(2,1)S(1)} collective-permute-done((bf16[1024,256]{1,0:T(8,128)(2,1)S(1)}, bf16[1024,256]{1,0:T(8,128)(2,1)S(1)}, u32[]{:S(2)}, u32[]{:S(2)}) %collective-permute-start.1) | collective-permute-done | bytes 524320 | tf_op jit(solution)/shard_map/ppermute | solution.py:29
  18.7 2.6 %fusion.6 = f32[2048,256]{1,0:T(8,128)} fusion(bf16[1024,256]{1,0:T(8,128)(2,1)S(1)} %collective-permute-done.1, s32[1024]{0:T(1024)S(1)} %iota_add_fusion, s32[2048]{0:T(1024)S(1)} %copy-done.2), kind=kOutput, calls=%fused_computation.10 | convolution fusion | flops 1075838976 | bytes 2633728 | tf_op jit(solution)/shard_map/dot_general | solution.py:65
  21.3 8.8 %collective-permute-done = bf16[1024,256]{1,0:T(8,128)(2,1)S(1)} collective-permute-done((bf16[1024,256]{1,0:T(8,128)(2,1)S(1)}, bf16[1024,256]{1,0:T(8,128)(2,1)S(1)}, u32[]{:S(2)}, u32[]{:S(2)}) %collective-permute-start) | collective-permute-done | bytes 524320 | tf_op jit(solution)/shard_map/ppermute | solution.py:29
  31.6 7.6 %all-to-all-start = ((bf16[32,16,256]{2,1,0:T(8,128)(2,1)}), bf16[32,16,256]{2,1,0:T(8,128)(2,1)S(1)}, u32[]{:S(2)}, u32[]{:S(2)}) async-start(bf16[32,16,256]{2,1,0:T(8,128)(2,1)} %broadcast_in_dim.7), calls=%async_computation | async-start | bytes 524288 | tf_op jit(solution)/shard_map/all_to_all | solution.py:77
  39.2 3.1 %fusion.44 = f32[2048,256]{1,0:T(8,128)S(1)} fusion(f32[2048,256]{1,0:T(8,128)} %fusion.10, bf16[1024,256]{1,0:T(8,128)(2,1)S(1)} %collective-permute-done, s32[2048]{0:T(1024)S(1)} %copy-done.2), kind=kOutput, calls=%fused_computation.54 | convolution fusion | flops 1076363264 | bytes 4726784 | tf_op jit(solution)/shard_map/dot_general | solution.py:65
  42.3 5.9 %convolution_bitcast_fusion.1 = f32[2048,256]{1,0:T(8,128)S(1)} fusion(bf16[2048,2048]{1,0:T(8,128)(2,1)} %param.8, f32[2048,256]{1,0:T(8,128)S(1)} %fusion.44, f32[2048,256]{1,0:T(8,128)S(1)} %copy-done.6, f32[2048]{0:T(1024)S(1)} %copy-done.1), kind=kOutput, calls=%fused_computation.47 | convolution fusion | flops 2149056512 | bytes 14688256 | tf_op jit(solution)/shard_map/dot_general | solution.py:82
  48.2 1.6 %all-to-all-done = bf16[32,16,256]{2,1,0:T(8,128)(2,1)S(1)} async-done(((bf16[32,16,256]{2,1,0:T(8,128)(2,1)}), bf16[32,16,256]{2,1,0:T(8,128)(2,1)S(1)}, u32[]{:S(2)}, u32[]{:S(2)}) %all-to-all-start) | async-done | bytes 262176 | tf_op jit(solution)/shard_map/all_to_all | solution.py:77
  50.6 1.3 fusion.55
  51.9 1.5 fusion.47
  53.4 1.3 collective-permute-start.2
  54.7 4.6 %collective-permute-start.3 = (bf16[1024,256]{1,0:T(8,128)(2,1)S(1)}, bf16[1024,256]{1,0:T(8,128)(2,1)S(1)}, u32[]{:S(2)}, u32[]{:S(2)}) collective-permute-start(bf16[1024,256]{1,0:T(8,128)(2,1)S(1)} %fusion.55), channel_id=1, source_target_pairs={{0,4},{4,8},{8,12},{12,16},{16,20},{20,24},{24,28},{1,5},{5,9},{9,... | collective-permute-start | bytes 1572872 | tf_op jit(solution)/shard_map/ppermute | solution.py:29
  59.3 1.3 fusion.49
  60.6 8.4 %collective-permute-done.2 = bf16[1024,256]{1,0:T(8,128)(2,1)S(1)} collective-permute-done((bf16[1024,256]{1,0:T(8,128)(2,1)S(1)}, bf16[1024,256]{1,0:T(8,128)(2,1)S(1)}, u32[]{:S(2)}, u32[]{:S(2)}) %collective-permute-start.2) | collective-permute-done | bytes 524320 | tf_op jit(solution)/shard_map/ppermute | solution.py:29
  69.0 10.1 %collective-permute-done.3 = bf16[1024,256]{1,0:T(8,128)(2,1)S(1)} collective-permute-done((bf16[1024,256]{1,0:T(8,128)(2,1)S(1)}, bf16[1024,256]{1,0:T(8,128)(2,1)S(1)}, u32[]{:S(2)}, u32[]{:S(2)}) %collective-permute-start.3) | collective-permute-done | bytes 524320 | tf_op jit(solution)/shard_map/ppermute | solution.py:29
  81.6 5.2 %collective-permute-start.4 = (bf16[1024,256]{1,0:T(8,128)(2,1)S(1)}, bf16[1024,256]{1,0:T(8,128)(2,1)S(1)}, u32[]{:S(2)}, u32[]{:S(2)}) collective-permute-start(bf16[1024,256]{1,0:T(8,128)(2,1)S(1)} %get-tuple-element.14), channel_id=1, source_target_pairs={{0,4},{4,8},{8,12},{12,16},{16,20},{20,24},{24,28},{1,5},{5,9},{9,... | collective-permute-start | bytes 1572872 | tf_op jit(solution)/shard_map/ppermute | solution.py:29
  86.8 2.6 %fusion.8 = f32[2048,256]{1,0:T(8,128)} fusion(bf16[1024,256]{1,0:T(8,128)(2,1)S(1)} %get-tuple-element.14, s32[1024]{0:T(1024)S(1)} %iota_add_fusion.1, s32[2048]{0:T(1024)S(1)} %copy-done.2), kind=kOutput, calls=%fused_computation.12 | convolution fusion | flops 1075838976 | bytes 2633728 | tf_op jit(solution)/shard_map/dot_general | solution.py:65
  89.4 7.4 %collective-permute-done.5 = bf16[1024,256]{1,0:T(8,128)(2,1)S(1)} collective-permute-done((bf16[1024,256]{1,0:T(8,128)(2,1)S(1)}, bf16[1024,256]{1,0:T(8,128)(2,1)S(1)}, u32[]{:S(2)}, u32[]{:S(2)}) %collective-permute-start.5) | collective-permute-done | bytes 524320 | tf_op jit(solution)/shard_map/ppermute | solution.py:29
  96.7 2.6 %fusion.4 = f32[2048,256]{1,0:T(8,128)} fusion(bf16[1024,256]{1,0:T(8,128)(2,1)S(1)} %collective-permute-done.5, s32[1024]{0:T(1024)S(1)} %iota_add_fusion, s32[2048]{0:T(1024)S(1)} %copy-done.2), kind=kOutput, calls=%fused_computation.8 | convolution fusion | flops 1075838976 | bytes 2633728 | tf_op jit(solution)/shard_map/dot_general | solution.py:65
  99.3 8.8 %collective-permute-done.4 = bf16[1024,256]{1,0:T(8,128)(2,1)S(1)} collective-permute-done((bf16[1024,256]{1,0:T(8,128)(2,1)S(1)}, bf16[1024,256]{1,0:T(8,128)(2,1)S(1)}, u32[]{:S(2)}, u32[]{:S(2)}) %collective-permute-start.4) | collective-permute-done | bytes 524320 | tf_op jit(solution)/shard_map/ppermute | solution.py:29
  109.6 6.1 %all-to-all-start.1 = ((bf16[32,16,256]{2,1,0:T(8,128)(2,1)}), bf16[32,16,256]{2,1,0:T(8,128)(2,1)S(1)}, u32[]{:S(2)}, u32[]{:S(2)}) async-start(bf16[32,16,256]{2,1,0:T(8,128)(2,1)} %broadcast_in_dim.8), calls=%async_computation.1 | async-start | bytes 524288 | tf_op jit(solution)/shard_map/all_to_all | solution.py:77
  115.7 1.7 %fusion.18 = f32[2048,256]{1,0:T(8,128)S(1)} fusion(bf16[1024,256]{1,0:T(8,128)(2,1)S(1)} %collective-permute-done.4, s32[2048]{0:T(1024)S(1)} %copy-done.2), kind=kOutput, calls=%fused_computation.24 | convolution fusion | flops 1075838976 | bytes 2629632 | tf_op jit(solution)/shard_map/dot_general | solution.py:65
  117.9 5.9 %convolution_bitcast_fusion = f32[2048,256]{1,0:T(8,128)S(1)} fusion(bf16[2048,2048]{1,0:T(8,128)(2,1)} %param.8, f32[2048,256]{1,0:T(8,128)S(1)} %copy-done.5, f32[2048,256]{1,0:T(8,128)S(1)} %copy-done.4, f32[2048,256]{1,0:T(8,128)S(1)} %fusion.18, f32[2048]{0:T(1024)S(1)} %copy-done.1), kind=kOutput, calls=%fused_computation.46 | convolution fusion | flops 2149580800 | bytes 16785408 | tf_op jit(solution)/shard_map/dot_general | solution.py:82
  123.8 2.5 %all-to-all-done.1 = bf16[32,16,256]{2,1,0:T(8,128)(2,1)S(1)} async-done(((bf16[32,16,256]{2,1,0:T(8,128)(2,1)}), bf16[32,16,256]{2,1,0:T(8,128)(2,1)S(1)}, u32[]{:S(2)}, u32[]{:S(2)}) %all-to-all-start.1) | async-done | bytes 262176 | tf_op jit(solution)/shard_map/all_to_all | solution.py:77
  127.1 1.3 fusion.58
  128.4 1.5 fusion.48
  131.2 4.6 %collective-permute-start.7 = (bf16[1024,256]{1,0:T(8,128)(2,1)S(1)}, bf16[1024,256]{1,0:T(8,128)(2,1)S(1)}, u32[]{:S(2)}, u32[]{:S(2)}) collective-permute-start(bf16[1024,256]{1,0:T(8,128)(2,1)S(1)} %fusion.58), channel_id=1, source_target_pairs={{0,4},{4,8},{8,12},{12,16},{16,20},{20,24},{24,28},{1,5},{5,9},{9,... | collective-permute-start | bytes 1572872 | tf_op jit(solution)/shard_map/ppermute | solution.py:29
  135.8 1.3 fusion.52
  137.1 8.4 %collective-permute-done.6 = bf16[1024,256]{1,0:T(8,128)(2,1)S(1)} collective-permute-done((bf16[1024,256]{1,0:T(8,128)(2,1)S(1)}, bf16[1024,256]{1,0:T(8,128)(2,1)S(1)}, u32[]{:S(2)}, u32[]{:S(2)}) %collective-permute-start.6) | collective-permute-done | bytes 524320 | tf_op jit(solution)/shard_map/ppermute | solution.py:29
  145.5 9.8 %collective-permute-done.7 = bf16[1024,256]{1,0:T(8,128)(2,1)S(1)} collective-permute-done((bf16[1024,256]{1,0:T(8,128)(2,1)S(1)}, bf16[1024,256]{1,0:T(8,128)(2,1)S(1)}, u32[]{:S(2)}, u32[]{:S(2)}) %collective-permute-start.7) | collective-permute-done | bytes 524320 | tf_op jit(solution)/shard_map/ppermute | solution.py:29
  (37 shorter events, 13.2 us)
Async XLA Ops:
  0.6 49.2 %copy-start = (bf16[16,2048]{1,0:T(8,128)(2,1)S(1)}, bf16[16,2048]{1,0:T(8,128)(2,1)}, u32[]{:S(2)}) copy-start(bf16[16,2048]{1,0:T(8,128)(2,1)} %param.9) | copy-start | bytes 196612
  2.0 16.8 %collective-permute-start.1 = (bf16[1024,256]{1,0:T(8,128)(2,1)S(1)}, bf16[1024,256]{1,0:T(8,128)(2,1)S(1)}, u32[]{:S(2)}, u32[]{:S(2)}) collective-permute-start(bf16[1024,256]{1,0:T(8,128)(2,1)S(1)} %convert_element_type.96), channel_id=1, source_target_pairs={{4,0},{8,4},{12,8},{16,12},{20,16},{24,20},{28,24},{5,1},{9,5},{13... | collective-permute-start | bytes 1572872 | tf_op jit(solution)/shard_map/ppermute | solution.py:29
  3.3 26.8 %collective-permute-start = (bf16[1024,256]{1,0:T(8,128)(2,1)S(1)}, bf16[1024,256]{1,0:T(8,128)(2,1)S(1)}, u32[]{:S(2)}, u32[]{:S(2)}) collective-permute-start(bf16[1024,256]{1,0:T(8,128)(2,1)S(1)} %convert_element_type.96), channel_id=1, source_target_pairs={{0,4},{4,8},{8,12},{12,16},{16,20},{20,24},{24,28},{1,5},{5,9},{9,... | collective-permute-start | bytes 1572872 | tf_op jit(solution)/shard_map/ppermute | solution.py:29
  9.4 3.3 %copy-start.2 = (s32[2048]{0:T(1024)S(1)}, s32[2048]{0:T(1024)}, u32[]{:S(2)}) copy-start(s32[2048]{0:T(1024)} %param.12) | copy-start | bytes 24580
  9.4 4.0 %copy-start.1 = (f32[2048]{0:T(1024)S(1)}, f32[2048]{0:T(1024)}, u32[]{:S(2)}) copy-start(f32[2048]{0:T(1024)} %param.10) | copy-start | bytes 24580
  31.6 18.2 %all-to-all-start = ((bf16[32,16,256]{2,1,0:T(8,128)(2,1)}), bf16[32,16,256]{2,1,0:T(8,128)(2,1)S(1)}, u32[]{:S(2)}, u32[]{:S(2)}) async-start(bf16[32,16,256]{2,1,0:T(8,128)(2,1)} %broadcast_in_dim.7), calls=%async_computation | async-start | bytes 524288 | tf_op jit(solution)/shard_map/all_to_all | solution.py:77
  39.2 3.1 %copy-start.6 = (f32[2048,256]{1,0:T(8,128)S(1)}, f32[2048,256]{1,0:T(8,128)}, u32[]{:S(2)}) copy-start(f32[2048,256]{1,0:T(8,128)} %fusion.6) | copy-start | bytes 6291460
  42.3 7.5 %copy-start.3 = (bf16[16,512]{1,0:T(8,128)(2,1)S(1)}, bf16[16,512]{1,0:T(8,128)(2,1)}, u32[]{:S(2)}) copy-start(bf16[16,512]{1,0:T(8,128)(2,1)} %param.11) | copy-start | bytes 49156
  53.4 15.6 %collective-permute-start.2 = (bf16[1024,256]{1,0:T(8,128)(2,1)S(1)}, bf16[1024,256]{1,0:T(8,128)(2,1)S(1)}, u32[]{:S(2)}, u32[]{:S(2)}) collective-permute-start(bf16[1024,256]{1,0:T(8,128)(2,1)S(1)} %fusion.47), channel_id=1, source_target_pairs={{4,0},{8,4},{12,8},{16,12},{20,16},{24,20},{28,24},{5,1},{9,5},{13... | collective-permute-start | bytes 1572872 | tf_op jit(solution)/shard_map/ppermute | solution.py:29
  54.7 24.4 %collective-permute-start.3 = (bf16[1024,256]{1,0:T(8,128)(2,1)S(1)}, bf16[1024,256]{1,0:T(8,128)(2,1)S(1)}, u32[]{:S(2)}, u32[]{:S(2)}) collective-permute-start(bf16[1024,256]{1,0:T(8,128)(2,1)S(1)} %fusion.55), channel_id=1, source_target_pairs={{0,4},{4,8},{8,12},{12,16},{16,20},{20,24},{24,28},{1,5},{5,9},{9,... | collective-permute-start | bytes 1572872 | tf_op jit(solution)/shard_map/ppermute | solution.py:29
  80.3 16.5 %collective-permute-start.5 = (bf16[1024,256]{1,0:T(8,128)(2,1)S(1)}, bf16[1024,256]{1,0:T(8,128)(2,1)S(1)}, u32[]{:S(2)}, u32[]{:S(2)}) collective-permute-start(bf16[1024,256]{1,0:T(8,128)(2,1)S(1)} %get-tuple-element.14), channel_id=1, source_target_pairs={{4,0},{8,4},{12,8},{16,12},{20,16},{24,20},{28,24},{5,1},{9,5},{13... | collective-permute-start | bytes 1572872 | tf_op jit(solution)/shard_map/ppermute | solution.py:29
  81.6 26.6 %collective-permute-start.4 = (bf16[1024,256]{1,0:T(8,128)(2,1)S(1)}, bf16[1024,256]{1,0:T(8,128)(2,1)S(1)}, u32[]{:S(2)}, u32[]{:S(2)}) collective-permute-start(bf16[1024,256]{1,0:T(8,128)(2,1)S(1)} %get-tuple-element.14), channel_id=1, source_target_pairs={{0,4},{4,8},{8,12},{12,16},{16,20},{20,24},{24,28},{1,5},{5,9},{9,... | collective-permute-start | bytes 1572872 | tf_op jit(solution)/shard_map/ppermute | solution.py:29
  109.6 16.7 %all-to-all-start.1 = ((bf16[32,16,256]{2,1,0:T(8,128)(2,1)}), bf16[32,16,256]{2,1,0:T(8,128)(2,1)S(1)}, u32[]{:S(2)}, u32[]{:S(2)}) async-start(bf16[32,16,256]{2,1,0:T(8,128)(2,1)} %broadcast_in_dim.8), calls=%async_computation.1 | async-start | bytes 524288 | tf_op jit(solution)/shard_map/all_to_all | solution.py:77
  115.7 1.7 %copy-start.4 = (f32[2048,256]{1,0:T(8,128)S(1)}, f32[2048,256]{1,0:T(8,128)}, u32[]{:S(2)}) copy-start(f32[2048,256]{1,0:T(8,128)} %fusion.8) | copy-start | bytes 6291460
  115.7 2.2 %copy-start.5 = (f32[2048,256]{1,0:T(8,128)S(1)}, f32[2048,256]{1,0:T(8,128)}, u32[]{:S(2)}) copy-start(f32[2048,256]{1,0:T(8,128)} %fusion.4) | copy-start | bytes 6291460
  129.9 15.6 %collective-permute-start.6 = (bf16[1024,256]{1,0:T(8,128)(2,1)S(1)}, bf16[1024,256]{1,0:T(8,128)(2,1)S(1)}, u32[]{:S(2)}, u32[]{:S(2)}) collective-permute-start(bf16[1024,256]{1,0:T(8,128)(2,1)S(1)} %fusion.48), channel_id=1, source_target_pairs={{4,0},{8,4},{12,8},{16,12},{20,16},{24,20},{28,24},{5,1},{9,5},{13... | collective-permute-start | bytes 1572872 | tf_op jit(solution)/shard_map/ppermute | solution.py:29
  131.2 24.2 %collective-permute-start.7 = (bf16[1024,256]{1,0:T(8,128)(2,1)S(1)}, bf16[1024,256]{1,0:T(8,128)(2,1)S(1)}, u32[]{:S(2)}, u32[]{:S(2)}) collective-permute-start(bf16[1024,256]{1,0:T(8,128)(2,1)S(1)} %fusion.58), channel_id=1, source_target_pairs={{0,4},{4,8},{8,12},{12,16},{16,20},{20,24},{24,28},{1,5},{5,9},{9,... | collective-permute-start | bytes 1572872 | tf_op jit(solution)/shard_map/ppermute | solution.py:29

commit v15 on v13

--- a/solution.py
+++ b/solution.py
@@ -72,10 +72,14 @@
         before, gathered_after = lax.optimization_barrier((before, gathered_after))
         padded = jnp.concatenate([before, rounded, after], axis=0)
         primal = (primal_scale * padded[primal_source].astype(jnp.float32)).astype(jnp.bfloat16)
-        count = lax.axis_size("sub") * lax.axis_size("grp")
+        group = lax.axis_size("grp")
+        primal_copies = jnp.broadcast_to(primal[None], (group,) + primal.shape)
+        in_group = lax.all_to_all(primal_copies, "grp", 0, 0, tiled=False)
+        chain = lax.axis_size("sub")
         primal_all = lax.all_to_all(
-            jnp.broadcast_to(primal[None], (count,) + primal.shape), AXES, 0, 0, tiled=False
+            jnp.broadcast_to(in_group[None], (chain,) + in_group.shape), "sub", 0, 0, tiled=False
         ).reshape(-1, primal.shape[1])
+        before, primal_copies = lax.optimization_barrier((before, primal_copies))
         gathered_own = lax.optimization_barrier(select(picks[1], rounded))
         gathered = gathered_own + select(picks[0], before) + gathered_after
         scaled = (scale_column * gathered).astype(jnp.bfloat16)

time: 160 us -> 171 us (1.069)
  starting transfers between devices: 38.7 us -> 47.7 us
  matrix products: 40.3 us -> 42.1 us
    all_to_all x2 -> x4, starting transfers between devices: 13.7 us -> 25.8 us  [the longest x2 19.2 us: precondition(): lax.all_to_all(jnp.broadcast_to(in_group[None], (chain,) + in_group.shape...]
    ppermute x8, starting transfers between devices: 25 us -> 22 us  [shifted(): return lax.ppermute(shard, axis, pairs)]
    ppermute x8, waiting for transfers between devices: 66.5 us -> 64.7 us  [shifted(): return lax.ppermute(shard, axis, pairs)]
    all_to_all x2 -> x4, waiting for transfers between devices: 4.34 us -> 4.84 us  [the longest x2 3.61 us: precondition(): lax.all_to_all(jnp.broadcast_to(in_group[None], (chain,) + in_group.shape...]
  transfers between devices with their start and end apart: 10 -> 12, of which waited for: 10 -> 9; matrix products, arithmetic and copies ran while one was open for 20% -> 21% of each run, Pallas kernels for 0% -> 0%
where the time goes in v15:
time: 171 us; the launch traced here: 169 us
  waiting for transfers between devices  69.6 us (41%)
  starting transfers between devices  47.7 us (28%)
  matrix products  42.1 us (25%)
  local copies, waits for them, and re-layouts  5.22 us (3%)
  other arithmetic  3.99 us (2%)
    ppermute x8, waiting for transfers between devices, shifted(): return lax.ppermute(shard, axis, pairs)  64.7 us
    dot_general x12, matrix products, select(): return jnp.dot(matrix, rows, preferred_element_type=jnp.float32)  25.8 us
    ppermute x8, starting transfers between devices, shifted(): return lax.ppermute(shard, axis, pairs)  22 us
    all_to_all x2, starting transfers between devices, precondition(): lax.all_to_all(jnp.broadcast_to(in_group[None], (chain,) + in_group.shape...  19.2 us
    dot_general x2, matrix products, precondition(): solved = jnp.dot(schur_inv, scaled, preferred_element_type=jnp.float32)  14.7 us
    all_to_all x2, starting transfers between devices, precondition(): in_group = lax.all_to_all(primal_copies, 'grp', 0, 0, tiled=False)  6.53 us
    all_to_all x2, waiting for transfers between devices, precondition(): lax.all_to_all(jnp.broadcast_to(in_group[None], (chain,) + in_group.shape...  3.61 us
  transfers between devices with their start and end apart: 12, of which 9 were waited for; matrix products, arithmetic and copies ran while one was open for 21% of the time, Pallas kernels for 0%

profile of v15, /device:TPU:0, one launch (start us, length us, event | category | flops | bytes accessed | tf_op | source)
XLA Modules:
  0.0 169.4 jit_solution(833767583393008487)
XLA Ops:
  0.6 1.3 convert_element_type.96
  2.0 4.9 %collective-permute-start = (bf16[1024,256]{1,0:T(8,128)(2,1)S(1)}, bf16[1024,256]{1,0:T(8,128)(2,1)S(1)}, u32[]{:S(2)}, u32[]{:S(2)}) collective-permute-start(bf16[1024,256]{1,0:T(8,128)(2,1)S(1)} %convert_element_type.96), channel_id=1, source_target_pairs={{0,4},{4,8},{8,12},{12,16},{16,20},{20,24},{24,28},{1,5},{5,9},{9,... | collective-permute-start | bytes 1572872 | tf_op jit(solution)/shard_map/ppermute | solution.py:29
  6.8 1.3 collective-permute-start.1
  8.2 3.3 %fusion.10 = f32[2048,256]{1,0:T(8,128)} fusion(bf16[1024,256]{1,0:T(8,128)(2,1)S(1)} %convert_element_type.96, s32[1024]{0:T(1024)S(1)} %iota_add_fusion.1, s32[2048]{0:T(1024)} %param.12), kind=kOutput, calls=%fused_computation.14 | convolution fusion | flops 1075838976 | bytes 2633728 | tf_op jit(solution)/shard_map/dot_general | solution.py:65
  12.8 9.3 %collective-permute-done.1 = bf16[1024,256]{1,0:T(8,128)(2,1)S(1)} collective-permute-done((bf16[1024,256]{1,0:T(8,128)(2,1)S(1)}, bf16[1024,256]{1,0:T(8,128)(2,1)S(1)}, u32[]{:S(2)}, u32[]{:S(2)}) %collective-permute-start.1) | collective-permute-done | bytes 524320 | tf_op jit(solution)/shard_map/ppermute | solution.py:29
  22.1 2.5 %fusion.6 = f32[2048,256]{1,0:T(8,128)} fusion(bf16[1024,256]{1,0:T(8,128)(2,1)S(1)} %collective-permute-done.1, s32[1024]{0:T(1024)S(1)} %iota_add_fusion, s32[2048]{0:T(1024)S(1)} %copy-done.2), kind=kOutput, calls=%fused_computation.10 | convolution fusion | flops 1075838976 | bytes 2633728 | tf_op jit(solution)/shard_map/dot_general | solution.py:65
  24.7 4.5 %collective-permute-done = bf16[1024,256]{1,0:T(8,128)(2,1)S(1)} collective-permute-done((bf16[1024,256]{1,0:T(8,128)(2,1)S(1)}, bf16[1024,256]{1,0:T(8,128)(2,1)S(1)}, u32[]{:S(2)}, u32[]{:S(2)}) %collective-permute-start) | collective-permute-done | bytes 524320 | tf_op jit(solution)/shard_map/ppermute | solution.py:29
  30.6 3.3 %all-to-all-start = ((bf16[4,16,256]{2,1,0:T(8,128)(2,1)}), bf16[4,16,256]{2,1,0:T(8,128)(2,1)S(1)}, u32[]{:S(2)}, u32[]{:S(2)}) async-start(bf16[4,16,256]{2,1,0:T(8,128)(2,1)} %broadcast_in_dim.11), calls=%async_computation | async-start | bytes 65536 | tf_op jit(solution)/shard_map/all_to_all | solution.py:77
  33.9 3.9 %fusion.44 = f32[2048,256]{1,0:T(8,128)} fusion(f32[2048,256]{1,0:T(8,128)} %fusion.10, bf16[1024,256]{1,0:T(8,128)(2,1)S(1)} %collective-permute-done, s32[2048]{0:T(1024)S(1)} %copy-done.2), kind=kOutput, calls=%fused_computation.54 | convolution fusion | flops 1076363264 | bytes 4726784 | tf_op jit(solution)/shard_map/dot_general | solution.py:65
  38.5 9.3 %all-to-all-start.1 = ((bf16[8,4,16,256]{3,2,1,0:T(8,128)(2,1)}), bf16[8,4,16,256]{3,2,1,0:T(8,128)(2,1)S(1)}, u32[]{:S(2)}, u32[]{:S(2)}) async-start(bf16[8,4,16,256]{3,2,1,0:T(8,128)(2,1)} %broadcast_in_dim.12), calls=%async_computation.1 | async-start | bytes 524288 | tf_op jit(solution)/shard_map/all_to_all | solution.py:79
  47.8 7.1 %convolution_bitcast_fusion.1 = f32[2048,256]{1,0:T(8,128)S(1)} fusion(bf16[2048,2048]{1,0:T(8,128)(2,1)} %param.8, f32[2048,256]{1,0:T(8,128)} %fusion.44, f32[2048,256]{1,0:T(8,128)} %fusion.6, f32[2048]{0:T(1024)S(1)} %copy-done.1), kind=kOutput, calls=%fused_computation.47 | convolution fusion | flops 2149056512 | bytes 14688256 | tf_op jit(solution)/shard_map/dot_general | solution.py:86
  54.9 2.5 %all-to-all-done.1 = bf16[8,4,16,256]{3,2,1,0:T(8,128)(2,1)S(1)} async-done(((bf16[8,4,16,256]{3,2,1,0:T(8,128)(2,1)}), bf16[8,4,16,256]{3,2,1,0:T(8,128)(2,1)S(1)}, u32[]{:S(2)}, u32[]{:S(2)}) %all-to-all-start.1) | async-done | bytes 262176 | tf_op jit(solution)/shard_map/all_to_all | solution.py:79
  58.2 1.3 fusion.55
  59.5 1.5 fusion.47
  61.0 3.3 %collective-permute-start.3 = (bf16[1024,256]{1,0:T(8,128)(2,1)S(1)}, bf16[1024,256]{1,0:T(8,128)(2,1)S(1)}, u32[]{:S(2)}, u32[]{:S(2)}) collective-permute-start(bf16[1024,256]{1,0:T(8,128)(2,1)S(1)} %fusion.55), channel_id=1, source_target_pairs={{0,4},{4,8},{8,12},{12,16},{16,20},{20,24},{24,28},{1,5},{5,9},{9,... | collective-permute-start | bytes 1572872 | tf_op jit(solution)/shard_map/ppermute | solution.py:29
  64.3 1.3 collective-permute-start.2
  65.6 1.3 fusion.49
  67.0 18.0 %collective-permute-done.3 = bf16[1024,256]{1,0:T(8,128)(2,1)S(1)} collective-permute-done((bf16[1024,256]{1,0:T(8,128)(2,1)S(1)}, bf16[1024,256]{1,0:T(8,128)(2,1)S(1)}, u32[]{:S(2)}, u32[]{:S(2)}) %collective-permute-start.3) | collective-permute-done | bytes 524320 | tf_op jit(solution)/shard_map/ppermute | solution.py:29
  87.4 5.2 %collective-permute-start.4 = (bf16[1024,256]{1,0:T(8,128)(2,1)S(1)}, bf16[1024,256]{1,0:T(8,128)(2,1)S(1)}, u32[]{:S(2)}, u32[]{:S(2)}) collective-permute-start(bf16[1024,256]{1,0:T(8,128)(2,1)S(1)} %get-tuple-element.14), channel_id=1, source_target_pairs={{0,4},{4,8},{8,12},{12,16},{16,20},{20,24},{24,28},{1,5},{5,9},{9,... | collective-permute-start | bytes 1572872 | tf_op jit(solution)/shard_map/ppermute | solution.py:29
  92.6 2.6 %fusion.8 = f32[2048,256]{1,0:T(8,128)} fusion(bf16[1024,256]{1,0:T(8,128)(2,1)S(1)} %get-tuple-element.14, s32[1024]{0:T(1024)S(1)} %iota_add_fusion.1, s32[2048]{0:T(1024)S(1)} %copy-done.2), kind=kOutput, calls=%fused_computation.12 | convolution fusion | flops 1075838976 | bytes 2633728 | tf_op jit(solution)/shard_map/dot_general | solution.py:65
  95.2 4.5 %collective-permute-done.5 = bf16[1024,256]{1,0:T(8,128)(2,1)S(1)} collective-permute-done((bf16[1024,256]{1,0:T(8,128)(2,1)S(1)}, bf16[1024,256]{1,0:T(8,128)(2,1)S(1)}, u32[]{:S(2)}, u32[]{:S(2)}) %collective-permute-start.5) | collective-permute-done | bytes 524320 | tf_op jit(solution)/shard_map/ppermute | solution.py:29
  99.7 2.5 %fusion.4 = f32[2048,256]{1,0:T(8,128)} fusion(bf16[1024,256]{1,0:T(8,128)(2,1)S(1)} %collective-permute-done.5, s32[1024]{0:T(1024)S(1)} %iota_add_fusion, s32[2048]{0:T(1024)S(1)} %copy-done.2), kind=kOutput, calls=%fused_computation.8 | convolution fusion | flops 1075838976 | bytes 2633728 | tf_op jit(solution)/shard_map/dot_general | solution.py:65
  102.3 9.9 %collective-permute-done.4 = bf16[1024,256]{1,0:T(8,128)(2,1)S(1)} collective-permute-done((bf16[1024,256]{1,0:T(8,128)(2,1)S(1)}, bf16[1024,256]{1,0:T(8,128)(2,1)S(1)}, u32[]{:S(2)}, u32[]{:S(2)}) %collective-permute-start.4) | collective-permute-done | bytes 524320 | tf_op jit(solution)/shard_map/ppermute | solution.py:29
  113.5 3.3 %all-to-all-start.2 = ((bf16[4,16,256]{2,1,0:T(8,128)(2,1)}), bf16[4,16,256]{2,1,0:T(8,128)(2,1)S(1)}, u32[]{:S(2)}, u32[]{:S(2)}) async-start(bf16[4,16,256]{2,1,0:T(8,128)(2,1)} %broadcast_in_dim.13), calls=%async_computation.2 | async-start | bytes 65536 | tf_op jit(solution)/shard_map/all_to_all | solution.py:77
  116.8 2.7 %fusion.18 = f32[2048,256]{1,0:T(8,128)} fusion(bf16[1024,256]{1,0:T(8,128)(2,1)S(1)} %collective-permute-done.4, s32[2048]{0:T(1024)S(1)} %copy-done.2), kind=kOutput, calls=%fused_computation.24 | convolution fusion | flops 1075838976 | bytes 2629632 | tf_op jit(solution)/shard_map/dot_general | solution.py:65
  121.4 9.9 %all-to-all-start.3 = ((bf16[8,4,16,256]{3,2,1,0:T(8,128)(2,1)}), bf16[8,4,16,256]{3,2,1,0:T(8,128)(2,1)S(1)}, u32[]{:S(2)}, u32[]{:S(2)}) async-start(bf16[8,4,16,256]{3,2,1,0:T(8,128)(2,1)} %broadcast_in_dim.14), calls=%async_computation.3 | async-start | bytes 524288 | tf_op jit(solution)/shard_map/all_to_all | solution.py:79
  131.4 7.7 %convolution_bitcast_fusion = f32[2048,256]{1,0:T(8,128)S(1)} fusion(bf16[2048,2048]{1,0:T(8,128)(2,1)} %param.8, f32[2048,256]{1,0:T(8,128)} %fusion.4, f32[2048,256]{1,0:T(8,128)} %fusion.8, f32[2048,256]{1,0:T(8,128)} %fusion.18, f32[2048]{0:T(1024)S(1)} %copy-done.1), kind=kOutput, calls=%fused_computation.46 | convolution fusion | flops 2149580800 | bytes 16785408 | tf_op jit(solution)/shard_map/dot_general | solution.py:86
  141.0 1.3 fusion.58
  142.3 1.5 fusion.48
  143.8 3.4 %collective-permute-start.7 = (bf16[1024,256]{1,0:T(8,128)(2,1)S(1)}, bf16[1024,256]{1,0:T(8,128)(2,1)S(1)}, u32[]{:S(2)}, u32[]{:S(2)}) collective-permute-start(bf16[1024,256]{1,0:T(8,128)(2,1)S(1)} %fusion.58), channel_id=1, source_target_pairs={{0,4},{4,8},{8,12},{12,16},{16,20},{20,24},{24,28},{1,5},{5,9},{9,... | collective-permute-start | bytes 1572872 | tf_op jit(solution)/shard_map/ppermute | solution.py:29
  148.4 1.3 fusion.52
  149.8 18.5 %collective-permute-done.7 = bf16[1024,256]{1,0:T(8,128)(2,1)S(1)} collective-permute-done((bf16[1024,256]{1,0:T(8,128)(2,1)S(1)}, bf16[1024,256]{1,0:T(8,128)(2,1)S(1)}, u32[]{:S(2)}, u32[]{:S(2)}) %collective-permute-start.7) | collective-permute-done | bytes 524320 | tf_op jit(solution)/shard_map/ppermute | solution.py:29
  (39 shorter events, 14.4 us)
Async XLA Ops:
  0.6 56.8 %copy-start = (bf16[16,2048]{1,0:T(8,128)(2,1)S(1)}, bf16[16,2048]{1,0:T(8,128)(2,1)}, u32[]{:S(2)}) copy-start(bf16[16,2048]{1,0:T(8,128)(2,1)} %param.9) | copy-start | bytes 196612
  2.0 27.2 %collective-permute-start = (bf16[1024,256]{1,0:T(8,128)(2,1)S(1)}, bf16[1024,256]{1,0:T(8,128)(2,1)S(1)}, u32[]{:S(2)}, u32[]{:S(2)}) collective-permute-start(bf16[1024,256]{1,0:T(8,128)(2,1)S(1)} %convert_element_type.96), channel_id=1, source_target_pairs={{0,4},{4,8},{8,12},{12,16},{16,20},{20,24},{24,28},{1,5},{5,9},{9,... | collective-permute-start | bytes 1572872 | tf_op jit(solution)/shard_map/ppermute | solution.py:29
  6.8 15.3 %collective-permute-start.1 = (bf16[1024,256]{1,0:T(8,128)(2,1)S(1)}, bf16[1024,256]{1,0:T(8,128)(2,1)S(1)}, u32[]{:S(2)}, u32[]{:S(2)}) collective-permute-start(bf16[1024,256]{1,0:T(8,128)(2,1)S(1)} %convert_element_type.96), channel_id=1, source_target_pairs={{4,0},{8,4},{12,8},{16,12},{20,16},{24,20},{28,24},{5,1},{9,5},{13... | collective-permute-start | bytes 1572872 | tf_op jit(solution)/shard_map/ppermute | solution.py:29
  8.2 3.3 %copy-start.4 = (s32[16]{0:T(128)S(1)}, s32[16]{0:T(128)}, u32[]{:S(2)}) copy-start(s32[16]{0:T(128)} %param.13) | copy-start | bytes 196
  8.2 3.3 %copy-start.2 = (s32[2048]{0:T(1024)S(1)}, s32[2048]{0:T(1024)}, u32[]{:S(2)}) copy-start(s32[2048]{0:T(1024)} %param.12) | copy-start | bytes 24580
  8.2 4.0 %copy-start.1 = (f32[2048]{0:T(1024)S(1)}, f32[2048]{0:T(1024)}, u32[]{:S(2)}) copy-start(f32[2048]{0:T(1024)} %param.10) | copy-start | bytes 24580
  30.6 7.2 %all-to-all-start = ((bf16[4,16,256]{2,1,0:T(8,128)(2,1)}), bf16[4,16,256]{2,1,0:T(8,128)(2,1)S(1)}, u32[]{:S(2)}, u32[]{:S(2)}) async-start(bf16[4,16,256]{2,1,0:T(8,128)(2,1)} %broadcast_in_dim.11), calls=%async_computation | async-start | bytes 65536 | tf_op jit(solution)/shard_map/all_to_all | solution.py:77
  38.5 18.9 %all-to-all-start.1 = ((bf16[8,4,16,256]{3,2,1,0:T(8,128)(2,1)}), bf16[8,4,16,256]{3,2,1,0:T(8,128)(2,1)S(1)}, u32[]{:S(2)}, u32[]{:S(2)}) async-start(bf16[8,4,16,256]{3,2,1,0:T(8,128)(2,1)} %broadcast_in_dim.12), calls=%async_computation.1 | async-start | bytes 524288 | tf_op jit(solution)/shard_map/all_to_all | solution.py:79
  47.8 9.6 %copy-start.3 = (bf16[16,512]{1,0:T(8,128)(2,1)S(1)}, bf16[16,512]{1,0:T(8,128)(2,1)}, u32[]{:S(2)}) copy-start(bf16[16,512]{1,0:T(8,128)(2,1)} %param.11) | copy-start | bytes 49156
  61.0 24.0 %collective-permute-start.3 = (bf16[1024,256]{1,0:T(8,128)(2,1)S(1)}, bf16[1024,256]{1,0:T(8,128)(2,1)S(1)}, u32[]{:S(2)}, u32[]{:S(2)}) collective-permute-start(bf16[1024,256]{1,0:T(8,128)(2,1)S(1)} %fusion.55), channel_id=1, source_target_pairs={{0,4},{4,8},{8,12},{12,16},{16,20},{20,24},{24,28},{1,5},{5,9},{9,... | collective-permute-start | bytes 1572872 | tf_op jit(solution)/shard_map/ppermute | solution.py:29
  64.3 20.6 %collective-permute-start.2 = (bf16[1024,256]{1,0:T(8,128)(2,1)S(1)}, bf16[1024,256]{1,0:T(8,128)(2,1)S(1)}, u32[]{:S(2)}, u32[]{:S(2)}) collective-permute-start(bf16[1024,256]{1,0:T(8,128)(2,1)S(1)} %fusion.47), channel_id=1, source_target_pairs={{4,0},{8,4},{12,8},{16,12},{20,16},{24,20},{28,24},{5,1},{9,5},{13... | collective-permute-start | bytes 1572872 | tf_op jit(solution)/shard_map/ppermute | solution.py:29
  86.1 13.6 %collective-permute-start.5 = (bf16[1024,256]{1,0:T(8,128)(2,1)S(1)}, bf16[1024,256]{1,0:T(8,128)(2,1)S(1)}, u32[]{:S(2)}, u32[]{:S(2)}) collective-permute-start(bf16[1024,256]{1,0:T(8,128)(2,1)S(1)} %get-tuple-element.14), channel_id=1, source_target_pairs={{4,0},{8,4},{12,8},{16,12},{20,16},{24,20},{28,24},{5,1},{9,5},{13... | collective-permute-start | bytes 1572872 | tf_op jit(solution)/shard_map/ppermute | solution.py:29
  87.4 24.7 %collective-permute-start.4 = (bf16[1024,256]{1,0:T(8,128)(2,1)S(1)}, bf16[1024,256]{1,0:T(8,128)(2,1)S(1)}, u32[]{:S(2)}, u32[]{:S(2)}) collective-permute-start(bf16[1024,256]{1,0:T(8,128)(2,1)S(1)} %get-tuple-element.14), channel_id=1, source_target_pairs={{0,4},{4,8},{8,12},{12,16},{16,20},{20,24},{24,28},{1,5},{5,9},{9,... | collective-permute-start | bytes 1572872 | tf_op jit(solution)/shard_map/ppermute | solution.py:29
  113.5 7.2 %all-to-all-start.2 = ((bf16[4,16,256]{2,1,0:T(8,128)(2,1)}), bf16[4,16,256]{2,1,0:T(8,128)(2,1)S(1)}, u32[]{:S(2)}, u32[]{:S(2)}) async-start(bf16[4,16,256]{2,1,0:T(8,128)(2,1)} %broadcast_in_dim.13), calls=%async_computation.2 | async-start | bytes 65536 | tf_op jit(solution)/shard_map/all_to_all | solution.py:77
  121.4 18.7 %all-to-all-start.3 = ((bf16[8,4,16,256]{3,2,1,0:T(8,128)(2,1)}), bf16[8,4,16,256]{3,2,1,0:T(8,128)(2,1)S(1)}, u32[]{:S(2)}, u32[]{:S(2)}) async-start(bf16[8,4,16,256]{3,2,1,0:T(8,128)(2,1)} %broadcast_in_dim.14), calls=%async_computation.3 | async-start | bytes 524288 | tf_op jit(solution)/shard_map/all_to_all | solution.py:79
  143.8 24.5 %collective-permute-start.7 = (bf16[1024,256]{1,0:T(8,128)(2,1)S(1)}, bf16[1024,256]{1,0:T(8,128)(2,1)S(1)}, u32[]{:S(2)}, u32[]{:S(2)}) collective-permute-start(bf16[1024,256]{1,0:T(8,128)(2,1)S(1)} %fusion.58), channel_id=1, source_target_pairs={{0,4},{4,8},{8,12},{12,16},{16,20},{20,24},{24,28},{1,5},{5,9},{9,... | collective-permute-start | bytes 1572872 | tf_op jit(solution)/shard_map/ppermute | solution.py:29
  147.1 21.2 %collective-permute-start.6 = (bf16[1024,256]{1,0:T(8,128)(2,1)S(1)}, bf16[1024,256]{1,0:T(8,128)(2,1)S(1)}, u32[]{:S(2)}, u32[]{:S(2)}) collective-permute-start(bf16[1024,256]{1,0:T(8,128)(2,1)S(1)} %fusion.48), channel_id=1, source_target_pairs={{4,0},{8,4},{12,8},{16,12},{20,16},{24,20},{28,24},{5,1},{9,5},{13... | collective-permute-start | bytes 1572872 | tf_op jit(solution)/shard_map/ppermute | solution.py:29

commit v16 on v14

--- a/solution.py
+++ b/solution.py
@@ -88,7 +88,8 @@
         )
         weighted = (scale_column * solved).astype(jnp.bfloat16)
         to_previous = select(places[0], weighted).astype(jnp.bfloat16)
-        to_next = select(places[2], weighted).astype(jnp.bfloat16)
+        weighted_next, to_previous = lax.optimization_barrier((weighted, to_previous))
+        to_next = select(places[2], weighted_next).astype(jnp.bfloat16)
         from_next = shifted(to_previous, "sub", -1)
         from_previous = shifted(to_next, "sub", 1)
         kept = lax.optimization_barrier(select(places[1], weighted).astype(jnp.bfloat16))

time: 157 us -> 158 us (level)
    ppermute x8, starting transfers between devices: 25 us -> 21.6 us  [shifted(): return lax.ppermute(shard, axis, pairs)]
    all_to_all x2, starting transfers between devices: 13.7 us -> 16.2 us  [precondition(): lax.all_to_all(primal_copies, AXES, 0, 0, tiled=False)]
  transfers between devices with their start and end apart: 10 -> 10, of which waited for: 10 -> 8; matrix products, arithmetic and copies ran while one was open for 21% -> 21% of each run, Pallas kernels for 0% -> 0%
where the time goes in v16:
time: 158 us; the launch traced here: 157 us
  waiting for transfers between devices  71.6 us (45%)
  starting transfers between devices  37.8 us (24%)
  matrix products  37.4 us (24%)
  other arithmetic  4.64 us (3%)
  local copies, waits for them, and re-layouts  4.46 us (3%)
    ppermute x8, waiting for transfers between devices, shifted(): return lax.ppermute(shard, axis, pairs)  67.6 us
    dot_general x12, matrix products, select(): return jnp.dot(matrix, rows, preferred_element_type=jnp.float32)  24.1 us
    ppermute x8, starting transfers between devices, shifted(): return lax.ppermute(shard, axis, pairs)  21.6 us
    all_to_all x2, starting transfers between devices, precondition(): lax.all_to_all(primal_copies, AXES, 0, 0, tiled=False)  16.2 us
    dot_general x2, matrix products, precondition(): solved = jnp.dot(schur_inv, scaled, preferred_element_type=jnp.float32)  11.8 us
    all_to_all x2, waiting for transfers between devices, precondition(): lax.all_to_all(primal_copies, AXES, 0, 0, tiled=False)  4.05 us
  transfers between devices with their start and end apart: 10, of which 8 were waited for; matrix products, arithmetic and copies ran while one was open for 21% of the time, Pallas kernels for 0%

profile of v16, /device:TPU:0, one launch (start us, length us, event | category | flops | bytes accessed | tf_op | source)
XLA Modules:
  0.0 156.8 jit_solution(13215568554687477273)
XLA Ops:
  0.6 1.3 convert_element_type.96
  2.0 1.3 collective-permute-start.1
  3.3 5.5 %collective-permute-start = (bf16[1024,256]{1,0:T(8,128)(2,1)S(1)}, bf16[1024,256]{1,0:T(8,128)(2,1)S(1)}, u32[]{:S(2)}, u32[]{:S(2)}) collective-permute-start(bf16[1024,256]{1,0:T(8,128)(2,1)S(1)} %convert_element_type.96), channel_id=1, source_target_pairs={{0,4},{4,8},{8,12},{12,16},{16,20},{20,24},{24,28},{1,5},{5,9},{9,... | collective-permute-start | bytes 1572872 | tf_op jit(solution)/shard_map/ppermute | solution.py:29
  9.4 3.3 %fusion.10 = f32[2048,256]{1,0:T(8,128)} fusion(bf16[1024,256]{1,0:T(8,128)(2,1)S(1)} %convert_element_type.96, s32[1024]{0:T(1024)S(1)} %iota_add_fusion.1, s32[2048]{0:T(1024)} %param.12), kind=kOutput, calls=%fused_computation.14 | convolution fusion | flops 1075838976 | bytes 2633728 | tf_op jit(solution)/shard_map/dot_general | solution.py:65
  14.1 4.6 %collective-permute-done.1 = bf16[1024,256]{1,0:T(8,128)(2,1)S(1)} collective-permute-done((bf16[1024,256]{1,0:T(8,128)(2,1)S(1)}, bf16[1024,256]{1,0:T(8,128)(2,1)S(1)}, u32[]{:S(2)}, u32[]{:S(2)}) %collective-permute-start.1) | collective-permute-done | bytes 524320 | tf_op jit(solution)/shard_map/ppermute | solution.py:29
  18.7 2.6 %fusion.6 = f32[2048,256]{1,0:T(8,128)} fusion(bf16[1024,256]{1,0:T(8,128)(2,1)S(1)} %collective-permute-done.1, s32[1024]{0:T(1024)S(1)} %iota_add_fusion, s32[2048]{0:T(1024)S(1)} %copy-done.2), kind=kOutput, calls=%fused_computation.10 | convolution fusion | flops 1075838976 | bytes 2633728 | tf_op jit(solution)/shard_map/dot_general | solution.py:65
  21.3 8.8 %collective-permute-done = bf16[1024,256]{1,0:T(8,128)(2,1)S(1)} collective-permute-done((bf16[1024,256]{1,0:T(8,128)(2,1)S(1)}, bf16[1024,256]{1,0:T(8,128)(2,1)S(1)}, u32[]{:S(2)}, u32[]{:S(2)}) %collective-permute-start) | collective-permute-done | bytes 524320 | tf_op jit(solution)/shard_map/ppermute | solution.py:29
  31.6 7.6 %all-to-all-start = ((bf16[32,16,256]{2,1,0:T(8,128)(2,1)}), bf16[32,16,256]{2,1,0:T(8,128)(2,1)S(1)}, u32[]{:S(2)}, u32[]{:S(2)}) async-start(bf16[32,16,256]{2,1,0:T(8,128)(2,1)} %broadcast_in_dim.7), calls=%async_computation | async-start | bytes 524288 | tf_op jit(solution)/shard_map/all_to_all | solution.py:77
  39.2 3.1 %fusion.44 = f32[2048,256]{1,0:T(8,128)S(1)} fusion(f32[2048,256]{1,0:T(8,128)} %fusion.10, bf16[1024,256]{1,0:T(8,128)(2,1)S(1)} %collective-permute-done, s32[2048]{0:T(1024)S(1)} %copy-done.2), kind=kOutput, calls=%fused_computation.54 | convolution fusion | flops 1076363264 | bytes 4726784 | tf_op jit(solution)/shard_map/dot_general | solution.py:65
  42.3 5.9 %convolution_bitcast_fusion.1 = f32[2048,256]{1,0:T(8,128)S(1)} fusion(bf16[2048,2048]{1,0:T(8,128)(2,1)} %param.8, f32[2048,256]{1,0:T(8,128)S(1)} %fusion.44, f32[2048,256]{1,0:T(8,128)S(1)} %copy-done.6, f32[2048]{0:T(1024)S(1)} %copy-done.1), kind=kOutput, calls=%fused_computation.47 | convolution fusion | flops 2149056512 | bytes 14688256 | tf_op jit(solution)/shard_map/dot_general | solution.py:82
  48.2 1.6 %all-to-all-done = bf16[32,16,256]{2,1,0:T(8,128)(2,1)S(1)} async-done(((bf16[32,16,256]{2,1,0:T(8,128)(2,1)}), bf16[32,16,256]{2,1,0:T(8,128)(2,1)S(1)}, u32[]{:S(2)}, u32[]{:S(2)}) %all-to-all-start) | async-done | bytes 262176 | tf_op jit(solution)/shard_map/all_to_all | solution.py:77
  50.6 1.5 fusion.47
  52.0 1.3 fusion.55
  53.4 2.8 %collective-permute-start.3 = (bf16[1024,256]{1,0:T(8,128)(2,1)S(1)}, bf16[1024,256]{1,0:T(8,128)(2,1)S(1)}, u32[]{:S(2)}, u32[]{:S(2)}) collective-permute-start(bf16[1024,256]{1,0:T(8,128)(2,1)S(1)} %fusion.55), channel_id=1, source_target_pairs={{0,4},{4,8},{8,12},{12,16},{16,20},{20,24},{24,28},{1,5},{5,9},{9,... | collective-permute-start | bytes 1572872 | tf_op jit(solution)/shard_map/ppermute | solution.py:29
  56.2 1.3 collective-permute-start.2
  57.5 1.3 fusion.49
  58.9 19.4 %collective-permute-done.3 = bf16[1024,256]{1,0:T(8,128)(2,1)S(1)} collective-permute-done((bf16[1024,256]{1,0:T(8,128)(2,1)S(1)}, bf16[1024,256]{1,0:T(8,128)(2,1)S(1)}, u32[]{:S(2)}, u32[]{:S(2)}) %collective-permute-start.3) | collective-permute-done | bytes 524320 | tf_op jit(solution)/shard_map/ppermute | solution.py:29
  80.7 5.2 %collective-permute-start.4 = (bf16[1024,256]{1,0:T(8,128)(2,1)S(1)}, bf16[1024,256]{1,0:T(8,128)(2,1)S(1)}, u32[]{:S(2)}, u32[]{:S(2)}) collective-permute-start(bf16[1024,256]{1,0:T(8,128)(2,1)S(1)} %get-tuple-element.22), channel_id=1, source_target_pairs={{0,4},{4,8},{8,12},{12,16},{16,20},{20,24},{24,28},{1,5},{5,9},{9,... | collective-permute-start | bytes 1572872 | tf_op jit(solution)/shard_map/ppermute | solution.py:29
  85.9 2.6 %fusion.8 = f32[2048,256]{1,0:T(8,128)} fusion(bf16[1024,256]{1,0:T(8,128)(2,1)S(1)} %get-tuple-element.22, s32[1024]{0:T(1024)S(1)} %iota_add_fusion.1, s32[2048]{0:T(1024)S(1)} %copy-done.2), kind=kOutput, calls=%fused_computation.12 | convolution fusion | flops 1075838976 | bytes 2633728 | tf_op jit(solution)/shard_map/dot_general | solution.py:65
  88.5 5.9 %collective-permute-done.5 = bf16[1024,256]{1,0:T(8,128)(2,1)S(1)} collective-permute-done((bf16[1024,256]{1,0:T(8,128)(2,1)S(1)}, bf16[1024,256]{1,0:T(8,128)(2,1)S(1)}, u32[]{:S(2)}, u32[]{:S(2)}) %collective-permute-start.5) | collective-permute-done | bytes 524320 | tf_op jit(solution)/shard_map/ppermute | solution.py:29
  94.4 2.6 %fusion.4 = f32[2048,256]{1,0:T(8,128)} fusion(bf16[1024,256]{1,0:T(8,128)(2,1)S(1)} %collective-permute-done.5, s32[1024]{0:T(1024)S(1)} %iota_add_fusion, s32[2048]{0:T(1024)S(1)} %copy-done.2), kind=kOutput, calls=%fused_computation.8 | convolution fusion | flops 1075838976 | bytes 2633728 | tf_op jit(solution)/shard_map/dot_general | solution.py:65
  96.9 9.9 %collective-permute-done.4 = bf16[1024,256]{1,0:T(8,128)(2,1)S(1)} collective-permute-done((bf16[1024,256]{1,0:T(8,128)(2,1)S(1)}, bf16[1024,256]{1,0:T(8,128)(2,1)S(1)}, u32[]{:S(2)}, u32[]{:S(2)}) %collective-permute-start.4) | collective-permute-done | bytes 524320 | tf_op jit(solution)/shard_map/ppermute | solution.py:29
  108.3 8.6 %all-to-all-start.1 = ((bf16[32,16,256]{2,1,0:T(8,128)(2,1)}), bf16[32,16,256]{2,1,0:T(8,128)(2,1)S(1)}, u32[]{:S(2)}, u32[]{:S(2)}) async-start(bf16[32,16,256]{2,1,0:T(8,128)(2,1)} %broadcast_in_dim.8), calls=%async_computation.1 | async-start | bytes 524288 | tf_op jit(solution)/shard_map/all_to_all | solution.py:77
  116.9 1.7 %fusion.18 = f32[2048,256]{1,0:T(8,128)S(1)} fusion(bf16[1024,256]{1,0:T(8,128)(2,1)S(1)} %collective-permute-done.4, s32[2048]{0:T(1024)S(1)} %copy-done.2), kind=kOutput, calls=%fused_computation.24 | convolution fusion | flops 1075838976 | bytes 2629632 | tf_op jit(solution)/shard_map/dot_general | solution.py:65
  119.2 5.9 %convolution_bitcast_fusion = f32[2048,256]{1,0:T(8,128)S(1)} fusion(bf16[2048,2048]{1,0:T(8,128)(2,1)} %param.8, f32[2048,256]{1,0:T(8,128)S(1)} %copy-done.5, f32[2048,256]{1,0:T(8,128)S(1)} %copy-done.4, f32[2048,256]{1,0:T(8,128)S(1)} %fusion.18, f32[2048]{0:T(1024)S(1)} %copy-done.1), kind=kOutput, calls=%fused_computation.46 | convolution fusion | flops 2149580800 | bytes 16785408 | tf_op jit(solution)/shard_map/dot_general | solution.py:82
  125.1 2.5 %all-to-all-done.1 = bf16[32,16,256]{2,1,0:T(8,128)(2,1)S(1)} async-done(((bf16[32,16,256]{2,1,0:T(8,128)(2,1)}), bf16[32,16,256]{2,1,0:T(8,128)(2,1)S(1)}, u32[]{:S(2)}, u32[]{:S(2)}) %all-to-all-start.1) | async-done | bytes 262176 | tf_op jit(solution)/shard_map/all_to_all | solution.py:77
  128.3 1.5 fusion.48
  129.8 1.3 fusion.58
  131.1 2.8 %collective-permute-start.7 = (bf16[1024,256]{1,0:T(8,128)(2,1)S(1)}, bf16[1024,256]{1,0:T(8,128)(2,1)S(1)}, u32[]{:S(2)}, u32[]{:S(2)}) collective-permute-start(bf16[1024,256]{1,0:T(8,128)(2,1)S(1)} %fusion.58), channel_id=1, source_target_pairs={{0,4},{4,8},{8,12},{12,16},{16,20},{20,24},{24,28},{1,5},{5,9},{9,... | collective-permute-start | bytes 1572872 | tf_op jit(solution)/shard_map/ppermute | solution.py:29
  134.0 1.3 collective-permute-start.6
  135.3 1.3 fusion.52
  136.6 19.1 %collective-permute-done.7 = bf16[1024,256]{1,0:T(8,128)(2,1)S(1)} collective-permute-done((bf16[1024,256]{1,0:T(8,128)(2,1)S(1)}, bf16[1024,256]{1,0:T(8,128)(2,1)S(1)}, u32[]{:S(2)}, u32[]{:S(2)}) %collective-permute-start.7) | collective-permute-done | bytes 524320 | tf_op jit(solution)/shard_map/ppermute | solution.py:29
  (37 shorter events, 10.6 us)
Async XLA Ops:
  0.6 49.2 %copy-start = (bf16[16,2048]{1,0:T(8,128)(2,1)S(1)}, bf16[16,2048]{1,0:T(8,128)(2,1)}, u32[]{:S(2)}) copy-start(bf16[16,2048]{1,0:T(8,128)(2,1)} %param.9) | copy-start | bytes 196612
  2.0 16.8 %collective-permute-start.1 = (bf16[1024,256]{1,0:T(8,128)(2,1)S(1)}, bf16[1024,256]{1,0:T(8,128)(2,1)S(1)}, u32[]{:S(2)}, u32[]{:S(2)}) collective-permute-start(bf16[1024,256]{1,0:T(8,128)(2,1)S(1)} %convert_element_type.96), channel_id=1, source_target_pairs={{4,0},{8,4},{12,8},{16,12},{20,16},{24,20},{28,24},{5,1},{9,5},{13... | collective-permute-start | bytes 1572872 | tf_op jit(solution)/shard_map/ppermute | solution.py:29
  3.3 26.8 %collective-permute-start = (bf16[1024,256]{1,0:T(8,128)(2,1)S(1)}, bf16[1024,256]{1,0:T(8,128)(2,1)S(1)}, u32[]{:S(2)}, u32[]{:S(2)}) collective-permute-start(bf16[1024,256]{1,0:T(8,128)(2,1)S(1)} %convert_element_type.96), channel_id=1, source_target_pairs={{0,4},{4,8},{8,12},{12,16},{16,20},{20,24},{24,28},{1,5},{5,9},{9,... | collective-permute-start | bytes 1572872 | tf_op jit(solution)/shard_map/ppermute | solution.py:29
  9.4 3.3 %copy-start.2 = (s32[2048]{0:T(1024)S(1)}, s32[2048]{0:T(1024)}, u32[]{:S(2)}) copy-start(s32[2048]{0:T(1024)} %param.12) | copy-start | bytes 24580
  9.4 4.0 %copy-start.1 = (f32[2048]{0:T(1024)S(1)}, f32[2048]{0:T(1024)}, u32[]{:S(2)}) copy-start(f32[2048]{0:T(1024)} %param.10) | copy-start | bytes 24580
  31.6 18.2 %all-to-all-start = ((bf16[32,16,256]{2,1,0:T(8,128)(2,1)}), bf16[32,16,256]{2,1,0:T(8,128)(2,1)S(1)}, u32[]{:S(2)}, u32[]{:S(2)}) async-start(bf16[32,16,256]{2,1,0:T(8,128)(2,1)} %broadcast_in_dim.7), calls=%async_computation | async-start | bytes 524288 | tf_op jit(solution)/shard_map/all_to_all | solution.py:77
  39.2 3.1 %copy-start.6 = (f32[2048,256]{1,0:T(8,128)S(1)}, f32[2048,256]{1,0:T(8,128)}, u32[]{:S(2)}) copy-start(f32[2048,256]{1,0:T(8,128)} %fusion.6) | copy-start | bytes 6291460
  42.3 7.5 %copy-start.3 = (bf16[16,512]{1,0:T(8,128)(2,1)S(1)}, bf16[16,512]{1,0:T(8,128)(2,1)}, u32[]{:S(2)}) copy-start(bf16[16,512]{1,0:T(8,128)(2,1)} %param.11) | copy-start | bytes 49156
  53.4 24.8 %collective-permute-start.3 = (bf16[1024,256]{1,0:T(8,128)(2,1)S(1)}, bf16[1024,256]{1,0:T(8,128)(2,1)S(1)}, u32[]{:S(2)}, u32[]{:S(2)}) collective-permute-start(bf16[1024,256]{1,0:T(8,128)(2,1)S(1)} %fusion.55), channel_id=1, source_target_pairs={{0,4},{4,8},{8,12},{12,16},{16,20},{20,24},{24,28},{1,5},{5,9},{9,... | collective-permute-start | bytes 1572872 | tf_op jit(solution)/shard_map/ppermute | solution.py:29
  56.2 22.0 %collective-permute-start.2 = (bf16[1024,256]{1,0:T(8,128)(2,1)S(1)}, bf16[1024,256]{1,0:T(8,128)(2,1)S(1)}, u32[]{:S(2)}, u32[]{:S(2)}) collective-permute-start(bf16[1024,256]{1,0:T(8,128)(2,1)S(1)} %fusion.47), channel_id=1, source_target_pairs={{4,0},{8,4},{12,8},{16,12},{20,16},{24,20},{28,24},{5,1},{9,5},{13... | collective-permute-start | bytes 1572872 | tf_op jit(solution)/shard_map/ppermute | solution.py:29
  79.4 15.0 %collective-permute-start.5 = (bf16[1024,256]{1,0:T(8,128)(2,1)S(1)}, bf16[1024,256]{1,0:T(8,128)(2,1)S(1)}, u32[]{:S(2)}, u32[]{:S(2)}) collective-permute-start(bf16[1024,256]{1,0:T(8,128)(2,1)S(1)} %get-tuple-element.22), channel_id=1, source_target_pairs={{4,0},{8,4},{12,8},{16,12},{20,16},{24,20},{28,24},{5,1},{9,5},{13... | collective-permute-start | bytes 1572872 | tf_op jit(solution)/shard_map/ppermute | solution.py:29
  80.7 26.1 %collective-permute-start.4 = (bf16[1024,256]{1,0:T(8,128)(2,1)S(1)}, bf16[1024,256]{1,0:T(8,128)(2,1)S(1)}, u32[]{:S(2)}, u32[]{:S(2)}) collective-permute-start(bf16[1024,256]{1,0:T(8,128)(2,1)S(1)} %get-tuple-element.22), channel_id=1, source_target_pairs={{0,4},{4,8},{8,12},{12,16},{16,20},{20,24},{24,28},{1,5},{5,9},{9,... | collective-permute-start | bytes 1572872 | tf_op jit(solution)/shard_map/ppermute | solution.py:29
  108.3 19.2 %all-to-all-start.1 = ((bf16[32,16,256]{2,1,0:T(8,128)(2,1)}), bf16[32,16,256]{2,1,0:T(8,128)(2,1)S(1)}, u32[]{:S(2)}, u32[]{:S(2)}) async-start(bf16[32,16,256]{2,1,0:T(8,128)(2,1)} %broadcast_in_dim.8), calls=%async_computation.1 | async-start | bytes 524288 | tf_op jit(solution)/shard_map/all_to_all | solution.py:77
  116.9 1.7 %copy-start.4 = (f32[2048,256]{1,0:T(8,128)S(1)}, f32[2048,256]{1,0:T(8,128)}, u32[]{:S(2)}) copy-start(f32[2048,256]{1,0:T(8,128)} %fusion.8) | copy-start | bytes 6291460
  116.9 2.2 %copy-start.5 = (f32[2048,256]{1,0:T(8,128)S(1)}, f32[2048,256]{1,0:T(8,128)}, u32[]{:S(2)}) copy-start(f32[2048,256]{1,0:T(8,128)} %fusion.4) | copy-start | bytes 6291460
  131.1 24.6 %collective-permute-start.7 = (bf16[1024,256]{1,0:T(8,128)(2,1)S(1)}, bf16[1024,256]{1,0:T(8,128)(2,1)S(1)}, u32[]{:S(2)}, u32[]{:S(2)}) collective-permute-start(bf16[1024,256]{1,0:T(8,128)(2,1)S(1)} %fusion.58), channel_id=1, source_target_pairs={{0,4},{4,8},{8,12},{12,16},{16,20},{20,24},{24,28},{1,5},{5,9},{9,... | collective-permute-start | bytes 1572872 | tf_op jit(solution)/shard_map/ppermute | solution.py:29
  134.0 21.7 %collective-permute-start.6 = (bf16[1024,256]{1,0:T(8,128)(2,1)S(1)}, bf16[1024,256]{1,0:T(8,128)(2,1)S(1)}, u32[]{:S(2)}, u32[]{:S(2)}) collective-permute-start(bf16[1024,256]{1,0:T(8,128)(2,1)S(1)} %fusion.48), channel_id=1, source_target_pairs={{4,0},{8,4},{12,8},{16,12},{20,16},{24,20},{28,24},{5,1},{9,5},{13... | collective-permute-start | bytes 1572872 | tf_op jit(solution)/shard_map/ppermute | solution.py:29

commit v17 on v14

--- a/solution.py
+++ b/solution.py
@@ -92,11 +92,8 @@
         from_next = shifted(to_previous, "sub", -1)
         from_previous = shifted(to_next, "sub", 1)
         kept = lax.optimization_barrier(select(places[1], weighted).astype(jnp.bfloat16))
-        return (
-            kept.astype(jnp.float32)
-            + from_next.astype(jnp.float32)
-            + from_previous.astype(jnp.float32)
-        )
+        partial = lax.optimization_barrier(kept.astype(jnp.float32) + from_next.astype(jnp.float32))
+        return partial + from_previous.astype(jnp.float32)
 
     first_apply = precondition(resid)
     second_apply = precondition(first_apply)

time: 157 us -> 154 us (0.981)
  waiting for transfers between devices: 70.4 us -> 67.5 us
    ppermute x8, waiting for transfers between devices: 66.3 us -> 63.5 us  [shifted(): return lax.ppermute(shard, axis, pairs)]
  transfers between devices with their start and end apart: 10 -> 10, of which waited for: 10 -> 10; matrix products, arithmetic and copies ran while one was open for 21% -> 23% of each run, Pallas kernels for 0% -> 0%
where the time goes in v17:
time: 154 us
  waiting for transfers between devices  67.5 us (44%)
  starting transfers between devices  38.7 us (25%)
  matrix products  37.4 us (24%)
  other arithmetic  4.83 us (3%)
  local copies, waits for them, and re-layouts  4.46 us (3%)
    ppermute x8, waiting for transfers between devices, shifted(): return lax.ppermute(shard, axis, pairs)  63.5 us
    ppermute x8, starting transfers between devices, shifted(): return lax.ppermute(shard, axis, pairs)  25 us
    dot_general x12, matrix products, select(): return jnp.dot(matrix, rows, preferred_element_type=jnp.float32)  24.1 us
    all_to_all x2, starting transfers between devices, precondition(): lax.all_to_all(primal_copies, AXES, 0, 0, tiled=False)  13.7 us
    dot_general x2, matrix products, precondition(): solved = jnp.dot(schur_inv, scaled, preferred_element_type=jnp.float32)  11.8 us
    all_to_all x2, waiting for transfers between devices, precondition(): lax.all_to_all(primal_copies, AXES, 0, 0, tiled=False)  4.05 us
  transfers between devices with their start and end apart: 10, of which 10 were waited for; matrix products, arithmetic and copies ran while one was open for 23% of the time, Pallas kernels for 0%

profile of v17, /device:TPU:0, one launch (start us, length us, event | category | flops | bytes accessed | tf_op | source)
XLA Modules:
  0.0 153.8 jit_solution(12002997886600977127)
XLA Ops:
  0.6 1.3 convert_element_type.96
  2.0 1.3 collective-permute-start.1
  3.3 5.5 %collective-permute-start = (bf16[1024,256]{1,0:T(8,128)(2,1)S(1)}, bf16[1024,256]{1,0:T(8,128)(2,1)S(1)}, u32[]{:S(2)}, u32[]{:S(2)}) collective-permute-start(bf16[1024,256]{1,0:T(8,128)(2,1)S(1)} %convert_element_type.96), channel_id=1, source_target_pairs={{0,4},{4,8},{8,12},{12,16},{16,20},{20,24},{24,28},{1,5},{5,9},{9,... | collective-permute-start | bytes 1572872 | tf_op jit(solution)/shard_map/ppermute | solution.py:29
  9.4 3.3 %fusion.10 = f32[2048,256]{1,0:T(8,128)} fusion(bf16[1024,256]{1,0:T(8,128)(2,1)S(1)} %convert_element_type.96, s32[1024]{0:T(1024)S(1)} %iota_add_fusion.1, s32[2048]{0:T(1024)} %param.12), kind=kOutput, calls=%fused_computation.14 | convolution fusion | flops 1075838976 | bytes 2633728 | tf_op jit(solution)/shard_map/dot_general | solution.py:65
  14.1 4.6 %collective-permute-done.1 = bf16[1024,256]{1,0:T(8,128)(2,1)S(1)} collective-permute-done((bf16[1024,256]{1,0:T(8,128)(2,1)S(1)}, bf16[1024,256]{1,0:T(8,128)(2,1)S(1)}, u32[]{:S(2)}, u32[]{:S(2)}) %collective-permute-start.1) | collective-permute-done | bytes 524320 | tf_op jit(solution)/shard_map/ppermute | solution.py:29
  18.7 2.6 %fusion.6 = f32[2048,256]{1,0:T(8,128)} fusion(bf16[1024,256]{1,0:T(8,128)(2,1)S(1)} %collective-permute-done.1, s32[1024]{0:T(1024)S(1)} %iota_add_fusion, s32[2048]{0:T(1024)S(1)} %copy-done.2), kind=kOutput, calls=%fused_computation.10 | convolution fusion | flops 1075838976 | bytes 2633728 | tf_op jit(solution)/shard_map/dot_general | solution.py:65
  21.3 8.8 %collective-permute-done = bf16[1024,256]{1,0:T(8,128)(2,1)S(1)} collective-permute-done((bf16[1024,256]{1,0:T(8,128)(2,1)S(1)}, bf16[1024,256]{1,0:T(8,128)(2,1)S(1)}, u32[]{:S(2)}, u32[]{:S(2)}) %collective-permute-start) | collective-permute-done | bytes 524320 | tf_op jit(solution)/shard_map/ppermute | solution.py:29
  31.6 7.6 %all-to-all-start = ((bf16[32,16,256]{2,1,0:T(8,128)(2,1)}), bf16[32,16,256]{2,1,0:T(8,128)(2,1)S(1)}, u32[]{:S(2)}, u32[]{:S(2)}) async-start(bf16[32,16,256]{2,1,0:T(8,128)(2,1)} %broadcast_in_dim.7), calls=%async_computation | async-start | bytes 524288 | tf_op jit(solution)/shard_map/all_to_all | solution.py:77
  39.2 3.1 %fusion.44 = f32[2048,256]{1,0:T(8,128)S(1)} fusion(f32[2048,256]{1,0:T(8,128)} %fusion.10, bf16[1024,256]{1,0:T(8,128)(2,1)S(1)} %collective-permute-done, s32[2048]{0:T(1024)S(1)} %copy-done.2), kind=kOutput, calls=%fused_computation.54 | convolution fusion | flops 1076363264 | bytes 4726784 | tf_op jit(solution)/shard_map/dot_general | solution.py:65
  42.3 5.9 %convolution_bitcast_fusion.1 = f32[2048,256]{1,0:T(8,128)S(1)} fusion(bf16[2048,2048]{1,0:T(8,128)(2,1)} %param.8, f32[2048,256]{1,0:T(8,128)S(1)} %fusion.44, f32[2048,256]{1,0:T(8,128)S(1)} %copy-done.6, f32[2048]{0:T(1024)S(1)} %copy-done.1), kind=kOutput, calls=%fused_computation.47 | convolution fusion | flops 2149056512 | bytes 14688256 | tf_op jit(solution)/shard_map/dot_general | solution.py:82
  48.2 1.6 %all-to-all-done = bf16[32,16,256]{2,1,0:T(8,128)(2,1)S(1)} async-done(((bf16[32,16,256]{2,1,0:T(8,128)(2,1)}), bf16[32,16,256]{2,1,0:T(8,128)(2,1)S(1)}, u32[]{:S(2)}, u32[]{:S(2)}) %all-to-all-start) | async-done | bytes 262176 | tf_op jit(solution)/shard_map/all_to_all | solution.py:77
  50.6 1.5 fusion.47
  53.3 1.3 fusion.55
  54.7 4.6 %collective-permute-start.3 = (bf16[1024,256]{1,0:T(8,128)(2,1)S(1)}, bf16[1024,256]{1,0:T(8,128)(2,1)S(1)}, u32[]{:S(2)}, u32[]{:S(2)}) collective-permute-start(bf16[1024,256]{1,0:T(8,128)(2,1)S(1)} %fusion.55), channel_id=1, source_target_pairs={{0,4},{4,8},{8,12},{12,16},{16,20},{20,24},{24,28},{1,5},{5,9},{9,... | collective-permute-start | bytes 1572872 | tf_op jit(solution)/shard_map/ppermute | solution.py:29
  59.3 1.3 fusion.49
  60.6 7.1 %collective-permute-done.2 = bf16[1024,256]{1,0:T(8,128)(2,1)S(1)} collective-permute-done((bf16[1024,256]{1,0:T(8,128)(2,1)S(1)}, bf16[1024,256]{1,0:T(8,128)(2,1)S(1)}, u32[]{:S(2)}, u32[]{:S(2)}) %collective-permute-start.2) | collective-permute-done | bytes 524320 | tf_op jit(solution)/shard_map/ppermute | solution.py:29
  67.8 10.0 %collective-permute-done.3 = bf16[1024,256]{1,0:T(8,128)(2,1)S(1)} collective-permute-done((bf16[1024,256]{1,0:T(8,128)(2,1)S(1)}, bf16[1024,256]{1,0:T(8,128)(2,1)S(1)}, u32[]{:S(2)}, u32[]{:S(2)}) %collective-permute-start.3) | collective-permute-done | bytes 524320 | tf_op jit(solution)/shard_map/ppermute | solution.py:29
  80.2 5.2 %collective-permute-start.4 = (bf16[1024,256]{1,0:T(8,128)(2,1)S(1)}, bf16[1024,256]{1,0:T(8,128)(2,1)S(1)}, u32[]{:S(2)}, u32[]{:S(2)}) collective-permute-start(bf16[1024,256]{1,0:T(8,128)(2,1)S(1)} %get-tuple-element.14), channel_id=1, source_target_pairs={{0,4},{4,8},{8,12},{12,16},{16,20},{20,24},{24,28},{1,5},{5,9},{9,... | collective-permute-start | bytes 1572872 | tf_op jit(solution)/shard_map/ppermute | solution.py:29
  85.5 2.6 %fusion.8 = f32[2048,256]{1,0:T(8,128)} fusion(bf16[1024,256]{1,0:T(8,128)(2,1)S(1)} %get-tuple-element.14, s32[1024]{0:T(1024)S(1)} %iota_add_fusion.1, s32[2048]{0:T(1024)S(1)} %copy-done.2), kind=kOutput, calls=%fused_computation.12 | convolution fusion | flops 1075838976 | bytes 2633728 | tf_op jit(solution)/shard_map/dot_general | solution.py:65
  88.0 7.4 %collective-permute-done.5 = bf16[1024,256]{1,0:T(8,128)(2,1)S(1)} collective-permute-done((bf16[1024,256]{1,0:T(8,128)(2,1)S(1)}, bf16[1024,256]{1,0:T(8,128)(2,1)S(1)}, u32[]{:S(2)}, u32[]{:S(2)}) %collective-permute-start.5) | collective-permute-done | bytes 524320 | tf_op jit(solution)/shard_map/ppermute | solution.py:29
  95.4 2.6 %fusion.4 = f32[2048,256]{1,0:T(8,128)} fusion(bf16[1024,256]{1,0:T(8,128)(2,1)S(1)} %collective-permute-done.5, s32[1024]{0:T(1024)S(1)} %iota_add_fusion, s32[2048]{0:T(1024)S(1)} %copy-done.2), kind=kOutput, calls=%fused_computation.8 | convolution fusion | flops 1075838976 | bytes 2633728 | tf_op jit(solution)/shard_map/dot_general | solution.py:65
  98.0 8.8 %collective-permute-done.4 = bf16[1024,256]{1,0:T(8,128)(2,1)S(1)} collective-permute-done((bf16[1024,256]{1,0:T(8,128)(2,1)S(1)}, bf16[1024,256]{1,0:T(8,128)(2,1)S(1)}, u32[]{:S(2)}, u32[]{:S(2)}) %collective-permute-start.4) | collective-permute-done | bytes 524320 | tf_op jit(solution)/shard_map/ppermute | solution.py:29
  108.3 6.1 %all-to-all-start.1 = ((bf16[32,16,256]{2,1,0:T(8,128)(2,1)}), bf16[32,16,256]{2,1,0:T(8,128)(2,1)S(1)}, u32[]{:S(2)}, u32[]{:S(2)}) async-start(bf16[32,16,256]{2,1,0:T(8,128)(2,1)} %broadcast_in_dim.8), calls=%async_computation.1 | async-start | bytes 524288 | tf_op jit(solution)/shard_map/all_to_all | solution.py:77
  114.4 1.7 %fusion.18 = f32[2048,256]{1,0:T(8,128)S(1)} fusion(bf16[1024,256]{1,0:T(8,128)(2,1)S(1)} %collective-permute-done.4, s32[2048]{0:T(1024)S(1)} %copy-done.2), kind=kOutput, calls=%fused_computation.24 | convolution fusion | flops 1075838976 | bytes 2629632 | tf_op jit(solution)/shard_map/dot_general | solution.py:65
  116.6 5.9 %convolution_bitcast_fusion = f32[2048,256]{1,0:T(8,128)S(1)} fusion(bf16[2048,2048]{1,0:T(8,128)(2,1)} %param.8, f32[2048,256]{1,0:T(8,128)S(1)} %copy-done.5, f32[2048,256]{1,0:T(8,128)S(1)} %copy-done.4, f32[2048,256]{1,0:T(8,128)S(1)} %fusion.18, f32[2048]{0:T(1024)S(1)} %copy-done.1), kind=kOutput, calls=%fused_computation.46 | convolution fusion | flops 2149580800 | bytes 16785408 | tf_op jit(solution)/shard_map/dot_general | solution.py:82
  122.5 2.5 %all-to-all-done.1 = bf16[32,16,256]{2,1,0:T(8,128)(2,1)S(1)} async-done(((bf16[32,16,256]{2,1,0:T(8,128)(2,1)}), bf16[32,16,256]{2,1,0:T(8,128)(2,1)S(1)}, u32[]{:S(2)}, u32[]{:S(2)}) %all-to-all-start.1) | async-done | bytes 262176 | tf_op jit(solution)/shard_map/all_to_all | solution.py:77
  125.8 1.5 fusion.48
  128.5 1.3 fusion.58
  129.8 4.6 %collective-permute-start.7 = (bf16[1024,256]{1,0:T(8,128)(2,1)S(1)}, bf16[1024,256]{1,0:T(8,128)(2,1)S(1)}, u32[]{:S(2)}, u32[]{:S(2)}) collective-permute-start(bf16[1024,256]{1,0:T(8,128)(2,1)S(1)} %fusion.58), channel_id=1, source_target_pairs={{0,4},{4,8},{8,12},{12,16},{16,20},{20,24},{24,28},{1,5},{5,9},{9,... | collective-permute-start | bytes 1572872 | tf_op jit(solution)/shard_map/ppermute | solution.py:29
  134.4 1.3 fusion.52
  135.8 7.1 %collective-permute-done.6 = bf16[1024,256]{1,0:T(8,128)(2,1)S(1)} collective-permute-done((bf16[1024,256]{1,0:T(8,128)(2,1)S(1)}, bf16[1024,256]{1,0:T(8,128)(2,1)S(1)}, u32[]{:S(2)}, u32[]{:S(2)}) %collective-permute-start.6) | collective-permute-done | bytes 524320 | tf_op jit(solution)/shard_map/ppermute | solution.py:29
  143.0 9.7 %collective-permute-done.7 = bf16[1024,256]{1,0:T(8,128)(2,1)S(1)} collective-permute-done((bf16[1024,256]{1,0:T(8,128)(2,1)S(1)}, bf16[1024,256]{1,0:T(8,128)(2,1)S(1)}, u32[]{:S(2)}, u32[]{:S(2)}) %collective-permute-start.7) | collective-permute-done | bytes 524320 | tf_op jit(solution)/shard_map/ppermute | solution.py:29
  (39 shorter events, 13.4 us)
Async XLA Ops:
  0.6 49.2 %copy-start = (bf16[16,2048]{1,0:T(8,128)(2,1)S(1)}, bf16[16,2048]{1,0:T(8,128)(2,1)}, u32[]{:S(2)}) copy-start(bf16[16,2048]{1,0:T(8,128)(2,1)} %param.9) | copy-start | bytes 196612
  2.0 16.8 %collective-permute-start.1 = (bf16[1024,256]{1,0:T(8,128)(2,1)S(1)}, bf16[1024,256]{1,0:T(8,128)(2,1)S(1)}, u32[]{:S(2)}, u32[]{:S(2)}) collective-permute-start(bf16[1024,256]{1,0:T(8,128)(2,1)S(1)} %convert_element_type.96), channel_id=1, source_target_pairs={{4,0},{8,4},{12,8},{16,12},{20,16},{24,20},{28,24},{5,1},{9,5},{13... | collective-permute-start | bytes 1572872 | tf_op jit(solution)/shard_map/ppermute | solution.py:29
  3.3 26.8 %collective-permute-start = (bf16[1024,256]{1,0:T(8,128)(2,1)S(1)}, bf16[1024,256]{1,0:T(8,128)(2,1)S(1)}, u32[]{:S(2)}, u32[]{:S(2)}) collective-permute-start(bf16[1024,256]{1,0:T(8,128)(2,1)S(1)} %convert_element_type.96), channel_id=1, source_target_pairs={{0,4},{4,8},{8,12},{12,16},{16,20},{20,24},{24,28},{1,5},{5,9},{9,... | collective-permute-start | bytes 1572872 | tf_op jit(solution)/shard_map/ppermute | solution.py:29
  9.4 3.3 %copy-start.2 = (s32[2048]{0:T(1024)S(1)}, s32[2048]{0:T(1024)}, u32[]{:S(2)}) copy-start(s32[2048]{0:T(1024)} %param.12) | copy-start | bytes 24580
  9.4 4.0 %copy-start.1 = (f32[2048]{0:T(1024)S(1)}, f32[2048]{0:T(1024)}, u32[]{:S(2)}) copy-start(f32[2048]{0:T(1024)} %param.10) | copy-start | bytes 24580
  31.6 18.2 %all-to-all-start = ((bf16[32,16,256]{2,1,0:T(8,128)(2,1)}), bf16[32,16,256]{2,1,0:T(8,128)(2,1)S(1)}, u32[]{:S(2)}, u32[]{:S(2)}) async-start(bf16[32,16,256]{2,1,0:T(8,128)(2,1)} %broadcast_in_dim.7), calls=%async_computation | async-start | bytes 524288 | tf_op jit(solution)/shard_map/all_to_all | solution.py:77
  39.2 3.1 %copy-start.6 = (f32[2048,256]{1,0:T(8,128)S(1)}, f32[2048,256]{1,0:T(8,128)}, u32[]{:S(2)}) copy-start(f32[2048,256]{1,0:T(8,128)} %fusion.6) | copy-start | bytes 6291460
  42.3 7.5 %copy-start.3 = (bf16[16,512]{1,0:T(8,128)(2,1)S(1)}, bf16[16,512]{1,0:T(8,128)(2,1)}, u32[]{:S(2)}) copy-start(bf16[16,512]{1,0:T(8,128)(2,1)} %param.11) | copy-start | bytes 49156
  52.0 15.6 %collective-permute-start.2 = (bf16[1024,256]{1,0:T(8,128)(2,1)S(1)}, bf16[1024,256]{1,0:T(8,128)(2,1)S(1)}, u32[]{:S(2)}, u32[]{:S(2)}) collective-permute-start(bf16[1024,256]{1,0:T(8,128)(2,1)S(1)} %fusion.47), channel_id=1, source_target_pairs={{4,0},{8,4},{12,8},{16,12},{20,16},{24,20},{28,24},{5,1},{9,5},{13... | collective-permute-start | bytes 1572872 | tf_op jit(solution)/shard_map/ppermute | solution.py:29
  54.7 23.1 %collective-permute-start.3 = (bf16[1024,256]{1,0:T(8,128)(2,1)S(1)}, bf16[1024,256]{1,0:T(8,128)(2,1)S(1)}, u32[]{:S(2)}, u32[]{:S(2)}) collective-permute-start(bf16[1024,256]{1,0:T(8,128)(2,1)S(1)} %fusion.55), channel_id=1, source_target_pairs={{0,4},{4,8},{8,12},{12,16},{16,20},{20,24},{24,28},{1,5},{5,9},{9,... | collective-permute-start | bytes 1572872 | tf_op jit(solution)/shard_map/ppermute | solution.py:29
  78.9 16.5 %collective-permute-start.5 = (bf16[1024,256]{1,0:T(8,128)(2,1)S(1)}, bf16[1024,256]{1,0:T(8,128)(2,1)S(1)}, u32[]{:S(2)}, u32[]{:S(2)}) collective-permute-start(bf16[1024,256]{1,0:T(8,128)(2,1)S(1)} %get-tuple-element.14), channel_id=1, source_target_pairs={{4,0},{8,4},{12,8},{16,12},{20,16},{24,20},{28,24},{5,1},{9,5},{13... | collective-permute-start | bytes 1572872 | tf_op jit(solution)/shard_map/ppermute | solution.py:29
  80.2 26.6 %collective-permute-start.4 = (bf16[1024,256]{1,0:T(8,128)(2,1)S(1)}, bf16[1024,256]{1,0:T(8,128)(2,1)S(1)}, u32[]{:S(2)}, u32[]{:S(2)}) collective-permute-start(bf16[1024,256]{1,0:T(8,128)(2,1)S(1)} %get-tuple-element.14), channel_id=1, source_target_pairs={{0,4},{4,8},{8,12},{12,16},{16,20},{20,24},{24,28},{1,5},{5,9},{9,... | collective-permute-start | bytes 1572872 | tf_op jit(solution)/shard_map/ppermute | solution.py:29
  108.3 16.7 %all-to-all-start.1 = ((bf16[32,16,256]{2,1,0:T(8,128)(2,1)}), bf16[32,16,256]{2,1,0:T(8,128)(2,1)S(1)}, u32[]{:S(2)}, u32[]{:S(2)}) async-start(bf16[32,16,256]{2,1,0:T(8,128)(2,1)} %broadcast_in_dim.8), calls=%async_computation.1 | async-start | bytes 524288 | tf_op jit(solution)/shard_map/all_to_all | solution.py:77
  114.4 1.7 %copy-start.4 = (f32[2048,256]{1,0:T(8,128)S(1)}, f32[2048,256]{1,0:T(8,128)}, u32[]{:S(2)}) copy-start(f32[2048,256]{1,0:T(8,128)} %fusion.8) | copy-start | bytes 6291460
  114.4 2.2 %copy-start.5 = (f32[2048,256]{1,0:T(8,128)S(1)}, f32[2048,256]{1,0:T(8,128)}, u32[]{:S(2)}) copy-start(f32[2048,256]{1,0:T(8,128)} %fusion.4) | copy-start | bytes 6291460
  127.2 15.6 %collective-permute-start.6 = (bf16[1024,256]{1,0:T(8,128)(2,1)S(1)}, bf16[1024,256]{1,0:T(8,128)(2,1)S(1)}, u32[]{:S(2)}, u32[]{:S(2)}) collective-permute-start(bf16[1024,256]{1,0:T(8,128)(2,1)S(1)} %fusion.48), channel_id=1, source_target_pairs={{4,0},{8,4},{12,8},{16,12},{20,16},{24,20},{28,24},{5,1},{9,5},{13... | collective-permute-start | bytes 1572872 | tf_op jit(solution)/shard_map/ppermute | solution.py:29
  129.8 22.8 %collective-permute-start.7 = (bf16[1024,256]{1,0:T(8,128)(2,1)S(1)}, bf16[1024,256]{1,0:T(8,128)(2,1)S(1)}, u32[]{:S(2)}, u32[]{:S(2)}) collective-permute-start(bf16[1024,256]{1,0:T(8,128)(2,1)S(1)} %fusion.58), channel_id=1, source_target_pairs={{0,4},{4,8},{8,12},{12,16},{16,20},{20,24},{24,28},{1,5},{5,9},{9,... | collective-permute-start | bytes 1572872 | tf_op jit(solution)/shard_map/ppermute | solution.py:29
